TPU v7x, 256 devices: a whole 4x4x8 slice. The times are simulated.
256 devices in a mesh: ta: 4 (over z_lo), row: 16 (over y, z_hi, core), col: 4 (over x).
Axes of the slice: x: 4, y: 4, z: 8 (z_hi: 2, z_lo: 4; z = z_hi * 4 + z_lo), core: 2. Of those that a mesh axis runs over, the one named last changes fastest.
Arguments:
- features: bfloat16 [32, 96, 128, 256], P(None, None, 'row', ('ta', 'col')), may hold values from -6 to 6
- conv_weight: bfloat16 [3, 3, 96, 96], replicated, may hold values from -0.21875 to 0.21875
- time_weight: float32 [96, 5], replicated, may hold values from -2.5 to 2.5
- band_out: bfloat16 [96, 28], replicated, may hold values from -0.625 to 0.625
- band_input_weight: bfloat16 [28, 96], replicated, may hold values from -0.25 to 0.25
- measured: float32 [32, 128, 310], P(('ta', 'col'), 'row'), may hold values from -24 to 24
- aperture: int32 [32, 128, 256], P(('ta', 'col'), 'row'), may hold values 0 or 1
- dispersion: int32 [28], replicated, may hold values from 0 to 54, as said below
- update_cot: bfloat16 [32, 96, 128, 256], P(('ta', 'col'), None, 'row'), may hold values from -6 to 6
Outputs:
- updated: bfloat16 [32, 96, 128, 256], P(('ta', 'col'), None, 'row')
- features_grad: bfloat16 [32, 96, 128, 256], P(None, None, 'row', ('ta', 'col'))
Inputs may be any that keep to these rules, and one draw needn't show every extreme that they name: `dispersion`: some band has shift 0 and some band shift 54.
All inputs are finite; a program needn't handle non-finite values. No bound on the sum of `aperture` on one device may be relied on, other than what follows from the above.
Results may differ from a plain program's by a relative error of at most 0.0059.
Values may be sent and summed in bfloat16 or wider, within the bound.
No kernel may reach another device: no remote copies, remote signals or barrier semaphores. Data moves between devices by JAX's collectives and lax.ppermute only.
A program may use at most 128 MiB of HBM per device.

v0:
```python
import jax
import jax.numpy as jnp
from jax import lax
from jax.sharding import PartitionSpec as P


def with_halo(array, sides, width):
    for axis, dim in sides:
        devices, length = (lax.axis_size(axis), array.shape[dim])
        up = [(i, (i + 1) % devices) for i in range(devices - 1)]
        down = [(j, i) for i, j in up]
        last = lax.slice_in_dim(array, length - width, length, axis=dim)
        initial = lax.slice_in_dim(array, 0, width, axis=dim)
        before = lax.ppermute(last, axis, up)
        after = lax.ppermute(initial, axis, down)
        array = jnp.concatenate([before, array, after], axis=dim)
    return array


def spatial_conv(field_in, kernel):
    row_number = field_in.shape[2]
    col_count = field_in.shape[3]
    padded = with_halo(field_in, (("row", 2), (("ta", "col"), 3)), 1)
    summed = None
    for row_tap in range(3):
        for col_tap in range(3):
            window = padded[:, :, row_tap : row_tap + row_number, col_tap : col_tap + col_count]
            partial_sum = jnp.einsum(
                "io,fiqw->foqw",
                kernel[row_tap, col_tap],
                window,
                preferred_element_type=jnp.float32,
            )
            summed = partial_sum if summed is None else summed + partial_sum
    return summed


def to_time(field_in):
    return lax.all_to_all(field_in, ("ta", "col"), split_axis=0, concat_axis=3, tiled=True)


def to_space(field_in):
    return lax.all_to_all(field_in, ("ta", "col"), split_axis=3, concat_axis=0, tiled=True)


def framed(field_in):
    return with_halo(field_in, ((("ta", "col"), 0),), 2)


def time_mix(padded, time_taps):
    frame_count = padded.shape[0] - 4
    summed = jnp.zeros((frame_count,) + padded.shape[1:], jnp.float32)
    for tap_index in range(5):
        summed = summed + time_taps[None, :, tap_index, None, None] * padded[
            tap_index : tap_index + frame_count
        ].astype(jnp.float32)
    return summed


def gelu_exact(values_in):
    return jax.nn.gelu(values_in, approximate=False)


def shift_table(dispersion, width_keep, width_wide):
    source_col = lax.broadcasted_iota(jnp.int32, (1, width_keep, width_wide), 1)
    target_col = lax.broadcasted_iota(jnp.int32, (1, width_keep, width_wide), 2)
    return (target_col == source_col + dispersion[:, None, None]).astype(jnp.float32)


def disperse(masked, table):
    return jnp.einsum(
        "fbqw,bwv->fqv",
        masked,
        table,
        precision=lax.Precision.HIGHEST,
        preferred_element_type=jnp.float32,
    )


def undisperse(field_in, table):
    return jnp.einsum(
        "fqv,bwv->fbqw",
        field_in,
        table,
        precision=lax.Precision.HIGHEST,
        preferred_element_type=jnp.float32,
    )


def on_device(
    features,
    conv_weight,
    time_weight,
    band_out,
    band_input_weight,
    measured,
    aperture,
    dispersion,
    update_cot,
):
    pre_act = spatial_conv(features, conv_weight)
    hidden_state = (features.astype(jnp.float32) + gelu_exact(pre_act)).astype(jnp.bfloat16)
    temporal = time_mix(framed(to_time(hidden_state)), time_weight).astype(jnp.bfloat16)
    width_keep = aperture.shape[-1]
    width_wide = measured.shape[-1]
    table = shift_table(dispersion, width_keep, width_wide)
    mask_float = aperture.astype(jnp.float32)[:, None]
    band_vals = jnp.einsum("fcqw,cb->fbqw", temporal, band_out, preferred_element_type=jnp.float32)
    masked_band_sum = disperse(band_vals * mask_float, table)
    residual_error = measured - masked_band_sum
    back_proj = (undisperse(residual_error, table) * mask_float).astype(jnp.bfloat16)
    updated = (
        temporal.astype(jnp.float32)
        + jnp.einsum(
            "fbqw,bc->fcqw", back_proj, band_input_weight, preferred_element_type=jnp.float32
        )
    ).astype(jnp.bfloat16)
    band_cot = jnp.einsum(
        "fcqw,bc->fbqw", update_cot, band_input_weight, preferred_element_type=jnp.float32
    )
    resid_grad = disperse(band_cot * mask_float, table)
    band_grad = (-(undisperse(resid_grad, table) * mask_float)).astype(jnp.bfloat16)
    cot_temporal = (
        update_cot.astype(jnp.float32)
        + jnp.einsum("fbqw,cb->fcqw", band_grad, band_out, preferred_element_type=jnp.float32)
    ).astype(jnp.bfloat16)
    flipped = time_weight[:, ::-1]
    cot_hidden = to_space(time_mix(framed(cot_temporal), flipped).astype(jnp.bfloat16))
    pullback = jax.vjp(gelu_exact, pre_act)[1]
    gate_grad = pullback(cot_hidden.astype(jnp.float32))[0].astype(jnp.bfloat16)
    kernel_flip = jnp.transpose(conv_weight[::-1, ::-1], (0, 1, 3, 2))
    features_grad = (cot_hidden.astype(jnp.float32) + spatial_conv(gate_grad, kernel_flip)).astype(
        jnp.bfloat16
    )
    return (updated, features_grad)


def solution(mesh):
    return jax.shard_map(
        on_device,
        mesh=mesh,
        in_specs=(
            P(None, None, "row", ("ta", "col")),
            P(),
            P(),
            P(),
            P(),
            P(("ta", "col"), "row", None),
            P(("ta", "col"), "row", None),
            P(),
            P(("ta", "col"), None, "row", None),
        ),
        out_specs=(P(("ta", "col"), None, "row", None), P(None, None, "row", ("ta", "col"))),
        check_vma=False,
    )
```

profile of v0, /device:TPU:48, one launch (start us, length us, event | category | flops | bytes accessed | tf_op | source)
XLA Modules:
  0.0 202.4 jit_solution(11668594038029512178)
XLA Ops:
  1.4 1.4 fusion.39
  2.8 4.8 %fusion.81 = f32[2,8,310,1]{2,1,0,3:T(8,128)S(1)} fusion(s32[28]{0:T(128)} %param.16, f32[2,28,8,256]{3,1,2,0:T(8,128)S(1)} %fusion.39), kind=kOutput, calls=%fused_computation.83 | convolution fusion | flops 431083520 | bytes 478704 | tf_op jit(solution)/shard_map/fbqw,bwv->fqv/dot_general | solution.py:71
  7.7 3.2 %fusion.59 = bf16[2,28,8,256]{3,2,0,1:T(8,128)(2,1)S(1)} fusion(f32[2,8,310,1]{2,1,0,3:T(8,128)S(1)} %fusion.81, s32[28]{0:T(128)S(1)} %copy-done.23, f32[2,8,256]{2,1,0:T(8,128)S(1)} %convert_element_type.92), kind=kOutput, calls=%fused_computation.65 | convolution fusion | flops 431427584 | bytes 265712 | tf_op jit(solution)/shard_map/fqv,bwv->fbqw/dot_general | solution.py:81
  12.3 4.2 %collective-permute-start.7 = (bf16[2,96,8,256]{3,1,2,0:T(8,128)(2,1)}, bf16[2,96,8,256]{3,1,2,0:T(8,128)(2,1)}, u32[]{:S(2)}, u32[]{:S(2)}) collective-permute-start(bf16[2,96,8,256]{3,1,2,0:T(8,128)(2,1)} %fusion.37), channel_id=1, source_target_pairs={{1,0},{2,1},{3,2},{64,3},{65,64},{66,65},{67,66},{128,67},{129,128... | collective-permute-start | bytes 2359304 | tf_op jit(solution)/shard_map/ppermute | solution.py:15
  16.5 1.9 collective-permute-start.6
  19.8 1.9 collective-permute-start
  21.7 8.4 %collective-permute-start.1 = (bf16[32,96,1,16]{1,0,3,2:T(8,128)(2,1)}, bf16[32,96,1,16]{1,0,3,2:T(8,128)(2,1)}, u32[]{:S(2)}, u32[]{:S(2)}) collective-permute-start(bf16[32,96,1,16]{1,0,3,2:T(8,128)(2,1)} %get-tuple-element.17), channel_id=1, source_target_pairs={{4,0},{8,4},{12,8},{16,12},{20,16},{24,20},{28,24},{32,28},{36,32}... | collective-permute-start | bytes 294920 | tf_op jit(solution)/shard_map/ppermute | solution.py:15
  30.4 2.2 %fusion.112 = f32[32,8,16,96]{3,0,2,1:T(8,128)} fusion(bf16[3,3,96,96]{3,2,1,0:T(8,128)(2,1)S(1)} %copy-done.8, bf16[32,96,8,16]{1,3,2,0:T(8,128)(2,1)S(1)} %copy-done.1), kind=kOutput, calls=%fused_computation.125 | convolution fusion | flops 75497472 | bytes 2646016 | tf_op jit(solution)/shard_map/io,fiqw->foqw/dot_general | solution.py:28
  33.3 9.4 %collective-permute-done = bf16[32,96,1,16]{1,0,3,2:T(8,128)(2,1)S(1)} collective-permute-done((bf16[32,96,1,16]{1,0,3,2:T(8,128)(2,1)S(1)}, bf16[32,96,1,16]{1,0,3,2:T(8,128)(2,1)S(1)}, u32[]{:S(2)}, u32[]{:S(2)}) %collective-permute-start) | collective-permute-done | bytes 98336 | tf_op jit(solution)/shard_map/ppermute | solution.py:14
  45.1 8.3 %collective-permute-start.3 = (bf16[32,96,10,1]{1,0,3,2:T(8,128)(2,1)}, bf16[32,96,10,1]{1,0,3,2:T(8,128)(2,1)}, u32[]{:S(2)}, u32[]{:S(2)}) collective-permute-start(bf16[32,96,10,1]{1,0,3,2:T(8,128)(2,1)} %get-tuple-element.12), channel_id=1, source_target_pairs={{1,0},{2,1},{3,2},{64,3},{65,64},{66,65},{67,66},{128,67},{129,128... | collective-permute-start | bytes 184328 | tf_op jit(solution)/shard_map/ppermute | solution.py:15
  53.4 2.1 %collective-permute-start.2 = (bf16[32,96,10,1]{1,0,3,2:T(8,128)(2,1)}, bf16[32,96,10,1]{1,0,3,2:T(8,128)(2,1)S(1)}, u32[]{:S(2)}, u32[]{:S(2)}) collective-permute-start(bf16[32,96,10,1]{1,0,3,2:T(8,128)(2,1)} %get-tuple-element.13), channel_id=1, source_target_pairs={{0,1},{1,2},{2,3},{3,64},{64,65},{65,66},{66,67},{67,128},{128,129... | collective-permute-start | bytes 184328 | tf_op jit(solution)/shard_map/ppermute | solution.py:14
  55.5 2.7 %fusion.66 = f32[32,8,16,96]{3,0,2,1:T(8,128)} fusion(bf16[32,96,1,16]{1,0,3,2:T(8,128)(2,1)} %collective-permute-done.1, bf16[32,96,8,16]{1,0,3,2:T(8,128)(2,1)S(1)} %copy.43, bf16[3,3,96,96]{3,2,1,0:T(8,128)(2,1)} %param.10), kind=kOutput, calls=%fused_computation.70 | convolution fusion | flops 77266944 | bytes 2514944 | tf_op jit(solution)/shard_map/io,fiqw->foqw/dot_general | solution.py:28
  58.2 3.8 %add_convert_fusion = bf16[2,96,8,256]{3,1,2,0:T(8,128)(2,1)} fusion(bf16[2,96,8,256]{3,1,2,0:T(8,128)(2,1)} %collective-permute-done.7, bf16[2,96,8,256]{3,1,2,0:T(8,128)(2,1)} %fusion.37, bf16[2,96,8,256]{3,1,2,0:T(8,128)(2,1)} %collective-permute-done.6, f32[96]{0:T(128)S(1)} %get-tuple-element.21, f32[96]{0:T(128)S(1)} %get-tuple-element.22, ...), kind=kLoop, calls=%fused_computation.49 | loop fusion | flops 6684672 | bytes 3147648 | tf_op jit(solution)/shard_map/convert_element_type | solution.py:128
  61.9 2.6 %copy.63 = bf16[2,96,8,256]{1,2,0,3:T(8,128)(2,1)} copy(bf16[2,96,8,256]{3,1,2,0:T(8,128)(2,1)} %add_convert_fusion) | data formatting | bytes 1572864 | tf_op jit(solution)/shard_map/convert_element_type | solution.py:128
  64.5 7.3 %all-to-all-start.1 = ((bf16[2,96,8,256]{1,2,0,3:T(8,128)(2,1)}), bf16[2,96,8,256]{1,2,0,3:T(8,128)(2,1)}, u32[]{:S(2)}, u32[]{:S(2)}) async-start(bf16[2,96,8,256]{1,2,0,3:T(8,128)(2,1)} %copy.63), calls=%async_computation.1 | async-start | bytes 2097152 | tf_op jit(solution)/shard_map/all_to_all | solution.py:43
  71.8 2.8 %fusion.62 = f32[32,8,16,96]{3,0,2,1:T(8,128)} fusion(bf16[32,96,8,16]{1,0,3,2:T(8,128)(2,1)S(1)} %copy.43, bf16[32,96,1,16]{1,0,3,2:T(8,128)(2,1)} %copy-done.10, bf16[3,3,96,96]{3,2,1,0:T(8,128)(2,1)} %param.10), kind=kOutput, calls=%fused_computation.66 | convolution fusion | flops 77266944 | bytes 2514944 | tf_op jit(solution)/shard_map/io,fiqw->foqw/dot_general | solution.py:28
  74.6 1.8 fusion.97
  76.4 1.8 fusion.96
  78.2 1.7 fusion.98
  80.0 2.6 %fusion.94 = f32[32,8,16,96]{3,0,2,1:T(8,128)} fusion(bf16[32,96,10,1]{1,0,3,2:T(8,128)(2,1)} %collective-permute-done.3, bf16[32,96,10,16]{1,0,3,2:T(8,128)(2,1)S(1)} %constant_dynamic-update-slice_fusion, bf16[3,3,96,96]{3,2,1,0:T(8,128)(2,1)S(1)} %copy-done.9), kind=kOutput, calls=%fused_computation.94 | convolution fusion | flops 77586432 | bytes 2969600 | tf_op jit(solution)/shard_map/io,fiqw->foqw/dot_general | solution.py:28
  82.5 2.6 %fusion.95 = f32[32,8,16,96]{3,0,2,1:T(8,128)} fusion(bf16[32,96,10,1]{1,0,3,2:T(8,128)(2,1)} %collective-permute-done.3, bf16[32,96,10,16]{1,0,3,2:T(8,128)(2,1)S(1)} %constant_dynamic-update-slice_fusion, bf16[3,3,96,96]{3,2,1,0:T(8,128)(2,1)S(1)} %copy-done.9), kind=kOutput, calls=%fused_computation.95 | convolution fusion | flops 77586432 | bytes 2969600 | tf_op jit(solution)/shard_map/io,fiqw->foqw/dot_general | solution.py:28
  85.1 13.4 %all-to-all-done.1 = bf16[2,96,8,256]{1,2,0,3:T(8,128)(2,1)} async-done(((bf16[2,96,8,256]{1,2,0,3:T(8,128)(2,1)}), bf16[2,96,8,256]{1,2,0,3:T(8,128)(2,1)}, u32[]{:S(2)}, u32[]{:S(2)}) %all-to-all-start.1) | async-done | bytes 786464 | tf_op jit(solution)/shard_map/all_to_all | solution.py:43
  98.5 1.6 copy.64
  100.4 1.6 copy.65
  103.0 8.1 %fusion.24 = (bf16[32,96,8,16]{1,0,3,2:T(8,128)(2,1)S(1)}, f32[32,96,8,16]{1,0,3,2:T(8,128)S(1)}, f32[32,8,16,96]{3,0,2,1:T(8,128)S(1)}) fusion(f32[32,96,8,16]{1,0,3,2:T(8,128)S(1)} %bitcast.318, bf16[3,3,96,96]{3,2,1,0:T(8,128)(2,1)} %param.10, bf16[32,96,10,1]{1,0,3,2:T(8,128)(2,1)} %collective-permute-done.3, ...), kind=kOutput, calls=%fused_computation.30 | convolution fusion | flops 109043712 | bytes 21274624 | tf_op jit(solution)/shard_map/io,fiqw->foqw/dot_general | solution.py:28
  113.6 5.4 %all-to-all-start = ((bf16[32,96,8,16]{1,3,2,0:T(8,128)(2,1)}), bf16[32,96,8,16]{1,3,2,0:T(8,128)(2,1)S(1)}, u32[]{:S(2)}, u32[]{:S(2)}) async-start(bf16[32,96,8,16]{1,3,2,0:T(8,128)(2,1)} %copy.50), calls=%async_computation | async-start | bytes 2097152 | tf_op jit(solution)/shard_map/all_to_all | solution.py:39
  119.0 1.9 collective-permute-start.8
  120.9 8.4 %collective-permute-start.9 = (bf16[32,96,1,16]{1,0,3,2:T(8,128)(2,1)S(1)}, bf16[32,96,1,16]{1,0,3,2:T(8,128)(2,1)S(1)}, u32[]{:S(2)}, u32[]{:S(2)}) collective-permute-start(bf16[32,96,1,16]{1,0,3,2:T(8,128)(2,1)S(1)} %get-tuple-element.15), channel_id=1, source_target_pairs={{4,0},{8,4},{12,8},{16,12},{20,16},{24,20},{28,24},{32,28},{36,32}... | collective-permute-start | bytes 294920 | tf_op jit(solution)/shard_map/ppermute | solution.py:15
  129.4 1.7 fusion.104
  131.1 6.6 %collective-permute-done.8 = bf16[32,96,1,16]{1,0,3,2:T(8,128)(2,1)S(1)} collective-permute-done((bf16[32,96,1,16]{1,0,3,2:T(8,128)(2,1)S(1)}, bf16[32,96,1,16]{1,0,3,2:T(8,128)(2,1)S(1)}, u32[]{:S(2)}, u32[]{:S(2)}) %collective-permute-start.8) | collective-permute-done | bytes 98336 | tf_op jit(solution)/shard_map/ppermute | solution.py:14
  137.8 9.8 %collective-permute-start.11 = (bf16[32,96,10,1]{1,0,3,2:T(8,128)(2,1)S(1)}, bf16[32,96,10,1]{1,0,3,2:T(8,128)(2,1)S(1)}, u32[]{:S(2)}, u32[]{:S(2)}) collective-permute-start(bf16[32,96,10,1]{1,0,3,2:T(8,128)(2,1)S(1)} %get-tuple-element.10), channel_id=1, source_target_pairs={{1,0},{2,1},{3,2},{64,3},{65,64},{66,65},{67,66},{128,67},{129,128... | collective-permute-start | bytes 184328 | tf_op jit(solution)/shard_map/ppermute | solution.py:15
  147.7 2.1 %collective-permute-start.10 = (bf16[32,96,10,1]{1,0,3,2:T(8,128)(2,1)S(1)}, bf16[32,96,10,1]{1,0,3,2:T(8,128)(2,1)S(1)}, u32[]{:S(2)}, u32[]{:S(2)}) collective-permute-start(bf16[32,96,10,1]{1,0,3,2:T(8,128)(2,1)S(1)} %get-tuple-element.11), channel_id=1, source_target_pairs={{0,1},{1,2},{2,3},{3,64},{64,65},{65,66},{66,67},{67,128},{128,129... | collective-permute-start | bytes 184328 | tf_op jit(solution)/shard_map/ppermute | solution.py:14
  149.8 1.8 fusion.74
  151.6 1.8 fusion.70
  153.4 2.9 %collective-permute-done.10 = bf16[32,96,10,1]{1,0,3,2:T(8,128)(2,1)S(1)} collective-permute-done((bf16[32,96,10,1]{1,0,3,2:T(8,128)(2,1)S(1)}, bf16[32,96,10,1]{1,0,3,2:T(8,128)(2,1)S(1)}, u32[]{:S(2)}, u32[]{:S(2)}) %collective-permute-start.10) | collective-permute-done | bytes 61472 | tf_op jit(solution)/shard_map/ppermute | solution.py:14
  156.3 1.8 fusion.105
  158.1 1.7 fusion.102
  159.9 1.7 fusion.107
  161.6 1.8 fusion.103
  163.4 1.7 fusion.106
  165.9 3.1 %collective-permute-start.5 = (bf16[2,96,8,256]{3,1,2,0:T(8,128)(2,1)S(1)}, bf16[2,96,8,256]{3,1,2,0:T(8,128)(2,1)S(1)}, u32[]{:S(2)}, u32[]{:S(2)}) collective-permute-start(bf16[2,96,8,256]{3,1,2,0:T(8,128)(2,1)S(1)} %copy.52), channel_id=1, source_target_pairs={{1,0},{2,1},{3,2},{64,3},{65,64},{66,65},{67,66},{128,67},{129,128... | collective-permute-start | bytes 2359304 | tf_op jit(solution)/shard_map/ppermute | solution.py:15
  169.0 2.7 %collective-permute-start.4 = (bf16[2,96,8,256]{3,1,2,0:T(8,128)(2,1)S(1)}, bf16[2,96,8,256]{3,1,2,0:T(8,128)(2,1)S(1)}, u32[]{:S(2)}, u32[]{:S(2)}) collective-permute-start(bf16[2,96,8,256]{3,1,2,0:T(8,128)(2,1)S(1)} %copy.52), channel_id=1, source_target_pairs={{0,1},{1,2},{2,3},{3,64},{64,65},{65,66},{66,67},{67,128},{128,129... | collective-permute-start | bytes 2359304 | tf_op jit(solution)/shard_map/ppermute | solution.py:14
  171.8 7.5 %fusion.15 = bf16[32,96,8,16]{1,0,3,2:T(8,128)(2,1)S(1)} fusion(f32[32,96,8,16]{1,0,3,2:T(8,128)} %bitcast.319, f32[32,8,16,96]{3,0,2,1:T(8,128)} %fusion.74, f32[32,8,16,96]{3,0,2,1:T(8,128)} %fusion.102, f32[32,8,16,96]{3,0,2,1:T(8,128)} %fusion.103, f32[32,8,16,96]{3,0,2,1:T(8,128)} %fusion.104, f32[32,8,16,96]{3,0,2,1:T(8,128)} %fusion.105, ...), kind=kOutput, calls=%fused_computation.15 | convolution fusion | flops 83607552 | bytes 20729856 | tf_op jit(solution)/shard_map/io,fiqw->foqw/dot_general | solution.py:28
  179.4 1.4 copy.68
  180.7 5.9 %collective-permute-done.5 = bf16[2,96,8,256]{3,1,2,0:T(8,128)(2,1)S(1)} collective-permute-done((bf16[2,96,8,256]{3,1,2,0:T(8,128)(2,1)S(1)}, bf16[2,96,8,256]{3,1,2,0:T(8,128)(2,1)S(1)}, u32[]{:S(2)}, u32[]{:S(2)}) %collective-permute-start.5) | collective-permute-done | bytes 786464 | tf_op jit(solution)/shard_map/ppermute | solution.py:15
  186.7 5.5 %collective-permute-done.4 = bf16[2,96,8,256]{3,1,2,0:T(8,128)(2,1)S(1)} collective-permute-done((bf16[2,96,8,256]{3,1,2,0:T(8,128)(2,1)S(1)}, bf16[2,96,8,256]{3,1,2,0:T(8,128)(2,1)S(1)}, u32[]{:S(2)}, u32[]{:S(2)}) %collective-permute-start.4) | collective-permute-done | bytes 786464 | tf_op jit(solution)/shard_map/ppermute | solution.py:14
  193.2 4.1 %fusion.87 = f32[2,8,310,1]{2,1,0,3:T(8,128)S(1)} fusion(f32[2,8,310]{2,1,0:T(8,128)S(1)} %copy-done.22, s32[28]{0:T(128)S(1)} %copy-done.24, f32[2,28,8,256]{3,1,2,0:T(8,128)S(1)} %fusion.40), kind=kOutput, calls=%fused_computation.85 | convolution fusion | flops 431088480 | bytes 498544 | tf_op jit(solution)/shard_map/fbqw,bwv->fqv/dot_general | solution.py:71
  197.4 3.2 %fusion.56 = bf16[2,28,8,256]{3,2,0,1:T(8,128)(2,1)S(1)} fusion(f32[2,8,310,1]{2,1,0,3:T(8,128)S(1)} %fusion.87, s32[28]{0:T(128)S(1)} %copy-done.24, f32[2,8,256]{2,1,0:T(8,128)S(1)} %copy-done.13), kind=kOutput, calls=%fused_computation.64 | convolution fusion | flops 431312896 | bytes 265712 | tf_op jit(solution)/shard_map/fqv,bwv->fbqw/dot_general | solution.py:81
  (80 shorter events, 13.9 us)
Async XLA Ops:
  0.6 10.3 %copy-start = (bf16[96,28]{0,1:T(8,128)(2,1)S(1)}, bf16[96,28]{0,1:T(8,128)(2,1)}, u32[]{:S(2)}) copy-start(bf16[96,28]{0,1:T(8,128)(2,1)} %param.12) | copy-start | bytes 16132
  1.4 6.3 %copy-start.12 = (f32[2,8,256]{2,1,0:T(8,128)}, f32[2,8,256]{2,1,0:T(8,128)S(1)}, u32[]{:S(2)}) copy-start(f32[2,8,256]{2,1,0:T(8,128)S(1)} %convert_element_type.92) | copy-start | bytes 49156
  2.8 4.9 %copy-start.23 = (s32[28]{0:T(128)S(1)}, s32[28]{0:T(128)}, u32[]{:S(2)}) copy-start(s32[28]{0:T(128)} %param.16) | copy-start | bytes 340
  7.7 3.2 %copy-start.3 = (bf16[2,96,8,256]{3,2,1,0:T(8,128)(2,1)S(1)}, bf16[2,96,8,256]{3,2,1,0:T(8,128)(2,1)}, u32[]{:S(2)}) copy-start(bf16[2,96,8,256]{3,2,1,0:T(8,128)(2,1)} %param.17) | copy-start | bytes 2359300
  10.9 7.5 %copy-start.1 = (bf16[32,96,8,16]{1,3,2,0:T(8,128)(2,1)S(1)}, bf16[32,96,8,16]{1,3,2,0:T(8,128)(2,1)}, u32[]{:S(2)}) copy-start(bf16[32,96,8,16]{1,3,2,0:T(8,128)(2,1)} %param.9) | copy-start | bytes 2359300
  10.9 19.2 %copy-start.8 = (bf16[3,3,96,96]{3,2,1,0:T(8,128)(2,1)S(1)}, bf16[3,3,96,96]{3,2,1,0:T(8,128)(2,1)}, u32[]{:S(2)}) copy-start(bf16[3,3,96,96]{3,2,1,0:T(8,128)(2,1)} %param.10) | copy-start | bytes 497668
  12.3 45.9 %collective-permute-start.7 = (bf16[2,96,8,256]{3,1,2,0:T(8,128)(2,1)}, bf16[2,96,8,256]{3,1,2,0:T(8,128)(2,1)}, u32[]{:S(2)}, u32[]{:S(2)}) collective-permute-start(bf16[2,96,8,256]{3,1,2,0:T(8,128)(2,1)} %fusion.37), channel_id=1, source_target_pairs={{1,0},{2,1},{3,2},{64,3},{65,64},{66,65},{67,66},{128,67},{129,128... | collective-permute-start | bytes 2359304 | tf_op jit(solution)/shard_map/ppermute | solution.py:15
  16.5 41.6 %collective-permute-start.6 = (bf16[2,96,8,256]{3,1,2,0:T(8,128)(2,1)}, bf16[2,96,8,256]{3,1,2,0:T(8,128)(2,1)}, u32[]{:S(2)}, u32[]{:S(2)}) collective-permute-start(bf16[2,96,8,256]{3,1,2,0:T(8,128)(2,1)} %fusion.37), channel_id=1, source_target_pairs={{0,1},{1,2},{2,3},{3,64},{64,65},{65,66},{66,67},{67,128},{128,129... | collective-permute-start | bytes 2359304 | tf_op jit(solution)/shard_map/ppermute | solution.py:14
  19.1 13.5 %copy-start.21 = (f32[96,5]{0,1:T(8,128)S(1)}, f32[96,5]{0,1:T(8,128)}, u32[]{:S(2)}) copy-start(f32[96,5]{0,1:T(8,128)} %param.11) | copy-start | bytes 5764
  19.8 22.9 %collective-permute-start = (bf16[32,96,1,16]{1,0,3,2:T(8,128)(2,1)S(1)}, bf16[32,96,1,16]{1,0,3,2:T(8,128)(2,1)S(1)}, u32[]{:S(2)}, u32[]{:S(2)}) collective-permute-start(bf16[32,96,1,16]{1,0,3,2:T(8,128)(2,1)S(1)} %get-tuple-element.16), channel_id=1, source_target_pairs={{0,4},{4,8},{8,12},{12,16},{16,20},{20,24},{24,28},{28,32},{32,36}... | collective-permute-start | bytes 294920 | tf_op jit(solution)/shard_map/ppermute | solution.py:14
  21.7 21.7 %collective-permute-start.1 = (bf16[32,96,1,16]{1,0,3,2:T(8,128)(2,1)}, bf16[32,96,1,16]{1,0,3,2:T(8,128)(2,1)}, u32[]{:S(2)}, u32[]{:S(2)}) collective-permute-start(bf16[32,96,1,16]{1,0,3,2:T(8,128)(2,1)} %get-tuple-element.17), channel_id=1, source_target_pairs={{4,0},{8,4},{12,8},{16,12},{20,16},{24,20},{28,24},{32,28},{36,32}... | collective-permute-start | bytes 294920 | tf_op jit(solution)/shard_map/ppermute | solution.py:15
  32.6 25.6 %copy-start.15 = (f32[96]{0:T(128)}, f32[96]{0:T(128)S(1)}, u32[]{:S(2)}) copy-start(f32[96]{0:T(128)S(1)} %get-tuple-element.20) | copy-start | bytes 1156
  32.6 25.6 %copy-start.17 = (f32[96]{0:T(128)}, f32[96]{0:T(128)S(1)}, u32[]{:S(2)}) copy-start(f32[96]{0:T(128)S(1)} %get-tuple-element.21) | copy-start | bytes 1156
  32.6 25.6 %copy-start.19 = (f32[96]{0:T(128)}, f32[96]{0:T(128)S(1)}, u32[]{:S(2)}) copy-start(f32[96]{0:T(128)S(1)} %get-tuple-element.22) | copy-start | bytes 1156
  42.7 10.7 %copy-start.10 = (bf16[32,96,1,16]{1,0,3,2:T(8,128)(2,1)}, bf16[32,96,1,16]{1,0,3,2:T(8,128)(2,1)S(1)}, u32[]{:S(2)}) copy-start(bf16[32,96,1,16]{1,0,3,2:T(8,128)(2,1)S(1)} %collective-permute-done) | copy-start | bytes 294916
  45.1 34.9 %collective-permute-start.3 = (bf16[32,96,10,1]{1,0,3,2:T(8,128)(2,1)}, bf16[32,96,10,1]{1,0,3,2:T(8,128)(2,1)}, u32[]{:S(2)}, u32[]{:S(2)}) collective-permute-start(bf16[32,96,10,1]{1,0,3,2:T(8,128)(2,1)} %get-tuple-element.12), channel_id=1, source_target_pairs={{1,0},{2,1},{3,2},{64,3},{65,64},{66,65},{67,66},{128,67},{129,128... | collective-permute-start | bytes 184328 | tf_op jit(solution)/shard_map/ppermute | solution.py:15
  53.4 21.3 %collective-permute-start.2 = (bf16[32,96,10,1]{1,0,3,2:T(8,128)(2,1)}, bf16[32,96,10,1]{1,0,3,2:T(8,128)(2,1)S(1)}, u32[]{:S(2)}, u32[]{:S(2)}) collective-permute-start(bf16[32,96,10,1]{1,0,3,2:T(8,128)(2,1)} %get-tuple-element.13), channel_id=1, source_target_pairs={{0,1},{1,2},{2,3},{3,64},{64,65},{65,66},{66,67},{67,128},{128,129... | collective-permute-start | bytes 184328 | tf_op jit(solution)/shard_map/ppermute | solution.py:14
  64.5 33.9 %all-to-all-start.1 = ((bf16[2,96,8,256]{1,2,0,3:T(8,128)(2,1)}), bf16[2,96,8,256]{1,2,0,3:T(8,128)(2,1)}, u32[]{:S(2)}, u32[]{:S(2)}) async-start(bf16[2,96,8,256]{1,2,0,3:T(8,128)(2,1)} %copy.63), calls=%async_computation.1 | async-start | bytes 2097152 | tf_op jit(solution)/shard_map/all_to_all | solution.py:43
  71.8 2.8 %copy-start.9 = (bf16[3,3,96,96]{3,2,1,0:T(8,128)(2,1)S(1)}, bf16[3,3,96,96]{3,2,1,0:T(8,128)(2,1)}, u32[]{:S(2)}) copy-start(bf16[3,3,96,96]{3,2,1,0:T(8,128)(2,1)} %param.10) | copy-start | bytes 497668
  98.5 3.6 %copy-start.7 = (f32[32,8,16,96]{3,0,2,1:T(8,128)S(1)}, f32[32,8,16,96]{3,0,2,1:T(8,128)}, u32[]{:S(2)}) copy-start(f32[32,8,16,96]{3,0,2,1:T(8,128)} %fusion.97) | copy-start | bytes 4718596
  100.1 1.9 copy-start.6
  100.4 2.0 %copy-start.4 = (f32[32,8,16,96]{3,0,2,1:T(8,128)S(1)}, f32[32,8,16,96]{3,0,2,1:T(8,128)}, u32[]{:S(2)}) copy-start(f32[32,8,16,96]{3,0,2,1:T(8,128)} %fusion.112) | copy-start | bytes 4718596
  100.4 2.6 %copy-start.5 = (f32[32,8,16,96]{3,0,2,1:T(8,128)S(1)}, f32[32,8,16,96]{3,0,2,1:T(8,128)}, u32[]{:S(2)}) copy-start(f32[32,8,16,96]{3,0,2,1:T(8,128)} %fusion.66) | copy-start | bytes 4718596
  102.0 9.1 %copy-start.2 = (f32[16,2,96,8,16]{2,1,0,4,3:T(2,128)}, f32[16,2,96,8,16]{2,1,0,4,3:T(2,128)S(1)}, u32[]{:S(2)}) copy-start(f32[16,2,96,8,16]{2,1,0,4,3:T(2,128)S(1)} %copy.65) | copy-start | bytes 4718596
  112.2 17.2 %copy-start.11 = (bf16[3,3,96,96]{3,2,1,0:T(8,128)(2,1)S(1)}, bf16[3,3,96,96]{3,2,1,0:T(8,128)(2,1)}, u32[]{:S(2)}) copy-start(bf16[3,3,96,96]{3,2,1,0:T(8,128)(2,1)} %reverse_bitcast_fusion) | copy-start | bytes 497668
  113.6 51.6 %all-to-all-start = ((bf16[32,96,8,16]{1,3,2,0:T(8,128)(2,1)}), bf16[32,96,8,16]{1,3,2,0:T(8,128)(2,1)S(1)}, u32[]{:S(2)}, u32[]{:S(2)}) async-start(bf16[32,96,8,16]{1,3,2,0:T(8,128)(2,1)} %copy.50), calls=%async_computation | async-start | bytes 2097152 | tf_op jit(solution)/shard_map/all_to_all | solution.py:39
  119.0 18.8 %collective-permute-start.8 = (bf16[32,96,1,16]{1,0,3,2:T(8,128)(2,1)S(1)}, bf16[32,96,1,16]{1,0,3,2:T(8,128)(2,1)S(1)}, u32[]{:S(2)}, u32[]{:S(2)}) collective-permute-start(bf16[32,96,1,16]{1,0,3,2:T(8,128)(2,1)S(1)} %get-tuple-element.14), channel_id=1, source_target_pairs={{0,4},{4,8},{8,12},{12,16},{16,20},{20,24},{24,28},{28,32},{32,36}... | collective-permute-start | bytes 294920 | tf_op jit(solution)/shard_map/ppermute | solution.py:14
  120.9 16.8 %collective-permute-start.9 = (bf16[32,96,1,16]{1,0,3,2:T(8,128)(2,1)S(1)}, bf16[32,96,1,16]{1,0,3,2:T(8,128)(2,1)S(1)}, u32[]{:S(2)}, u32[]{:S(2)}) collective-permute-start(bf16[32,96,1,16]{1,0,3,2:T(8,128)(2,1)S(1)} %get-tuple-element.15), channel_id=1, source_target_pairs={{4,0},{8,4},{12,8},{16,12},{20,16},{24,20},{28,24},{32,28},{36,32}... | collective-permute-start | bytes 294920 | tf_op jit(solution)/shard_map/ppermute | solution.py:15
  137.8 23.8 %collective-permute-start.11 = (bf16[32,96,10,1]{1,0,3,2:T(8,128)(2,1)S(1)}, bf16[32,96,10,1]{1,0,3,2:T(8,128)(2,1)S(1)}, u32[]{:S(2)}, u32[]{:S(2)}) collective-permute-start(bf16[32,96,10,1]{1,0,3,2:T(8,128)(2,1)S(1)} %get-tuple-element.10), channel_id=1, source_target_pairs={{1,0},{2,1},{3,2},{64,3},{65,64},{66,65},{67,66},{128,67},{129,128... | collective-permute-start | bytes 184328 | tf_op jit(solution)/shard_map/ppermute | solution.py:15
  147.7 8.6 %collective-permute-start.10 = (bf16[32,96,10,1]{1,0,3,2:T(8,128)(2,1)S(1)}, bf16[32,96,10,1]{1,0,3,2:T(8,128)(2,1)S(1)}, u32[]{:S(2)}, u32[]{:S(2)}) collective-permute-start(bf16[32,96,10,1]{1,0,3,2:T(8,128)(2,1)S(1)} %get-tuple-element.11), channel_id=1, source_target_pairs={{0,1},{1,2},{2,3},{3,64},{64,65},{65,66},{66,67},{67,128},{128,129... | collective-permute-start | bytes 184328 | tf_op jit(solution)/shard_map/ppermute | solution.py:14
  165.9 20.8 %collective-permute-start.5 = (bf16[2,96,8,256]{3,1,2,0:T(8,128)(2,1)S(1)}, bf16[2,96,8,256]{3,1,2,0:T(8,128)(2,1)S(1)}, u32[]{:S(2)}, u32[]{:S(2)}) collective-permute-start(bf16[2,96,8,256]{3,1,2,0:T(8,128)(2,1)S(1)} %copy.52), channel_id=1, source_target_pairs={{1,0},{2,1},{3,2},{64,3},{65,64},{66,65},{67,66},{128,67},{129,128... | collective-permute-start | bytes 2359304 | tf_op jit(solution)/shard_map/ppermute | solution.py:15
  169.0 23.2 %collective-permute-start.4 = (bf16[2,96,8,256]{3,1,2,0:T(8,128)(2,1)S(1)}, bf16[2,96,8,256]{3,1,2,0:T(8,128)(2,1)S(1)}, u32[]{:S(2)}, u32[]{:S(2)}) collective-permute-start(bf16[2,96,8,256]{3,1,2,0:T(8,128)(2,1)S(1)} %copy.52), channel_id=1, source_target_pairs={{0,1},{1,2},{2,3},{3,64},{64,65},{65,66},{66,67},{67,128},{128,129... | collective-permute-start | bytes 2359304 | tf_op jit(solution)/shard_map/ppermute | solution.py:14
  179.3 12.9 %copy-start.16 = (f32[96]{0:T(128)S(1)}, f32[96]{0:T(128)}, u32[]{:S(2)}) copy-start(f32[96]{0:T(128)} %copy-done.15) | copy-start | bytes 1156
  179.3 12.9 %copy-start.18 = (f32[96]{0:T(128)S(1)}, f32[96]{0:T(128)}, u32[]{:S(2)}) copy-start(f32[96]{0:T(128)} %copy-done.17) | copy-start | bytes 1156
  179.3 12.9 %copy-start.20 = (f32[96]{0:T(128)S(1)}, f32[96]{0:T(128)}, u32[]{:S(2)}) copy-start(f32[96]{0:T(128)} %copy-done.19) | copy-start | bytes 1156
  180.7 12.2 %copy-start.13 = (f32[2,8,256]{2,1,0:T(8,128)S(1)}, f32[2,8,256]{2,1,0:T(8,128)}, u32[]{:S(2)}) copy-start(f32[2,8,256]{2,1,0:T(8,128)} %copy-done.12) | copy-start | bytes 49156
  180.7 12.5 %copy-start.22 = (f32[2,8,310]{2,1,0:T(8,128)S(1)}, f32[2,8,310]{2,1,0:T(8,128)}, u32[]{:S(2)}) copy-start(f32[2,8,310]{2,1,0:T(8,128)} %param.14) | copy-start | bytes 59524
  180.7 12.5 %copy-start.24 = (s32[28]{0:T(128)S(1)}, s32[28]{0:T(128)}, u32[]{:S(2)}) copy-start(s32[28]{0:T(128)} %param.16) | copy-start | bytes 340
  197.3 3.2 %copy-start.14 = (bf16[28,96]{1,0:T(8,128)(2,1)S(1)}, bf16[28,96]{1,0:T(8,128)(2,1)}, u32[]{:S(2)}) copy-start(bf16[28,96]{1,0:T(8,128)(2,1)} %param.13) | copy-start | bytes 16132
where the time goes:
time: 203 us; the launch traced here: 202 us
  starting transfers between devices  67.7 us (33%)
  matrix products  66.7 us (33%)
  waiting for transfers between devices  43.8 us (22%)
  local copies, waits for them, and re-layouts  16.4 us (8%)
  other arithmetic  6.53 us (3%)
    dot_general x18, matrix products, spatial_conv(): jnp.einsum('io,fiqw->foqw', kernel[row_tap, col_tap], window, preferred_e...  47.9 us
    ppermute x6, starting transfers between devices, with_halo(): after = lax.ppermute(initial, axis, down)  42.3 us
    ppermute x6, waiting for transfers between devices, with_halo(): before = lax.ppermute(last, axis, up)  24.5 us
    all_to_all x1, waiting for transfers between devices, to_space(): lax.all_to_all(field_in, ('ta', 'col'), split_axis=3, concat_axis=0, tile...  13.4 us
    ppermute x6, starting transfers between devices, with_halo(): before = lax.ppermute(last, axis, up)  12.7 us
    dot_general x2, matrix products, disperse(): jnp.einsum('fbqw,bwv->fqv', masked, table, precision=lax.Precision.HIGHES...  8.97 us
    all_to_all x1, starting transfers between devices, to_space(): lax.all_to_all(field_in, ('ta', 'col'), split_axis=3, concat_axis=0, tile...  7.28 us
    dot_general x2, matrix products, undisperse(): jnp.einsum('fqv,bwv->fbqw', field_in, table, precision=lax.Precision.HIGH...  6.43 us
  transfers between devices with their start and end apart: 14, of which 6 were waited for; matrix products, arithmetic and copies ran while one was open for 26% of the time, Pallas kernels for 0%

commit v1 on v0

--- a/solution.py
+++ b/solution.py
@@ -18,21 +18,15 @@
 
 
 def spatial_conv(field_in, kernel):
-    row_number = field_in.shape[2]
-    col_count = field_in.shape[3]
     padded = with_halo(field_in, (("row", 2), (("ta", "col"), 3)), 1)
-    summed = None
-    for row_tap in range(3):
-        for col_tap in range(3):
-            window = padded[:, :, row_tap : row_tap + row_number, col_tap : col_tap + col_count]
-            partial_sum = jnp.einsum(
-                "io,fiqw->foqw",
-                kernel[row_tap, col_tap],
-                window,
-                preferred_element_type=jnp.float32,
-            )
-            summed = partial_sum if summed is None else summed + partial_sum
-    return summed
+    return lax.conv_general_dilated(
+        padded,
+        kernel,
+        window_strides=(1, 1),
+        padding="VALID",
+        dimension_numbers=("NCHW", "HWIO", "NCHW"),
+        preferred_element_type=jnp.float32,
+    )
 
 
 def to_time(field_in):
@@ -43,13 +37,10 @@
     return lax.all_to_all(field_in, ("ta", "col"), split_axis=3, concat_axis=0, tiled=True)
 
 
-def framed(field_in):
-    return with_halo(field_in, ((("ta", "col"), 0),), 2)
-
-
-def time_mix(padded, time_taps):
-    frame_count = padded.shape[0] - 4
-    summed = jnp.zeros((frame_count,) + padded.shape[1:], jnp.float32)
+def time_mix(frames_in, time_taps):
+    frame_count = frames_in.shape[0]
+    padded = jnp.pad(frames_in, ((2, 2), (0, 0), (0, 0), (0, 0)))
+    summed = jnp.zeros(frames_in.shape, jnp.float32)
     for tap_index in range(5):
         summed = summed + time_taps[None, :, tap_index, None, None] * padded[
             tap_index : tap_index + frame_count
@@ -100,7 +91,7 @@
 ):
     pre_act = spatial_conv(features, conv_weight)
     hidden_state = (features.astype(jnp.float32) + gelu_exact(pre_act)).astype(jnp.bfloat16)
-    temporal = time_mix(framed(to_time(hidden_state)), time_weight).astype(jnp.bfloat16)
+    temporal = to_time(time_mix(hidden_state, time_weight).astype(jnp.bfloat16))
     width_keep = aperture.shape[-1]
     width_wide = measured.shape[-1]
     table = shift_table(dispersion, width_keep, width_wide)
@@ -125,7 +116,7 @@
         + jnp.einsum("fbqw,cb->fcqw", band_grad, band_out, preferred_element_type=jnp.float32)
     ).astype(jnp.bfloat16)
     flipped = time_weight[:, ::-1]
-    cot_hidden = to_space(time_mix(framed(cot_temporal), flipped).astype(jnp.bfloat16))
+    cot_hidden = time_mix(to_space(cot_temporal), flipped).astype(jnp.bfloat16)
     pullback = jax.vjp(gelu_exact, pre_act)[1]
     gate_grad = pullback(cot_hidden.astype(jnp.float32))[0].astype(jnp.bfloat16)
     kernel_flip = jnp.transpose(conv_weight[::-1, ::-1], (0, 1, 3, 2))

time: 203 us -> 131 us (0.65)
  the two profiles are of different devices: /device:TPU:48 before, /device:TPU:86 now
where the time goes in v1:
time: 131 us; the launch traced here: 130 us
  starting transfers between devices  63.2 us (48%)
  matrix products  30 us (23%)
  waiting for transfers between devices  24.1 us (18%)
  local copies, waits for them, and re-layouts  8.4 us (6%)
  other arithmetic  3.41 us (3%)
    ppermute x4, starting transfers between devices, with_halo(): before = lax.ppermute(last, axis, up)  27.7 us
    ppermute x4, starting transfers between devices, with_halo(): after = lax.ppermute(initial, axis, down)  21.1 us
    ppermute x4, waiting for transfers between devices, with_halo(): before = lax.ppermute(last, axis, up)  12.3 us
    conv_general_dilated x2, matrix products, spatial_conv(): lax.conv_general_dilated(padded, kernel, window_strides=(1, 1), padding='...  11.9 us
    ppermute x4, waiting for transfers between devices, with_halo(): after = lax.ppermute(initial, axis, down)  11.8 us
    dot_general x2, matrix products, disperse(): jnp.einsum('fbqw,bwv->fqv', masked, table, precision=lax.Precision.HIGHES...  8.97 us
    all_to_all x1, starting transfers between devices, to_space(): lax.all_to_all(field_in, ('ta', 'col'), split_axis=3, concat_axis=0, tile...  7.95 us
    all_to_all x1, starting transfers between devices, to_time(): lax.all_to_all(field_in, ('ta', 'col'), split_axis=0, concat_axis=3, tile...  6.46 us
  transfers between devices with their start and end apart: 10, of which 4 were waited for; matrix products, arithmetic and copies ran while one was open for 4% of the time, Pallas kernels for 0%

profile of v1, /device:TPU:86, one launch (start us, length us, event | category | flops | bytes accessed | tf_op | source)
XLA Modules:
  0.0 130.2 jit_solution(13495990683557551393)
XLA Ops:
  0.6 0.0 copy-start
  0.6 0.8 convert_element_type.86
  1.4 1.4 %fusion.46 = f32[2,28,8,256]{3,1,2,0:T(8,128)S(1)} fusion(bf16[2,96,8,256]{3,2,1,0:T(8,128)(2,1)} %param.17, f32[2,8,256]{2,1,0:T(8,128)S(1)} %convert_element_type.86, bf16[28,96]{1,0:T(8,128)(2,1)} %param.13), kind=kOutput, calls=%fused_computation.70 | convolution fusion | flops 22134784 | bytes 1266944 | tf_op jit(solution)/shard_map/fcqw,bc->fbqw/dot_general | solution.py:109
  2.8 4.8 %fusion.71 = f32[2,8,310,1]{2,1,0,3:T(8,128)S(1)} fusion(s32[28]{0:T(128)} %param.16, f32[2,28,8,256]{3,1,2,0:T(8,128)S(1)} %fusion.46), kind=kOutput, calls=%fused_computation.79 | convolution fusion | flops 431083520 | bytes 478704 | tf_op jit(solution)/shard_map/fbqw,bwv->fqv/dot_general | solution.py:62
  7.7 0.0 copy-start.2
  7.7 0.0 copy-start.5
  7.7 3.2 %fusion.65 = bf16[2,28,8,256]{3,2,0,1:T(8,128)(2,1)S(1)} fusion(f32[2,8,310,1]{2,1,0,3:T(8,128)S(1)} %fusion.71, s32[28]{0:T(128)S(1)} %copy-done.9, f32[2,8,256]{2,1,0:T(8,128)S(1)} %convert_element_type.86), kind=kOutput, calls=%fused_computation.77 | convolution fusion | flops 431427584 | bytes 265712 | tf_op jit(solution)/shard_map/fqv,bwv->fbqw/dot_general | solution.py:72
  11.0 0.4 fusion.28
  11.4 0.0 copy-start.1
  11.4 1.7 %copy.45 = bf16[2,96,8,256]{1,2,0,3:T(8,128)(2,1)} copy(bf16[2,96,8,256]{3,1,2,0:T(8,128)(2,1)S(1)} %fusion.28) | data formatting | bytes 1572864 | tf_op jit(solution)/shard_map/convert_element_type | solution.py:117
  13.2 7.9 %all-to-all-start.1 = ((bf16[2,96,8,256]{1,2,0,3:T(8,128)(2,1)}), bf16[2,96,8,256]{1,2,0,3:T(8,128)(2,1)S(1)}, u32[]{:S(2)}, u32[]{:S(2)}) async-start(bf16[2,96,8,256]{1,2,0,3:T(8,128)(2,1)} %copy.45), calls=%async_computation.1 | async-start | bytes 2097152 | tf_op jit(solution)/shard_map/all_to_all | solution.py:37
  21.1 0.0 copy-start.7
  21.2 1.9 %collective-permute-start = (bf16[32,96,1,16]{1,0,3,2:T(8,128)(2,1)S(1)}, bf16[32,96,1,16]{1,0,3,2:T(8,128)(2,1)S(1)}, u32[]{:S(2)}, u32[]{:S(2)}) collective-permute-start(bf16[32,96,1,16]{1,0,3,2:T(8,128)(2,1)S(1)} %copy.72), channel_id=1, source_target_pairs={{0,4},{4,8},{8,12},{12,16},{16,20},{20,24},{24,28},{28,32},{32,36}... | collective-permute-start | bytes 294920 | tf_op jit(solution)/shard_map/ppermute | solution.py:14
  23.2 8.4 %collective-permute-start.1 = (bf16[32,96,1,16]{1,0,3,2:T(8,128)(2,1)S(1)}, bf16[32,96,1,16]{1,0,3,2:T(8,128)(2,1)S(1)}, u32[]{:S(2)}, u32[]{:S(2)}) collective-permute-start(bf16[32,96,1,16]{1,0,3,2:T(8,128)(2,1)S(1)} %copy.73), channel_id=1, source_target_pairs={{4,0},{8,4},{12,8},{16,12},{20,16},{24,20},{28,24},{32,28},{36,32}... | collective-permute-start | bytes 294920 | tf_op jit(solution)/shard_map/ppermute | solution.py:15
  31.6 6.7 %collective-permute-done = bf16[32,96,1,16]{1,0,3,2:T(8,128)(2,1)S(1)} collective-permute-done((bf16[32,96,1,16]{1,0,3,2:T(8,128)(2,1)S(1)}, bf16[32,96,1,16]{1,0,3,2:T(8,128)(2,1)S(1)}, u32[]{:S(2)}, u32[]{:S(2)}) %collective-permute-start) | collective-permute-done | bytes 98336 | tf_op jit(solution)/shard_map/ppermute | solution.py:14
  38.3 0.7 constant_dynamic-update-slice_fusion.1
  39.1 0.0 collective-permute-done.1
  39.1 12.1 %collective-permute-start.2 = (bf16[32,96,10,1]{1,0,3,2:T(8,128)(2,1)S(1)}, bf16[32,96,10,1]{1,0,3,2:T(8,128)(2,1)S(1)}, u32[]{:S(2)}, u32[]{:S(2)}) collective-permute-start(bf16[32,96,10,1]{1,0,3,2:T(8,128)(2,1)S(1)} %get-tuple-element.13), channel_id=1, source_target_pairs={{0,1},{1,2},{2,3},{3,64},{64,65},{65,66},{66,67},{67,128},{128,129... | collective-permute-start | bytes 184328 | tf_op jit(solution)/shard_map/ppermute | solution.py:14
  51.3 2.1 %collective-permute-start.3 = (bf16[32,96,10,1]{1,0,3,2:T(8,128)(2,1)S(1)}, bf16[32,96,10,1]{1,0,3,2:T(8,128)(2,1)S(1)}, u32[]{:S(2)}, u32[]{:S(2)}) collective-permute-start(bf16[32,96,10,1]{1,0,3,2:T(8,128)(2,1)S(1)} %get-tuple-element.14), channel_id=1, source_target_pairs={{1,0},{2,1},{3,2},{64,3},{65,64},{66,65},{67,66},{128,67},{129,128... | collective-permute-start | bytes 184328 | tf_op jit(solution)/shard_map/ppermute | solution.py:15
  53.4 0.0 all-to-all-done.1
  53.4 0.8 copy.47
  54.3 0.0 collective-permute-done.2
  54.3 5.6 %collective-permute-done.3 = bf16[32,96,10,1]{1,0,3,2:T(8,128)(2,1)S(1)} collective-permute-done((bf16[32,96,10,1]{1,0,3,2:T(8,128)(2,1)S(1)}, bf16[32,96,10,1]{1,0,3,2:T(8,128)(2,1)S(1)}, u32[]{:S(2)}, u32[]{:S(2)}) %collective-permute-start.3) | collective-permute-done | bytes 61472 | tf_op jit(solution)/shard_map/ppermute | solution.py:15
  59.8 9.2 %fusion.20 = (bf16[32,96,8,16]{1,0,3,2:T(8,128)(2,1)S(1)}, bf16[32,96,8,16]{1,0,3,2:T(8,128)(2,1)}, f32[32,96,8,16]{1,0,3,2:T(8,128)S(1)}, f32[32,96,8,16]{1,0,3,2:T(8,128)S(1)}) fusion(f32[96]{0:T(128)S(1)} %get-tuple-element.22, f32[96]{0:T(128)S(1)} %get-tuple-element.21, bf16[32,96,8,16]{1,0,3,2:T(8,128)(2,1)S(1)} %bitcast.111, ...), kind=kOutput, calls=%fused_computation.21 | convolution fusion | flops 715186176 | bytes 6778752 | tf_op jit(solution)/shard_map/conv_general_dilated | solution.py:22
  69.1 1.0 add_convert_fusion.2
  70.1 1.6 %add_convert_fusion.1 = bf16[32,96,8,16]{1,0,3,2:T(8,128)(2,1)S(1)} fusion(bf16[32,96,8,16]{1,0,3,2:T(8,128)(2,1)S(1)} %add_convert_fusion.2, f32[96]{0:T(128)S(1)} %get-tuple-element.19, f32[96]{0:T(128)S(1)} %get-tuple-element.23, f32[96]{0:T(128)S(1)} %get-tuple-element.20, f32[96]{0:T(128)S(1)} %get-tuple-element.21, f32[96]{0:T(128)S(1)} %get-tuple-element.22), kind=kLoop, calls=%fused_computation.25 | loop fusion | flops 5898240 | bytes 1574784 | tf_op jit(solution)/shard_map/convert_element_type | solution.py:94
  71.7 1.4 %copy.35 = bf16[32,96,8,16]{1,3,2,0:T(8,128)(2,1)} copy(bf16[32,96,8,16]{1,0,3,2:T(8,128)(2,1)S(1)} %add_convert_fusion.1) | data formatting | bytes 1572864 | tf_op jit(solution)/shard_map/convert_element_type | solution.py:94
  73.1 6.5 %all-to-all-start = ((bf16[32,96,8,16]{1,3,2,0:T(8,128)(2,1)}), bf16[32,96,8,16]{1,3,2,0:T(8,128)(2,1)S(1)}, u32[]{:S(2)}, u32[]{:S(2)}) async-start(bf16[32,96,8,16]{1,3,2,0:T(8,128)(2,1)} %copy.35), calls=%async_computation | async-start | bytes 2097152 | tf_op jit(solution)/shard_map/all_to_all | solution.py:33
  79.6 1.9 %collective-permute-start.4 = (bf16[32,96,1,16]{1,0,3,2:T(8,128)(2,1)S(1)}, bf16[32,96,1,16]{1,0,3,2:T(8,128)(2,1)S(1)}, u32[]{:S(2)}, u32[]{:S(2)}) collective-permute-start(bf16[32,96,1,16]{1,0,3,2:T(8,128)(2,1)S(1)} %get-tuple-element.15), channel_id=1, source_target_pairs={{0,4},{4,8},{8,12},{12,16},{16,20},{20,24},{24,28},{28,32},{32,36}... | collective-permute-start | bytes 294920 | tf_op jit(solution)/shard_map/ppermute | solution.py:14
  81.5 8.4 %collective-permute-start.5 = (bf16[32,96,1,16]{1,0,3,2:T(8,128)(2,1)S(1)}, bf16[32,96,1,16]{1,0,3,2:T(8,128)(2,1)S(1)}, u32[]{:S(2)}, u32[]{:S(2)}) collective-permute-start(bf16[32,96,1,16]{1,0,3,2:T(8,128)(2,1)S(1)} %get-tuple-element.16), channel_id=1, source_target_pairs={{4,0},{8,4},{12,8},{16,12},{20,16},{24,20},{28,24},{32,28},{36,32}... | collective-permute-start | bytes 294920 | tf_op jit(solution)/shard_map/ppermute | solution.py:15
  90.0 5.6 %collective-permute-done.4 = bf16[32,96,1,16]{1,0,3,2:T(8,128)(2,1)S(1)} collective-permute-done((bf16[32,96,1,16]{1,0,3,2:T(8,128)(2,1)S(1)}, bf16[32,96,1,16]{1,0,3,2:T(8,128)(2,1)S(1)}, u32[]{:S(2)}, u32[]{:S(2)}) %collective-permute-start.4) | collective-permute-done | bytes 98336 | tf_op jit(solution)/shard_map/ppermute | solution.py:14
  95.6 0.0 collective-permute-done.5
  95.6 11.7 %collective-permute-start.6 = (bf16[32,96,10,1]{1,0,3,2:T(8,128)(2,1)S(1)}, bf16[32,96,10,1]{1,0,3,2:T(8,128)(2,1)S(1)}, u32[]{:S(2)}, u32[]{:S(2)}) collective-permute-start(bf16[32,96,10,1]{1,0,3,2:T(8,128)(2,1)S(1)} %get-tuple-element.11), channel_id=1, source_target_pairs={{0,1},{1,2},{2,3},{3,64},{64,65},{65,66},{66,67},{67,128},{128,129... | collective-permute-start | bytes 184328 | tf_op jit(solution)/shard_map/ppermute | solution.py:14
  107.3 2.1 %collective-permute-start.7 = (bf16[32,96,10,1]{1,0,3,2:T(8,128)(2,1)S(1)}, bf16[32,96,10,1]{1,0,3,2:T(8,128)(2,1)S(1)}, u32[]{:S(2)}, u32[]{:S(2)}) collective-permute-start(bf16[32,96,10,1]{1,0,3,2:T(8,128)(2,1)S(1)} %get-tuple-element.12), channel_id=1, source_target_pairs={{1,0},{2,1},{3,2},{64,3},{65,64},{66,65},{67,66},{128,67},{129,128... | collective-permute-start | bytes 184328 | tf_op jit(solution)/shard_map/ppermute | solution.py:15
  109.5 0.0 collective-permute-done.6
  109.5 6.3 %collective-permute-done.7 = bf16[32,96,10,1]{1,0,3,2:T(8,128)(2,1)S(1)} collective-permute-done((bf16[32,96,10,1]{1,0,3,2:T(8,128)(2,1)S(1)}, bf16[32,96,10,1]{1,0,3,2:T(8,128)(2,1)S(1)}, u32[]{:S(2)}, u32[]{:S(2)}) %collective-permute-start.7) | collective-permute-done | bytes 61472 | tf_op jit(solution)/shard_map/ppermute | solution.py:15
  115.8 2.6 %fusion.22 = bf16[32,96,8,16]{1,0,3,2:T(8,128)(2,1)S(1)} fusion(bf16[32,96,8,16]{1,0,3,2:T(8,128)(2,1)S(1)} %copy-done.10, bf16[3,3,96,96]{3,2,1,0:T(8,128)(2,1)S(1)} %copy-done, bf16[32,96,10,1]{1,0,3,2:T(8,128)(2,1)S(1)} %collective-permute-done.7, bf16[32,96,1,16]{1,0,3,2:T(8,128)(2,1)S(1)} %collective-permute-done.5, ...), kind=kOutput, calls=%fused_computation.23 | convolution fusion | flops 682868736 | bytes 2844672 | tf_op jit(solution)/shard_map/conv_general_dilated | solution.py:22
  118.5 1.4 %copy.49 = bf16[32,96,8,16]{1,3,2,0:T(8,128)(2,1)} copy(bf16[32,96,8,16]{1,0,3,2:T(8,128)(2,1)S(1)} %fusion.22) | data formatting | bytes 1572864
  119.8 0.0 all-to-all-done
  119.8 0.2 copy.36
  120.1 0.0 copy-start.8
  120.1 0.4 fusion.45
  120.5 0.5 copy.37
  121.1 4.1 %fusion.77 = f32[2,8,310,1]{2,1,0,3:T(8,128)S(1)} fusion(f32[2,8,310]{2,1,0:T(8,128)S(1)} %copy-done.8, s32[28]{0:T(128)S(1)} %copy-done.9, f32[2,28,8,256]{3,1,2,0:T(8,128)S(1)} %fusion.45), kind=kOutput, calls=%fused_computation.81 | convolution fusion | flops 431088480 | bytes 498544 | tf_op jit(solution)/shard_map/fbqw,bwv->fqv/dot_general | solution.py:62
  125.2 0.0 copy-start.6
  125.2 3.2 %fusion.62 = bf16[2,28,8,256]{3,2,0,1:T(8,128)(2,1)S(1)} fusion(f32[2,8,310,1]{2,1,0,3:T(8,128)S(1)} %fusion.77, s32[28]{0:T(128)S(1)} %copy-done.9, f32[2,8,256]{2,1,0:T(8,128)S(1)} %convert_element_type.86), kind=kOutput, calls=%fused_computation.76 | convolution fusion | flops 431312896 | bytes 265712 | tf_op jit(solution)/shard_map/fqv,bwv->fbqw/dot_general | solution.py:72
  128.5 0.4 fusion.29
  128.9 1.3 %copy.48 = bf16[2,96,8,256]{3,2,1,0:T(8,128)(2,1)} copy(bf16[2,96,8,256]{3,1,2,0:T(8,128)(2,1)S(1)} %fusion.29) | data formatting | bytes 1572864
  (24 shorter events, 0.2 us)
Async XLA Ops:
  0.6 59.2 %copy-start = (bf16[3,3,96,96]{3,2,1,0:T(8,128)(2,1)S(1)}, bf16[3,3,96,96]{3,2,1,0:T(8,128)(2,1)}, u32[]{:S(2)}) copy-start(bf16[3,3,96,96]{3,2,1,0:T(8,128)(2,1)} %param.10) | copy-start | bytes 497668
  2.8 4.9 %copy-start.9 = (s32[28]{0:T(128)S(1)}, s32[28]{0:T(128)}, u32[]{:S(2)}) copy-start(s32[28]{0:T(128)} %param.16) | copy-start | bytes 340
  7.7 3.3 %copy-start.2 = (bf16[2,96,8,256]{3,2,1,0:T(8,128)(2,1)S(1)}, bf16[2,96,8,256]{3,2,1,0:T(8,128)(2,1)}, u32[]{:S(2)}) copy-start(bf16[2,96,8,256]{3,2,1,0:T(8,128)(2,1)} %param.17) | copy-start | bytes 2359300
  7.7 3.2 %copy-start.5 = (bf16[96,28]{0,1:T(8,128)(2,1)S(1)}, bf16[96,28]{0,1:T(8,128)(2,1)}, u32[]{:S(2)}) copy-start(bf16[96,28]{0,1:T(8,128)(2,1)} %param.12) | copy-start | bytes 16132
  11.4 9.7 %copy-start.1 = (bf16[32,96,8,16]{1,3,2,0:T(8,128)(2,1)S(1)}, bf16[32,96,8,16]{1,3,2,0:T(8,128)(2,1)}, u32[]{:S(2)}) copy-start(bf16[32,96,8,16]{1,3,2,0:T(8,128)(2,1)} %param.9) | copy-start | bytes 2359300
  13.2 40.3 %all-to-all-start.1 = ((bf16[2,96,8,256]{1,2,0,3:T(8,128)(2,1)}), bf16[2,96,8,256]{1,2,0,3:T(8,128)(2,1)S(1)}, u32[]{:S(2)}, u32[]{:S(2)}) async-start(bf16[2,96,8,256]{1,2,0,3:T(8,128)(2,1)} %copy.45), calls=%async_computation.1 | async-start | bytes 2097152 | tf_op jit(solution)/shard_map/all_to_all | solution.py:37
  21.1 32.3 %copy-start.7 = (f32[96,5]{0,1:T(8,128)S(1)}, f32[96,5]{0,1:T(8,128)}, u32[]{:S(2)}) copy-start(f32[96,5]{0,1:T(8,128)} %param.11) | copy-start | bytes 5764
  21.2 17.1 %collective-permute-start = (bf16[32,96,1,16]{1,0,3,2:T(8,128)(2,1)S(1)}, bf16[32,96,1,16]{1,0,3,2:T(8,128)(2,1)S(1)}, u32[]{:S(2)}, u32[]{:S(2)}) collective-permute-start(bf16[32,96,1,16]{1,0,3,2:T(8,128)(2,1)S(1)} %copy.72), channel_id=1, source_target_pairs={{0,4},{4,8},{8,12},{12,16},{16,20},{20,24},{24,28},{28,32},{32,36}... | collective-permute-start | bytes 294920 | tf_op jit(solution)/shard_map/ppermute | solution.py:14
  23.2 15.9 %collective-permute-start.1 = (bf16[32,96,1,16]{1,0,3,2:T(8,128)(2,1)S(1)}, bf16[32,96,1,16]{1,0,3,2:T(8,128)(2,1)S(1)}, u32[]{:S(2)}, u32[]{:S(2)}) collective-permute-start(bf16[32,96,1,16]{1,0,3,2:T(8,128)(2,1)S(1)} %copy.73), channel_id=1, source_target_pairs={{4,0},{8,4},{12,8},{16,12},{20,16},{24,20},{28,24},{32,28},{36,32}... | collective-permute-start | bytes 294920 | tf_op jit(solution)/shard_map/ppermute | solution.py:15
  39.1 14.3 %copy-start.3 = (bf16[32,96,10,16]{1,0,3,2:T(8,128)(2,1)}, bf16[32,96,10,16]{1,0,3,2:T(8,128)(2,1)S(1)}, u32[]{:S(2)}) copy-start(bf16[32,96,10,16]{1,0,3,2:T(8,128)(2,1)S(1)} %constant_dynamic-update-slice_fusion) | copy-start | bytes 2949124
  39.1 15.1 %collective-permute-start.2 = (bf16[32,96,10,1]{1,0,3,2:T(8,128)(2,1)S(1)}, bf16[32,96,10,1]{1,0,3,2:T(8,128)(2,1)S(1)}, u32[]{:S(2)}, u32[]{:S(2)}) collective-permute-start(bf16[32,96,10,1]{1,0,3,2:T(8,128)(2,1)S(1)} %get-tuple-element.13), channel_id=1, source_target_pairs={{0,1},{1,2},{2,3},{3,64},{64,65},{65,66},{66,67},{67,128},{128,129... | collective-permute-start | bytes 184328 | tf_op jit(solution)/shard_map/ppermute | solution.py:14
  51.3 8.5 %collective-permute-start.3 = (bf16[32,96,10,1]{1,0,3,2:T(8,128)(2,1)S(1)}, bf16[32,96,10,1]{1,0,3,2:T(8,128)(2,1)S(1)}, u32[]{:S(2)}, u32[]{:S(2)}) collective-permute-start(bf16[32,96,10,1]{1,0,3,2:T(8,128)(2,1)S(1)} %get-tuple-element.14), channel_id=1, source_target_pairs={{1,0},{2,1},{3,2},{64,3},{65,64},{66,65},{67,66},{128,67},{129,128... | collective-permute-start | bytes 184328 | tf_op jit(solution)/shard_map/ppermute | solution.py:15
  53.4 6.4 %copy-start.4 = (bf16[32,96,10,16]{1,0,3,2:T(8,128)(2,1)S(1)}, bf16[32,96,10,16]{1,0,3,2:T(8,128)(2,1)}, u32[]{:S(2)}) copy-start(bf16[32,96,10,16]{1,0,3,2:T(8,128)(2,1)} %copy-done.3) | copy-start | bytes 2949124
  73.1 42.7 %copy-start.10 = (bf16[32,96,8,16]{1,0,3,2:T(8,128)(2,1)S(1)}, bf16[32,96,8,16]{1,0,3,2:T(8,128)(2,1)}, u32[]{:S(2)}) copy-start(bf16[32,96,8,16]{1,0,3,2:T(8,128)(2,1)} %get-tuple-element.9) | copy-start | bytes 2359300
  73.1 46.7 %all-to-all-start = ((bf16[32,96,8,16]{1,3,2,0:T(8,128)(2,1)}), bf16[32,96,8,16]{1,3,2,0:T(8,128)(2,1)S(1)}, u32[]{:S(2)}, u32[]{:S(2)}) async-start(bf16[32,96,8,16]{1,3,2,0:T(8,128)(2,1)} %copy.35), calls=%async_computation | async-start | bytes 2097152 | tf_op jit(solution)/shard_map/all_to_all | solution.py:33
  79.6 16.0 %collective-permute-start.4 = (bf16[32,96,1,16]{1,0,3,2:T(8,128)(2,1)S(1)}, bf16[32,96,1,16]{1,0,3,2:T(8,128)(2,1)S(1)}, u32[]{:S(2)}, u32[]{:S(2)}) collective-permute-start(bf16[32,96,1,16]{1,0,3,2:T(8,128)(2,1)S(1)} %get-tuple-element.15), channel_id=1, source_target_pairs={{0,4},{4,8},{8,12},{12,16},{16,20},{20,24},{24,28},{28,32},{32,36}... | collective-permute-start | bytes 294920 | tf_op jit(solution)/shard_map/ppermute | solution.py:14
  81.5 14.1 %collective-permute-start.5 = (bf16[32,96,1,16]{1,0,3,2:T(8,128)(2,1)S(1)}, bf16[32,96,1,16]{1,0,3,2:T(8,128)(2,1)S(1)}, u32[]{:S(2)}, u32[]{:S(2)}) collective-permute-start(bf16[32,96,1,16]{1,0,3,2:T(8,128)(2,1)S(1)} %get-tuple-element.16), channel_id=1, source_target_pairs={{4,0},{8,4},{12,8},{16,12},{20,16},{24,20},{28,24},{32,28},{36,32}... | collective-permute-start | bytes 294920 | tf_op jit(solution)/shard_map/ppermute | solution.py:15
  95.6 13.9 %collective-permute-start.6 = (bf16[32,96,10,1]{1,0,3,2:T(8,128)(2,1)S(1)}, bf16[32,96,10,1]{1,0,3,2:T(8,128)(2,1)S(1)}, u32[]{:S(2)}, u32[]{:S(2)}) collective-permute-start(bf16[32,96,10,1]{1,0,3,2:T(8,128)(2,1)S(1)} %get-tuple-element.11), channel_id=1, source_target_pairs={{0,1},{1,2},{2,3},{3,64},{64,65},{65,66},{66,67},{67,128},{128,129... | collective-permute-start | bytes 184328 | tf_op jit(solution)/shard_map/ppermute | solution.py:14
  107.3 8.4 %collective-permute-start.7 = (bf16[32,96,10,1]{1,0,3,2:T(8,128)(2,1)S(1)}, bf16[32,96,10,1]{1,0,3,2:T(8,128)(2,1)S(1)}, u32[]{:S(2)}, u32[]{:S(2)}) collective-permute-start(bf16[32,96,10,1]{1,0,3,2:T(8,128)(2,1)S(1)} %get-tuple-element.12), channel_id=1, source_target_pairs={{1,0},{2,1},{3,2},{64,3},{65,64},{66,65},{67,66},{128,67},{129,128... | collective-permute-start | bytes 184328 | tf_op jit(solution)/shard_map/ppermute | solution.py:15
  120.1 1.0 copy-start.8
  125.2 3.2 %copy-start.6 = (bf16[28,96]{1,0:T(8,128)(2,1)S(1)}, bf16[28,96]{1,0:T(8,128)(2,1)}, u32[]{:S(2)}) copy-start(bf16[28,96]{1,0:T(8,128)(2,1)} %param.13) | copy-start | bytes 16132

commit v2 on v1

--- a/solution.py
+++ b/solution.py
@@ -17,8 +17,7 @@
     return array
 
 
-def spatial_conv(field_in, kernel):
-    padded = with_halo(field_in, (("row", 2), (("ta", "col"), 3)), 1)
+def valid_conv(padded, kernel):
     return lax.conv_general_dilated(
         padded,
         kernel,
@@ -29,12 +28,20 @@
     )
 
 
+def to_space_haloed(field_in):
+    blocks = lax.axis_size(("ta", "col"))
+    rows = with_halo(field_in, (("row", 2),), 1)
+    wide = jnp.pad(rows, ((0, 0), (0, 0), (0, 0), (1, 1)))
+    block_cols = field_in.shape[3] // blocks
+    windows = jnp.stack(
+        [wide[..., j * block_cols : j * block_cols + block_cols + 2] for j in range(blocks)]
+    )
+    gathered = lax.all_to_all(windows, ("ta", "col"), split_axis=0, concat_axis=1, tiled=True)
+    return gathered[0]
+
+
 def to_time(field_in):
     return lax.all_to_all(field_in, ("ta", "col"), split_axis=0, concat_axis=3, tiled=True)
-
-
-def to_space(field_in):
-    return lax.all_to_all(field_in, ("ta", "col"), split_axis=3, concat_axis=0, tiled=True)
 
 
 def time_mix(frames_in, time_taps):
@@ -89,7 +96,9 @@
     dispersion,
     update_cot,
 ):
-    pre_act = spatial_conv(features, conv_weight)
+    feature_halo = with_halo(features, (("row", 2), (("ta", "col"), 3)), 2)
+    pre_act_wide = valid_conv(feature_halo, conv_weight)
+    pre_act = pre_act_wide[:, :, 1:-1, 1:-1]
     hidden_state = (features.astype(jnp.float32) + gelu_exact(pre_act)).astype(jnp.bfloat16)
     temporal = to_time(time_mix(hidden_state, time_weight).astype(jnp.bfloat16))
     width_keep = aperture.shape[-1]
@@ -116,13 +125,14 @@
         + jnp.einsum("fbqw,cb->fcqw", band_grad, band_out, preferred_element_type=jnp.float32)
     ).astype(jnp.bfloat16)
     flipped = time_weight[:, ::-1]
-    cot_hidden = time_mix(to_space(cot_temporal), flipped).astype(jnp.bfloat16)
-    pullback = jax.vjp(gelu_exact, pre_act)[1]
-    gate_grad = pullback(cot_hidden.astype(jnp.float32))[0].astype(jnp.bfloat16)
+    cot_hidden_wide = time_mix(to_space_haloed(cot_temporal), flipped).astype(jnp.bfloat16)
+    pullback = jax.vjp(gelu_exact, pre_act_wide)[1]
+    gate_grad_wide = pullback(cot_hidden_wide.astype(jnp.float32))[0].astype(jnp.bfloat16)
     kernel_flip = jnp.transpose(conv_weight[::-1, ::-1], (0, 1, 3, 2))
-    features_grad = (cot_hidden.astype(jnp.float32) + spatial_conv(gate_grad, kernel_flip)).astype(
-        jnp.bfloat16
-    )
+    cot_hidden = cot_hidden_wide[:, :, 1:-1, 1:-1]
+    features_grad = (
+        cot_hidden.astype(jnp.float32) + valid_conv(gate_grad_wide, kernel_flip)
+    ).astype(jnp.bfloat16)
     return (updated, features_grad)
 
 

time: 131 us -> 155 us (1.18)
  the two profiles are of different devices: /device:TPU:86 before, /device:TPU:56 now
where the time goes in v2:
time: 155 us; the launch traced here: 154 us
  starting transfers between devices  43.7 us (28%)
  waiting for transfers between devices  35.5 us (23%)
  local copies, waits for them, and re-layouts  33.5 us (22%)
  matrix products  30.7 us (20%)
  other arithmetic  9.64 us (6%)
    all_to_all x1, waiting for transfers between devices, to_space_haloed(): lax.all_to_all(windows, ('ta', 'col'), split_axis=0, concat_axis=1, tiled...  22.3 us
    ppermute x3, starting transfers between devices, with_halo(): after = lax.ppermute(initial, axis, down)  21.6 us
    unnamed x63, local copies, waits for them, and re-layouts  18.6 us
    conv_general_dilated x2, matrix products, valid_conv(): lax.conv_general_dilated(padded, kernel, window_strides=(1, 1), padding='...  11.8 us
    all_to_all x1, waiting for transfers between devices, to_time(): lax.all_to_all(field_in, ('ta', 'col'), split_axis=0, concat_axis=3, tile...  10.4 us
    another operation x2, local copies, waits for them, and re-layouts, to_space_haloed(): jnp.stack([wide[..., j * block_cols:j * block_cols + block_cols + 2] for...  10.2 us
    dot_general x2, matrix products, disperse(): jnp.einsum('fbqw,bwv->fqv', masked, table, precision=lax.Precision.HIGHES...  9.67 us
    all_to_all x1, starting transfers between devices, to_time(): lax.all_to_all(field_in, ('ta', 'col'), split_axis=0, concat_axis=3, tile...  9.18 us
  transfers between devices with their start and end apart: 8, of which 4 were waited for; matrix products, arithmetic and copies ran while one was open for 25% of the time, Pallas kernels for 0%

profile of v2, /device:TPU:56, one launch (start us, length us, event | category | flops | bytes accessed | tf_op | source)
XLA Modules:
  0.0 154.2 jit_solution(16316758206754858525)
XLA Ops:
  0.6 0.8 convert_element_type.91
  1.4 1.4 fusion.50
  2.8 4.8 %fusion.75 = f32[2,8,310,1]{2,1,0,3:T(8,128)S(1)} fusion(s32[28]{0:T(128)} %param.16, f32[2,28,8,256]{3,1,2,0:T(8,128)S(1)} %fusion.50), kind=kOutput, calls=%fused_computation.92 | convolution fusion | flops 431083520 | bytes 478704 | tf_op jit(solution)/shard_map/fbqw,bwv->fqv/dot_general | solution.py:69
  7.7 3.2 %fusion.69 = bf16[2,28,8,256]{3,2,0,1:T(8,128)(2,1)S(1)} fusion(f32[2,8,310,1]{2,1,0,3:T(8,128)S(1)} %fusion.75, s32[28]{0:T(128)S(1)} %copy-done.19, f32[2,8,256]{2,1,0:T(8,128)S(1)} %convert_element_type.91), kind=kOutput, calls=%fused_computation.90 | convolution fusion | flops 431427584 | bytes 265712 | tf_op jit(solution)/shard_map/fqv,bwv->fbqw/dot_general | solution.py:79
  11.4 1.9 %collective-permute-start.4 = (bf16[2,96,1,256]{3,1,2,0:T(8,128)(2,1)S(1)}, bf16[2,96,1,256]{3,1,2,0:T(8,128)(2,1)S(1)}, u32[]{:S(2)}, u32[]{:S(2)}) collective-permute-start(bf16[2,96,1,256]{3,1,2,0:T(8,128)(2,1)S(1)} %get-tuple-element.14), channel_id=1, source_target_pairs={{0,4},{4,8},{8,12},{12,16},{16,20},{20,24},{24,28},{28,32},{32,36}... | collective-permute-start | bytes 294920 | tf_op jit(solution)/shard_map/ppermute | solution.py:14
  13.3 8.4 %collective-permute-start.5 = (bf16[2,96,1,256]{3,1,2,0:T(8,128)(2,1)S(1)}, bf16[2,96,1,256]{3,1,2,0:T(8,128)(2,1)S(1)}, u32[]{:S(2)}, u32[]{:S(2)}) collective-permute-start(bf16[2,96,1,256]{3,1,2,0:T(8,128)(2,1)S(1)} %get-tuple-element.15), channel_id=1, source_target_pairs={{4,0},{8,4},{12,8},{16,12},{20,16},{24,20},{28,24},{32,28},{36,32}... | collective-permute-start | bytes 294920 | tf_op jit(solution)/shard_map/ppermute | solution.py:15
  21.9 1.9 %collective-permute-start = (bf16[32,96,2,16]{1,0,3,2:T(8,128)(2,1)S(1)}, bf16[32,96,2,16]{1,0,3,2:T(8,128)(2,1)S(1)}, u32[]{:S(2)}, u32[]{:S(2)}) collective-permute-start(bf16[32,96,2,16]{1,0,3,2:T(8,128)(2,1)S(1)} %copy.101), channel_id=1, source_target_pairs={{0,4},{4,8},{8,12},{12,16},{16,20},{20,24},{24,28},{28,32},{32,36}... | collective-permute-start | bytes 589832 | tf_op jit(solution)/shard_map/ppermute | solution.py:14
  24.0 8.4 %collective-permute-start.1 = (bf16[32,96,2,16]{1,0,3,2:T(8,128)(2,1)S(1)}, bf16[32,96,2,16]{1,0,3,2:T(8,128)(2,1)S(1)}, u32[]{:S(2)}, u32[]{:S(2)}) collective-permute-start(bf16[32,96,2,16]{1,0,3,2:T(8,128)(2,1)S(1)} %copy.102), channel_id=1, source_target_pairs={{4,0},{8,4},{12,8},{16,12},{20,16},{24,20},{28,24},{32,28},{36,32}... | collective-permute-start | bytes 589832 | tf_op jit(solution)/shard_map/ppermute | solution.py:15
  32.7 1.0 fusion.86
  33.7 1.0 fusion.102
  34.6 1.0 fusion.101
  35.6 1.0 fusion.100
  36.6 1.0 fusion.99
  37.6 1.0 fusion.98
  38.6 1.0 fusion.97
  39.6 1.0 fusion.96
  40.6 0.7 constant_dynamic-update-slice_fusion.1
  41.4 3.4 %collective-permute-start.2 = (bf16[32,96,12,2]{1,0,3,2:T(8,128)(2,1)S(1)}, bf16[32,96,12,2]{1,0,3,2:T(8,128)(2,1)S(1)}, u32[]{:S(2)}, u32[]{:S(2)}) collective-permute-start(bf16[32,96,12,2]{1,0,3,2:T(8,128)(2,1)S(1)} %get-tuple-element.10), channel_id=1, source_target_pairs={{0,1},{1,2},{2,3},{3,64},{64,65},{65,66},{66,67},{67,128},{128,129... | collective-permute-start | bytes 442376 | tf_op jit(solution)/shard_map/ppermute | solution.py:14
  44.8 4.7 %collective-permute-start.3 = (bf16[32,96,12,2]{1,0,3,2:T(8,128)(2,1)S(1)}, bf16[32,96,12,2]{1,0,3,2:T(8,128)(2,1)S(1)}, u32[]{:S(2)}, u32[]{:S(2)}) collective-permute-start(bf16[32,96,12,2]{1,0,3,2:T(8,128)(2,1)S(1)} %get-tuple-element.11), channel_id=1, source_target_pairs={{1,0},{2,1},{3,2},{64,3},{65,64},{66,65},{67,66},{128,67},{129,128... | collective-permute-start | bytes 442376 | tf_op jit(solution)/shard_map/ppermute | solution.py:15
  49.6 1.0 fusion.95
  50.6 1.6 %collective-permute-done.2 = bf16[32,96,12,2]{1,0,3,2:T(8,128)(2,1)S(1)} collective-permute-done((bf16[32,96,12,2]{1,0,3,2:T(8,128)(2,1)S(1)}, bf16[32,96,12,2]{1,0,3,2:T(8,128)(2,1)S(1)}, u32[]{:S(2)}, u32[]{:S(2)}) %collective-permute-start.2) | collective-permute-done | bytes 147488 | tf_op jit(solution)/shard_map/ppermute | solution.py:14
  52.1 1.2 collective-permute-done.3
  53.3 2.9 %fusion.40 = f32[32,96,10,18]{1,0,3,2:T(8,128)S(1)} fusion(bf16[3,3,96,96]{3,2,1,0:T(8,128)(2,1)S(1)} %copy-done, bf16[32,96,12,2]{1,0,3,2:T(8,128)(2,1)S(1)} %collective-permute-done.3, bf16[32,96,12,16]{1,0,3,2:T(8,128)(2,1)S(1)} %constant_dynamic-update-slice_fusion, bf16[32,96,12,2]{1,0,3,2:T(8,128)(2,1)S(1)} %collective-permute-done.2), kind=kOutput, calls=%fused_computation.60 | convolution fusion | flops 956989440 | bytes 3852288 | tf_op jit(solution)/shard_map/conv_general_dilated | solution.py:21
  56.3 4.8 %fusion.32 = bf16[32,96,8,16]{1,0,3,2:T(8,128)(2,1)S(1)} fusion(f32[32,96,10,18]{1,0,3,2:T(8,128)S(1)} %fusion.40, bf16[32,96,8,16]{1,3,2,0:T(8,128)(2,1)S(1)} %copy-done.1), kind=kLoop, calls=%fused_computation.42 | loop fusion | flops 26345472 | bytes 3145728 | tf_op jit(solution)/shard_map/convert_element_type | solution.py:102
  61.2 1.6 %add_convert_fusion.2 = bf16[32,96,8,16]{1,0,3,2:T(8,128)(2,1)S(1)} fusion(bf16[32,96,8,16]{1,0,3,2:T(8,128)(2,1)S(1)} %fusion.32, f32[96]{0:T(128)S(1)} %get-tuple-element.19, f32[96]{0:T(128)S(1)} %get-tuple-element.20, f32[96]{0:T(128)S(1)} %get-tuple-element.17, f32[96]{0:T(128)S(1)} %get-tuple-element.18, f32[96]{0:T(128)S(1)} %get-tuple-element.16), kind=kLoop, calls=%fused_computation.44 | loop fusion | flops 5898240 | bytes 1574784 | tf_op jit(solution)/shard_map/convert_element_type | solution.py:103
  62.8 1.4 copy.68
  64.1 9.2 %all-to-all-start = ((bf16[32,96,8,16]{1,3,2,0:T(8,128)(2,1)}), bf16[32,96,8,16]{1,3,2,0:T(8,128)(2,1)S(1)}, u32[]{:S(2)}, u32[]{:S(2)}) async-start(bf16[32,96,8,16]{1,3,2,0:T(8,128)(2,1)} %copy.68), calls=%async_computation | async-start | bytes 2097152 | tf_op jit(solution)/shard_map/all_to_all | solution.py:44
  73.3 1.0 fusion.94
  74.3 1.0 fusion.93
  75.3 1.0 fusion.92
  76.3 1.0 fusion.91
  77.3 1.0 fusion.90
  78.3 1.0 fusion.89
  79.3 1.0 fusion.88
  80.3 9.2 %copy.78 = bf16[16,2,96,10,18]{2,1,4,3,0:T(2,128)(2,1)} copy(bf16[16,2,96,10,18]{4,2,3,1,0:T(8,128)(2,1)} %fusion.88) | data formatting | bytes 2211840 | tf_op jit(solution)/shard_map/stack | solution.py:36
  89.5 10.4 %all-to-all-done = bf16[32,96,8,16]{1,3,2,0:T(8,128)(2,1)S(1)} async-done(((bf16[32,96,8,16]{1,3,2,0:T(8,128)(2,1)}), bf16[32,96,8,16]{1,3,2,0:T(8,128)(2,1)S(1)}, u32[]{:S(2)}, u32[]{:S(2)}) %all-to-all-start) | async-done | bytes 786464 | tf_op jit(solution)/shard_map/all_to_all | solution.py:44
  99.9 5.7 %all-to-all-start.1 = ((bf16[16,2,96,10,18]{2,1,4,3,0:T(2,128)(2,1)}), bf16[16,2,96,10,18]{2,1,4,3,0:T(2,128)(2,1)S(1)}, u32[]{:S(2)}, u32[]{:S(2)}) async-start(bf16[16,2,96,10,18]{2,1,4,3,0:T(2,128)(2,1)} %copy.78), calls=%async_computation.1 | async-start | bytes 2949120 | tf_op jit(solution)/shard_map/all_to_all | solution.py:39
  105.6 1.5 copy.69
  107.1 0.5 copy.70
  108.1 4.9 %fusion.81 = f32[2,8,310,1]{2,1,0,3:T(8,128)S(1)} fusion(f32[2,8,310]{2,1,0:T(8,128)} %param.14, s32[28]{0:T(128)} %param.16, f32[2,28,8,256]{3,1,2,0:T(8,128)S(1)} %fusion.49), kind=kOutput, calls=%fused_computation.94 | convolution fusion | flops 431088480 | bytes 498544 | tf_op jit(solution)/shard_map/fbqw,bwv->fqv/dot_general | solution.py:69
  113.0 3.2 %fusion.66 = bf16[2,28,8,256]{3,2,0,1:T(8,128)(2,1)S(1)} fusion(f32[2,8,310,1]{2,1,0,3:T(8,128)S(1)} %fusion.81, s32[28]{0:T(128)S(1)} %copy-done.20, f32[2,8,256]{2,1,0:T(8,128)S(1)} %convert_element_type.91), kind=kOutput, calls=%fused_computation.89 | convolution fusion | flops 431312896 | bytes 265712 | tf_op jit(solution)/shard_map/fqv,bwv->fbqw/dot_general | solution.py:79
  116.3 0.4 fusion.47
  116.7 1.3 copy.80
  118.0 22.3 %all-to-all-done.1 = bf16[16,2,96,10,18]{2,1,4,3,0:T(2,128)(2,1)S(1)} async-done(((bf16[16,2,96,10,18]{2,1,4,3,0:T(2,128)(2,1)}), bf16[16,2,96,10,18]{2,1,4,3,0:T(2,128)(2,1)S(1)}, u32[]{:S(2)}, u32[]{:S(2)}) %all-to-all-start.1) | async-done | bytes 1105952 | tf_op jit(solution)/shard_map/all_to_all | solution.py:39
  140.4 1.2 copy.79
  141.6 2.3 %add_convert_fusion = bf16[32,96,10,18]{1,0,3,2:T(8,128)(2,1)S(1)} fusion(bf16[32,96,10,18]{1,0,3,2:T(8,128)(2,1)S(1)} %bitcast.170, f32[96]{0:T(128)S(1)} %copy-done.9, f32[96]{0:T(128)S(1)} %copy-done.13, f32[96]{0:T(128)S(1)} %copy-done.11, f32[96]{0:T(128)S(1)} %copy-done.17, f32[96]{0:T(128)S(1)} %copy-done.15), kind=kLoop, calls=%fused_computation.35 | loop fusion | flops 8294400 | bytes 2213760 | tf_op jit(solution)/shard_map/convert_element_type | solution.py:128
  144.0 8.9 %add_convert_fusion.1 = bf16[32,96,8,16]{1,0,3,2:T(8,128)(2,1)S(1)} fusion(bf16[3,3,96,96]{3,2,1,0:T(8,128)(2,1)S(1)} %copy-done, bf16[32,96,10,18]{1,0,3,2:T(8,128)(2,1)S(1)} %add_convert_fusion, f32[32,96,10,18]{1,0,3,2:T(8,128)S(1)} %copy-done.5), kind=kOutput, calls=%fused_computation.43 | convolution fusion | flops 721022976 | bytes 6479872 | tf_op jit(solution)/shard_map/conv_general_dilated | solution.py:21
  152.8 1.4 copy.81
  (57 shorter events, 1.5 us)
Async XLA Ops:
  0.6 52.7 %copy-start = (bf16[3,3,96,96]{3,2,1,0:T(8,128)(2,1)S(1)}, bf16[3,3,96,96]{3,2,1,0:T(8,128)(2,1)}, u32[]{:S(2)}) copy-start(bf16[3,3,96,96]{3,2,1,0:T(8,128)(2,1)} %param.10) | copy-start | bytes 497668
  1.4 6.2 %copy-start.19 = (s32[28]{0:T(128)S(1)}, s32[28]{0:T(128)}, u32[]{:S(2)}) copy-start(s32[28]{0:T(128)} %param.16) | copy-start | bytes 340
  7.6 3.3 %copy-start.3 = (bf16[2,96,8,256]{3,2,1,0:T(8,128)(2,1)S(1)}, bf16[2,96,8,256]{3,2,1,0:T(8,128)(2,1)}, u32[]{:S(2)}) copy-start(bf16[2,96,8,256]{3,2,1,0:T(8,128)(2,1)} %param.17) | copy-start | bytes 2359300
  7.6 3.3 %copy-start.6 = (bf16[96,28]{0,1:T(8,128)(2,1)S(1)}, bf16[96,28]{0,1:T(8,128)(2,1)}, u32[]{:S(2)}) copy-start(bf16[96,28]{0,1:T(8,128)(2,1)} %param.12) | copy-start | bytes 16132
  7.7 14.1 %copy-start.1 = (bf16[32,96,8,16]{1,3,2,0:T(8,128)(2,1)S(1)}, bf16[32,96,8,16]{1,3,2,0:T(8,128)(2,1)}, u32[]{:S(2)}) copy-start(bf16[32,96,8,16]{1,3,2,0:T(8,128)(2,1)} %param.9) | copy-start | bytes 2359300
  10.9 21.5 %copy-start.18 = (f32[96,5]{0,1:T(8,128)S(1)}, f32[96,5]{0,1:T(8,128)}, u32[]{:S(2)}) copy-start(f32[96,5]{0,1:T(8,128)} %param.11) | copy-start | bytes 5764
  11.4 21.1 %collective-permute-start.4 = (bf16[2,96,1,256]{3,1,2,0:T(8,128)(2,1)S(1)}, bf16[2,96,1,256]{3,1,2,0:T(8,128)(2,1)S(1)}, u32[]{:S(2)}, u32[]{:S(2)}) collective-permute-start(bf16[2,96,1,256]{3,1,2,0:T(8,128)(2,1)S(1)} %get-tuple-element.14), channel_id=1, source_target_pairs={{0,4},{4,8},{8,12},{12,16},{16,20},{20,24},{24,28},{28,32},{32,36}... | collective-permute-start | bytes 294920 | tf_op jit(solution)/shard_map/ppermute | solution.py:14
  13.3 19.2 %collective-permute-start.5 = (bf16[2,96,1,256]{3,1,2,0:T(8,128)(2,1)S(1)}, bf16[2,96,1,256]{3,1,2,0:T(8,128)(2,1)S(1)}, u32[]{:S(2)}, u32[]{:S(2)}) collective-permute-start(bf16[2,96,1,256]{3,1,2,0:T(8,128)(2,1)S(1)} %get-tuple-element.15), channel_id=1, source_target_pairs={{4,0},{8,4},{12,8},{16,12},{20,16},{24,20},{28,24},{32,28},{36,32}... | collective-permute-start | bytes 294920 | tf_op jit(solution)/shard_map/ppermute | solution.py:15
  21.9 18.6 %collective-permute-start = (bf16[32,96,2,16]{1,0,3,2:T(8,128)(2,1)S(1)}, bf16[32,96,2,16]{1,0,3,2:T(8,128)(2,1)S(1)}, u32[]{:S(2)}, u32[]{:S(2)}) collective-permute-start(bf16[32,96,2,16]{1,0,3,2:T(8,128)(2,1)S(1)} %copy.101), channel_id=1, source_target_pairs={{0,4},{4,8},{8,12},{12,16},{16,20},{20,24},{24,28},{28,32},{32,36}... | collective-permute-start | bytes 589832 | tf_op jit(solution)/shard_map/ppermute | solution.py:14
  24.0 17.3 %collective-permute-start.1 = (bf16[32,96,2,16]{1,0,3,2:T(8,128)(2,1)S(1)}, bf16[32,96,2,16]{1,0,3,2:T(8,128)(2,1)S(1)}, u32[]{:S(2)}, u32[]{:S(2)}) collective-permute-start(bf16[32,96,2,16]{1,0,3,2:T(8,128)(2,1)S(1)} %copy.102), channel_id=1, source_target_pairs={{4,0},{8,4},{12,8},{16,12},{20,16},{24,20},{28,24},{32,28},{36,32}... | collective-permute-start | bytes 589832 | tf_op jit(solution)/shard_map/ppermute | solution.py:15
  32.5 28.7 %copy-start.8 = (f32[96]{0:T(128)}, f32[96]{0:T(128)S(1)}, u32[]{:S(2)}) copy-start(f32[96]{0:T(128)S(1)} %get-tuple-element.16) | copy-start | bytes 1156
  32.5 28.7 %copy-start.10 = (f32[96]{0:T(128)}, f32[96]{0:T(128)S(1)}, u32[]{:S(2)}) copy-start(f32[96]{0:T(128)S(1)} %get-tuple-element.17) | copy-start | bytes 1156
  32.5 28.7 %copy-start.12 = (f32[96]{0:T(128)}, f32[96]{0:T(128)S(1)}, u32[]{:S(2)}) copy-start(f32[96]{0:T(128)S(1)} %get-tuple-element.18) | copy-start | bytes 1156
  32.5 28.7 %copy-start.14 = (f32[96]{0:T(128)}, f32[96]{0:T(128)S(1)}, u32[]{:S(2)}) copy-start(f32[96]{0:T(128)S(1)} %get-tuple-element.19) | copy-start | bytes 1156
  32.5 28.7 %copy-start.16 = (f32[96]{0:T(128)}, f32[96]{0:T(128)S(1)}, u32[]{:S(2)}) copy-start(f32[96]{0:T(128)S(1)} %get-tuple-element.20) | copy-start | bytes 1156
  41.4 10.7 %collective-permute-start.2 = (bf16[32,96,12,2]{1,0,3,2:T(8,128)(2,1)S(1)}, bf16[32,96,12,2]{1,0,3,2:T(8,128)(2,1)S(1)}, u32[]{:S(2)}, u32[]{:S(2)}) collective-permute-start(bf16[32,96,12,2]{1,0,3,2:T(8,128)(2,1)S(1)} %get-tuple-element.10), channel_id=1, source_target_pairs={{0,1},{1,2},{2,3},{3,64},{64,65},{65,66},{66,67},{67,128},{128,129... | collective-permute-start | bytes 442376 | tf_op jit(solution)/shard_map/ppermute | solution.py:14
  44.8 8.5 %collective-permute-start.3 = (bf16[32,96,12,2]{1,0,3,2:T(8,128)(2,1)S(1)}, bf16[32,96,12,2]{1,0,3,2:T(8,128)(2,1)S(1)}, u32[]{:S(2)}, u32[]{:S(2)}) collective-permute-start(bf16[32,96,12,2]{1,0,3,2:T(8,128)(2,1)S(1)} %get-tuple-element.11), channel_id=1, source_target_pairs={{1,0},{2,1},{3,2},{64,3},{65,64},{66,65},{67,66},{128,67},{129,128... | collective-permute-start | bytes 442376 | tf_op jit(solution)/shard_map/ppermute | solution.py:15
  56.3 4.9 %copy-start.4 = (f32[32,96,10,18]{1,0,3,2:T(8,128)}, f32[32,96,10,18]{1,0,3,2:T(8,128)S(1)}, u32[]{:S(2)}) copy-start(f32[32,96,10,18]{1,0,3,2:T(8,128)S(1)} %fusion.40) | copy-start | bytes 6635524
  64.1 35.7 %all-to-all-start = ((bf16[32,96,8,16]{1,3,2,0:T(8,128)(2,1)}), bf16[32,96,8,16]{1,3,2,0:T(8,128)(2,1)S(1)}, u32[]{:S(2)}, u32[]{:S(2)}) async-start(bf16[32,96,8,16]{1,3,2,0:T(8,128)(2,1)} %copy.68), calls=%async_computation | async-start | bytes 2097152 | tf_op jit(solution)/shard_map/all_to_all | solution.py:44
  99.9 5.7 %copy-start.2 = (bf16[32,96,8,16]{1,3,2,0:T(8,128)(2,1)}, bf16[32,96,8,16]{1,3,2,0:T(8,128)(2,1)S(1)}, u32[]{:S(2)}) copy-start(bf16[32,96,8,16]{1,3,2,0:T(8,128)(2,1)S(1)} %all-to-all-done) | copy-start | bytes 2359300
  99.9 40.5 %all-to-all-start.1 = ((bf16[16,2,96,10,18]{2,1,4,3,0:T(2,128)(2,1)}), bf16[16,2,96,10,18]{2,1,4,3,0:T(2,128)(2,1)S(1)}, u32[]{:S(2)}, u32[]{:S(2)}) async-start(bf16[16,2,96,10,18]{2,1,4,3,0:T(2,128)(2,1)} %copy.78), calls=%async_computation.1 | async-start | bytes 2949120 | tf_op jit(solution)/shard_map/all_to_all | solution.py:39
  107.6 5.4 %copy-start.20 = (s32[28]{0:T(128)S(1)}, s32[28]{0:T(128)}, u32[]{:S(2)}) copy-start(s32[28]{0:T(128)} %param.16) | copy-start | bytes 340
  113.0 3.2 %copy-start.7 = (bf16[28,96]{1,0:T(8,128)(2,1)S(1)}, bf16[28,96]{1,0:T(8,128)(2,1)}, u32[]{:S(2)}) copy-start(bf16[28,96]{1,0:T(8,128)(2,1)} %param.13) | copy-start | bytes 16132
  116.2 25.4 %copy-start.9 = (f32[96]{0:T(128)S(1)}, f32[96]{0:T(128)}, u32[]{:S(2)}) copy-start(f32[96]{0:T(128)} %copy-done.8) | copy-start | bytes 1156
  116.2 25.4 %copy-start.11 = (f32[96]{0:T(128)S(1)}, f32[96]{0:T(128)}, u32[]{:S(2)}) copy-start(f32[96]{0:T(128)} %copy-done.10) | copy-start | bytes 1156
  116.2 25.4 %copy-start.13 = (f32[96]{0:T(128)S(1)}, f32[96]{0:T(128)}, u32[]{:S(2)}) copy-start(f32[96]{0:T(128)} %copy-done.12) | copy-start | bytes 1156
  116.3 25.4 %copy-start.15 = (f32[96]{0:T(128)S(1)}, f32[96]{0:T(128)}, u32[]{:S(2)}) copy-start(f32[96]{0:T(128)} %copy-done.14) | copy-start | bytes 1156
  116.3 25.4 %copy-start.17 = (f32[96]{0:T(128)S(1)}, f32[96]{0:T(128)}, u32[]{:S(2)}) copy-start(f32[96]{0:T(128)} %copy-done.16) | copy-start | bytes 1156
  140.4 3.6 %copy-start.5 = (f32[32,96,10,18]{1,0,3,2:T(8,128)S(1)}, f32[32,96,10,18]{1,0,3,2:T(8,128)}, u32[]{:S(2)}) copy-start(f32[32,96,10,18]{1,0,3,2:T(8,128)} %copy-done.4) | copy-start | bytes 6635524

commit v3 on v2

--- a/solution.py
+++ b/solution.py
@@ -31,11 +31,11 @@
 def to_space_haloed(field_in):
     blocks = lax.axis_size(("ta", "col"))
     rows = with_halo(field_in, (("row", 2),), 1)
-    wide = jnp.pad(rows, ((0, 0), (0, 0), (0, 0), (1, 1)))
-    block_cols = field_in.shape[3] // blocks
-    windows = jnp.stack(
-        [wide[..., j * block_cols : j * block_cols + block_cols + 2] for j in range(blocks)]
-    )
+    lead = rows.shape[:3]
+    split = rows.reshape(lead + (blocks, rows.shape[3] // blocks))
+    left = jnp.pad(split[..., :-1, -1:], ((0, 0),) * 3 + ((1, 0), (0, 0)))
+    right = jnp.pad(split[..., 1:, :1], ((0, 0),) * 3 + ((0, 1), (0, 0)))
+    windows = jnp.moveaxis(jnp.concatenate([left, split, right], axis=-1), 3, 0)
     gathered = lax.all_to_all(windows, ("ta", "col"), split_axis=0, concat_axis=1, tiled=True)
     return gathered[0]
 
@@ -98,8 +98,11 @@
 ):
     feature_halo = with_halo(features, (("row", 2), (("ta", "col"), 3)), 2)
     pre_act_wide = valid_conv(feature_halo, conv_weight)
-    pre_act = pre_act_wide[:, :, 1:-1, 1:-1]
-    hidden_state = (features.astype(jnp.float32) + gelu_exact(pre_act)).astype(jnp.bfloat16)
+    gelu_wide, pullback = jax.vjp(gelu_exact, pre_act_wide)
+    slope_wide = pullback(jnp.ones_like(pre_act_wide))[0]
+    hidden_state = (
+        features.astype(jnp.float32) + gelu_wide[:, :, 1:-1, 1:-1]
+    ).astype(jnp.bfloat16)
     temporal = to_time(time_mix(hidden_state, time_weight).astype(jnp.bfloat16))
     width_keep = aperture.shape[-1]
     width_wide = measured.shape[-1]
@@ -126,8 +129,9 @@
     ).astype(jnp.bfloat16)
     flipped = time_weight[:, ::-1]
     cot_hidden_wide = time_mix(to_space_haloed(cot_temporal), flipped).astype(jnp.bfloat16)
-    pullback = jax.vjp(gelu_exact, pre_act_wide)[1]
-    gate_grad_wide = pullback(cot_hidden_wide.astype(jnp.float32))[0].astype(jnp.bfloat16)
+    gate_grad_wide = lax.optimization_barrier(
+        (slope_wide * cot_hidden_wide.astype(jnp.float32)).astype(jnp.bfloat16)
+    )
     kernel_flip = jnp.transpose(conv_weight[::-1, ::-1], (0, 1, 3, 2))
     cot_hidden = cot_hidden_wide[:, :, 1:-1, 1:-1]
     features_grad = (

time: 155 us -> 149 us (0.961)
  the two profiles are of different devices: /device:TPU:56 before, /device:TPU:40 now
where the time goes in v3:
time: 149 us
  starting transfers between devices  51.4 us (34%)
  waiting for transfers between devices  45.1 us (30%)
  matrix products  35.1 us (24%)
  local copies, waits for them, and re-layouts  11.6 us (8%)
  other arithmetic  4.68 us (3%)
    ppermute x3, starting transfers between devices, with_halo(): after = lax.ppermute(initial, axis, down)  23.5 us
    ppermute x3, waiting for transfers between devices, with_halo(): before = lax.ppermute(last, axis, up)  22.7 us
    all_to_all x1, waiting for transfers between devices, to_time(): lax.all_to_all(field_in, ('ta', 'col'), split_axis=0, concat_axis=3, tile...  19.4 us
    conv_general_dilated x2, matrix products, valid_conv(): lax.conv_general_dilated(padded, kernel, window_strides=(1, 1), padding='...  17 us
    ppermute x3, starting transfers between devices, with_halo(): before = lax.ppermute(last, axis, up)  10.6 us
    dot_general x2, matrix products, disperse(): jnp.einsum('fbqw,bwv->fqv', masked, table, precision=lax.Precision.HIGHES...  8.91 us
    all_to_all x1, starting transfers between devices, to_time(): lax.all_to_all(field_in, ('ta', 'col'), split_axis=0, concat_axis=3, tile...  8.88 us
    all_to_all x1, starting transfers between devices, to_space_haloed(): lax.all_to_all(windows, ('ta', 'col'), split_axis=0, concat_axis=1, tiled...  8.48 us
  transfers between devices with their start and end apart: 8, of which 6 were waited for; matrix products, arithmetic and copies ran while one was open for 5% of the time, Pallas kernels for 0%

profile of v3, /device:TPU:40, one launch (start us, length us, event | category | flops | bytes accessed | tf_op | source)
XLA Modules:
  0.0 148.9 jit_solution(366381280450253980)
XLA Ops:
  0.6 0.0 copy-start
  0.6 0.8 convert_element_type.93
  1.4 1.4 fusion.36
  2.8 4.8 %fusion.61 = f32[2,8,310,1]{2,1,0,3:T(8,128)S(1)} fusion(s32[28]{0:T(128)} %param.16, f32[2,28,8,256]{3,1,2,0:T(8,128)S(1)} %fusion.36), kind=kOutput, calls=%fused_computation.71 | convolution fusion | flops 431083520 | bytes 478704 | tf_op jit(solution)/shard_map/fbqw,bwv->fqv/dot_general | solution.py:69
  7.6 0.0 copy-start.2
  7.6 0.0 copy-start.5
  7.7 3.2 %fusion.55 = bf16[2,28,8,256]{3,2,0,1:T(8,128)(2,1)S(1)} fusion(f32[2,8,310,1]{2,1,0,3:T(8,128)S(1)} %fusion.61, s32[28]{0:T(128)S(1)} %copy-done.9, f32[2,8,256]{2,1,0:T(8,128)S(1)} %convert_element_type.93), kind=kOutput, calls=%fused_computation.69 | convolution fusion | flops 431427584 | bytes 265712 | tf_op jit(solution)/shard_map/fqv,bwv->fbqw/dot_general | solution.py:79
  10.9 0.4 fusion.33
  11.4 1.9 %collective-permute-start.4 = (bf16[2,96,1,256]{3,1,2,0:T(8,128)(2,1)S(1)}, bf16[2,96,1,256]{3,1,2,0:T(8,128)(2,1)S(1)}, u32[]{:S(2)}, u32[]{:S(2)}) collective-permute-start(bf16[2,96,1,256]{3,1,2,0:T(8,128)(2,1)S(1)} %get-tuple-element.17), channel_id=1, source_target_pairs={{0,4},{4,8},{8,12},{12,16},{16,20},{20,24},{24,28},{28,32},{32,36}... | collective-permute-start | bytes 294920 | tf_op jit(solution)/shard_map/ppermute | solution.py:14
  13.3 8.4 %collective-permute-start.5 = (bf16[2,96,1,256]{3,1,2,0:T(8,128)(2,1)S(1)}, bf16[2,96,1,256]{3,1,2,0:T(8,128)(2,1)S(1)}, u32[]{:S(2)}, u32[]{:S(2)}) collective-permute-start(bf16[2,96,1,256]{3,1,2,0:T(8,128)(2,1)S(1)} %get-tuple-element.18), channel_id=1, source_target_pairs={{4,0},{8,4},{12,8},{16,12},{20,16},{24,20},{28,24},{32,28},{36,32}... | collective-permute-start | bytes 294920 | tf_op jit(solution)/shard_map/ppermute | solution.py:15
  21.8 0.4 collective-permute-done.4
  22.1 1.8 %collective-permute-done.5 = bf16[2,96,1,256]{3,1,2,0:T(8,128)(2,1)S(1)} collective-permute-done((bf16[2,96,1,256]{3,1,2,0:T(8,128)(2,1)S(1)}, bf16[2,96,1,256]{3,1,2,0:T(8,128)(2,1)S(1)}, u32[]{:S(2)}, u32[]{:S(2)}) %collective-permute-start.5) | collective-permute-done | bytes 98336 | tf_op jit(solution)/shard_map/ppermute | solution.py:15
  24.0 0.1 pad_maximum_fusion
  24.1 0.8 copy.47
  24.9 0.2 fusion.82
  25.1 1.2 fusion.25
  26.3 0.0 copy-start.1
  26.3 3.4 %copy.48 = bf16[16,2,96,10,18]{2,1,4,3,0:T(2,128)(2,1)} copy(bf16[16,2,96,10,18]{2,4,0,3,1:T(8,128)(2,1)S(1)} %fusion.25) | data formatting | bytes 2211840 | tf_op jit(solution)/shard_map/transpose | solution.py:38
  29.7 8.5 %all-to-all-start.1 = ((bf16[16,2,96,10,18]{2,1,4,3,0:T(2,128)(2,1)}), bf16[16,2,96,10,18]{2,1,4,3,0:T(2,128)(2,1)S(1)}, u32[]{:S(2)}, u32[]{:S(2)}) async-start(bf16[16,2,96,10,18]{2,1,4,3,0:T(2,128)(2,1)} %copy.48), calls=%async_computation.1 | async-start | bytes 2949120 | tf_op jit(solution)/shard_map/all_to_all | solution.py:39
  38.2 0.0 copy-start.7
  38.2 0.1 copy.73
  38.4 5.3 %collective-permute-start = (bf16[32,96,2,16]{1,0,3,2:T(8,128)(2,1)S(1)}, bf16[32,96,2,16]{1,0,3,2:T(8,128)(2,1)S(1)}, u32[]{:S(2)}, u32[]{:S(2)}) collective-permute-start(bf16[32,96,2,16]{1,0,3,2:T(8,128)(2,1)S(1)} %copy.73), channel_id=1, source_target_pairs={{0,4},{4,8},{8,12},{12,16},{16,20},{20,24},{24,28},{28,32},{32,36}... | collective-permute-start | bytes 589832 | tf_op jit(solution)/shard_map/ppermute | solution.py:14
  43.6 0.1 copy.74
  43.8 5.1 %collective-permute-start.1 = (bf16[32,96,2,16]{1,0,3,2:T(8,128)(2,1)S(1)}, bf16[32,96,2,16]{1,0,3,2:T(8,128)(2,1)S(1)}, u32[]{:S(2)}, u32[]{:S(2)}) collective-permute-start(bf16[32,96,2,16]{1,0,3,2:T(8,128)(2,1)S(1)} %copy.74), channel_id=1, source_target_pairs={{4,0},{8,4},{12,8},{16,12},{20,16},{24,20},{28,24},{32,28},{36,32}... | collective-permute-start | bytes 589832 | tf_op jit(solution)/shard_map/ppermute | solution.py:15
  48.8 19.9 %collective-permute-done = bf16[32,96,2,16]{1,0,3,2:T(8,128)(2,1)S(1)} collective-permute-done((bf16[32,96,2,16]{1,0,3,2:T(8,128)(2,1)S(1)}, bf16[32,96,2,16]{1,0,3,2:T(8,128)(2,1)S(1)}, u32[]{:S(2)}, u32[]{:S(2)}) %collective-permute-start) | collective-permute-done | bytes 196640 | tf_op jit(solution)/shard_map/ppermute | solution.py:14
  68.8 0.7 constant_dynamic-update-slice_fusion.1
  69.6 3.4 %collective-permute-start.2 = (bf16[32,96,12,2]{1,0,3,2:T(8,128)(2,1)S(1)}, bf16[32,96,12,2]{1,0,3,2:T(8,128)(2,1)S(1)}, u32[]{:S(2)}, u32[]{:S(2)}) collective-permute-start(bf16[32,96,12,2]{1,0,3,2:T(8,128)(2,1)S(1)} %get-tuple-element.11), channel_id=1, source_target_pairs={{0,1},{1,2},{2,3},{3,64},{64,65},{65,66},{66,67},{67,128},{128,129... | collective-permute-start | bytes 442376 | tf_op jit(solution)/shard_map/ppermute | solution.py:14
  73.0 9.9 %collective-permute-start.3 = (bf16[32,96,12,2]{1,0,3,2:T(8,128)(2,1)S(1)}, bf16[32,96,12,2]{1,0,3,2:T(8,128)(2,1)}, u32[]{:S(2)}, u32[]{:S(2)}) collective-permute-start(bf16[32,96,12,2]{1,0,3,2:T(8,128)(2,1)S(1)} %get-tuple-element.12), channel_id=1, source_target_pairs={{1,0},{2,1},{3,2},{64,3},{65,64},{66,65},{67,66},{128,67},{129,128... | collective-permute-start | bytes 442376 | tf_op jit(solution)/shard_map/ppermute | solution.py:15
  83.0 1.2 all-to-all-done.1
  84.2 1.2 copy.49
  85.3 2.4 %collective-permute-done.2 = bf16[32,96,12,2]{1,0,3,2:T(8,128)(2,1)S(1)} collective-permute-done((bf16[32,96,12,2]{1,0,3,2:T(8,128)(2,1)S(1)}, bf16[32,96,12,2]{1,0,3,2:T(8,128)(2,1)S(1)}, u32[]{:S(2)}, u32[]{:S(2)}) %collective-permute-start.2) | collective-permute-done | bytes 147488 | tf_op jit(solution)/shard_map/ppermute | solution.py:14
  87.8 0.0 collective-permute-done.3
  87.8 13.2 %multiply_convert_fusion = (bf16[32,96,10,18]{1,0,3,2:T(8,128)(2,1)}, bf16[32,96,10,18]{1,0,3,2:T(8,128)(2,1)}, f32[32,96,10,18]{1,0,3,2:T(8,128)S(1)}, f32[32,96,10,18]{1,0,3,2:T(8,128)S(1)}) fusion(f32[96]{0:T(128)S(1)} %get-tuple-element.22, f32[96]{0:T(128)S(1)} %get-tuple-element.21, bf16[32,96,10,18]{1,0,3,2:T(8,128)(2,1)S(1)} %bitcast.113, ...), kind=kOutput, calls=%fused_computation.17 | convolution fusion | flops 1004544000 | bytes 9383808 | tf_op jit(solution)/shard_map/conv_general_dilated | solution.py:21
  101.0 1.0 fusion.23
  102.0 1.6 %add_convert_fusion.2 = bf16[32,96,8,16]{1,0,3,2:T(8,128)(2,1)S(1)} fusion(bf16[32,96,8,16]{1,0,3,2:T(8,128)(2,1)S(1)} %fusion.23, f32[96]{0:T(128)S(1)} %get-tuple-element.19, f32[96]{0:T(128)S(1)} %get-tuple-element.23, f32[96]{0:T(128)S(1)} %get-tuple-element.20, f32[96]{0:T(128)S(1)} %get-tuple-element.21, f32[96]{0:T(128)S(1)} %get-tuple-element.22), kind=kLoop, calls=%fused_computation.37 | loop fusion | flops 5898240 | bytes 1574784 | tf_op jit(solution)/shard_map/convert_element_type | solution.py:106
  103.6 1.4 copy.37
  105.0 8.9 %all-to-all-start = ((bf16[32,96,8,16]{1,3,2,0:T(8,128)(2,1)}), bf16[32,96,8,16]{1,3,2,0:T(8,128)(2,1)S(1)}, u32[]{:S(2)}, u32[]{:S(2)}) async-start(bf16[32,96,8,16]{1,3,2,0:T(8,128)(2,1)} %copy.37), calls=%async_computation | async-start | bytes 2097152 | tf_op jit(solution)/shard_map/all_to_all | solution.py:44
  113.9 3.8 %add_convert_fusion.1 = bf16[32,96,8,16]{1,0,3,2:T(8,128)(2,1)S(1)} fusion(bf16[32,96,10,18]{1,0,3,2:T(8,128)(2,1)S(1)} %copy-done.10, bf16[3,3,96,96]{3,2,1,0:T(8,128)(2,1)S(1)} %copy-done, bf16[32,96,10,18]{1,0,3,2:T(8,128)(2,1)} %get-tuple-element.9), kind=kOutput, calls=%fused_computation.36 | convolution fusion | flops 680656896 | bytes 2844672 | tf_op jit(solution)/shard_map/conv_general_dilated | solution.py:21
  117.7 1.4 copy.51
  119.1 19.4 %all-to-all-done = bf16[32,96,8,16]{1,3,2,0:T(8,128)(2,1)S(1)} async-done(((bf16[32,96,8,16]{1,3,2,0:T(8,128)(2,1)}), bf16[32,96,8,16]{1,3,2,0:T(8,128)(2,1)S(1)}, u32[]{:S(2)}, u32[]{:S(2)}) %all-to-all-start) | async-done | bytes 786464 | tf_op jit(solution)/shard_map/all_to_all | solution.py:44
  138.5 0.2 copy.38
  138.7 0.4 fusion.35
  139.2 0.5 copy.39
  139.7 4.1 %fusion.67 = f32[2,8,310,1]{2,1,0,3:T(8,128)S(1)} fusion(f32[2,8,310]{2,1,0:T(8,128)S(1)} %copy-done.8, s32[28]{0:T(128)S(1)} %copy-done.9, f32[2,28,8,256]{3,1,2,0:T(8,128)S(1)} %fusion.35), kind=kOutput, calls=%fused_computation.73 | convolution fusion | flops 431088480 | bytes 498544 | tf_op jit(solution)/shard_map/fbqw,bwv->fqv/dot_general | solution.py:69
  143.9 0.0 copy-start.6
  143.9 3.2 %fusion.52 = bf16[2,28,8,256]{3,2,0,1:T(8,128)(2,1)S(1)} fusion(f32[2,8,310,1]{2,1,0,3:T(8,128)S(1)} %fusion.67, s32[28]{0:T(128)S(1)} %copy-done.9, f32[2,8,256]{2,1,0:T(8,128)S(1)} %convert_element_type.93), kind=kOutput, calls=%fused_computation.68 | convolution fusion | flops 431312896 | bytes 265712 | tf_op jit(solution)/shard_map/fqv,bwv->fbqw/dot_general | solution.py:79
  147.1 0.4 fusion.34
  147.6 1.3 copy.50
  (23 shorter events, 0.2 us)
Async XLA Ops:
  0.6 87.2 %copy-start = (bf16[3,3,96,96]{3,2,1,0:T(8,128)(2,1)S(1)}, bf16[3,3,96,96]{3,2,1,0:T(8,128)(2,1)}, u32[]{:S(2)}) copy-start(bf16[3,3,96,96]{3,2,1,0:T(8,128)(2,1)} %param.10) | copy-start | bytes 497668
  1.4 6.2 %copy-start.9 = (s32[28]{0:T(128)S(1)}, s32[28]{0:T(128)}, u32[]{:S(2)}) copy-start(s32[28]{0:T(128)} %param.16) | copy-start | bytes 340
  7.6 3.3 %copy-start.2 = (bf16[2,96,8,256]{3,2,1,0:T(8,128)(2,1)S(1)}, bf16[2,96,8,256]{3,2,1,0:T(8,128)(2,1)}, u32[]{:S(2)}) copy-start(bf16[2,96,8,256]{3,2,1,0:T(8,128)(2,1)} %param.17) | copy-start | bytes 2359300
  7.6 3.3 %copy-start.5 = (bf16[96,28]{0,1:T(8,128)(2,1)S(1)}, bf16[96,28]{0,1:T(8,128)(2,1)}, u32[]{:S(2)}) copy-start(bf16[96,28]{0,1:T(8,128)(2,1)} %param.12) | copy-start | bytes 16132
  11.4 10.8 %collective-permute-start.4 = (bf16[2,96,1,256]{3,1,2,0:T(8,128)(2,1)S(1)}, bf16[2,96,1,256]{3,1,2,0:T(8,128)(2,1)S(1)}, u32[]{:S(2)}, u32[]{:S(2)}) collective-permute-start(bf16[2,96,1,256]{3,1,2,0:T(8,128)(2,1)S(1)} %get-tuple-element.17), channel_id=1, source_target_pairs={{0,4},{4,8},{8,12},{12,16},{16,20},{20,24},{24,28},{28,32},{32,36}... | collective-permute-start | bytes 294920 | tf_op jit(solution)/shard_map/ppermute | solution.py:14
  13.3 10.6 %collective-permute-start.5 = (bf16[2,96,1,256]{3,1,2,0:T(8,128)(2,1)S(1)}, bf16[2,96,1,256]{3,1,2,0:T(8,128)(2,1)S(1)}, u32[]{:S(2)}, u32[]{:S(2)}) collective-permute-start(bf16[2,96,1,256]{3,1,2,0:T(8,128)(2,1)S(1)} %get-tuple-element.18), channel_id=1, source_target_pairs={{4,0},{8,4},{12,8},{16,12},{20,16},{24,20},{28,24},{32,28},{36,32}... | collective-permute-start | bytes 294920 | tf_op jit(solution)/shard_map/ppermute | solution.py:15
  26.3 11.9 %copy-start.1 = (bf16[32,96,8,16]{1,3,2,0:T(8,128)(2,1)S(1)}, bf16[32,96,8,16]{1,3,2,0:T(8,128)(2,1)}, u32[]{:S(2)}) copy-start(bf16[32,96,8,16]{1,3,2,0:T(8,128)(2,1)} %param.9) | copy-start | bytes 2359300
  29.7 54.5 %all-to-all-start.1 = ((bf16[16,2,96,10,18]{2,1,4,3,0:T(2,128)(2,1)}), bf16[16,2,96,10,18]{2,1,4,3,0:T(2,128)(2,1)S(1)}, u32[]{:S(2)}, u32[]{:S(2)}) async-start(bf16[16,2,96,10,18]{2,1,4,3,0:T(2,128)(2,1)} %copy.48), calls=%async_computation.1 | async-start | bytes 2949120 | tf_op jit(solution)/shard_map/all_to_all | solution.py:39
  38.2 44.8 %copy-start.7 = (f32[96,5]{0,1:T(8,128)S(1)}, f32[96,5]{0,1:T(8,128)}, u32[]{:S(2)}) copy-start(f32[96,5]{0,1:T(8,128)} %param.11) | copy-start | bytes 5764
  38.4 30.4 %collective-permute-start = (bf16[32,96,2,16]{1,0,3,2:T(8,128)(2,1)S(1)}, bf16[32,96,2,16]{1,0,3,2:T(8,128)(2,1)S(1)}, u32[]{:S(2)}, u32[]{:S(2)}) collective-permute-start(bf16[32,96,2,16]{1,0,3,2:T(8,128)(2,1)S(1)} %copy.73), channel_id=1, source_target_pairs={{0,4},{4,8},{8,12},{12,16},{16,20},{20,24},{24,28},{28,32},{32,36}... | collective-permute-start | bytes 589832 | tf_op jit(solution)/shard_map/ppermute | solution.py:14
  43.8 25.8 %collective-permute-start.1 = (bf16[32,96,2,16]{1,0,3,2:T(8,128)(2,1)S(1)}, bf16[32,96,2,16]{1,0,3,2:T(8,128)(2,1)S(1)}, u32[]{:S(2)}, u32[]{:S(2)}) collective-permute-start(bf16[32,96,2,16]{1,0,3,2:T(8,128)(2,1)S(1)} %copy.74), channel_id=1, source_target_pairs={{4,0},{8,4},{12,8},{16,12},{20,16},{24,20},{28,24},{32,28},{36,32}... | collective-permute-start | bytes 589832 | tf_op jit(solution)/shard_map/ppermute | solution.py:15
  69.6 13.4 %copy-start.3 = (bf16[32,96,12,16]{1,0,3,2:T(8,128)(2,1)}, bf16[32,96,12,16]{1,0,3,2:T(8,128)(2,1)S(1)}, u32[]{:S(2)}) copy-start(bf16[32,96,12,16]{1,0,3,2:T(8,128)(2,1)S(1)} %constant_dynamic-update-slice_fusion) | copy-start | bytes 3538948
  69.6 18.1 %collective-permute-start.2 = (bf16[32,96,12,2]{1,0,3,2:T(8,128)(2,1)S(1)}, bf16[32,96,12,2]{1,0,3,2:T(8,128)(2,1)S(1)}, u32[]{:S(2)}, u32[]{:S(2)}) collective-permute-start(bf16[32,96,12,2]{1,0,3,2:T(8,128)(2,1)S(1)} %get-tuple-element.11), channel_id=1, source_target_pairs={{0,1},{1,2},{2,3},{3,64},{64,65},{65,66},{66,67},{67,128},{128,129... | collective-permute-start | bytes 442376 | tf_op jit(solution)/shard_map/ppermute | solution.py:14
  73.0 14.8 %collective-permute-start.3 = (bf16[32,96,12,2]{1,0,3,2:T(8,128)(2,1)S(1)}, bf16[32,96,12,2]{1,0,3,2:T(8,128)(2,1)}, u32[]{:S(2)}, u32[]{:S(2)}) collective-permute-start(bf16[32,96,12,2]{1,0,3,2:T(8,128)(2,1)S(1)} %get-tuple-element.12), channel_id=1, source_target_pairs={{1,0},{2,1},{3,2},{64,3},{65,64},{66,65},{67,66},{128,67},{129,128... | collective-permute-start | bytes 442376 | tf_op jit(solution)/shard_map/ppermute | solution.py:15
  84.2 3.6 %copy-start.4 = (bf16[32,96,12,16]{1,0,3,2:T(8,128)(2,1)S(1)}, bf16[32,96,12,16]{1,0,3,2:T(8,128)(2,1)}, u32[]{:S(2)}) copy-start(bf16[32,96,12,16]{1,0,3,2:T(8,128)(2,1)} %copy-done.3) | copy-start | bytes 3538948
  103.6 10.3 %copy-start.10 = (bf16[32,96,10,18]{1,0,3,2:T(8,128)(2,1)S(1)}, bf16[32,96,10,18]{1,0,3,2:T(8,128)(2,1)}, u32[]{:S(2)}) copy-start(bf16[32,96,10,18]{1,0,3,2:T(8,128)(2,1)} %get-tuple-element.8) | copy-start | bytes 3317764
  105.0 33.5 %all-to-all-start = ((bf16[32,96,8,16]{1,3,2,0:T(8,128)(2,1)}), bf16[32,96,8,16]{1,3,2,0:T(8,128)(2,1)S(1)}, u32[]{:S(2)}, u32[]{:S(2)}) async-start(bf16[32,96,8,16]{1,3,2,0:T(8,128)(2,1)} %copy.37), calls=%async_computation | async-start | bytes 2097152 | tf_op jit(solution)/shard_map/all_to_all | solution.py:44
  119.1 20.6 %copy-start.8 = (f32[2,8,310]{2,1,0:T(8,128)S(1)}, f32[2,8,310]{2,1,0:T(8,128)}, u32[]{:S(2)}) copy-start(f32[2,8,310]{2,1,0:T(8,128)} %param.14) | copy-start | bytes 59524
  143.9 3.2 %copy-start.6 = (bf16[28,96]{1,0:T(8,128)(2,1)S(1)}, bf16[28,96]{1,0:T(8,128)(2,1)}, u32[]{:S(2)}) copy-start(bf16[28,96]{1,0:T(8,128)(2,1)} %param.13) | copy-start | bytes 16132

commit v4 on v1

--- a/solution.py
+++ b/solution.py
@@ -52,30 +52,29 @@
     return jax.nn.gelu(values_in, approximate=False)
 
 
-def shift_table(dispersion, width_keep, width_wide):
-    source_col = lax.broadcasted_iota(jnp.int32, (1, width_keep, width_wide), 1)
-    target_col = lax.broadcasted_iota(jnp.int32, (1, width_keep, width_wide), 2)
-    return (target_col == source_col + dispersion[:, None, None]).astype(jnp.float32)
+def shift_bits(dispersion, largest):
+    bits = largest.bit_length()
+    return [((dispersion >> k) & 1).astype(bool)[None, :, None, None] for k in range(bits)]
 
 
-def disperse(masked, table):
-    return jnp.einsum(
-        "fbqw,bwv->fqv",
-        masked,
-        table,
-        precision=lax.Precision.HIGHEST,
-        preferred_element_type=jnp.float32,
-    )
+def disperse(masked, bits, width_wide):
+    moved = jnp.pad(masked, ((0, 0),) * 3 + ((0, width_wide - masked.shape[-1]),))
+    for k, bit in enumerate(bits):
+        step = 1 << k
+        later = jnp.pad(moved[..., :-step], ((0, 0),) * 3 + ((step, 0),))
+        moved = jnp.where(bit, later, moved)
+    return jnp.sum(moved, axis=1)
 
 
-def undisperse(field_in, table):
-    return jnp.einsum(
-        "fqv,bwv->fbqw",
-        field_in,
-        table,
-        precision=lax.Precision.HIGHEST,
-        preferred_element_type=jnp.float32,
+def undisperse(field_in, bits, width_keep):
+    moved = jnp.broadcast_to(
+        field_in[:, None], (field_in.shape[0], bits[0].shape[1]) + field_in.shape[1:]
     )
+    for k, bit in enumerate(bits):
+        step = 1 << k
+        earlier = jnp.pad(moved[..., step:], ((0, 0),) * 3 + ((0, step),))
+        moved = jnp.where(bit, earlier, moved)
+    return moved[..., :width_keep]
 
 
 def on_device(
@@ -94,12 +93,12 @@
     temporal = to_time(time_mix(hidden_state, time_weight).astype(jnp.bfloat16))
     width_keep = aperture.shape[-1]
     width_wide = measured.shape[-1]
-    table = shift_table(dispersion, width_keep, width_wide)
+    bits = shift_bits(dispersion, width_wide - width_keep)
     mask_float = aperture.astype(jnp.float32)[:, None]
     band_vals = jnp.einsum("fcqw,cb->fbqw", temporal, band_out, preferred_element_type=jnp.float32)
-    masked_band_sum = disperse(band_vals * mask_float, table)
+    masked_band_sum = disperse(band_vals * mask_float, bits, width_wide)
     residual_error = measured - masked_band_sum
-    back_proj = (undisperse(residual_error, table) * mask_float).astype(jnp.bfloat16)
+    back_proj = (undisperse(residual_error, bits, width_keep) * mask_float).astype(jnp.bfloat16)
     updated = (
         temporal.astype(jnp.float32)
         + jnp.einsum(
@@ -109,8 +108,8 @@
     band_cot = jnp.einsum(
         "fcqw,bc->fbqw", update_cot, band_input_weight, preferred_element_type=jnp.float32
     )
-    resid_grad = disperse(band_cot * mask_float, table)
-    band_grad = (-(undisperse(resid_grad, table) * mask_float)).astype(jnp.bfloat16)
+    resid_grad = disperse(band_cot * mask_float, bits, width_wide)
+    band_grad = (-(undisperse(resid_grad, bits, width_keep) * mask_float)).astype(jnp.bfloat16)
     cot_temporal = (
         update_cot.astype(jnp.float32)
         + jnp.einsum("fbqw,cb->fcqw", band_grad, band_out, preferred_element_type=jnp.float32)

time: 131 us -> 155 us (1.18)
  the two profiles are of different devices: /device:TPU:86 before, /device:TPU:7 now
where the time goes in v4:
time: 155 us
  starting transfers between devices  43.4 us (28%)
  waiting for transfers between devices  40.4 us (26%)
  blocking collectives  30.3 us (20%)
  local copies, waits for them, and re-layouts  16 us (10%)
  matrix products  13.9 us (9%)
  other arithmetic  9.6 us (6%)
    ppermute x4, starting transfers between devices, with_halo(): before = lax.ppermute(last, axis, up)  31 us
    all_to_all x1, blocking collectives, to_space(): lax.all_to_all(field_in, ('ta', 'col'), split_axis=3, concat_axis=0, tile...  30.3 us
    ppermute x4, waiting for transfers between devices, with_halo(): after = lax.ppermute(initial, axis, down)  20.5 us
    all_to_all x1, waiting for transfers between devices, to_time(): lax.all_to_all(field_in, ('ta', 'col'), split_axis=0, concat_axis=3, tile...  18.6 us
    conv_general_dilated x2, matrix products, spatial_conv(): lax.conv_general_dilated(padded, kernel, window_strides=(1, 1), padding='...  11.4 us
    ppermute x4, starting transfers between devices, with_halo(): after = lax.ppermute(initial, axis, down)  8.03 us
    unnamed x34, local copies, waits for them, and re-layouts  5.57 us
    all_to_all x1, starting transfers between devices, to_time(): lax.all_to_all(field_in, ('ta', 'col'), split_axis=0, concat_axis=3, tile...  4.42 us
  transfers between devices with their start and end apart: 9, of which 6 were waited for; matrix products, arithmetic and copies ran while one was open for 4% of the time, Pallas kernels for 0%

profile of v4, /device:TPU:7, one launch (start us, length us, event | category | flops | bytes accessed | tf_op | source)
XLA Modules:
  0.0 154.7 jit_solution(662968992393793340)
XLA Ops:
  0.7 1.1 fusion.56
  1.8 9.4 %collective-permute-start = (bf16[32,96,1,16]{1,0,3,2:T(8,128)(2,1)S(1)}, bf16[32,96,1,16]{1,0,3,2:T(8,128)(2,1)S(1)}, u32[]{:S(2)}, u32[]{:S(2)}) collective-permute-start(bf16[32,96,1,16]{1,0,3,2:T(8,128)(2,1)S(1)} %copy.58), channel_id=1, source_target_pairs={{0,4},{4,8},{8,12},{12,16},{16,20},{20,24},{24,28},{28,32},{32,36}... | collective-permute-start | bytes 294920 | tf_op jit(solution)/shard_map/ppermute | solution.py:14
  11.2 1.9 %collective-permute-start.1 = (bf16[32,96,1,16]{1,0,3,2:T(8,128)(2,1)S(1)}, bf16[32,96,1,16]{1,0,3,2:T(8,128)(2,1)S(1)}, u32[]{:S(2)}, u32[]{:S(2)}) collective-permute-start(bf16[32,96,1,16]{1,0,3,2:T(8,128)(2,1)S(1)} %copy.59), channel_id=1, source_target_pairs={{4,0},{8,4},{12,8},{16,12},{20,16},{24,20},{28,24},{32,28},{36,32}... | collective-permute-start | bytes 294920 | tf_op jit(solution)/shard_map/ppermute | solution.py:15
  13.2 1.3 collective-permute-done
  14.5 2.0 %constant_dynamic-update-slice_fusion.1 = bf16[32,96,10,16]{1,0,3,2:T(8,128)(2,1)S(1)} fusion(bf16[32,96,10,16]{1,0,3,2:T(8,128)(2,1)S(1)} %constant_dynamic-update-slice_fusion.2, bf16[32,96,8,16]{1,3,2,0:T(8,128)(2,1)} %param.9), kind=kLoop, calls=%fused_computation.100 | loop fusion | bytes 1835008
  16.5 5.1 %collective-permute-done.1 = bf16[32,96,1,16]{1,0,3,2:T(8,128)(2,1)S(1)} collective-permute-done((bf16[32,96,1,16]{1,0,3,2:T(8,128)(2,1)S(1)}, bf16[32,96,1,16]{1,0,3,2:T(8,128)(2,1)S(1)}, u32[]{:S(2)}, u32[]{:S(2)}) %collective-permute-start.1) | collective-permute-done | bytes 98336 | tf_op jit(solution)/shard_map/ppermute | solution.py:15
  21.6 3.9 %collective-permute-start.2 = (bf16[32,96,10,1]{1,0,3,2:T(8,128)(2,1)S(1)}, bf16[32,96,10,1]{1,0,3,2:T(8,128)(2,1)S(1)}, u32[]{:S(2)}, u32[]{:S(2)}) collective-permute-start(bf16[32,96,10,1]{1,0,3,2:T(8,128)(2,1)S(1)} %get-tuple-element.16), channel_id=1, source_target_pairs={{0,1},{1,2},{2,3},{3,64},{64,65},{65,66},{66,67},{67,128},{128,129... | collective-permute-start | bytes 184328 | tf_op jit(solution)/shard_map/ppermute | solution.py:14
  25.5 1.9 %collective-permute-start.3 = (bf16[32,96,10,1]{1,0,3,2:T(8,128)(2,1)S(1)}, bf16[32,96,10,1]{1,0,3,2:T(8,128)(2,1)S(1)}, u32[]{:S(2)}, u32[]{:S(2)}) collective-permute-start(bf16[32,96,10,1]{1,0,3,2:T(8,128)(2,1)S(1)} %get-tuple-element.17), channel_id=1, source_target_pairs={{1,0},{2,1},{3,2},{64,3},{65,64},{66,65},{67,66},{128,67},{129,128... | collective-permute-start | bytes 184328 | tf_op jit(solution)/shard_map/ppermute | solution.py:15
  27.4 5.3 %collective-permute-done.3 = bf16[32,96,10,1]{1,0,3,2:T(8,128)(2,1)S(1)} collective-permute-done((bf16[32,96,10,1]{1,0,3,2:T(8,128)(2,1)S(1)}, bf16[32,96,10,1]{1,0,3,2:T(8,128)(2,1)S(1)}, u32[]{:S(2)}, u32[]{:S(2)}) %collective-permute-start.3) | collective-permute-done | bytes 61472 | tf_op jit(solution)/shard_map/ppermute | solution.py:15
  32.8 8.7 %add_convert_fusion.2 = (bf16[32,96,8,16]{1,0,3,2:T(8,128)(2,1)S(1)}, f32[32,96,8,16]{1,0,3,2:T(8,128)}, f32[32,96,8,16]{1,0,3,2:T(8,128)}) fusion(bf16[32,96,8,16]{1,3,2,0:T(8,128)(2,1)S(1)} %copy-done.6, bf16[3,3,96,96]{3,2,1,0:T(8,128)(2,1)S(1)} %copy-done, bf16[32,96,10,1]{1,0,3,2:T(8,128)(2,1)S(1)} %collective-permute-done.3, ...), kind=kOutput, calls=%fused_computation.15 | convolution fusion | flops 706928640 | bytes 5990400 | tf_op jit(solution)/shard_map/conv_general_dilated | solution.py:22
  41.4 1.6 %add_convert_fusion.1 = bf16[32,96,8,16]{1,0,3,2:T(8,128)(2,1)S(1)} fusion(bf16[32,96,8,16]{1,0,3,2:T(8,128)(2,1)S(1)} %get-tuple-element.12, f32[96]{0:T(128)S(1)} %get-tuple-element.25, f32[96]{0:T(128)S(1)} %get-tuple-element.26, f32[96]{0:T(128)S(1)} %get-tuple-element.23, f32[96]{0:T(128)S(1)} %get-tuple-element.24, f32[96]{0:T(128)S(1)} %get-tuple-element.22), kind=kLoop, calls=%fused_computation.14 | loop fusion | flops 5898240 | bytes 1574784 | tf_op jit(solution)/shard_map/convert_element_type | solution.py:93
  43.1 1.4 copy.38
  44.4 4.4 %all-to-all-start = ((bf16[32,96,8,16]{1,3,2,0:T(8,128)(2,1)}), bf16[32,96,8,16]{1,3,2,0:T(8,128)(2,1)S(1)}, u32[]{:S(2)}, u32[]{:S(2)}) async-start(bf16[32,96,8,16]{1,3,2,0:T(8,128)(2,1)} %copy.38), calls=%async_computation | async-start | bytes 2097152 | tf_op jit(solution)/shard_map/all_to_all | solution.py:33
  49.2 18.6 %all-to-all-done = bf16[32,96,8,16]{1,3,2,0:T(8,128)(2,1)S(1)} async-done(((bf16[32,96,8,16]{1,3,2,0:T(8,128)(2,1)}), bf16[32,96,8,16]{1,3,2,0:T(8,128)(2,1)S(1)}, u32[]{:S(2)}, u32[]{:S(2)}) %all-to-all-start) | async-done | bytes 786464 | tf_op jit(solution)/shard_map/all_to_all | solution.py:33
  68.1 0.4 fusion.31
  68.6 0.5 pad_select_fusion.1
  69.2 0.5 pad_select_fusion.19
  69.7 0.5 pad_select_fusion.18
  70.1 0.5 pad_select_fusion.17
  70.6 0.5 pad_select_fusion.16
  71.1 0.5 select_reduce_fusion
  72.4 0.3 slice.224
  72.7 0.3 slice.212
  72.9 0.4 pad_select_fusion.5
  73.6 0.3 slice.213
  73.9 0.3 pad_select_fusion.4
  74.5 0.3 slice.214
  74.8 0.3 pad_select_fusion.3
  75.4 0.3 slice.215
  75.6 0.3 pad_select_fusion.2
  76.2 0.6 copy-done.3
  76.8 1.4 fusion.14
  78.1 1.9 %copy.44 = bf16[2,96,8,256]{1,2,0,3:T(8,128)(2,1)S(1)} copy(bf16[2,96,8,256]{3,1,2,0:T(8,128)(2,1)} %fusion.14) | data formatting | bytes 1572864 | tf_op jit(solution)/shard_map/convert_element_type | solution.py:116
  80.0 30.3 %all_to_all.36 = bf16[2,96,8,256]{1,2,0,3:T(8,128)(2,1)S(1)} all-to-all(bf16[2,96,8,256]{1,2,0,3:T(8,128)(2,1)S(1)} %copy.44), channel_id=1, replica_groups=mesh['ta'=4,'row'=16,'col'=4] {'ta','col'}, dimensions={3} | all-to-all | bytes 1572864 | tf_op jit(solution)/shard_map/all_to_all | solution.py:37
  110.3 0.8 copy.46
  111.2 3.4 %fusion.6 = (bf16[32,96,8,16]{1,0,3,2:T(8,128)(2,1)S(1)}, bf16[32,96,8,16]{1,0,3,2:T(8,128)(2,1)}) fusion(f32[32,96,8,16]{1,0,3,2:T(8,128)S(1)} %copy-done.4, f32[32,96,8,16]{1,0,3,2:T(8,128)S(1)} %copy-done.5, f32[96]{0:T(128)S(1)} %get-tuple-element.22, f32[96]{0:T(128)S(1)} %get-tuple-element.24, bf16[32,96,8,16]{1,0,3,2:T(8,128)(2,1)S(1)} %bitcast.71, ...), kind=kLoop, calls=%fused_computation.10 | loop fusion | flops 11796480 | bytes 5506944 | tf_op jit(solution)/shard_map/convert_element_type | solution.py:120
  114.6 0.7 fusion.55
  115.2 12.0 %collective-permute-start.4 = (bf16[32,96,1,16]{1,0,3,2:T(8,128)(2,1)}, bf16[32,96,1,16]{1,0,3,2:T(8,128)(2,1)S(1)}, u32[]{:S(2)}, u32[]{:S(2)}) collective-permute-start(bf16[32,96,1,16]{1,0,3,2:T(8,128)(2,1)} %get-tuple-element.18), channel_id=1, source_target_pairs={{0,4},{4,8},{8,12},{12,16},{16,20},{20,24},{24,28},{28,32},{32,36}... | collective-permute-start | bytes 294920 | tf_op jit(solution)/shard_map/ppermute | solution.py:14
  127.2 1.9 %collective-permute-start.5 = (bf16[32,96,1,16]{1,0,3,2:T(8,128)(2,1)S(1)}, bf16[32,96,1,16]{1,0,3,2:T(8,128)(2,1)S(1)}, u32[]{:S(2)}, u32[]{:S(2)}) collective-permute-start(bf16[32,96,1,16]{1,0,3,2:T(8,128)(2,1)S(1)} %get-tuple-element.19), channel_id=1, source_target_pairs={{4,0},{8,4},{12,8},{16,12},{20,16},{24,20},{28,24},{32,28},{36,32}... | collective-permute-start | bytes 294920 | tf_op jit(solution)/shard_map/ppermute | solution.py:15
  129.1 1.2 copy.40
  130.7 6.7 %collective-permute-done.5 = bf16[32,96,1,16]{1,0,3,2:T(8,128)(2,1)S(1)} collective-permute-done((bf16[32,96,1,16]{1,0,3,2:T(8,128)(2,1)S(1)}, bf16[32,96,1,16]{1,0,3,2:T(8,128)(2,1)S(1)}, u32[]{:S(2)}, u32[]{:S(2)}) %collective-permute-start.5) | collective-permute-done | bytes 98336 | tf_op jit(solution)/shard_map/ppermute | solution.py:15
  137.5 5.8 %collective-permute-start.6 = (bf16[32,96,10,1]{1,0,3,2:T(8,128)(2,1)S(1)}, bf16[32,96,10,1]{1,0,3,2:T(8,128)(2,1)S(1)}, u32[]{:S(2)}, u32[]{:S(2)}) collective-permute-start(bf16[32,96,10,1]{1,0,3,2:T(8,128)(2,1)S(1)} %get-tuple-element.14), channel_id=1, source_target_pairs={{0,1},{1,2},{2,3},{3,64},{64,65},{65,66},{66,67},{67,128},{128,129... | collective-permute-start | bytes 184328 | tf_op jit(solution)/shard_map/ppermute | solution.py:14
  143.2 2.3 %collective-permute-start.7 = (bf16[32,96,10,1]{1,0,3,2:T(8,128)(2,1)S(1)}, bf16[32,96,10,1]{1,0,3,2:T(8,128)(2,1)S(1)}, u32[]{:S(2)}, u32[]{:S(2)}) collective-permute-start(bf16[32,96,10,1]{1,0,3,2:T(8,128)(2,1)S(1)} %get-tuple-element.15), channel_id=1, source_target_pairs={{1,0},{2,1},{3,2},{64,3},{65,64},{66,65},{67,66},{128,67},{129,128... | collective-permute-start | bytes 184328 | tf_op jit(solution)/shard_map/ppermute | solution.py:15
  145.5 0.5 fusion.15
  146.0 1.3 copy.47
  147.3 3.3 %collective-permute-done.7 = bf16[32,96,10,1]{1,0,3,2:T(8,128)(2,1)S(1)} collective-permute-done((bf16[32,96,10,1]{1,0,3,2:T(8,128)(2,1)S(1)}, bf16[32,96,10,1]{1,0,3,2:T(8,128)(2,1)S(1)}, u32[]{:S(2)}, u32[]{:S(2)}) %collective-permute-start.7) | collective-permute-done | bytes 61472 | tf_op jit(solution)/shard_map/ppermute | solution.py:15
  150.7 2.7 %fusion.8 = bf16[32,96,8,16]{1,0,3,2:T(8,128)(2,1)S(1)} fusion(bf16[32,96,8,16]{1,0,3,2:T(8,128)(2,1)S(1)} %copy-done.7, bf16[3,3,96,96]{3,2,1,0:T(8,128)(2,1)S(1)} %copy-done, bf16[32,96,10,1]{1,0,3,2:T(8,128)(2,1)S(1)} %collective-permute-done.7, bf16[32,96,1,16]{1,0,3,2:T(8,128)(2,1)S(1)} %collective-permute-done.5, ...), kind=kOutput, calls=%fused_computation.12 | convolution fusion | flops 682868736 | bytes 2844672 | tf_op jit(solution)/shard_map/conv_general_dilated | solution.py:22
  153.3 1.4 copy.48
  (53 shorter events, 2.9 us)
Async XLA Ops:
  0.6 32.1 %copy-start = (bf16[3,3,96,96]{3,2,1,0:T(8,128)(2,1)S(1)}, bf16[3,3,96,96]{3,2,1,0:T(8,128)(2,1)}, u32[]{:S(2)}) copy-start(bf16[3,3,96,96]{3,2,1,0:T(8,128)(2,1)} %param.10) | copy-start | bytes 497668
  0.6 32.1 %copy-start.6 = (bf16[32,96,8,16]{1,3,2,0:T(8,128)(2,1)S(1)}, bf16[32,96,8,16]{1,3,2,0:T(8,128)(2,1)}, u32[]{:S(2)}) copy-start(bf16[32,96,8,16]{1,3,2,0:T(8,128)(2,1)} %param.9) | copy-start | bytes 2359300
  0.7 26.7 %copy-start.12 = (f32[96,5]{0,1:T(8,128)S(1)}, f32[96,5]{0,1:T(8,128)}, u32[]{:S(2)}) copy-start(f32[96,5]{0,1:T(8,128)} %param.11) | copy-start | bytes 5764
  1.8 12.7 %collective-permute-start = (bf16[32,96,1,16]{1,0,3,2:T(8,128)(2,1)S(1)}, bf16[32,96,1,16]{1,0,3,2:T(8,128)(2,1)S(1)}, u32[]{:S(2)}, u32[]{:S(2)}) collective-permute-start(bf16[32,96,1,16]{1,0,3,2:T(8,128)(2,1)S(1)} %copy.58), channel_id=1, source_target_pairs={{0,4},{4,8},{8,12},{12,16},{16,20},{20,24},{24,28},{28,32},{32,36}... | collective-permute-start | bytes 294920 | tf_op jit(solution)/shard_map/ppermute | solution.py:14
  11.2 10.3 %collective-permute-start.1 = (bf16[32,96,1,16]{1,0,3,2:T(8,128)(2,1)S(1)}, bf16[32,96,1,16]{1,0,3,2:T(8,128)(2,1)S(1)}, u32[]{:S(2)}, u32[]{:S(2)}) collective-permute-start(bf16[32,96,1,16]{1,0,3,2:T(8,128)(2,1)S(1)} %copy.59), channel_id=1, source_target_pairs={{4,0},{8,4},{12,8},{16,12},{20,16},{24,20},{28,24},{32,28},{36,32}... | collective-permute-start | bytes 294920 | tf_op jit(solution)/shard_map/ppermute | solution.py:15
  21.6 5.8 %collective-permute-start.2 = (bf16[32,96,10,1]{1,0,3,2:T(8,128)(2,1)S(1)}, bf16[32,96,10,1]{1,0,3,2:T(8,128)(2,1)S(1)}, u32[]{:S(2)}, u32[]{:S(2)}) collective-permute-start(bf16[32,96,10,1]{1,0,3,2:T(8,128)(2,1)S(1)} %get-tuple-element.16), channel_id=1, source_target_pairs={{0,1},{1,2},{2,3},{3,64},{64,65},{65,66},{66,67},{67,128},{128,129... | collective-permute-start | bytes 184328 | tf_op jit(solution)/shard_map/ppermute | solution.py:14
  25.5 7.3 %collective-permute-start.3 = (bf16[32,96,10,1]{1,0,3,2:T(8,128)(2,1)S(1)}, bf16[32,96,10,1]{1,0,3,2:T(8,128)(2,1)S(1)}, u32[]{:S(2)}, u32[]{:S(2)}) collective-permute-start(bf16[32,96,10,1]{1,0,3,2:T(8,128)(2,1)S(1)} %get-tuple-element.17), channel_id=1, source_target_pairs={{1,0},{2,1},{3,2},{64,3},{65,64},{66,65},{67,66},{128,67},{129,128... | collective-permute-start | bytes 184328 | tf_op jit(solution)/shard_map/ppermute | solution.py:15
  43.0 5.9 %copy-start.11 = (s32[2,8,256]{2,1,0:T(8,128)S(1)}, s32[2,8,256]{2,1,0:T(8,128)}, u32[]{:S(2)}) copy-start(s32[2,8,256]{2,1,0:T(8,128)} %param.15) | copy-start | bytes 49156
  43.0 5.9 %copy-start.13 = (s32[28]{0:T(128)S(1)}, s32[28]{0:T(128)}, u32[]{:S(2)}) copy-start(s32[28]{0:T(128)} %param.16) | copy-start | bytes 340
  43.0 5.9 %copy-start.2 = (bf16[2,96,8,256]{3,2,1,0:T(8,128)(2,1)S(1)}, bf16[2,96,8,256]{3,2,1,0:T(8,128)(2,1)}, u32[]{:S(2)}) copy-start(bf16[2,96,8,256]{3,2,1,0:T(8,128)(2,1)} %param.17) | copy-start | bytes 2359300
  43.1 5.9 %copy-start.9 = (bf16[28,96]{1,0:T(8,128)(2,1)S(1)}, bf16[28,96]{1,0:T(8,128)(2,1)}, u32[]{:S(2)}) copy-start(bf16[28,96]{1,0:T(8,128)(2,1)} %param.13) | copy-start | bytes 16132
  44.4 23.4 %all-to-all-start = ((bf16[32,96,8,16]{1,3,2,0:T(8,128)(2,1)}), bf16[32,96,8,16]{1,3,2,0:T(8,128)(2,1)S(1)}, u32[]{:S(2)}, u32[]{:S(2)}) async-start(bf16[32,96,8,16]{1,3,2,0:T(8,128)(2,1)} %copy.38), calls=%async_computation | async-start | bytes 2097152 | tf_op jit(solution)/shard_map/all_to_all | solution.py:33
  48.9 19.2 %copy-start.8 = (bf16[96,28]{0,1:T(8,128)(2,1)S(1)}, bf16[96,28]{0,1:T(8,128)(2,1)}, u32[]{:S(2)}) copy-start(bf16[96,28]{0,1:T(8,128)(2,1)} %param.12) | copy-start | bytes 16132
  71.1 0.7 copy-start.10
  75.6 1.1 copy-start.3
  80.0 31.1 %copy-start.4 = (f32[32,96,8,16]{1,0,3,2:T(8,128)S(1)}, f32[32,96,8,16]{1,0,3,2:T(8,128)}, u32[]{:S(2)}) copy-start(f32[32,96,8,16]{1,0,3,2:T(8,128)} %get-tuple-element.13) | copy-start | bytes 4718596
  80.0 31.1 %copy-start.5 = (f32[32,96,8,16]{1,0,3,2:T(8,128)S(1)}, f32[32,96,8,16]{1,0,3,2:T(8,128)}, u32[]{:S(2)}) copy-start(f32[32,96,8,16]{1,0,3,2:T(8,128)} %get-tuple-element.53) | copy-start | bytes 4718596
  115.2 15.4 %collective-permute-start.4 = (bf16[32,96,1,16]{1,0,3,2:T(8,128)(2,1)}, bf16[32,96,1,16]{1,0,3,2:T(8,128)(2,1)S(1)}, u32[]{:S(2)}, u32[]{:S(2)}) collective-permute-start(bf16[32,96,1,16]{1,0,3,2:T(8,128)(2,1)} %get-tuple-element.18), channel_id=1, source_target_pairs={{0,4},{4,8},{8,12},{12,16},{16,20},{20,24},{24,28},{28,32},{32,36}... | collective-permute-start | bytes 294920 | tf_op jit(solution)/shard_map/ppermute | solution.py:14
  127.2 10.2 %collective-permute-start.5 = (bf16[32,96,1,16]{1,0,3,2:T(8,128)(2,1)S(1)}, bf16[32,96,1,16]{1,0,3,2:T(8,128)(2,1)S(1)}, u32[]{:S(2)}, u32[]{:S(2)}) collective-permute-start(bf16[32,96,1,16]{1,0,3,2:T(8,128)(2,1)S(1)} %get-tuple-element.19), channel_id=1, source_target_pairs={{4,0},{8,4},{12,8},{16,12},{20,16},{24,20},{28,24},{32,28},{36,32}... | collective-permute-start | bytes 294920 | tf_op jit(solution)/shard_map/ppermute | solution.py:15
  130.4 15.1 %copy-start.1 = (bf16[2,96,8,256]{3,1,2,0:T(8,128)(2,1)S(1)}, bf16[2,96,8,256]{3,1,2,0:T(8,128)(2,1)}, u32[]{:S(2)}) copy-start(bf16[2,96,8,256]{3,1,2,0:T(8,128)(2,1)} %copy.40) | copy-start | bytes 2359300
  137.5 9.9 %collective-permute-start.6 = (bf16[32,96,10,1]{1,0,3,2:T(8,128)(2,1)S(1)}, bf16[32,96,10,1]{1,0,3,2:T(8,128)(2,1)S(1)}, u32[]{:S(2)}, u32[]{:S(2)}) collective-permute-start(bf16[32,96,10,1]{1,0,3,2:T(8,128)(2,1)S(1)} %get-tuple-element.14), channel_id=1, source_target_pairs={{0,1},{1,2},{2,3},{3,64},{64,65},{65,66},{66,67},{67,128},{128,129... | collective-permute-start | bytes 184328 | tf_op jit(solution)/shard_map/ppermute | solution.py:14
  143.2 7.4 %copy-start.7 = (bf16[32,96,8,16]{1,0,3,2:T(8,128)(2,1)S(1)}, bf16[32,96,8,16]{1,0,3,2:T(8,128)(2,1)}, u32[]{:S(2)}) copy-start(bf16[32,96,8,16]{1,0,3,2:T(8,128)(2,1)} %get-tuple-element.11) | copy-start | bytes 2359300
  143.2 7.4 %collective-permute-start.7 = (bf16[32,96,10,1]{1,0,3,2:T(8,128)(2,1)S(1)}, bf16[32,96,10,1]{1,0,3,2:T(8,128)(2,1)S(1)}, u32[]{:S(2)}, u32[]{:S(2)}) collective-permute-start(bf16[32,96,10,1]{1,0,3,2:T(8,128)(2,1)S(1)} %get-tuple-element.15), channel_id=1, source_target_pairs={{1,0},{2,1},{3,2},{64,3},{65,64},{66,65},{67,66},{128,67},{129,128... | collective-permute-start | bytes 184328 | tf_op jit(solution)/shard_map/ppermute | solution.py:15

commit v5 on v4

--- a/solution.py
+++ b/solution.py
@@ -88,13 +88,23 @@
     dispersion,
     update_cot,
 ):
-    pre_act = spatial_conv(features, conv_weight)
-    hidden_state = (features.astype(jnp.float32) + gelu_exact(pre_act)).astype(jnp.bfloat16)
-    temporal = to_time(time_mix(hidden_state, time_weight).astype(jnp.bfloat16))
     width_keep = aperture.shape[-1]
     width_wide = measured.shape[-1]
     bits = shift_bits(dispersion, width_wide - width_keep)
     mask_float = aperture.astype(jnp.float32)[:, None]
+    band_cot = jnp.einsum(
+        "fcqw,bc->fbqw", update_cot, band_input_weight, preferred_element_type=jnp.float32
+    )
+    resid_grad = disperse(band_cot * mask_float, bits, width_wide)
+    band_grad = (-(undisperse(resid_grad, bits, width_keep) * mask_float)).astype(jnp.bfloat16)
+    cot_temporal = (
+        update_cot.astype(jnp.float32)
+        + jnp.einsum("fbqw,cb->fcqw", band_grad, band_out, preferred_element_type=jnp.float32)
+    ).astype(jnp.bfloat16)
+    features, cot_temporal = lax.optimization_barrier((features, cot_temporal))
+    pre_act = spatial_conv(features, conv_weight)
+    hidden_state = (features.astype(jnp.float32) + gelu_exact(pre_act)).astype(jnp.bfloat16)
+    temporal = to_time(time_mix(hidden_state, time_weight).astype(jnp.bfloat16))
     band_vals = jnp.einsum("fcqw,cb->fbqw", temporal, band_out, preferred_element_type=jnp.float32)
     masked_band_sum = disperse(band_vals * mask_float, bits, width_wide)
     residual_error = measured - masked_band_sum
@@ -104,15 +114,6 @@
         + jnp.einsum(
             "fbqw,bc->fcqw", back_proj, band_input_weight, preferred_element_type=jnp.float32
         )
-    ).astype(jnp.bfloat16)
-    band_cot = jnp.einsum(
-        "fcqw,bc->fbqw", update_cot, band_input_weight, preferred_element_type=jnp.float32
-    )
-    resid_grad = disperse(band_cot * mask_float, bits, width_wide)
-    band_grad = (-(undisperse(resid_grad, bits, width_keep) * mask_float)).astype(jnp.bfloat16)
-    cot_temporal = (
-        update_cot.astype(jnp.float32)
-        + jnp.einsum("fbqw,cb->fcqw", band_grad, band_out, preferred_element_type=jnp.float32)
     ).astype(jnp.bfloat16)
     flipped = time_weight[:, ::-1]
     cot_hidden = time_mix(to_space(cot_temporal), flipped).astype(jnp.bfloat16)

time: 155 us -> 126 us (0.81)
  the two profiles are of different devices: /device:TPU:7 before, /device:TPU:86 now
where the time goes in v5:
time: 126 us; the launch traced here: 125 us
  starting transfers between devices  63.2 us (50%)
  waiting for transfers between devices  23.5 us (19%)
  matrix products  14.7 us (12%)
  local copies, waits for them, and re-layouts  13.2 us (10%)
  other arithmetic  9.37 us (7%)
    ppermute x4, starting transfers between devices, with_halo(): before = lax.ppermute(last, axis, up)  27.7 us
    ppermute x4, starting transfers between devices, with_halo(): after = lax.ppermute(initial, axis, down)  21.1 us
    conv_general_dilated x2, matrix products, spatial_conv(): lax.conv_general_dilated(padded, kernel, window_strides=(1, 1), padding='...  11.9 us
    ppermute x4, waiting for transfers between devices, with_halo(): after = lax.ppermute(initial, axis, down)  11.8 us
    ppermute x4, waiting for transfers between devices, with_halo(): before = lax.ppermute(last, axis, up)  11.7 us
    all_to_all x1, starting transfers between devices, to_space(): lax.all_to_all(field_in, ('ta', 'col'), split_axis=3, concat_axis=0, tile...  7.95 us
    all_to_all x1, starting transfers between devices, to_time(): lax.all_to_all(field_in, ('ta', 'col'), split_axis=0, concat_axis=3, tile...  6.46 us
    unnamed x24, local copies, waits for them, and re-layouts  4.58 us
  transfers between devices with their start and end apart: 10, of which 4 were waited for; matrix products, arithmetic and copies ran while one was open for 5% of the time, Pallas kernels for 0%

profile of v5, /device:TPU:86, one launch (start us, length us, event | category | flops | bytes accessed | tf_op | source)
XLA Modules:
  0.0 125.1 jit_solution(12486609926850711557)
XLA Ops:
  0.6 0.7 and_compare_fusion.5
  1.4 0.7 convert_element_type.140
  2.1 1.4 %fusion.32 = f32[2,28,8,256]{3,1,2,0:T(8,128)S(1)} fusion(bf16[2,96,8,256]{3,2,1,0:T(8,128)(2,1)} %param.17, f32[2,8,256]{2,1,0:T(8,128)S(1)} %convert_element_type.140, bf16[28,96]{1,0:T(8,128)(2,1)} %param.13), kind=kOutput, calls=%fused_computation.59 | convolution fusion | flops 22134784 | bytes 1266944 | tf_op jit(solution)/shard_map/fcqw,bc->fbqw/dot_general | solution.py:95
  3.6 0.3 pad_select_fusion.1
  3.8 0.3 pad_select_fusion.19
  4.1 0.3 pad_select_fusion.18
  4.4 0.3 pad_select_fusion.17
  4.7 0.3 pad_select_fusion.16
  5.0 0.3 select_reduce_fusion.1
  5.6 0.3 slice.208
  6.3 0.3 pad_select_fusion.13
  7.8 0.7 copy-done.2
  8.5 0.5 fusion.15
  9.0 1.7 %copy.44 = bf16[2,96,8,256]{1,2,0,3:T(8,128)(2,1)} copy(bf16[2,96,8,256]{3,1,2,0:T(8,128)(2,1)S(1)} %fusion.15) | data formatting | bytes 1572864 | tf_op jit(solution)/shard_map/optimization_barrier | solution.py:104
  10.7 7.9 %all-to-all-start.1 = ((bf16[2,96,8,256]{1,2,0,3:T(8,128)(2,1)}), bf16[2,96,8,256]{1,2,0,3:T(8,128)(2,1)S(1)}, u32[]{:S(2)}, u32[]{:S(2)}) async-start(bf16[2,96,8,256]{1,2,0,3:T(8,128)(2,1)} %copy.44), calls=%async_computation.1 | async-start | bytes 2097152 | tf_op jit(solution)/shard_map/all_to_all | solution.py:37
  18.7 0.7 copy.36
  19.4 1.9 %collective-permute-start = (bf16[32,96,1,16]{1,0,3,2:T(8,128)(2,1)S(1)}, bf16[32,96,1,16]{1,0,3,2:T(8,128)(2,1)S(1)}, u32[]{:S(2)}, u32[]{:S(2)}) collective-permute-start(bf16[32,96,1,16]{1,0,3,2:T(8,128)(2,1)S(1)} %get-tuple-element.22), channel_id=1, source_target_pairs={{0,4},{4,8},{8,12},{12,16},{16,20},{20,24},{24,28},{28,32},{32,36}... | collective-permute-start | bytes 294920 | tf_op jit(solution)/shard_map/ppermute | solution.py:14
  21.3 8.4 %collective-permute-start.1 = (bf16[32,96,1,16]{1,0,3,2:T(8,128)(2,1)S(1)}, bf16[32,96,1,16]{1,0,3,2:T(8,128)(2,1)S(1)}, u32[]{:S(2)}, u32[]{:S(2)}) collective-permute-start(bf16[32,96,1,16]{1,0,3,2:T(8,128)(2,1)S(1)} %get-tuple-element.21), channel_id=1, source_target_pairs={{4,0},{8,4},{12,8},{16,12},{20,16},{24,20},{28,24},{32,28},{36,32}... | collective-permute-start | bytes 294920 | tf_op jit(solution)/shard_map/ppermute | solution.py:15
  29.8 6.1 %collective-permute-done = bf16[32,96,1,16]{1,0,3,2:T(8,128)(2,1)S(1)} collective-permute-done((bf16[32,96,1,16]{1,0,3,2:T(8,128)(2,1)S(1)}, bf16[32,96,1,16]{1,0,3,2:T(8,128)(2,1)S(1)}, u32[]{:S(2)}, u32[]{:S(2)}) %collective-permute-start) | collective-permute-done | bytes 98336 | tf_op jit(solution)/shard_map/ppermute | solution.py:14
  35.8 0.7 constant_dynamic-update-slice_fusion.1
  36.7 12.1 %collective-permute-start.2 = (bf16[32,96,10,1]{1,0,3,2:T(8,128)(2,1)S(1)}, bf16[32,96,10,1]{1,0,3,2:T(8,128)(2,1)S(1)}, u32[]{:S(2)}, u32[]{:S(2)}) collective-permute-start(bf16[32,96,10,1]{1,0,3,2:T(8,128)(2,1)S(1)} %get-tuple-element.17), channel_id=1, source_target_pairs={{0,1},{1,2},{2,3},{3,64},{64,65},{65,66},{66,67},{67,128},{128,129... | collective-permute-start | bytes 184328 | tf_op jit(solution)/shard_map/ppermute | solution.py:14
  48.8 2.1 %collective-permute-start.3 = (bf16[32,96,10,1]{1,0,3,2:T(8,128)(2,1)S(1)}, bf16[32,96,10,1]{1,0,3,2:T(8,128)(2,1)S(1)}, u32[]{:S(2)}, u32[]{:S(2)}) collective-permute-start(bf16[32,96,10,1]{1,0,3,2:T(8,128)(2,1)S(1)} %get-tuple-element.18), channel_id=1, source_target_pairs={{1,0},{2,1},{3,2},{64,3},{65,64},{66,65},{67,66},{128,67},{129,128... | collective-permute-start | bytes 184328 | tf_op jit(solution)/shard_map/ppermute | solution.py:15
  51.0 0.8 copy.46
  51.8 5.6 %collective-permute-done.3 = bf16[32,96,10,1]{1,0,3,2:T(8,128)(2,1)S(1)} collective-permute-done((bf16[32,96,10,1]{1,0,3,2:T(8,128)(2,1)S(1)}, bf16[32,96,10,1]{1,0,3,2:T(8,128)(2,1)S(1)}, u32[]{:S(2)}, u32[]{:S(2)}) %collective-permute-start.3) | collective-permute-done | bytes 61472 | tf_op jit(solution)/shard_map/ppermute | solution.py:15
  57.4 9.2 %fusion.6 = (bf16[32,96,8,16]{1,0,3,2:T(8,128)(2,1)S(1)}, bf16[32,96,8,16]{1,0,3,2:T(8,128)(2,1)}, f32[32,96,8,16]{1,0,3,2:T(8,128)S(1)}, f32[32,96,8,16]{1,0,3,2:T(8,128)S(1)}) fusion(f32[96]{0:T(128)S(1)} %get-tuple-element.26, f32[96]{0:T(128)S(1)} %get-tuple-element.25, bf16[32,96,8,16]{1,0,3,2:T(8,128)(2,1)S(1)} %bitcast.71, ...), kind=kOutput, calls=%fused_computation.10 | convolution fusion | flops 715186176 | bytes 6778752 | tf_op jit(solution)/shard_map/conv_general_dilated | solution.py:22
  66.6 1.0 add_convert_fusion.2
  67.6 1.6 %add_convert_fusion.1 = bf16[32,96,8,16]{1,0,3,2:T(8,128)(2,1)S(1)} fusion(bf16[32,96,8,16]{1,0,3,2:T(8,128)(2,1)S(1)} %add_convert_fusion.2, f32[96]{0:T(128)S(1)} %get-tuple-element.23, f32[96]{0:T(128)S(1)} %get-tuple-element.27, f32[96]{0:T(128)S(1)} %get-tuple-element.24, f32[96]{0:T(128)S(1)} %get-tuple-element.25, f32[96]{0:T(128)S(1)} %get-tuple-element.26), kind=kLoop, calls=%fused_computation.14 | loop fusion | flops 5898240 | bytes 1574784 | tf_op jit(solution)/shard_map/convert_element_type | solution.py:107
  69.2 1.4 %copy.40 = bf16[32,96,8,16]{1,3,2,0:T(8,128)(2,1)} copy(bf16[32,96,8,16]{1,0,3,2:T(8,128)(2,1)S(1)} %add_convert_fusion.1) | data formatting | bytes 1572864 | tf_op jit(solution)/shard_map/convert_element_type | solution.py:107
  70.6 6.5 %all-to-all-start = ((bf16[32,96,8,16]{1,3,2,0:T(8,128)(2,1)}), bf16[32,96,8,16]{1,3,2,0:T(8,128)(2,1)S(1)}, u32[]{:S(2)}, u32[]{:S(2)}) async-start(bf16[32,96,8,16]{1,3,2,0:T(8,128)(2,1)} %copy.40), calls=%async_computation | async-start | bytes 2097152 | tf_op jit(solution)/shard_map/all_to_all | solution.py:33
  77.1 1.9 %collective-permute-start.4 = (bf16[32,96,1,16]{1,0,3,2:T(8,128)(2,1)S(1)}, bf16[32,96,1,16]{1,0,3,2:T(8,128)(2,1)S(1)}, u32[]{:S(2)}, u32[]{:S(2)}) collective-permute-start(bf16[32,96,1,16]{1,0,3,2:T(8,128)(2,1)S(1)} %get-tuple-element.19), channel_id=1, source_target_pairs={{0,4},{4,8},{8,12},{12,16},{16,20},{20,24},{24,28},{28,32},{32,36}... | collective-permute-start | bytes 294920 | tf_op jit(solution)/shard_map/ppermute | solution.py:14
  79.0 8.4 %collective-permute-start.5 = (bf16[32,96,1,16]{1,0,3,2:T(8,128)(2,1)S(1)}, bf16[32,96,1,16]{1,0,3,2:T(8,128)(2,1)S(1)}, u32[]{:S(2)}, u32[]{:S(2)}) collective-permute-start(bf16[32,96,1,16]{1,0,3,2:T(8,128)(2,1)S(1)} %get-tuple-element.20), channel_id=1, source_target_pairs={{4,0},{8,4},{12,8},{16,12},{20,16},{24,20},{28,24},{32,28},{36,32}... | collective-permute-start | bytes 294920 | tf_op jit(solution)/shard_map/ppermute | solution.py:15
  87.5 5.6 %collective-permute-done.4 = bf16[32,96,1,16]{1,0,3,2:T(8,128)(2,1)S(1)} collective-permute-done((bf16[32,96,1,16]{1,0,3,2:T(8,128)(2,1)S(1)}, bf16[32,96,1,16]{1,0,3,2:T(8,128)(2,1)S(1)}, u32[]{:S(2)}, u32[]{:S(2)}) %collective-permute-start.4) | collective-permute-done | bytes 98336 | tf_op jit(solution)/shard_map/ppermute | solution.py:14
  93.2 11.7 %collective-permute-start.6 = (bf16[32,96,10,1]{1,0,3,2:T(8,128)(2,1)S(1)}, bf16[32,96,10,1]{1,0,3,2:T(8,128)(2,1)S(1)}, u32[]{:S(2)}, u32[]{:S(2)}) collective-permute-start(bf16[32,96,10,1]{1,0,3,2:T(8,128)(2,1)S(1)} %get-tuple-element.15), channel_id=1, source_target_pairs={{0,1},{1,2},{2,3},{3,64},{64,65},{65,66},{66,67},{67,128},{128,129... | collective-permute-start | bytes 184328 | tf_op jit(solution)/shard_map/ppermute | solution.py:14
  104.9 2.1 %collective-permute-start.7 = (bf16[32,96,10,1]{1,0,3,2:T(8,128)(2,1)S(1)}, bf16[32,96,10,1]{1,0,3,2:T(8,128)(2,1)S(1)}, u32[]{:S(2)}, u32[]{:S(2)}) collective-permute-start(bf16[32,96,10,1]{1,0,3,2:T(8,128)(2,1)S(1)} %get-tuple-element.16), channel_id=1, source_target_pairs={{1,0},{2,1},{3,2},{64,3},{65,64},{66,65},{67,66},{128,67},{129,128... | collective-permute-start | bytes 184328 | tf_op jit(solution)/shard_map/ppermute | solution.py:15
  107.0 6.3 %collective-permute-done.7 = bf16[32,96,10,1]{1,0,3,2:T(8,128)(2,1)S(1)} collective-permute-done((bf16[32,96,10,1]{1,0,3,2:T(8,128)(2,1)S(1)}, bf16[32,96,10,1]{1,0,3,2:T(8,128)(2,1)S(1)}, u32[]{:S(2)}, u32[]{:S(2)}) %collective-permute-start.7) | collective-permute-done | bytes 61472 | tf_op jit(solution)/shard_map/ppermute | solution.py:15
  113.3 2.7 %fusion.8 = bf16[32,96,8,16]{1,0,3,2:T(8,128)(2,1)S(1)} fusion(bf16[32,96,8,16]{1,0,3,2:T(8,128)(2,1)S(1)} %copy-done.9, bf16[3,3,96,96]{3,2,1,0:T(8,128)(2,1)S(1)} %copy-done, bf16[32,96,10,1]{1,0,3,2:T(8,128)(2,1)S(1)} %collective-permute-done.7, bf16[32,96,1,16]{1,0,3,2:T(8,128)(2,1)S(1)} %collective-permute-done.5, ...), kind=kOutput, calls=%fused_computation.12 | convolution fusion | flops 682868736 | bytes 2844672 | tf_op jit(solution)/shard_map/conv_general_dilated | solution.py:22
  116.0 1.4 %copy.48 = bf16[32,96,8,16]{1,3,2,0:T(8,128)(2,1)} copy(bf16[32,96,8,16]{1,0,3,2:T(8,128)(2,1)S(1)} %fusion.8) | data formatting | bytes 1572864
  117.6 0.4 fusion.31
  118.1 0.5 copy.42
  118.7 0.3 pad_select_fusion
  119.0 0.3 pad_select_fusion.10
  119.3 0.3 pad_select_fusion.9
  119.6 0.3 pad_select_fusion.8
  119.9 0.3 pad_select_fusion.7
  120.1 0.3 select_reduce_fusion
  121.6 0.3 pad_select_fusion.4
  123.4 0.4 fusion.14
  123.8 1.3 %copy.47 = bf16[2,96,8,256]{3,2,1,0:T(8,128)(2,1)} copy(bf16[2,96,8,256]{3,1,2,0:T(8,128)(2,1)S(1)} %fusion.14) | data formatting | bytes 1572864
  (57 shorter events, 5.1 us)
Async XLA Ops:
  0.6 56.7 %copy-start = (bf16[3,3,96,96]{3,2,1,0:T(8,128)(2,1)S(1)}, bf16[3,3,96,96]{3,2,1,0:T(8,128)(2,1)}, u32[]{:S(2)}) copy-start(bf16[3,3,96,96]{3,2,1,0:T(8,128)(2,1)} %param.10) | copy-start | bytes 497668
  7.3 1.1 copy-start.2
  7.3 1.1 copy-start.5
  8.9 9.7 %copy-start.1 = (bf16[32,96,8,16]{1,3,2,0:T(8,128)(2,1)S(1)}, bf16[32,96,8,16]{1,3,2,0:T(8,128)(2,1)}, u32[]{:S(2)}) copy-start(bf16[32,96,8,16]{1,3,2,0:T(8,128)(2,1)} %param.9) | copy-start | bytes 2359300
  10.7 40.3 %all-to-all-start.1 = ((bf16[2,96,8,256]{1,2,0,3:T(8,128)(2,1)}), bf16[2,96,8,256]{1,2,0,3:T(8,128)(2,1)S(1)}, u32[]{:S(2)}, u32[]{:S(2)}) async-start(bf16[2,96,8,256]{1,2,0,3:T(8,128)(2,1)} %copy.44), calls=%async_computation.1 | async-start | bytes 2097152 | tf_op jit(solution)/shard_map/all_to_all | solution.py:37
  19.3 31.6 %copy-start.8 = (f32[96,5]{0,1:T(8,128)S(1)}, f32[96,5]{0,1:T(8,128)}, u32[]{:S(2)}) copy-start(f32[96,5]{0,1:T(8,128)} %param.11) | copy-start | bytes 5764
  19.4 16.5 %collective-permute-start = (bf16[32,96,1,16]{1,0,3,2:T(8,128)(2,1)S(1)}, bf16[32,96,1,16]{1,0,3,2:T(8,128)(2,1)S(1)}, u32[]{:S(2)}, u32[]{:S(2)}) collective-permute-start(bf16[32,96,1,16]{1,0,3,2:T(8,128)(2,1)S(1)} %get-tuple-element.22), channel_id=1, source_target_pairs={{0,4},{4,8},{8,12},{12,16},{16,20},{20,24},{24,28},{28,32},{32,36}... | collective-permute-start | bytes 294920 | tf_op jit(solution)/shard_map/ppermute | solution.py:14
  21.3 15.3 %collective-permute-start.1 = (bf16[32,96,1,16]{1,0,3,2:T(8,128)(2,1)S(1)}, bf16[32,96,1,16]{1,0,3,2:T(8,128)(2,1)S(1)}, u32[]{:S(2)}, u32[]{:S(2)}) collective-permute-start(bf16[32,96,1,16]{1,0,3,2:T(8,128)(2,1)S(1)} %get-tuple-element.21), channel_id=1, source_target_pairs={{4,0},{8,4},{12,8},{16,12},{20,16},{24,20},{28,24},{32,28},{36,32}... | collective-permute-start | bytes 294920 | tf_op jit(solution)/shard_map/ppermute | solution.py:15
  36.6 14.3 %copy-start.3 = (bf16[32,96,10,16]{1,0,3,2:T(8,128)(2,1)}, bf16[32,96,10,16]{1,0,3,2:T(8,128)(2,1)S(1)}, u32[]{:S(2)}) copy-start(bf16[32,96,10,16]{1,0,3,2:T(8,128)(2,1)S(1)} %constant_dynamic-update-slice_fusion) | copy-start | bytes 2949124
  36.7 15.1 %collective-permute-start.2 = (bf16[32,96,10,1]{1,0,3,2:T(8,128)(2,1)S(1)}, bf16[32,96,10,1]{1,0,3,2:T(8,128)(2,1)S(1)}, u32[]{:S(2)}, u32[]{:S(2)}) collective-permute-start(bf16[32,96,10,1]{1,0,3,2:T(8,128)(2,1)S(1)} %get-tuple-element.17), channel_id=1, source_target_pairs={{0,1},{1,2},{2,3},{3,64},{64,65},{65,66},{66,67},{67,128},{128,129... | collective-permute-start | bytes 184328 | tf_op jit(solution)/shard_map/ppermute | solution.py:14
  48.8 8.5 %collective-permute-start.3 = (bf16[32,96,10,1]{1,0,3,2:T(8,128)(2,1)S(1)}, bf16[32,96,10,1]{1,0,3,2:T(8,128)(2,1)S(1)}, u32[]{:S(2)}, u32[]{:S(2)}) collective-permute-start(bf16[32,96,10,1]{1,0,3,2:T(8,128)(2,1)S(1)} %get-tuple-element.18), channel_id=1, source_target_pairs={{1,0},{2,1},{3,2},{64,3},{65,64},{66,65},{67,66},{128,67},{129,128... | collective-permute-start | bytes 184328 | tf_op jit(solution)/shard_map/ppermute | solution.py:15
  51.0 6.4 %copy-start.4 = (bf16[32,96,10,16]{1,0,3,2:T(8,128)(2,1)S(1)}, bf16[32,96,10,16]{1,0,3,2:T(8,128)(2,1)}, u32[]{:S(2)}) copy-start(bf16[32,96,10,16]{1,0,3,2:T(8,128)(2,1)} %copy-done.3) | copy-start | bytes 2949124
  70.6 42.7 %copy-start.9 = (bf16[32,96,8,16]{1,0,3,2:T(8,128)(2,1)S(1)}, bf16[32,96,8,16]{1,0,3,2:T(8,128)(2,1)}, u32[]{:S(2)}) copy-start(bf16[32,96,8,16]{1,0,3,2:T(8,128)(2,1)} %get-tuple-element.13) | copy-start | bytes 2359300
  70.6 46.8 %all-to-all-start = ((bf16[32,96,8,16]{1,3,2,0:T(8,128)(2,1)}), bf16[32,96,8,16]{1,3,2,0:T(8,128)(2,1)S(1)}, u32[]{:S(2)}, u32[]{:S(2)}) async-start(bf16[32,96,8,16]{1,3,2,0:T(8,128)(2,1)} %copy.40), calls=%async_computation | async-start | bytes 2097152 | tf_op jit(solution)/shard_map/all_to_all | solution.py:33
  77.1 16.0 %collective-permute-start.4 = (bf16[32,96,1,16]{1,0,3,2:T(8,128)(2,1)S(1)}, bf16[32,96,1,16]{1,0,3,2:T(8,128)(2,1)S(1)}, u32[]{:S(2)}, u32[]{:S(2)}) collective-permute-start(bf16[32,96,1,16]{1,0,3,2:T(8,128)(2,1)S(1)} %get-tuple-element.19), channel_id=1, source_target_pairs={{0,4},{4,8},{8,12},{12,16},{16,20},{20,24},{24,28},{28,32},{32,36}... | collective-permute-start | bytes 294920 | tf_op jit(solution)/shard_map/ppermute | solution.py:14
  79.0 14.1 %collective-permute-start.5 = (bf16[32,96,1,16]{1,0,3,2:T(8,128)(2,1)S(1)}, bf16[32,96,1,16]{1,0,3,2:T(8,128)(2,1)S(1)}, u32[]{:S(2)}, u32[]{:S(2)}) collective-permute-start(bf16[32,96,1,16]{1,0,3,2:T(8,128)(2,1)S(1)} %get-tuple-element.20), channel_id=1, source_target_pairs={{4,0},{8,4},{12,8},{16,12},{20,16},{24,20},{28,24},{32,28},{36,32}... | collective-permute-start | bytes 294920 | tf_op jit(solution)/shard_map/ppermute | solution.py:15
  93.2 13.9 %collective-permute-start.6 = (bf16[32,96,10,1]{1,0,3,2:T(8,128)(2,1)S(1)}, bf16[32,96,10,1]{1,0,3,2:T(8,128)(2,1)S(1)}, u32[]{:S(2)}, u32[]{:S(2)}) collective-permute-start(bf16[32,96,10,1]{1,0,3,2:T(8,128)(2,1)S(1)} %get-tuple-element.15), channel_id=1, source_target_pairs={{0,1},{1,2},{2,3},{3,64},{64,65},{65,66},{66,67},{67,128},{128,129... | collective-permute-start | bytes 184328 | tf_op jit(solution)/shard_map/ppermute | solution.py:14
  104.9 8.4 %collective-permute-start.7 = (bf16[32,96,10,1]{1,0,3,2:T(8,128)(2,1)S(1)}, bf16[32,96,10,1]{1,0,3,2:T(8,128)(2,1)S(1)}, u32[]{:S(2)}, u32[]{:S(2)}) collective-permute-start(bf16[32,96,10,1]{1,0,3,2:T(8,128)(2,1)S(1)} %get-tuple-element.16), channel_id=1, source_target_pairs={{1,0},{2,1},{3,2},{64,3},{65,64},{66,65},{67,66},{128,67},{129,128... | collective-permute-start | bytes 184328 | tf_op jit(solution)/shard_map/ppermute | solution.py:15
  119.8 0.7 copy-start.7
  122.7 0.7 copy-start.6

commit v6 on v5

--- a/solution.py
+++ b/solution.py
@@ -17,8 +17,12 @@
     return array
 
 
-def spatial_conv(field_in, kernel):
-    padded = with_halo(field_in, (("row", 2), (("ta", "col"), 3)), 1)
+def row_halo(field_in):
+    return with_halo(field_in, (("row", 2),), 1)
+
+
+def halo_conv(rows, kernel):
+    padded = with_halo(rows, ((("ta", "col"), 3),), 1)
     return lax.conv_general_dilated(
         padded,
         kernel,
@@ -101,8 +105,9 @@
         update_cot.astype(jnp.float32)
         + jnp.einsum("fbqw,cb->fcqw", band_grad, band_out, preferred_element_type=jnp.float32)
     ).astype(jnp.bfloat16)
-    features, cot_temporal = lax.optimization_barrier((features, cot_temporal))
-    pre_act = spatial_conv(features, conv_weight)
+    feature_rows = row_halo(features)
+    feature_rows, cot_temporal = lax.optimization_barrier((feature_rows, cot_temporal))
+    pre_act = halo_conv(feature_rows, conv_weight)
     hidden_state = (features.astype(jnp.float32) + gelu_exact(pre_act)).astype(jnp.bfloat16)
     temporal = to_time(time_mix(hidden_state, time_weight).astype(jnp.bfloat16))
     band_vals = jnp.einsum("fcqw,cb->fbqw", temporal, band_out, preferred_element_type=jnp.float32)
@@ -120,7 +125,9 @@
     pullback = jax.vjp(gelu_exact, pre_act)[1]
     gate_grad = pullback(cot_hidden.astype(jnp.float32))[0].astype(jnp.bfloat16)
     kernel_flip = jnp.transpose(conv_weight[::-1, ::-1], (0, 1, 3, 2))
-    features_grad = (cot_hidden.astype(jnp.float32) + spatial_conv(gate_grad, kernel_flip)).astype(
+    gate_rows = row_halo(gate_grad)
+    gate_rows, updated = lax.optimization_barrier((gate_rows, updated))
+    features_grad = (cot_hidden.astype(jnp.float32) + halo_conv(gate_rows, kernel_flip)).astype(
         jnp.bfloat16
     )
     return (updated, features_grad)

time: 126 us -> 134 us (1.063)
  the two profiles are of different devices: /device:TPU:86 before, /device:TPU:14 now
where the time goes in v6:
time: 134 us
  starting transfers between devices  51.1 us (38%)
  waiting for transfers between devices  36.8 us (27%)
  local copies, waits for them, and re-layouts  15.4 us (11%)
  other arithmetic  15 us (11%)
  matrix products  14.3 us (11%)
    ppermute x4, starting transfers between devices, with_halo(): after = lax.ppermute(initial, axis, down)  21.1 us
    all_to_all x1, waiting for transfers between devices, to_space(): lax.all_to_all(field_in, ('ta', 'col'), split_axis=3, concat_axis=0, tile...  14.2 us
    ppermute x4, starting transfers between devices, with_halo(): before = lax.ppermute(last, axis, up)  13 us
    conv_general_dilated x2, matrix products, halo_conv(): lax.conv_general_dilated(padded, kernel, window_strides=(1, 1), padding='...  12.7 us
    ppermute x4, waiting for transfers between devices, with_halo(): before = lax.ppermute(last, axis, up)  10.4 us
    all_to_all x1, starting transfers between devices, to_space(): lax.all_to_all(field_in, ('ta', 'col'), split_axis=3, concat_axis=0, tile...  9.19 us
    convert_element_type x1, other arithmetic, on_device(): gate_grad = pullback(cot_hidden.astype(jnp.float32))[0].astype(jnp.bfloat16)  8.04 us
    all_to_all x1, starting transfers between devices, to_time(): lax.all_to_all(field_in, ('ta', 'col'), split_axis=0, concat_axis=3, tile...  7.83 us
  transfers between devices with their start and end apart: 10, of which 5 were waited for; matrix products, arithmetic and copies ran while one was open for 15% of the time, Pallas kernels for 0%

profile of v6, /device:TPU:14, one launch (start us, length us, event | category | flops | bytes accessed | tf_op | source)
XLA Modules:
  0.0 133.8 jit_solution(9808506432232971618)
XLA Ops:
  0.7 2.0 %copy.34 = bf16[32,96,8,16]{1,0,3,2:T(8,128)(2,1)S(1)} copy(bf16[32,96,8,16]{1,3,2,0:T(8,128)(2,1)} %param.9) | data formatting | bytes 1572864 | tf_op args[0]
  2.7 1.9 %collective-permute-start = (bf16[32,96,1,16]{1,0,3,2:T(8,128)(2,1)S(1)}, bf16[32,96,1,16]{1,0,3,2:T(8,128)(2,1)S(1)}, u32[]{:S(2)}, u32[]{:S(2)}) collective-permute-start(bf16[32,96,1,16]{1,0,3,2:T(8,128)(2,1)S(1)} %get-tuple-element.26), channel_id=1, source_target_pairs={{0,4},{4,8},{8,12},{12,16},{16,20},{20,24},{24,28},{28,32},{32,36}... | collective-permute-start | bytes 294920 | tf_op jit(solution)/shard_map/ppermute | solution.py:14
  4.6 8.4 %collective-permute-start.1 = (bf16[32,96,1,16]{1,0,3,2:T(8,128)(2,1)S(1)}, bf16[32,96,1,16]{1,0,3,2:T(8,128)(2,1)S(1)}, u32[]{:S(2)}, u32[]{:S(2)}) collective-permute-start(bf16[32,96,1,16]{1,0,3,2:T(8,128)(2,1)S(1)} %get-tuple-element.27), channel_id=1, source_target_pairs={{4,0},{8,4},{12,8},{16,12},{20,16},{24,20},{28,24},{32,28},{36,32}... | collective-permute-start | bytes 294920 | tf_op jit(solution)/shard_map/ppermute | solution.py:15
  13.5 0.3 pad_select_fusion.1
  13.8 0.3 pad_select_fusion.19
  14.1 0.3 pad_select_fusion.18
  14.4 0.3 pad_select_fusion.17
  14.6 0.3 pad_select_fusion.16
  14.9 0.3 select_reduce_fusion.1
  15.5 0.3 slice.210
  16.3 0.3 pad_select_fusion.13
  18.0 0.5 fusion.15
  18.5 0.3 pad_maximum_fusion
  18.8 1.1 copy-done.4
  19.9 3.7 %collective-permute-start.2 = (bf16[32,96,10,1]{1,0,3,2:T(8,128)(2,1)S(1)}, bf16[32,96,10,1]{1,0,3,2:T(8,128)(2,1)S(1)}, u32[]{:S(2)}, u32[]{:S(2)}) collective-permute-start(bf16[32,96,10,1]{1,0,3,2:T(8,128)(2,1)S(1)} %get-tuple-element.22), channel_id=1, source_target_pairs={{0,1},{1,2},{2,3},{3,64},{64,65},{65,66},{66,67},{67,128},{128,129... | collective-permute-start | bytes 184328 | tf_op jit(solution)/shard_map/ppermute | solution.py:14
  23.6 2.1 %collective-permute-start.3 = (bf16[32,96,10,1]{1,0,3,2:T(8,128)(2,1)S(1)}, bf16[32,96,10,1]{1,0,3,2:T(8,128)(2,1)}, u32[]{:S(2)}, u32[]{:S(2)}) collective-permute-start(bf16[32,96,10,1]{1,0,3,2:T(8,128)(2,1)S(1)} %get-tuple-element.23), channel_id=1, source_target_pairs={{1,0},{2,1},{3,2},{64,3},{65,64},{66,65},{67,66},{128,67},{129,128... | collective-permute-start | bytes 184328 | tf_op jit(solution)/shard_map/ppermute | solution.py:15
  25.8 1.8 %copy.39 = bf16[2,96,8,256]{1,2,0,3:T(8,128)(2,1)} copy(bf16[2,96,8,256]{3,1,2,0:T(8,128)(2,1)S(1)} %fusion.15) | data formatting | bytes 1572864 | tf_op jit(solution)/shard_map/optimization_barrier | solution.py:109
  27.5 9.2 %all-to-all-start = ((bf16[2,96,8,256]{1,2,0,3:T(8,128)(2,1)}), bf16[2,96,8,256]{1,2,0,3:T(8,128)(2,1)S(1)}, u32[]{:S(2)}, u32[]{:S(2)}) async-start(bf16[2,96,8,256]{1,2,0,3:T(8,128)(2,1)} %copy.39), calls=%async_computation | async-start | bytes 2097152 | tf_op jit(solution)/shard_map/all_to_all | solution.py:41
  36.7 10.0 %add_convert_fusion.1 = (bf16[32,96,8,16]{1,0,3,2:T(8,128)(2,1)}, f32[32,96,8,16]{1,0,3,2:T(8,128)S(1)}, f32[32,96,8,16]{1,0,3,2:T(8,128)}) fusion(bf16[32,96,8,16]{1,3,2,0:T(8,128)(2,1)} %param.9, bf16[3,3,96,96]{3,2,1,0:T(8,128)(2,1)S(1)} %copy-done, bf16[32,96,10,1]{1,0,3,2:T(8,128)(2,1)} %collective-permute-done.3, ...), kind=kOutput, calls=%fused_computation.14 | convolution fusion | flops 706928640 | bytes 5990400 | tf_op jit(solution)/shard_map/conv_general_dilated | solution.py:26
  46.7 14.2 %all-to-all-done = bf16[2,96,8,256]{1,2,0,3:T(8,128)(2,1)S(1)} async-done(((bf16[2,96,8,256]{1,2,0,3:T(8,128)(2,1)}), bf16[2,96,8,256]{1,2,0,3:T(8,128)(2,1)S(1)}, u32[]{:S(2)}, u32[]{:S(2)}) %all-to-all-start) | async-done | bytes 786464 | tf_op jit(solution)/shard_map/all_to_all | solution.py:41
  61.0 0.8 copy.41
  61.8 0.8 copy-done.2
  62.6 8.0 %fusion.5 = (bf16[32,96,8,16]{1,0,3,2:T(8,128)(2,1)S(1)}, bf16[32,96,8,16]{1,0,3,2:T(8,128)(2,1)}, bf16[32,96,8,16]{1,0,3,2:T(8,128)(2,1)S(1)}) fusion(f32[32,96,8,16]{1,0,3,2:T(8,128)S(1)} %get-tuple-element.17, f32[32,96,8,16]{1,0,3,2:T(8,128)S(1)} %copy-done.2, f32[96]{0:T(128)S(1)} %get-tuple-element.31, f32[96]{0:T(128)S(1)} %get-tuple-element.32, ...), kind=kLoop, calls=%fused_computation.9 | loop fusion | flops 17694720 | bytes 7079808 | tf_op jit(solution)/shard_map/convert_element_type | solution.py:126
  70.6 1.4 %copy.43 = bf16[32,96,8,16]{1,3,2,0:T(8,128)(2,1)} copy(bf16[32,96,8,16]{1,0,3,2:T(8,128)(2,1)S(1)} %get-tuple-element.33) | data formatting | bytes 1572864 | tf_op jit(solution)/shard_map/convert_element_type | solution.py:112
  72.0 7.8 %all-to-all-start.1 = ((bf16[32,96,8,16]{1,3,2,0:T(8,128)(2,1)}), bf16[32,96,8,16]{1,3,2,0:T(8,128)(2,1)S(1)}, u32[]{:S(2)}, u32[]{:S(2)}) async-start(bf16[32,96,8,16]{1,3,2,0:T(8,128)(2,1)} %copy.43), calls=%async_computation.1 | async-start | bytes 2097152 | tf_op jit(solution)/shard_map/all_to_all | solution.py:37
  79.8 1.9 %collective-permute-start.4 = (bf16[32,96,1,16]{1,0,3,2:T(8,128)(2,1)S(1)}, bf16[32,96,1,16]{1,0,3,2:T(8,128)(2,1)S(1)}, u32[]{:S(2)}, u32[]{:S(2)}) collective-permute-start(bf16[32,96,1,16]{1,0,3,2:T(8,128)(2,1)S(1)} %get-tuple-element.24), channel_id=1, source_target_pairs={{0,4},{4,8},{8,12},{12,16},{16,20},{20,24},{24,28},{28,32},{32,36}... | collective-permute-start | bytes 294920 | tf_op jit(solution)/shard_map/ppermute | solution.py:14
  81.8 8.7 %collective-permute-start.5 = (bf16[32,96,1,16]{1,0,3,2:T(8,128)(2,1)S(1)}, bf16[32,96,1,16]{1,0,3,2:T(8,128)(2,1)S(1)}, u32[]{:S(2)}, u32[]{:S(2)}) collective-permute-start(bf16[32,96,1,16]{1,0,3,2:T(8,128)(2,1)S(1)} %get-tuple-element.25), channel_id=1, source_target_pairs={{4,0},{8,4},{12,8},{16,12},{20,16},{24,20},{28,24},{32,28},{36,32}... | collective-permute-start | bytes 294920 | tf_op jit(solution)/shard_map/ppermute | solution.py:15
  90.4 10.4 %collective-permute-done.4 = bf16[32,96,1,16]{1,0,3,2:T(8,128)(2,1)S(1)} collective-permute-done((bf16[32,96,1,16]{1,0,3,2:T(8,128)(2,1)S(1)}, bf16[32,96,1,16]{1,0,3,2:T(8,128)(2,1)S(1)}, u32[]{:S(2)}, u32[]{:S(2)}) %collective-permute-start.4) | collective-permute-done | bytes 98336 | tf_op jit(solution)/shard_map/ppermute | solution.py:14
  100.8 1.4 %collective-permute-done.5 = bf16[32,96,1,16]{1,0,3,2:T(8,128)(2,1)S(1)} collective-permute-done((bf16[32,96,1,16]{1,0,3,2:T(8,128)(2,1)S(1)}, bf16[32,96,1,16]{1,0,3,2:T(8,128)(2,1)S(1)}, u32[]{:S(2)}, u32[]{:S(2)}) %collective-permute-start.5) | collective-permute-done | bytes 98336 | tf_op jit(solution)/shard_map/ppermute | solution.py:15
  102.2 1.4 %pad_maximum_fusion.1 = bf16[32,96,10,16]{1,0,3,2:T(8,128)(2,1)} fusion(bf16[32,96,1,16]{1,0,3,2:T(8,128)(2,1)S(1)} %collective-permute-done.5, bf16[32,96,8,16]{1,0,3,2:T(8,128)(2,1)S(1)} %get-tuple-element.18, bf16[32,96,1,16]{1,0,3,2:T(8,128)(2,1)S(1)} %collective-permute-done.4), kind=kLoop, calls=%fused_computation.45 | loop fusion | flops 983040 | bytes 1966080 | tf_op jit(solution)/shard_map/concatenate | solution.py:16
  103.6 5.6 %all-to-all-done.1 = bf16[32,96,8,16]{1,3,2,0:T(8,128)(2,1)S(1)} async-done(((bf16[32,96,8,16]{1,3,2,0:T(8,128)(2,1)}), bf16[32,96,8,16]{1,3,2,0:T(8,128)(2,1)S(1)}, u32[]{:S(2)}, u32[]{:S(2)}) %all-to-all-start.1) | async-done | bytes 786464 | tf_op jit(solution)/shard_map/all_to_all | solution.py:37
  109.4 0.4 fusion.27
  109.8 0.5 copy.45
  110.5 0.3 pad_select_fusion
  110.7 0.3 pad_select_fusion.10
  111.0 0.3 pad_select_fusion.9
  111.3 0.3 pad_select_fusion.8
  111.6 0.3 pad_select_fusion.7
  111.9 0.3 select_reduce_fusion
  113.4 0.3 pad_select_fusion.4
  114.9 0.5 fusion.14
  115.3 0.6 copy-done.3
  115.9 5.4 %collective-permute-start.6 = (bf16[32,96,10,1]{1,0,3,2:T(8,128)(2,1)S(1)}, bf16[32,96,10,1]{1,0,3,2:T(8,128)(2,1)S(1)}, u32[]{:S(2)}, u32[]{:S(2)}) collective-permute-start(bf16[32,96,10,1]{1,0,3,2:T(8,128)(2,1)S(1)} %get-tuple-element.20), channel_id=1, source_target_pairs={{0,1},{1,2},{2,3},{3,64},{64,65},{65,66},{66,67},{67,128},{128,129... | collective-permute-start | bytes 184328 | tf_op jit(solution)/shard_map/ppermute | solution.py:14
  121.3 1.9 %collective-permute-start.7 = (bf16[32,96,10,1]{1,0,3,2:T(8,128)(2,1)S(1)}, bf16[32,96,10,1]{1,0,3,2:T(8,128)(2,1)S(1)}, u32[]{:S(2)}, u32[]{:S(2)}) collective-permute-start(bf16[32,96,10,1]{1,0,3,2:T(8,128)(2,1)S(1)} %get-tuple-element.21), channel_id=1, source_target_pairs={{1,0},{2,1},{3,2},{64,3},{65,64},{66,65},{67,66},{128,67},{129,128... | collective-permute-start | bytes 184328 | tf_op jit(solution)/shard_map/ppermute | solution.py:15
  123.2 1.3 copy.47
  124.6 5.2 %collective-permute-done.7 = bf16[32,96,10,1]{1,0,3,2:T(8,128)(2,1)S(1)} collective-permute-done((bf16[32,96,10,1]{1,0,3,2:T(8,128)(2,1)S(1)}, bf16[32,96,10,1]{1,0,3,2:T(8,128)(2,1)S(1)}, u32[]{:S(2)}, u32[]{:S(2)}) %collective-permute-start.7) | collective-permute-done | bytes 61472 | tf_op jit(solution)/shard_map/ppermute | solution.py:15
  129.8 2.7 %fusion.7 = bf16[32,96,8,16]{1,0,3,2:T(8,128)(2,1)S(1)} fusion(bf16[32,96,8,16]{1,0,3,2:T(8,128)(2,1)S(1)} %copy-done.5, bf16[3,3,96,96]{3,2,1,0:T(8,128)(2,1)S(1)} %copy-done, bf16[32,96,10,1]{1,0,3,2:T(8,128)(2,1)S(1)} %collective-permute-done.7, bf16[32,96,10,16]{1,0,3,2:T(8,128)(2,1)S(1)} %copy-done.3, ...), kind=kOutput, calls=%fused_computation.11 | convolution fusion | flops 681762816 | bytes 2844672 | tf_op jit(solution)/shard_map/conv_general_dilated | solution.py:26
  132.4 1.4 %copy.48 = bf16[32,96,8,16]{1,3,2,0:T(8,128)(2,1)} copy(bf16[32,96,8,16]{1,0,3,2:T(8,128)(2,1)S(1)} %fusion.7) | data formatting | bytes 1572864
  (59 shorter events, 5.2 us)
Async XLA Ops:
  0.6 36.1 %copy-start = (bf16[3,3,96,96]{3,2,1,0:T(8,128)(2,1)S(1)}, bf16[3,3,96,96]{3,2,1,0:T(8,128)(2,1)}, u32[]{:S(2)}) copy-start(bf16[3,3,96,96]{3,2,1,0:T(8,128)(2,1)} %param.10) | copy-start | bytes 497668
  0.6 12.4 %copy-start.11 = (s32[28]{0:T(128)S(1)}, s32[28]{0:T(128)}, u32[]{:S(2)}) copy-start(s32[28]{0:T(128)} %param.16) | copy-start | bytes 340
  0.7 12.5 %copy-start.9 = (s32[2,8,256]{2,1,0:T(8,128)S(1)}, s32[2,8,256]{2,1,0:T(8,128)}, u32[]{:S(2)}) copy-start(s32[2,8,256]{2,1,0:T(8,128)} %param.15) | copy-start | bytes 49156
  0.7 12.5 %copy-start.1 = (bf16[2,96,8,256]{3,2,1,0:T(8,128)(2,1)S(1)}, bf16[2,96,8,256]{3,2,1,0:T(8,128)(2,1)}, u32[]{:S(2)}) copy-start(bf16[2,96,8,256]{3,2,1,0:T(8,128)(2,1)} %param.17) | copy-start | bytes 2359300
  0.7 12.5 %copy-start.7 = (bf16[28,96]{1,0:T(8,128)(2,1)S(1)}, bf16[28,96]{1,0:T(8,128)(2,1)}, u32[]{:S(2)}) copy-start(bf16[28,96]{1,0:T(8,128)(2,1)} %param.13) | copy-start | bytes 16132
  2.7 15.8 %collective-permute-start = (bf16[32,96,1,16]{1,0,3,2:T(8,128)(2,1)S(1)}, bf16[32,96,1,16]{1,0,3,2:T(8,128)(2,1)S(1)}, u32[]{:S(2)}, u32[]{:S(2)}) collective-permute-start(bf16[32,96,1,16]{1,0,3,2:T(8,128)(2,1)S(1)} %get-tuple-element.26), channel_id=1, source_target_pairs={{0,4},{4,8},{8,12},{12,16},{16,20},{20,24},{24,28},{28,32},{32,36}... | collective-permute-start | bytes 294920 | tf_op jit(solution)/shard_map/ppermute | solution.py:14
  4.6 13.8 %collective-permute-start.1 = (bf16[32,96,1,16]{1,0,3,2:T(8,128)(2,1)S(1)}, bf16[32,96,1,16]{1,0,3,2:T(8,128)(2,1)S(1)}, u32[]{:S(2)}, u32[]{:S(2)}) collective-permute-start(bf16[32,96,1,16]{1,0,3,2:T(8,128)(2,1)S(1)} %get-tuple-element.27), channel_id=1, source_target_pairs={{4,0},{8,4},{12,8},{16,12},{20,16},{24,20},{28,24},{32,28},{36,32}... | collective-permute-start | bytes 294920 | tf_op jit(solution)/shard_map/ppermute | solution.py:15
  17.3 0.7 copy-start.6
  18.4 7.3 %copy-start.10 = (f32[96,5]{0,1:T(8,128)S(1)}, f32[96,5]{0,1:T(8,128)}, u32[]{:S(2)}) copy-start(f32[96,5]{0,1:T(8,128)} %param.11) | copy-start | bytes 5764
  18.8 1.1 copy-start.4
  19.9 16.8 %collective-permute-start.2 = (bf16[32,96,10,1]{1,0,3,2:T(8,128)(2,1)S(1)}, bf16[32,96,10,1]{1,0,3,2:T(8,128)(2,1)S(1)}, u32[]{:S(2)}, u32[]{:S(2)}) collective-permute-start(bf16[32,96,10,1]{1,0,3,2:T(8,128)(2,1)S(1)} %get-tuple-element.22), channel_id=1, source_target_pairs={{0,1},{1,2},{2,3},{3,64},{64,65},{65,66},{66,67},{67,128},{128,129... | collective-permute-start | bytes 184328 | tf_op jit(solution)/shard_map/ppermute | solution.py:14
  23.6 13.1 %collective-permute-start.3 = (bf16[32,96,10,1]{1,0,3,2:T(8,128)(2,1)S(1)}, bf16[32,96,10,1]{1,0,3,2:T(8,128)(2,1)}, u32[]{:S(2)}, u32[]{:S(2)}) collective-permute-start(bf16[32,96,10,1]{1,0,3,2:T(8,128)(2,1)S(1)} %get-tuple-element.23), channel_id=1, source_target_pairs={{1,0},{2,1},{3,2},{64,3},{65,64},{66,65},{67,66},{128,67},{129,128... | collective-permute-start | bytes 184328 | tf_op jit(solution)/shard_map/ppermute | solution.py:15
  27.5 33.4 %all-to-all-start = ((bf16[2,96,8,256]{1,2,0,3:T(8,128)(2,1)}), bf16[2,96,8,256]{1,2,0,3:T(8,128)(2,1)S(1)}, u32[]{:S(2)}, u32[]{:S(2)}) async-start(bf16[2,96,8,256]{1,2,0,3:T(8,128)(2,1)} %copy.39), calls=%async_computation | async-start | bytes 2097152 | tf_op jit(solution)/shard_map/all_to_all | solution.py:41
  61.0 1.6 %copy-start.2 = (f32[32,96,8,16]{1,0,3,2:T(8,128)S(1)}, f32[32,96,8,16]{1,0,3,2:T(8,128)}, u32[]{:S(2)}) copy-start(f32[32,96,8,16]{1,0,3,2:T(8,128)} %get-tuple-element.40) | copy-start | bytes 4718596
  72.0 37.2 %all-to-all-start.1 = ((bf16[32,96,8,16]{1,3,2,0:T(8,128)(2,1)}), bf16[32,96,8,16]{1,3,2,0:T(8,128)(2,1)S(1)}, u32[]{:S(2)}, u32[]{:S(2)}) async-start(bf16[32,96,8,16]{1,3,2,0:T(8,128)(2,1)} %copy.43), calls=%async_computation.1 | async-start | bytes 2097152 | tf_op jit(solution)/shard_map/all_to_all | solution.py:37
  79.8 21.0 %collective-permute-start.4 = (bf16[32,96,1,16]{1,0,3,2:T(8,128)(2,1)S(1)}, bf16[32,96,1,16]{1,0,3,2:T(8,128)(2,1)S(1)}, u32[]{:S(2)}, u32[]{:S(2)}) collective-permute-start(bf16[32,96,1,16]{1,0,3,2:T(8,128)(2,1)S(1)} %get-tuple-element.24), channel_id=1, source_target_pairs={{0,4},{4,8},{8,12},{12,16},{16,20},{20,24},{24,28},{28,32},{32,36}... | collective-permute-start | bytes 294920 | tf_op jit(solution)/shard_map/ppermute | solution.py:14
  81.8 20.4 %collective-permute-start.5 = (bf16[32,96,1,16]{1,0,3,2:T(8,128)(2,1)S(1)}, bf16[32,96,1,16]{1,0,3,2:T(8,128)(2,1)S(1)}, u32[]{:S(2)}, u32[]{:S(2)}) collective-permute-start(bf16[32,96,1,16]{1,0,3,2:T(8,128)(2,1)S(1)} %get-tuple-element.25), channel_id=1, source_target_pairs={{4,0},{8,4},{12,8},{16,12},{20,16},{24,20},{28,24},{32,28},{36,32}... | collective-permute-start | bytes 294920 | tf_op jit(solution)/shard_map/ppermute | solution.py:15
  111.6 0.7 copy-start.8
  114.6 1.3 copy-start.3
  114.8 14.9 %copy-start.5 = (bf16[32,96,8,16]{1,0,3,2:T(8,128)(2,1)S(1)}, bf16[32,96,8,16]{1,0,3,2:T(8,128)(2,1)}, u32[]{:S(2)}) copy-start(bf16[32,96,8,16]{1,0,3,2:T(8,128)(2,1)} %get-tuple-element.19) | copy-start | bytes 2359300
  115.9 8.7 %collective-permute-start.6 = (bf16[32,96,10,1]{1,0,3,2:T(8,128)(2,1)S(1)}, bf16[32,96,10,1]{1,0,3,2:T(8,128)(2,1)S(1)}, u32[]{:S(2)}, u32[]{:S(2)}) collective-permute-start(bf16[32,96,10,1]{1,0,3,2:T(8,128)(2,1)S(1)} %get-tuple-element.20), channel_id=1, source_target_pairs={{0,1},{1,2},{2,3},{3,64},{64,65},{65,66},{66,67},{67,128},{128,129... | collective-permute-start | bytes 184328 | tf_op jit(solution)/shard_map/ppermute | solution.py:14
  121.3 8.4 %collective-permute-start.7 = (bf16[32,96,10,1]{1,0,3,2:T(8,128)(2,1)S(1)}, bf16[32,96,10,1]{1,0,3,2:T(8,128)(2,1)S(1)}, u32[]{:S(2)}, u32[]{:S(2)}) collective-permute-start(bf16[32,96,10,1]{1,0,3,2:T(8,128)(2,1)S(1)} %get-tuple-element.21), channel_id=1, source_target_pairs={{1,0},{2,1},{3,2},{64,3},{65,64},{66,65},{67,66},{128,67},{129,128... | collective-permute-start | bytes 184328 | tf_op jit(solution)/shard_map/ppermute | solution.py:15

commit v7 on v6

--- a/solution.py
+++ b/solution.py
@@ -31,6 +31,10 @@
         dimension_numbers=("NCHW", "HWIO", "NCHW"),
         preferred_element_type=jnp.float32,
     )
+
+
+def spatial_conv(field_in, kernel):
+    return halo_conv(row_halo(field_in), kernel)
 
 
 def to_time(field_in):
@@ -108,7 +112,9 @@
     feature_rows = row_halo(features)
     feature_rows, cot_temporal = lax.optimization_barrier((feature_rows, cot_temporal))
     pre_act = halo_conv(feature_rows, conv_weight)
-    hidden_state = (features.astype(jnp.float32) + gelu_exact(pre_act)).astype(jnp.bfloat16)
+    gelu_value, pullback = jax.vjp(gelu_exact, pre_act)
+    slope = pullback(jnp.ones_like(pre_act))[0]
+    hidden_state = (features.astype(jnp.float32) + gelu_value).astype(jnp.bfloat16)
     temporal = to_time(time_mix(hidden_state, time_weight).astype(jnp.bfloat16))
     band_vals = jnp.einsum("fcqw,cb->fbqw", temporal, band_out, preferred_element_type=jnp.float32)
     masked_band_sum = disperse(band_vals * mask_float, bits, width_wide)
@@ -122,12 +128,9 @@
     ).astype(jnp.bfloat16)
     flipped = time_weight[:, ::-1]
     cot_hidden = time_mix(to_space(cot_temporal), flipped).astype(jnp.bfloat16)
-    pullback = jax.vjp(gelu_exact, pre_act)[1]
-    gate_grad = pullback(cot_hidden.astype(jnp.float32))[0].astype(jnp.bfloat16)
+    gate_grad = (slope * cot_hidden.astype(jnp.float32)).astype(jnp.bfloat16)
     kernel_flip = jnp.transpose(conv_weight[::-1, ::-1], (0, 1, 3, 2))
-    gate_rows = row_halo(gate_grad)
-    gate_rows, updated = lax.optimization_barrier((gate_rows, updated))
-    features_grad = (cot_hidden.astype(jnp.float32) + halo_conv(gate_rows, kernel_flip)).astype(
+    features_grad = (cot_hidden.astype(jnp.float32) + spatial_conv(gate_grad, kernel_flip)).astype(
         jnp.bfloat16
     )
     return (updated, features_grad)

time: 134 us -> 125 us (0.933)
  the two profiles are of different devices: /device:TPU:14 before, /device:TPU:86 now
where the time goes in v7:
time: 125 us; the launch traced here: 124 us
  starting transfers between devices  56.7 us (45%)
  waiting for transfers between devices  30.3 us (24%)
  matrix products  14.7 us (12%)
  local copies, waits for them, and re-layouts  13 us (10%)
  other arithmetic  8.2 us (7%)
    ppermute x4, starting transfers between devices, with_halo(): after = lax.ppermute(initial, axis, down)  21.7 us
    ppermute x4, starting transfers between devices, with_halo(): before = lax.ppermute(last, axis, up)  18.7 us
    all_to_all x1, waiting for transfers between devices, to_space(): lax.all_to_all(field_in, ('ta', 'col'), split_axis=3, concat_axis=0, tile...  17.1 us
    conv_general_dilated x2, matrix products, halo_conv(): lax.conv_general_dilated(padded, kernel, window_strides=(1, 1), padding='...  13 us
    all_to_all x1, starting transfers between devices, to_time(): lax.all_to_all(field_in, ('ta', 'col'), split_axis=0, concat_axis=3, tile...  8.42 us
    all_to_all x1, starting transfers between devices, to_space(): lax.all_to_all(field_in, ('ta', 'col'), split_axis=3, concat_axis=0, tile...  7.95 us
    ppermute x4, waiting for transfers between devices, with_halo(): before = lax.ppermute(last, axis, up)  6.9 us
    ppermute x4, waiting for transfers between devices, with_halo(): after = lax.ppermute(initial, axis, down)  6.23 us
  transfers between devices with their start and end apart: 10, of which 4 were waited for; matrix products, arithmetic and copies ran while one was open for 9% of the time, Pallas kernels for 0%

profile of v7, /device:TPU:86, one launch (start us, length us, event | category | flops | bytes accessed | tf_op | source)
XLA Modules:
  0.0 124.1 jit_solution(12205112395090420941)
XLA Ops:
  0.7 2.0 %copy.34 = bf16[32,96,8,16]{1,0,3,2:T(8,128)(2,1)S(1)} copy(bf16[32,96,8,16]{1,3,2,0:T(8,128)(2,1)} %param.9) | data formatting | bytes 1572864 | tf_op args[0]
  2.7 1.9 %collective-permute-start = (bf16[32,96,1,16]{1,0,3,2:T(8,128)(2,1)S(1)}, bf16[32,96,1,16]{1,0,3,2:T(8,128)(2,1)S(1)}, u32[]{:S(2)}, u32[]{:S(2)}) collective-permute-start(bf16[32,96,1,16]{1,0,3,2:T(8,128)(2,1)S(1)} %get-tuple-element.21), channel_id=1, source_target_pairs={{0,4},{4,8},{8,12},{12,16},{16,20},{20,24},{24,28},{28,32},{32,36}... | collective-permute-start | bytes 294920 | tf_op jit(solution)/shard_map/ppermute | solution.py:14
  4.6 8.4 %collective-permute-start.1 = (bf16[32,96,1,16]{1,0,3,2:T(8,128)(2,1)S(1)}, bf16[32,96,1,16]{1,0,3,2:T(8,128)(2,1)S(1)}, u32[]{:S(2)}, u32[]{:S(2)}) collective-permute-start(bf16[32,96,1,16]{1,0,3,2:T(8,128)(2,1)S(1)} %get-tuple-element.22), channel_id=1, source_target_pairs={{4,0},{8,4},{12,8},{16,12},{20,16},{24,20},{28,24},{32,28},{36,32}... | collective-permute-start | bytes 294920 | tf_op jit(solution)/shard_map/ppermute | solution.py:15
  13.5 0.3 pad_select_fusion.1
  13.8 0.3 pad_select_fusion.19
  14.1 0.3 pad_select_fusion.18
  14.4 0.3 pad_select_fusion.17
  14.6 0.3 pad_select_fusion.16
  14.9 0.3 select_reduce_fusion.1
  15.5 0.3 slice.210
  16.0 0.3 slice.211
  16.2 0.3 pad_select_fusion.13
  16.5 0.3 slice.212
  17.0 0.3 slice.213
  17.9 0.5 fusion.9
  18.4 0.3 pad_maximum_fusion
  18.7 1.7 %copy.44 = bf16[2,96,8,256]{1,2,0,3:T(8,128)(2,1)} copy(bf16[2,96,8,256]{3,1,2,0:T(8,128)(2,1)S(1)} %fusion.9) | data formatting | bytes 1572864 | tf_op jit(solution)/shard_map/optimization_barrier | solution.py:113
  20.5 7.9 %all-to-all-start.1 = ((bf16[2,96,8,256]{1,2,0,3:T(8,128)(2,1)}), bf16[2,96,8,256]{1,2,0,3:T(8,128)(2,1)S(1)}, u32[]{:S(2)}, u32[]{:S(2)}) async-start(bf16[2,96,8,256]{1,2,0,3:T(8,128)(2,1)} %copy.44), calls=%async_computation.1 | async-start | bytes 2097152 | tf_op jit(solution)/shard_map/all_to_all | solution.py:45
  28.5 3.4 %collective-permute-start.2 = (bf16[32,96,10,1]{1,0,3,2:T(8,128)(2,1)S(1)}, bf16[32,96,10,1]{1,0,3,2:T(8,128)(2,1)S(1)}, u32[]{:S(2)}, u32[]{:S(2)}) collective-permute-start(bf16[32,96,10,1]{1,0,3,2:T(8,128)(2,1)S(1)} %get-tuple-element.17), channel_id=1, source_target_pairs={{0,1},{1,2},{2,3},{3,64},{64,65},{65,66},{66,67},{67,128},{128,129... | collective-permute-start | bytes 184328 | tf_op jit(solution)/shard_map/ppermute | solution.py:14
  31.8 2.7 %collective-permute-start.3 = (bf16[32,96,10,1]{1,0,3,2:T(8,128)(2,1)S(1)}, bf16[32,96,10,1]{1,0,3,2:T(8,128)(2,1)S(1)}, u32[]{:S(2)}, u32[]{:S(2)}) collective-permute-start(bf16[32,96,10,1]{1,0,3,2:T(8,128)(2,1)S(1)} %get-tuple-element.18), channel_id=1, source_target_pairs={{1,0},{2,1},{3,2},{64,3},{65,64},{66,65},{67,66},{128,67},{129,128... | collective-permute-start | bytes 184328 | tf_op jit(solution)/shard_map/ppermute | solution.py:15
  34.5 17.1 %all-to-all-done.1 = bf16[2,96,8,256]{1,2,0,3:T(8,128)(2,1)S(1)} async-done(((bf16[2,96,8,256]{1,2,0,3:T(8,128)(2,1)}), bf16[2,96,8,256]{1,2,0,3:T(8,128)(2,1)S(1)}, u32[]{:S(2)}, u32[]{:S(2)}) %all-to-all-start.1) | async-done | bytes 786464 | tf_op jit(solution)/shard_map/all_to_all | solution.py:45
  51.7 0.8 copy.46
  52.5 9.2 %fusion = (bf16[32,96,8,16]{1,0,3,2:T(8,128)(2,1)S(1)}, bf16[32,96,8,16]{1,0,3,2:T(8,128)(2,1)}, f32[32,96,8,16]{1,0,3,2:T(8,128)S(1)}, f32[32,96,8,16]{1,0,3,2:T(8,128)S(1)}) fusion(f32[96]{0:T(128)S(1)} %get-tuple-element.26, f32[96]{0:T(128)S(1)} %get-tuple-element.25, bf16[32,96,8,16]{1,0,3,2:T(8,128)(2,1)S(1)} %bitcast.71, ...), kind=kOutput, calls=%fused_computation.3 | convolution fusion | flops 714399744 | bytes 6778752 | tf_op jit(solution)/shard_map/conv_general_dilated | solution.py:26
  61.7 1.0 add_convert_fusion.2
  62.7 1.6 %add_convert_fusion.1 = bf16[32,96,8,16]{1,0,3,2:T(8,128)(2,1)S(1)} fusion(bf16[32,96,8,16]{1,0,3,2:T(8,128)(2,1)S(1)} %add_convert_fusion.2, f32[96]{0:T(128)S(1)} %get-tuple-element.23, f32[96]{0:T(128)S(1)} %get-tuple-element.27, f32[96]{0:T(128)S(1)} %get-tuple-element.24, f32[96]{0:T(128)S(1)} %get-tuple-element.25, f32[96]{0:T(128)S(1)} %get-tuple-element.26), kind=kLoop, calls=%fused_computation.7 | loop fusion | flops 5898240 | bytes 1574784 | tf_op jit(solution)/shard_map/convert_element_type | solution.py:118
  64.3 1.4 %copy.40 = bf16[32,96,8,16]{1,3,2,0:T(8,128)(2,1)} copy(bf16[32,96,8,16]{1,0,3,2:T(8,128)(2,1)S(1)} %add_convert_fusion.1) | data formatting | bytes 1572864 | tf_op jit(solution)/shard_map/convert_element_type | solution.py:118
  65.7 8.4 %all-to-all-start = ((bf16[32,96,8,16]{1,3,2,0:T(8,128)(2,1)}), bf16[32,96,8,16]{1,3,2,0:T(8,128)(2,1)S(1)}, u32[]{:S(2)}, u32[]{:S(2)}) async-start(bf16[32,96,8,16]{1,3,2,0:T(8,128)(2,1)} %copy.40), calls=%async_computation | async-start | bytes 2097152 | tf_op jit(solution)/shard_map/all_to_all | solution.py:41
  74.1 1.9 %collective-permute-start.4 = (bf16[32,96,1,16]{1,0,3,2:T(8,128)(2,1)S(1)}, bf16[32,96,1,16]{1,0,3,2:T(8,128)(2,1)S(1)}, u32[]{:S(2)}, u32[]{:S(2)}) collective-permute-start(bf16[32,96,1,16]{1,0,3,2:T(8,128)(2,1)S(1)} %get-tuple-element.19), channel_id=1, source_target_pairs={{0,4},{4,8},{8,12},{12,16},{16,20},{20,24},{24,28},{28,32},{32,36}... | collective-permute-start | bytes 294920 | tf_op jit(solution)/shard_map/ppermute | solution.py:14
  76.1 8.4 %collective-permute-start.5 = (bf16[32,96,1,16]{1,0,3,2:T(8,128)(2,1)S(1)}, bf16[32,96,1,16]{1,0,3,2:T(8,128)(2,1)S(1)}, u32[]{:S(2)}, u32[]{:S(2)}) collective-permute-start(bf16[32,96,1,16]{1,0,3,2:T(8,128)(2,1)S(1)} %get-tuple-element.20), channel_id=1, source_target_pairs={{4,0},{8,4},{12,8},{16,12},{20,16},{24,20},{28,24},{32,28},{36,32}... | collective-permute-start | bytes 294920 | tf_op jit(solution)/shard_map/ppermute | solution.py:15
  84.5 6.5 %collective-permute-done.4 = bf16[32,96,1,16]{1,0,3,2:T(8,128)(2,1)S(1)} collective-permute-done((bf16[32,96,1,16]{1,0,3,2:T(8,128)(2,1)S(1)}, bf16[32,96,1,16]{1,0,3,2:T(8,128)(2,1)S(1)}, u32[]{:S(2)}, u32[]{:S(2)}) %collective-permute-start.4) | collective-permute-done | bytes 98336 | tf_op jit(solution)/shard_map/ppermute | solution.py:14
  91.1 11.5 %collective-permute-start.6 = (bf16[32,96,10,1]{1,0,3,2:T(8,128)(2,1)S(1)}, bf16[32,96,10,1]{1,0,3,2:T(8,128)(2,1)S(1)}, u32[]{:S(2)}, u32[]{:S(2)}) collective-permute-start(bf16[32,96,10,1]{1,0,3,2:T(8,128)(2,1)S(1)} %get-tuple-element.15), channel_id=1, source_target_pairs={{0,1},{1,2},{2,3},{3,64},{64,65},{65,66},{66,67},{67,128},{128,129... | collective-permute-start | bytes 184328 | tf_op jit(solution)/shard_map/ppermute | solution.py:14
  102.6 2.1 %collective-permute-start.7 = (bf16[32,96,10,1]{1,0,3,2:T(8,128)(2,1)S(1)}, bf16[32,96,10,1]{1,0,3,2:T(8,128)(2,1)S(1)}, u32[]{:S(2)}, u32[]{:S(2)}) collective-permute-start(bf16[32,96,10,1]{1,0,3,2:T(8,128)(2,1)S(1)} %get-tuple-element.16), channel_id=1, source_target_pairs={{1,0},{2,1},{3,2},{64,3},{65,64},{66,65},{67,66},{128,67},{129,128... | collective-permute-start | bytes 184328 | tf_op jit(solution)/shard_map/ppermute | solution.py:15
  104.7 0.3 collective-permute-done.6
  105.1 6.2 %collective-permute-done.7 = bf16[32,96,10,1]{1,0,3,2:T(8,128)(2,1)S(1)} collective-permute-done((bf16[32,96,10,1]{1,0,3,2:T(8,128)(2,1)S(1)}, bf16[32,96,10,1]{1,0,3,2:T(8,128)(2,1)S(1)}, u32[]{:S(2)}, u32[]{:S(2)}) %collective-permute-start.7) | collective-permute-done | bytes 61472 | tf_op jit(solution)/shard_map/ppermute | solution.py:15
  111.3 3.8 %fusion.1 = bf16[32,96,8,16]{1,0,3,2:T(8,128)(2,1)S(1)} fusion(bf16[32,96,8,16]{1,0,3,2:T(8,128)(2,1)} %get-tuple-element.13, bf16[3,3,96,96]{3,2,1,0:T(8,128)(2,1)S(1)} %copy-done, bf16[32,96,10,1]{1,0,3,2:T(8,128)(2,1)S(1)} %collective-permute-done.7, bf16[32,96,1,16]{1,0,3,2:T(8,128)(2,1)S(1)} %collective-permute-done.5, ...), kind=kOutput, calls=%fused_computation.4 | convolution fusion | flops 682868736 | bytes 2844672 | tf_op jit(solution)/shard_map/conv_general_dilated | solution.py:26
  115.2 1.4 %copy.48 = bf16[32,96,8,16]{1,3,2,0:T(8,128)(2,1)} copy(bf16[32,96,8,16]{1,0,3,2:T(8,128)(2,1)S(1)} %fusion.1) | data formatting | bytes 1572864
  116.8 0.4 fusion.25
  117.2 0.5 copy.42
  117.9 0.3 pad_select_fusion
  118.1 0.3 pad_select_fusion.10
  118.4 0.3 pad_select_fusion.9
  118.7 0.3 pad_select_fusion.8
  119.0 0.3 pad_select_fusion.7
  119.3 0.3 select_reduce_fusion
  120.0 0.3 slice.222
  120.8 0.3 pad_select_fusion.4
  122.2 0.5 fusion.8
  122.8 1.3 %copy.47 = bf16[2,96,8,256]{3,2,1,0:T(8,128)(2,1)} copy(bf16[2,96,8,256]{3,1,2,0:T(8,128)(2,1)S(1)} %fusion.8) | data formatting | bytes 1572864
  (53 shorter events, 4.2 us)
Async XLA Ops:
  0.6 51.9 %copy-start = (bf16[3,3,96,96]{3,2,1,0:T(8,128)(2,1)S(1)}, bf16[3,3,96,96]{3,2,1,0:T(8,128)(2,1)}, u32[]{:S(2)}) copy-start(bf16[3,3,96,96]{3,2,1,0:T(8,128)(2,1)} %param.10) | copy-start | bytes 497668
  0.6 12.4 %copy-start.8 = (s32[28]{0:T(128)S(1)}, s32[28]{0:T(128)}, u32[]{:S(2)}) copy-start(s32[28]{0:T(128)} %param.16) | copy-start | bytes 340
  0.7 12.5 %copy-start.6 = (s32[2,8,256]{2,1,0:T(8,128)S(1)}, s32[2,8,256]{2,1,0:T(8,128)}, u32[]{:S(2)}) copy-start(s32[2,8,256]{2,1,0:T(8,128)} %param.15) | copy-start | bytes 49156
  0.7 12.5 %copy-start.2 = (bf16[2,96,8,256]{3,2,1,0:T(8,128)(2,1)S(1)}, bf16[2,96,8,256]{3,2,1,0:T(8,128)(2,1)}, u32[]{:S(2)}) copy-start(bf16[2,96,8,256]{3,2,1,0:T(8,128)(2,1)} %param.17) | copy-start | bytes 2359300
  0.7 12.5 %copy-start.4 = (bf16[28,96]{1,0:T(8,128)(2,1)S(1)}, bf16[28,96]{1,0:T(8,128)(2,1)}, u32[]{:S(2)}) copy-start(bf16[28,96]{1,0:T(8,128)(2,1)} %param.13) | copy-start | bytes 16132
  2.7 15.7 %collective-permute-start = (bf16[32,96,1,16]{1,0,3,2:T(8,128)(2,1)S(1)}, bf16[32,96,1,16]{1,0,3,2:T(8,128)(2,1)S(1)}, u32[]{:S(2)}, u32[]{:S(2)}) collective-permute-start(bf16[32,96,1,16]{1,0,3,2:T(8,128)(2,1)S(1)} %get-tuple-element.21), channel_id=1, source_target_pairs={{0,4},{4,8},{8,12},{12,16},{16,20},{20,24},{24,28},{28,32},{32,36}... | collective-permute-start | bytes 294920 | tf_op jit(solution)/shard_map/ppermute | solution.py:14
  4.6 13.8 %collective-permute-start.1 = (bf16[32,96,1,16]{1,0,3,2:T(8,128)(2,1)S(1)}, bf16[32,96,1,16]{1,0,3,2:T(8,128)(2,1)S(1)}, u32[]{:S(2)}, u32[]{:S(2)}) collective-permute-start(bf16[32,96,1,16]{1,0,3,2:T(8,128)(2,1)S(1)} %get-tuple-element.22), channel_id=1, source_target_pairs={{4,0},{8,4},{12,8},{16,12},{20,16},{24,20},{28,24},{32,28},{36,32}... | collective-permute-start | bytes 294920 | tf_op jit(solution)/shard_map/ppermute | solution.py:15
  17.2 0.7 copy-start.3
  18.7 15.8 %copy-start.7 = (f32[96,5]{0,1:T(8,128)S(1)}, f32[96,5]{0,1:T(8,128)}, u32[]{:S(2)}) copy-start(f32[96,5]{0,1:T(8,128)} %param.11) | copy-start | bytes 5764
  20.5 31.2 %all-to-all-start.1 = ((bf16[2,96,8,256]{1,2,0,3:T(8,128)(2,1)}), bf16[2,96,8,256]{1,2,0,3:T(8,128)(2,1)S(1)}, u32[]{:S(2)}, u32[]{:S(2)}) async-start(bf16[2,96,8,256]{1,2,0,3:T(8,128)(2,1)} %copy.44), calls=%async_computation.1 | async-start | bytes 2097152 | tf_op jit(solution)/shard_map/all_to_all | solution.py:45
  28.5 24.0 %collective-permute-start.2 = (bf16[32,96,10,1]{1,0,3,2:T(8,128)(2,1)S(1)}, bf16[32,96,10,1]{1,0,3,2:T(8,128)(2,1)S(1)}, u32[]{:S(2)}, u32[]{:S(2)}) collective-permute-start(bf16[32,96,10,1]{1,0,3,2:T(8,128)(2,1)S(1)} %get-tuple-element.17), channel_id=1, source_target_pairs={{0,1},{1,2},{2,3},{3,64},{64,65},{65,66},{66,67},{67,128},{128,129... | collective-permute-start | bytes 184328 | tf_op jit(solution)/shard_map/ppermute | solution.py:14
  31.8 20.7 %collective-permute-start.3 = (bf16[32,96,10,1]{1,0,3,2:T(8,128)(2,1)S(1)}, bf16[32,96,10,1]{1,0,3,2:T(8,128)(2,1)S(1)}, u32[]{:S(2)}, u32[]{:S(2)}) collective-permute-start(bf16[32,96,10,1]{1,0,3,2:T(8,128)(2,1)S(1)} %get-tuple-element.18), channel_id=1, source_target_pairs={{1,0},{2,1},{3,2},{64,3},{65,64},{66,65},{67,66},{128,67},{129,128... | collective-permute-start | bytes 184328 | tf_op jit(solution)/shard_map/ppermute | solution.py:15
  52.5 9.2 %copy-start.1 = (bf16[32,96,8,16]{1,3,2,0:T(8,128)(2,1)S(1)}, bf16[32,96,8,16]{1,3,2,0:T(8,128)(2,1)}, u32[]{:S(2)}) copy-start(bf16[32,96,8,16]{1,3,2,0:T(8,128)(2,1)} %param.9) | copy-start | bytes 2359300
  65.7 50.8 %all-to-all-start = ((bf16[32,96,8,16]{1,3,2,0:T(8,128)(2,1)}), bf16[32,96,8,16]{1,3,2,0:T(8,128)(2,1)S(1)}, u32[]{:S(2)}, u32[]{:S(2)}) async-start(bf16[32,96,8,16]{1,3,2,0:T(8,128)(2,1)} %copy.40), calls=%async_computation | async-start | bytes 2097152 | tf_op jit(solution)/shard_map/all_to_all | solution.py:41
  74.1 16.9 %collective-permute-start.4 = (bf16[32,96,1,16]{1,0,3,2:T(8,128)(2,1)S(1)}, bf16[32,96,1,16]{1,0,3,2:T(8,128)(2,1)S(1)}, u32[]{:S(2)}, u32[]{:S(2)}) collective-permute-start(bf16[32,96,1,16]{1,0,3,2:T(8,128)(2,1)S(1)} %get-tuple-element.19), channel_id=1, source_target_pairs={{0,4},{4,8},{8,12},{12,16},{16,20},{20,24},{24,28},{28,32},{32,36}... | collective-permute-start | bytes 294920 | tf_op jit(solution)/shard_map/ppermute | solution.py:14
  76.1 15.0 %collective-permute-start.5 = (bf16[32,96,1,16]{1,0,3,2:T(8,128)(2,1)S(1)}, bf16[32,96,1,16]{1,0,3,2:T(8,128)(2,1)S(1)}, u32[]{:S(2)}, u32[]{:S(2)}) collective-permute-start(bf16[32,96,1,16]{1,0,3,2:T(8,128)(2,1)S(1)} %get-tuple-element.20), channel_id=1, source_target_pairs={{4,0},{8,4},{12,8},{16,12},{20,16},{24,20},{28,24},{32,28},{36,32}... | collective-permute-start | bytes 294920 | tf_op jit(solution)/shard_map/ppermute | solution.py:15
  91.1 14.0 %collective-permute-start.6 = (bf16[32,96,10,1]{1,0,3,2:T(8,128)(2,1)S(1)}, bf16[32,96,10,1]{1,0,3,2:T(8,128)(2,1)S(1)}, u32[]{:S(2)}, u32[]{:S(2)}) collective-permute-start(bf16[32,96,10,1]{1,0,3,2:T(8,128)(2,1)S(1)} %get-tuple-element.15), channel_id=1, source_target_pairs={{0,1},{1,2},{2,3},{3,64},{64,65},{65,66},{66,67},{67,128},{128,129... | collective-permute-start | bytes 184328 | tf_op jit(solution)/shard_map/ppermute | solution.py:14
  102.6 8.7 %collective-permute-start.7 = (bf16[32,96,10,1]{1,0,3,2:T(8,128)(2,1)S(1)}, bf16[32,96,10,1]{1,0,3,2:T(8,128)(2,1)S(1)}, u32[]{:S(2)}, u32[]{:S(2)}) collective-permute-start(bf16[32,96,10,1]{1,0,3,2:T(8,128)(2,1)S(1)} %get-tuple-element.16), channel_id=1, source_target_pairs={{1,0},{2,1},{3,2},{64,3},{65,64},{66,65},{67,66},{128,67},{129,128... | collective-permute-start | bytes 184328 | tf_op jit(solution)/shard_map/ppermute | solution.py:15
  119.0 0.7 copy-start.5

commit v8 on v7

--- a/solution.py
+++ b/solution.py
@@ -127,7 +127,8 @@
         )
     ).astype(jnp.bfloat16)
     flipped = time_weight[:, ::-1]
-    cot_hidden = time_mix(to_space(cot_temporal), flipped).astype(jnp.bfloat16)
+    cot_space, slope = lax.optimization_barrier((to_space(cot_temporal), slope))
+    cot_hidden = time_mix(cot_space, flipped).astype(jnp.bfloat16)
     gate_grad = (slope * cot_hidden.astype(jnp.float32)).astype(jnp.bfloat16)
     kernel_flip = jnp.transpose(conv_weight[::-1, ::-1], (0, 1, 3, 2))
     features_grad = (cot_hidden.astype(jnp.float32) + spatial_conv(gate_grad, kernel_flip)).astype(

time: 125 us -> 121 us (0.968)
  waiting for transfers between devices: 30.3 us -> 27.5 us
  matrix products: 14.7 us -> 12.3 us
  other arithmetic: 8.2 us -> 9.88 us
  starting transfers between devices: 56.7 us -> 55.3 us
    conv_general_dilated x2, matrix products: 13 us -> 10.7 us  [halo_conv(): lax.conv_general_dilated(padded, kernel, window_strides=(1, 1), padding='...]
    all_to_all x1, waiting for transfers between devices: 17.1 us -> 15 us  [to_space(): lax.all_to_all(field_in, ('ta', 'col'), split_axis=3, concat_axis=0, tile...]
    convert_element_type x1, other arithmetic: 1.56 us -> 3.4 us  [on_device(): gate_grad = (slope * cot_hidden.astype(jnp.float32)).astype(jnp.bfloat16)]
    unnamed x21 -> x23, local copies, waits for them, and re-layouts: 5.13 us -> 5.91 us
  transfers between devices with their start and end apart: 10 -> 10, of which waited for: 4 -> 4; matrix products, arithmetic and copies ran while one was open for 9% -> 16% of each run, Pallas kernels for 0% -> 0%
where the time goes in v8:
time: 121 us; the launch traced here: 120 us
  starting transfers between devices  55.3 us (46%)
  waiting for transfers between devices  27.5 us (23%)
  local copies, waits for them, and re-layouts  13.8 us (11%)
  matrix products  12.3 us (10%)
  other arithmetic  9.88 us (8%)
    ppermute x4, starting transfers between devices, with_halo(): after = lax.ppermute(initial, axis, down)  21.1 us
    ppermute x4, starting transfers between devices, with_halo(): before = lax.ppermute(last, axis, up)  17.9 us
    all_to_all x1, waiting for transfers between devices, to_space(): lax.all_to_all(field_in, ('ta', 'col'), split_axis=3, concat_axis=0, tile...  15 us
    conv_general_dilated x2, matrix products, halo_conv(): lax.conv_general_dilated(padded, kernel, window_strides=(1, 1), padding='...  10.7 us
    all_to_all x1, starting transfers between devices, to_time(): lax.all_to_all(field_in, ('ta', 'col'), split_axis=0, concat_axis=3, tile...  8.33 us
    all_to_all x1, starting transfers between devices, to_space(): lax.all_to_all(field_in, ('ta', 'col'), split_axis=3, concat_axis=0, tile...  7.95 us
    ppermute x4, waiting for transfers between devices, with_halo(): after = lax.ppermute(initial, axis, down)  6.41 us
    ppermute x4, waiting for transfers between devices, with_halo(): before = lax.ppermute(last, axis, up)  6.09 us
  transfers between devices with their start and end apart: 10, of which 4 were waited for; matrix products, arithmetic and copies ran while one was open for 16% of the time, Pallas kernels for 0%

profile of v8, /device:TPU:86, one launch (start us, length us, event | category | flops | bytes accessed | tf_op | source)
XLA Modules:
  0.0 120.0 jit_solution(4766448071632746042)
XLA Ops:
  0.7 2.0 %copy.34 = bf16[32,96,8,16]{1,0,3,2:T(8,128)(2,1)S(1)} copy(bf16[32,96,8,16]{1,3,2,0:T(8,128)(2,1)} %param.9) | data formatting | bytes 1572864 | tf_op args[0]
  2.7 1.9 %collective-permute-start = (bf16[32,96,1,16]{1,0,3,2:T(8,128)(2,1)S(1)}, bf16[32,96,1,16]{1,0,3,2:T(8,128)(2,1)S(1)}, u32[]{:S(2)}, u32[]{:S(2)}) collective-permute-start(bf16[32,96,1,16]{1,0,3,2:T(8,128)(2,1)S(1)} %get-tuple-element.26), channel_id=1, source_target_pairs={{0,4},{4,8},{8,12},{12,16},{16,20},{20,24},{24,28},{28,32},{32,36}... | collective-permute-start | bytes 294920 | tf_op jit(solution)/shard_map/ppermute | solution.py:14
  4.6 8.4 %collective-permute-start.1 = (bf16[32,96,1,16]{1,0,3,2:T(8,128)(2,1)S(1)}, bf16[32,96,1,16]{1,0,3,2:T(8,128)(2,1)S(1)}, u32[]{:S(2)}, u32[]{:S(2)}) collective-permute-start(bf16[32,96,1,16]{1,0,3,2:T(8,128)(2,1)S(1)} %get-tuple-element.27), channel_id=1, source_target_pairs={{4,0},{8,4},{12,8},{16,12},{20,16},{24,20},{28,24},{32,28},{36,32}... | collective-permute-start | bytes 294920 | tf_op jit(solution)/shard_map/ppermute | solution.py:15
  13.5 0.3 pad_select_fusion.1
  13.8 0.3 pad_select_fusion.19
  14.1 0.3 pad_select_fusion.18
  14.4 0.3 pad_select_fusion.17
  14.6 0.3 pad_select_fusion.16
  14.9 0.3 select_reduce_fusion.1
  15.5 0.3 slice.210
  16.0 0.3 slice.211
  16.2 0.3 pad_select_fusion.13
  16.5 0.3 slice.212
  17.9 0.5 fusion.9
  18.4 0.3 pad_maximum_fusion
  18.8 3.7 %collective-permute-start.2 = (bf16[32,96,10,1]{1,0,3,2:T(8,128)(2,1)S(1)}, bf16[32,96,10,1]{1,0,3,2:T(8,128)(2,1)S(1)}, u32[]{:S(2)}, u32[]{:S(2)}) collective-permute-start(bf16[32,96,10,1]{1,0,3,2:T(8,128)(2,1)S(1)} %get-tuple-element.22), channel_id=1, source_target_pairs={{0,1},{1,2},{2,3},{3,64},{64,65},{65,66},{66,67},{67,128},{128,129... | collective-permute-start | bytes 184328 | tf_op jit(solution)/shard_map/ppermute | solution.py:14
  22.5 2.1 %collective-permute-start.3 = (bf16[32,96,10,1]{1,0,3,2:T(8,128)(2,1)S(1)}, bf16[32,96,10,1]{1,0,3,2:T(8,128)(2,1)S(1)}, u32[]{:S(2)}, u32[]{:S(2)}) collective-permute-start(bf16[32,96,10,1]{1,0,3,2:T(8,128)(2,1)S(1)} %get-tuple-element.23), channel_id=1, source_target_pairs={{1,0},{2,1},{3,2},{64,3},{65,64},{66,65},{67,66},{128,67},{129,128... | collective-permute-start | bytes 184328 | tf_op jit(solution)/shard_map/ppermute | solution.py:15
  24.6 1.7 %copy.44 = bf16[2,96,8,256]{1,2,0,3:T(8,128)(2,1)} copy(bf16[2,96,8,256]{3,1,2,0:T(8,128)(2,1)S(1)} %fusion.9) | data formatting | bytes 1572864 | tf_op jit(solution)/shard_map/optimization_barrier | solution.py:113
  26.4 7.9 %all-to-all-start.1 = ((bf16[2,96,8,256]{1,2,0,3:T(8,128)(2,1)}), bf16[2,96,8,256]{1,2,0,3:T(8,128)(2,1)S(1)}, u32[]{:S(2)}, u32[]{:S(2)}) async-start(bf16[2,96,8,256]{1,2,0,3:T(8,128)(2,1)} %copy.44), calls=%async_computation.1 | async-start | bytes 2097152 | tf_op jit(solution)/shard_map/all_to_all | solution.py:45
  34.4 8.0 %multiply_add_fusion = (f32[32,96,8,16]{1,0,3,2:T(8,128)}, f32[32,96,8,16]{1,0,3,2:T(8,128)S(1)}, f32[32,96,8,16]{1,0,3,2:T(8,128)S(1)}) fusion(bf16[3,3,96,96]{3,2,1,0:T(8,128)(2,1)S(1)} %copy-done, bf16[32,96,10,1]{1,0,3,2:T(8,128)(2,1)S(1)} %collective-permute-done.3, bf16[32,96,10,16]{1,0,3,2:T(8,128)(2,1)S(1)} %pad_maximum_fusion, ...), kind=kOutput, calls=%fused_computation.7 | convolution fusion | flops 707321856 | bytes 5990400 | tf_op jit(solution)/shard_map/conv_general_dilated | solution.py:26
  42.4 0.9 add_convert_fusion.2
  43.3 15.0 %all-to-all-done.1 = bf16[2,96,8,256]{1,2,0,3:T(8,128)(2,1)S(1)} async-done(((bf16[2,96,8,256]{1,2,0,3:T(8,128)(2,1)}), bf16[2,96,8,256]{1,2,0,3:T(8,128)(2,1)S(1)}, u32[]{:S(2)}, u32[]{:S(2)}) %all-to-all-start.1) | async-done | bytes 786464 | tf_op jit(solution)/shard_map/all_to_all | solution.py:45
  58.3 0.8 copy.46
  59.1 0.8 copy-done.3
  59.9 3.4 %fusion = (bf16[32,96,8,16]{1,0,3,2:T(8,128)(2,1)S(1)}, bf16[32,96,8,16]{1,0,3,2:T(8,128)(2,1)S(1)}, bf16[32,96,8,16]{1,0,3,2:T(8,128)(2,1)S(1)}) fusion(f32[32,96,8,16]{1,0,3,2:T(8,128)S(1)} %copy-done.3, f32[96]{0:T(128)S(1)} %get-tuple-element.28, f32[96]{0:T(128)S(1)} %get-tuple-element.30, bf16[32,96,8,16]{1,0,3,2:T(8,128)(2,1)S(1)} %bitcast.71, ...), kind=kLoop, calls=%fused_computation.3 | loop fusion | flops 12976128 | bytes 5506944 | tf_op jit(solution)/shard_map/convert_element_type | solution.py:132
  63.3 1.4 %copy.40 = bf16[32,96,8,16]{1,3,2,0:T(8,128)(2,1)} copy(bf16[32,96,8,16]{1,0,3,2:T(8,128)(2,1)S(1)} %get-tuple-element.33) | data formatting | bytes 1572864 | tf_op jit(solution)/shard_map/convert_element_type | solution.py:118
  64.7 8.3 %all-to-all-start = ((bf16[32,96,8,16]{1,3,2,0:T(8,128)(2,1)}), bf16[32,96,8,16]{1,3,2,0:T(8,128)(2,1)S(1)}, u32[]{:S(2)}, u32[]{:S(2)}) async-start(bf16[32,96,8,16]{1,3,2,0:T(8,128)(2,1)} %copy.40), calls=%async_computation | async-start | bytes 2097152 | tf_op jit(solution)/shard_map/all_to_all | solution.py:41
  73.0 1.9 %collective-permute-start.4 = (bf16[32,96,1,16]{1,0,3,2:T(8,128)(2,1)S(1)}, bf16[32,96,1,16]{1,0,3,2:T(8,128)(2,1)S(1)}, u32[]{:S(2)}, u32[]{:S(2)}) collective-permute-start(bf16[32,96,1,16]{1,0,3,2:T(8,128)(2,1)S(1)} %get-tuple-element.24), channel_id=1, source_target_pairs={{0,4},{4,8},{8,12},{12,16},{16,20},{20,24},{24,28},{28,32},{32,36}... | collective-permute-start | bytes 294920 | tf_op jit(solution)/shard_map/ppermute | solution.py:14
  75.0 8.4 %collective-permute-start.5 = (bf16[32,96,1,16]{1,0,3,2:T(8,128)(2,1)S(1)}, bf16[32,96,1,16]{1,0,3,2:T(8,128)(2,1)S(1)}, u32[]{:S(2)}, u32[]{:S(2)}) collective-permute-start(bf16[32,96,1,16]{1,0,3,2:T(8,128)(2,1)S(1)} %get-tuple-element.25), channel_id=1, source_target_pairs={{4,0},{8,4},{12,8},{16,12},{20,16},{24,20},{28,24},{32,28},{36,32}... | collective-permute-start | bytes 294920 | tf_op jit(solution)/shard_map/ppermute | solution.py:15
  83.4 5.4 %collective-permute-done.4 = bf16[32,96,1,16]{1,0,3,2:T(8,128)(2,1)S(1)} collective-permute-done((bf16[32,96,1,16]{1,0,3,2:T(8,128)(2,1)S(1)}, bf16[32,96,1,16]{1,0,3,2:T(8,128)(2,1)S(1)}, u32[]{:S(2)}, u32[]{:S(2)}) %collective-permute-start.4) | collective-permute-done | bytes 98336 | tf_op jit(solution)/shard_map/ppermute | solution.py:14
  88.9 10.3 %collective-permute-start.6 = (bf16[32,96,10,1]{1,0,3,2:T(8,128)(2,1)S(1)}, bf16[32,96,10,1]{1,0,3,2:T(8,128)(2,1)S(1)}, u32[]{:S(2)}, u32[]{:S(2)}) collective-permute-start(bf16[32,96,10,1]{1,0,3,2:T(8,128)(2,1)S(1)} %get-tuple-element.20), channel_id=1, source_target_pairs={{0,1},{1,2},{2,3},{3,64},{64,65},{65,66},{66,67},{67,128},{128,129... | collective-permute-start | bytes 184328 | tf_op jit(solution)/shard_map/ppermute | solution.py:14
  99.2 2.1 %collective-permute-start.7 = (bf16[32,96,10,1]{1,0,3,2:T(8,128)(2,1)S(1)}, bf16[32,96,10,1]{1,0,3,2:T(8,128)(2,1)S(1)}, u32[]{:S(2)}, u32[]{:S(2)}) collective-permute-start(bf16[32,96,10,1]{1,0,3,2:T(8,128)(2,1)S(1)} %get-tuple-element.21), channel_id=1, source_target_pairs={{1,0},{2,1},{3,2},{64,3},{65,64},{66,65},{67,66},{128,67},{129,128... | collective-permute-start | bytes 184328 | tf_op jit(solution)/shard_map/ppermute | solution.py:15
  101.3 0.7 collective-permute-done.6
  102.0 6.4 %collective-permute-done.7 = bf16[32,96,10,1]{1,0,3,2:T(8,128)(2,1)S(1)} collective-permute-done((bf16[32,96,10,1]{1,0,3,2:T(8,128)(2,1)S(1)}, bf16[32,96,10,1]{1,0,3,2:T(8,128)(2,1)S(1)}, u32[]{:S(2)}, u32[]{:S(2)}) %collective-permute-start.7) | collective-permute-done | bytes 61472 | tf_op jit(solution)/shard_map/ppermute | solution.py:15
  108.4 2.7 %fusion.1 = bf16[32,96,8,16]{1,0,3,2:T(8,128)(2,1)S(1)} fusion(bf16[32,96,8,16]{1,0,3,2:T(8,128)(2,1)S(1)} %get-tuple-element.17, bf16[3,3,96,96]{3,2,1,0:T(8,128)(2,1)S(1)} %copy-done, bf16[32,96,10,1]{1,0,3,2:T(8,128)(2,1)S(1)} %collective-permute-done.7, bf16[32,96,1,16]{1,0,3,2:T(8,128)(2,1)S(1)} %collective-permute-done.5, ...), kind=kOutput, calls=%fused_computation.4 | convolution fusion | flops 682868736 | bytes 2844672 | tf_op jit(solution)/shard_map/conv_general_dilated | solution.py:26
  111.1 1.4 %copy.48 = bf16[32,96,8,16]{1,3,2,0:T(8,128)(2,1)} copy(bf16[32,96,8,16]{1,0,3,2:T(8,128)(2,1)S(1)} %fusion.1) | data formatting | bytes 1572864
  112.7 0.4 fusion.25
  113.2 0.5 copy.42
  113.8 0.3 pad_select_fusion
  114.1 0.3 pad_select_fusion.10
  114.3 0.3 pad_select_fusion.9
  114.6 0.3 pad_select_fusion.8
  114.9 0.3 pad_select_fusion.7
  115.2 0.3 select_reduce_fusion
  115.9 0.3 slice.222
  116.7 0.3 pad_select_fusion.4
  118.2 0.5 fusion.8
  118.7 1.3 %copy.47 = bf16[2,96,8,256]{3,2,1,0:T(8,128)(2,1)} copy(bf16[2,96,8,256]{3,1,2,0:T(8,128)(2,1)S(1)} %fusion.8) | data formatting | bytes 1572864
  (55 shorter events, 4.4 us)
Async XLA Ops:
  0.6 33.7 %copy-start = (bf16[3,3,96,96]{3,2,1,0:T(8,128)(2,1)S(1)}, bf16[3,3,96,96]{3,2,1,0:T(8,128)(2,1)}, u32[]{:S(2)}) copy-start(bf16[3,3,96,96]{3,2,1,0:T(8,128)(2,1)} %param.10) | copy-start | bytes 497668
  0.6 12.4 %copy-start.9 = (s32[28]{0:T(128)S(1)}, s32[28]{0:T(128)}, u32[]{:S(2)}) copy-start(s32[28]{0:T(128)} %param.16) | copy-start | bytes 340
  0.7 12.5 %copy-start.7 = (s32[2,8,256]{2,1,0:T(8,128)S(1)}, s32[2,8,256]{2,1,0:T(8,128)}, u32[]{:S(2)}) copy-start(s32[2,8,256]{2,1,0:T(8,128)} %param.15) | copy-start | bytes 49156
  0.7 12.5 %copy-start.5 = (bf16[28,96]{1,0:T(8,128)(2,1)S(1)}, bf16[28,96]{1,0:T(8,128)(2,1)}, u32[]{:S(2)}) copy-start(bf16[28,96]{1,0:T(8,128)(2,1)} %param.13) | copy-start | bytes 16132
  0.7 12.5 %copy-start.2 = (bf16[2,96,8,256]{3,2,1,0:T(8,128)(2,1)S(1)}, bf16[2,96,8,256]{3,2,1,0:T(8,128)(2,1)}, u32[]{:S(2)}) copy-start(bf16[2,96,8,256]{3,2,1,0:T(8,128)(2,1)} %param.17) | copy-start | bytes 2359300
  2.7 15.7 %collective-permute-start = (bf16[32,96,1,16]{1,0,3,2:T(8,128)(2,1)S(1)}, bf16[32,96,1,16]{1,0,3,2:T(8,128)(2,1)S(1)}, u32[]{:S(2)}, u32[]{:S(2)}) collective-permute-start(bf16[32,96,1,16]{1,0,3,2:T(8,128)(2,1)S(1)} %get-tuple-element.26), channel_id=1, source_target_pairs={{0,4},{4,8},{8,12},{12,16},{16,20},{20,24},{24,28},{28,32},{32,36}... | collective-permute-start | bytes 294920 | tf_op jit(solution)/shard_map/ppermute | solution.py:14
  4.6 13.8 %collective-permute-start.1 = (bf16[32,96,1,16]{1,0,3,2:T(8,128)(2,1)S(1)}, bf16[32,96,1,16]{1,0,3,2:T(8,128)(2,1)S(1)}, u32[]{:S(2)}, u32[]{:S(2)}) collective-permute-start(bf16[32,96,1,16]{1,0,3,2:T(8,128)(2,1)S(1)} %get-tuple-element.27), channel_id=1, source_target_pairs={{4,0},{8,4},{12,8},{16,12},{20,16},{24,20},{28,24},{32,28},{36,32}... | collective-permute-start | bytes 294920 | tf_op jit(solution)/shard_map/ppermute | solution.py:15
  17.2 0.7 copy-start.4
  18.4 6.2 %copy-start.8 = (f32[96,5]{0,1:T(8,128)S(1)}, f32[96,5]{0,1:T(8,128)}, u32[]{:S(2)}) copy-start(f32[96,5]{0,1:T(8,128)} %param.11) | copy-start | bytes 5764
  18.8 15.6 %collective-permute-start.2 = (bf16[32,96,10,1]{1,0,3,2:T(8,128)(2,1)S(1)}, bf16[32,96,10,1]{1,0,3,2:T(8,128)(2,1)S(1)}, u32[]{:S(2)}, u32[]{:S(2)}) collective-permute-start(bf16[32,96,10,1]{1,0,3,2:T(8,128)(2,1)S(1)} %get-tuple-element.22), channel_id=1, source_target_pairs={{0,1},{1,2},{2,3},{3,64},{64,65},{65,66},{66,67},{67,128},{128,129... | collective-permute-start | bytes 184328 | tf_op jit(solution)/shard_map/ppermute | solution.py:14
  22.5 11.9 %collective-permute-start.3 = (bf16[32,96,10,1]{1,0,3,2:T(8,128)(2,1)S(1)}, bf16[32,96,10,1]{1,0,3,2:T(8,128)(2,1)S(1)}, u32[]{:S(2)}, u32[]{:S(2)}) collective-permute-start(bf16[32,96,10,1]{1,0,3,2:T(8,128)(2,1)S(1)} %get-tuple-element.23), channel_id=1, source_target_pairs={{1,0},{2,1},{3,2},{64,3},{65,64},{66,65},{67,66},{128,67},{129,128... | collective-permute-start | bytes 184328 | tf_op jit(solution)/shard_map/ppermute | solution.py:15
  26.4 31.9 %all-to-all-start.1 = ((bf16[2,96,8,256]{1,2,0,3:T(8,128)(2,1)}), bf16[2,96,8,256]{1,2,0,3:T(8,128)(2,1)S(1)}, u32[]{:S(2)}, u32[]{:S(2)}) async-start(bf16[2,96,8,256]{1,2,0,3:T(8,128)(2,1)} %copy.44), calls=%async_computation.1 | async-start | bytes 2097152 | tf_op jit(solution)/shard_map/all_to_all | solution.py:45
  34.3 8.0 %copy-start.1 = (bf16[32,96,8,16]{1,3,2,0:T(8,128)(2,1)S(1)}, bf16[32,96,8,16]{1,3,2,0:T(8,128)(2,1)}, u32[]{:S(2)}) copy-start(bf16[32,96,8,16]{1,3,2,0:T(8,128)(2,1)} %param.9) | copy-start | bytes 2359300
  58.3 1.6 %copy-start.3 = (f32[32,96,8,16]{1,0,3,2:T(8,128)S(1)}, f32[32,96,8,16]{1,0,3,2:T(8,128)}, u32[]{:S(2)}) copy-start(f32[32,96,8,16]{1,0,3,2:T(8,128)} %get-tuple-element.9) | copy-start | bytes 4718596
  64.7 47.8 %all-to-all-start = ((bf16[32,96,8,16]{1,3,2,0:T(8,128)(2,1)}), bf16[32,96,8,16]{1,3,2,0:T(8,128)(2,1)S(1)}, u32[]{:S(2)}, u32[]{:S(2)}) async-start(bf16[32,96,8,16]{1,3,2,0:T(8,128)(2,1)} %copy.40), calls=%async_computation | async-start | bytes 2097152 | tf_op jit(solution)/shard_map/all_to_all | solution.py:41
  73.0 15.8 %collective-permute-start.4 = (bf16[32,96,1,16]{1,0,3,2:T(8,128)(2,1)S(1)}, bf16[32,96,1,16]{1,0,3,2:T(8,128)(2,1)S(1)}, u32[]{:S(2)}, u32[]{:S(2)}) collective-permute-start(bf16[32,96,1,16]{1,0,3,2:T(8,128)(2,1)S(1)} %get-tuple-element.24), channel_id=1, source_target_pairs={{0,4},{4,8},{8,12},{12,16},{16,20},{20,24},{24,28},{28,32},{32,36}... | collective-permute-start | bytes 294920 | tf_op jit(solution)/shard_map/ppermute | solution.py:14
  75.0 13.9 %collective-permute-start.5 = (bf16[32,96,1,16]{1,0,3,2:T(8,128)(2,1)S(1)}, bf16[32,96,1,16]{1,0,3,2:T(8,128)(2,1)S(1)}, u32[]{:S(2)}, u32[]{:S(2)}) collective-permute-start(bf16[32,96,1,16]{1,0,3,2:T(8,128)(2,1)S(1)} %get-tuple-element.25), channel_id=1, source_target_pairs={{4,0},{8,4},{12,8},{16,12},{20,16},{24,20},{28,24},{32,28},{36,32}... | collective-permute-start | bytes 294920 | tf_op jit(solution)/shard_map/ppermute | solution.py:15
  88.9 13.1 %collective-permute-start.6 = (bf16[32,96,10,1]{1,0,3,2:T(8,128)(2,1)S(1)}, bf16[32,96,10,1]{1,0,3,2:T(8,128)(2,1)S(1)}, u32[]{:S(2)}, u32[]{:S(2)}) collective-permute-start(bf16[32,96,10,1]{1,0,3,2:T(8,128)(2,1)S(1)} %get-tuple-element.20), channel_id=1, source_target_pairs={{0,1},{1,2},{2,3},{3,64},{64,65},{65,66},{66,67},{67,128},{128,129... | collective-permute-start | bytes 184328 | tf_op jit(solution)/shard_map/ppermute | solution.py:14
  99.2 9.2 %collective-permute-start.7 = (bf16[32,96,10,1]{1,0,3,2:T(8,128)(2,1)S(1)}, bf16[32,96,10,1]{1,0,3,2:T(8,128)(2,1)S(1)}, u32[]{:S(2)}, u32[]{:S(2)}) collective-permute-start(bf16[32,96,10,1]{1,0,3,2:T(8,128)(2,1)S(1)} %get-tuple-element.21), channel_id=1, source_target_pairs={{1,0},{2,1},{3,2},{64,3},{65,64},{66,65},{67,66},{128,67},{129,128... | collective-permute-start | bytes 184328 | tf_op jit(solution)/shard_map/ppermute | solution.py:15
  114.9 0.7 copy-start.6

commit v9 on v8

--- a/solution.py
+++ b/solution.py
@@ -115,7 +115,12 @@
     gelu_value, pullback = jax.vjp(gelu_exact, pre_act)
     slope = pullback(jnp.ones_like(pre_act))[0]
     hidden_state = (features.astype(jnp.float32) + gelu_value).astype(jnp.bfloat16)
-    temporal = to_time(time_mix(hidden_state, time_weight).astype(jnp.bfloat16))
+    temporal_space = time_mix(hidden_state, time_weight).astype(jnp.bfloat16)
+    flipped = time_weight[:, ::-1]
+    cot_space, slope, temporal_space = lax.optimization_barrier(
+        (to_space(cot_temporal), slope, temporal_space)
+    )
+    temporal = to_time(temporal_space)
     band_vals = jnp.einsum("fcqw,cb->fbqw", temporal, band_out, preferred_element_type=jnp.float32)
     masked_band_sum = disperse(band_vals * mask_float, bits, width_wide)
     residual_error = measured - masked_band_sum
@@ -126,8 +131,6 @@
             "fbqw,bc->fcqw", back_proj, band_input_weight, preferred_element_type=jnp.float32
         )
     ).astype(jnp.bfloat16)
-    flipped = time_weight[:, ::-1]
-    cot_space, slope = lax.optimization_barrier((to_space(cot_temporal), slope))
     cot_hidden = time_mix(cot_space, flipped).astype(jnp.bfloat16)
     gate_grad = (slope * cot_hidden.astype(jnp.float32)).astype(jnp.bfloat16)
     kernel_flip = jnp.transpose(conv_weight[::-1, ::-1], (0, 1, 3, 2))

time: 121 us -> 120 us (level)
  waiting for transfers between devices: 27.5 us -> 22.4 us
  local copies, waits for them, and re-layouts: 13.8 us -> 16.6 us
    all_to_all x1, waiting for transfers between devices: 15 us -> 12 us  [to_space(): lax.all_to_all(field_in, ('ta', 'col'), split_axis=3, concat_axis=0, tile...]
    convert_element_type x1, other arithmetic: 0.89 us -> 3.09 us  [on_device(): temporal_space = time_mix(hidden_state, time_weight).astype(jnp.bfloat16)]
    ppermute x4, waiting for transfers between devices: 6.09 us -> 3.98 us  [with_halo(): before = lax.ppermute(last, axis, up)]
    convert_element_type x1, other arithmetic: 3.4 us -> 1.76 us  [on_device(): gate_grad = (slope * cot_hidden.astype(jnp.float32)).astype(jnp.bfloat16)]
    convert_element_type x1 -> x0, local copies, waits for them, and re-layouts: 1.4 us -> none  [on_device(): temporal = to_time(time_mix(hidden_state, time_weight).astype(jnp.bfloat16))]
    optimization_barrier x0 -> x1, local copies, waits for them, and re-layouts: none -> 1.39 us  [on_device(): lax.optimization_barrier((to_space(cot_temporal), slope, temporal_space))]
    all_to_all x1, local copies, waits for them, and re-layouts: 0.81 us -> 2.12 us  [to_space(): lax.all_to_all(field_in, ('ta', 'col'), split_axis=3, concat_axis=0, tile...]
    all_to_all x2, local copies, waits for them, and re-layouts: 0.76 us -> 2.01 us  [to_time(): lax.all_to_all(field_in, ('ta', 'col'), split_axis=0, concat_axis=3, tile...]
  transfers between devices with their start and end apart: 10 -> 10, of which waited for: 4 -> 4; matrix products, arithmetic and copies ran while one was open for 16% -> 21% of each run, Pallas kernels for 0% -> 0%
where the time goes in v9:
time: 120 us; the launch traced here: 119 us
  starting transfers between devices  55.4 us (46%)
  waiting for transfers between devices  22.4 us (19%)
  local copies, waits for them, and re-layouts  16.6 us (14%)
  matrix products  12.9 us (11%)
  other arithmetic  10.4 us (9%)
  between operations  1.45 us (1%)
    ppermute x4, starting transfers between devices, with_halo(): after = lax.ppermute(initial, axis, down)  21.1 us
    ppermute x4, starting transfers between devices, with_halo(): before = lax.ppermute(last, axis, up)  17.6 us
    all_to_all x1, waiting for transfers between devices, to_space(): lax.all_to_all(field_in, ('ta', 'col'), split_axis=3, concat_axis=0, tile...  12 us
    conv_general_dilated x2, matrix products, halo_conv(): lax.conv_general_dilated(padded, kernel, window_strides=(1, 1), padding='...  11.2 us
    all_to_all x1, starting transfers between devices, to_time(): lax.all_to_all(field_in, ('ta', 'col'), split_axis=0, concat_axis=3, tile...  8.39 us
    all_to_all x1, starting transfers between devices, to_space(): lax.all_to_all(field_in, ('ta', 'col'), split_axis=3, concat_axis=0, tile...  8.29 us
    ppermute x4, waiting for transfers between devices, with_halo(): after = lax.ppermute(initial, axis, down)  6.38 us
    unnamed x63, local copies, waits for them, and re-layouts  5.53 us
  transfers between devices with their start and end apart: 10, of which 4 were waited for; matrix products, arithmetic and copies ran while one was open for 21% of the time, Pallas kernels for 0%

profile of v9, /device:TPU:86, one launch (start us, length us, event | category | flops | bytes accessed | tf_op | source)
XLA Modules:
  0.0 119.1 jit_solution(12345825788118262587)
XLA Ops:
  0.7 2.0 %copy.34 = bf16[32,96,8,16]{1,0,3,2:T(8,128)(2,1)S(1)} copy(bf16[32,96,8,16]{1,3,2,0:T(8,128)(2,1)} %param.9) | data formatting | bytes 1572864 | tf_op args[0]
  2.7 1.9 %collective-permute-start = (bf16[32,96,1,16]{1,0,3,2:T(8,128)(2,1)S(1)}, bf16[32,96,1,16]{1,0,3,2:T(8,128)(2,1)S(1)}, u32[]{:S(2)}, u32[]{:S(2)}) collective-permute-start(bf16[32,96,1,16]{1,0,3,2:T(8,128)(2,1)S(1)} %get-tuple-element.28), channel_id=1, source_target_pairs={{0,4},{4,8},{8,12},{12,16},{16,20},{20,24},{24,28},{28,32},{32,36}... | collective-permute-start | bytes 294920 | tf_op jit(solution)/shard_map/ppermute | solution.py:14
  4.6 8.4 %collective-permute-start.1 = (bf16[32,96,1,16]{1,0,3,2:T(8,128)(2,1)S(1)}, bf16[32,96,1,16]{1,0,3,2:T(8,128)(2,1)S(1)}, u32[]{:S(2)}, u32[]{:S(2)}) collective-permute-start(bf16[32,96,1,16]{1,0,3,2:T(8,128)(2,1)S(1)} %get-tuple-element.29), channel_id=1, source_target_pairs={{4,0},{8,4},{12,8},{16,12},{20,16},{24,20},{28,24},{32,28},{36,32}... | collective-permute-start | bytes 294920 | tf_op jit(solution)/shard_map/ppermute | solution.py:15
  13.6 0.3 pad_select_fusion.1
  13.8 0.3 pad_select_fusion.19
  14.1 0.3 pad_select_fusion.18
  14.4 0.3 pad_select_fusion.17
  14.7 0.3 pad_select_fusion.16
  15.0 0.3 select_reduce_fusion.1
  15.5 0.3 slice.210
  16.3 0.3 pad_select_fusion.13
  17.5 0.3 slice.214
  18.0 0.5 fusion.9
  18.5 0.3 pad_maximum_fusion
  18.8 3.9 %collective-permute-start.2 = (bf16[32,96,10,1]{1,0,3,2:T(8,128)(2,1)S(1)}, bf16[32,96,10,1]{1,0,3,2:T(8,128)(2,1)}, u32[]{:S(2)}, u32[]{:S(2)}) collective-permute-start(bf16[32,96,10,1]{1,0,3,2:T(8,128)(2,1)S(1)} %get-tuple-element.24), channel_id=1, source_target_pairs={{0,1},{1,2},{2,3},{3,64},{64,65},{65,66},{66,67},{67,128},{128,129... | collective-permute-start | bytes 184328 | tf_op jit(solution)/shard_map/ppermute | solution.py:14
  22.7 2.1 %collective-permute-start.3 = (bf16[32,96,10,1]{1,0,3,2:T(8,128)(2,1)S(1)}, bf16[32,96,10,1]{1,0,3,2:T(8,128)(2,1)}, u32[]{:S(2)}, u32[]{:S(2)}) collective-permute-start(bf16[32,96,10,1]{1,0,3,2:T(8,128)(2,1)S(1)} %get-tuple-element.25), channel_id=1, source_target_pairs={{1,0},{2,1},{3,2},{64,3},{65,64},{66,65},{67,66},{128,67},{129,128... | collective-permute-start | bytes 184328 | tf_op jit(solution)/shard_map/ppermute | solution.py:15
  24.8 0.6 slice_bitcast_fusion.4
  25.4 1.7 %copy.39 = bf16[2,96,8,256]{1,2,0,3:T(8,128)(2,1)} copy(bf16[2,96,8,256]{3,1,2,0:T(8,128)(2,1)S(1)} %fusion.9) | data formatting | bytes 1572864 | tf_op jit(solution)/shard_map/optimization_barrier | solution.py:113
  27.2 8.3 %all-to-all-start = ((bf16[2,96,8,256]{1,2,0,3:T(8,128)(2,1)}), bf16[2,96,8,256]{1,2,0,3:T(8,128)(2,1)}, u32[]{:S(2)}, u32[]{:S(2)}) async-start(bf16[2,96,8,256]{1,2,0,3:T(8,128)(2,1)} %copy.39), calls=%async_computation | async-start | bytes 2097152 | tf_op jit(solution)/shard_map/all_to_all | solution.py:45
  35.6 8.5 %add_convert_fusion.2 = (bf16[32,96,8,16]{1,0,3,2:T(8,128)(2,1)S(1)}, f32[32,96,8,16]{1,0,3,2:T(8,128)S(1)}, f32[32,96,8,16]{1,0,3,2:T(8,128)S(1)}) fusion(bf16[32,96,8,16]{1,3,2,0:T(8,128)(2,1)S(1)} %copy-done.3, bf16[3,3,96,96]{3,2,1,0:T(8,128)(2,1)S(1)} %copy-done, bf16[32,96,10,1]{1,0,3,2:T(8,128)(2,1)} %collective-permute-done.3, ...), kind=kOutput, calls=%fused_computation.8 | convolution fusion | flops 706928640 | bytes 5990400 | tf_op jit(solution)/shard_map/conv_general_dilated | solution.py:26
  44.1 3.1 %add_convert_fusion.1 = (bf16[32,96,8,16]{1,0,3,2:T(8,128)(2,1)}, f32[32,96,8,16]{1,0,3,2:T(8,128)S(1)}) fusion(bf16[32,96,8,16]{1,0,3,2:T(8,128)(2,1)S(1)} %get-tuple-element.20, f32[96]{0:T(128)S(1)} %copy-done.24, f32[96]{0:T(128)S(1)} %copy-done.26, f32[96]{0:T(128)S(1)} %copy-done.20, f32[96]{0:T(128)S(1)} %copy-done.22, f32[96]{0:T(128)S(1)} %copy-done.18, ...), kind=kLoop, calls=%fused_computation.7 | loop fusion | flops 9830400 | bytes 6293376 | tf_op jit(solution)/shard_map/convert_element_type | solution.py:118
  47.2 12.0 %all-to-all-done = bf16[2,96,8,256]{1,2,0,3:T(8,128)(2,1)} async-done(((bf16[2,96,8,256]{1,2,0,3:T(8,128)(2,1)}), bf16[2,96,8,256]{1,2,0,3:T(8,128)(2,1)}, u32[]{:S(2)}, u32[]{:S(2)}) %all-to-all-start) | async-done | bytes 786464 | tf_op jit(solution)/shard_map/all_to_all | solution.py:45
  59.3 2.1 %copy.41 = bf16[16,2,96,8,16]{2,1,0,4,3:T(2,128)(2,1)S(1)} copy(bf16[16,2,96,8,16]{2,3,1,4,0:T(8,128)(2,1)} %bitcast.8) | data formatting | bytes 1572864 | tf_op jit(solution)/shard_map/all_to_all | solution.py:45
  61.4 1.4 %copy.43 = bf16[32,96,8,16]{1,3,2,0:T(8,128)(2,1)} copy(bf16[32,96,8,16]{1,0,3,2:T(8,128)(2,1)S(1)} %copy-done.1) | data formatting | bytes 1572864 | tf_op jit(solution)/shard_map/optimization_barrier | solution.py:120
  62.8 8.4 %all-to-all-start.1 = ((bf16[32,96,8,16]{1,3,2,0:T(8,128)(2,1)}), bf16[32,96,8,16]{1,3,2,0:T(8,128)(2,1)}, u32[]{:S(2)}, u32[]{:S(2)}) async-start(bf16[32,96,8,16]{1,3,2,0:T(8,128)(2,1)} %copy.43), calls=%async_computation.1 | async-start | bytes 2097152 | tf_op jit(solution)/shard_map/all_to_all | solution.py:41
  71.3 1.8 %fusion = (bf16[32,96,8,16]{1,0,3,2:T(8,128)(2,1)S(1)}, bf16[32,96,8,16]{1,0,3,2:T(8,128)(2,1)S(1)}) fusion(f32[32,96,8,16]{1,0,3,2:T(8,128)S(1)} %get-tuple-element.11, f32[96]{0:T(128)S(1)} %copy-done.19, f32[96]{0:T(128)S(1)} %copy-done.23, bf16[32,96,8,16]{1,0,3,2:T(8,128)(2,1)S(1)} %bitcast.69, f32[96]{0:T(128)S(1)} %copy-done.21, f32[96]{0:T(128)S(1)} %copy-done.27, ...), kind=kLoop, calls=%fused_computation.3 | loop fusion | flops 7077888 | bytes 3934080 | tf_op jit(solution)/shard_map/convert_element_type | solution.py:135
  73.1 1.9 %collective-permute-start.4 = (bf16[32,96,1,16]{1,0,3,2:T(8,128)(2,1)S(1)}, bf16[32,96,1,16]{1,0,3,2:T(8,128)(2,1)S(1)}, u32[]{:S(2)}, u32[]{:S(2)}) collective-permute-start(bf16[32,96,1,16]{1,0,3,2:T(8,128)(2,1)S(1)} %get-tuple-element.26), channel_id=1, source_target_pairs={{0,4},{4,8},{8,12},{12,16},{16,20},{20,24},{24,28},{28,32},{32,36}... | collective-permute-start | bytes 294920 | tf_op jit(solution)/shard_map/ppermute | solution.py:14
  75.0 8.4 %collective-permute-start.5 = (bf16[32,96,1,16]{1,0,3,2:T(8,128)(2,1)S(1)}, bf16[32,96,1,16]{1,0,3,2:T(8,128)(2,1)S(1)}, u32[]{:S(2)}, u32[]{:S(2)}) collective-permute-start(bf16[32,96,1,16]{1,0,3,2:T(8,128)(2,1)S(1)} %get-tuple-element.27), channel_id=1, source_target_pairs={{4,0},{8,4},{12,8},{16,12},{20,16},{24,20},{28,24},{32,28},{36,32}... | collective-permute-start | bytes 294920 | tf_op jit(solution)/shard_map/ppermute | solution.py:15
  83.4 3.7 %collective-permute-done.4 = bf16[32,96,1,16]{1,0,3,2:T(8,128)(2,1)S(1)} collective-permute-done((bf16[32,96,1,16]{1,0,3,2:T(8,128)(2,1)S(1)}, bf16[32,96,1,16]{1,0,3,2:T(8,128)(2,1)S(1)}, u32[]{:S(2)}, u32[]{:S(2)}) %collective-permute-start.4) | collective-permute-done | bytes 98336 | tf_op jit(solution)/shard_map/ppermute | solution.py:14
  87.2 9.9 %collective-permute-start.6 = (bf16[32,96,10,1]{1,0,3,2:T(8,128)(2,1)S(1)}, bf16[32,96,10,1]{1,0,3,2:T(8,128)(2,1)S(1)}, u32[]{:S(2)}, u32[]{:S(2)}) collective-permute-start(bf16[32,96,10,1]{1,0,3,2:T(8,128)(2,1)S(1)} %get-tuple-element.22), channel_id=1, source_target_pairs={{0,1},{1,2},{2,3},{3,64},{64,65},{65,66},{66,67},{67,128},{128,129... | collective-permute-start | bytes 184328 | tf_op jit(solution)/shard_map/ppermute | solution.py:14
  97.1 2.1 %collective-permute-start.7 = (bf16[32,96,10,1]{1,0,3,2:T(8,128)(2,1)S(1)}, bf16[32,96,10,1]{1,0,3,2:T(8,128)(2,1)S(1)}, u32[]{:S(2)}, u32[]{:S(2)}) collective-permute-start(bf16[32,96,10,1]{1,0,3,2:T(8,128)(2,1)S(1)} %get-tuple-element.23), channel_id=1, source_target_pairs={{1,0},{2,1},{3,2},{64,3},{65,64},{66,65},{67,66},{128,67},{129,128... | collective-permute-start | bytes 184328 | tf_op jit(solution)/shard_map/ppermute | solution.py:15
  99.5 6.4 %collective-permute-done.7 = bf16[32,96,10,1]{1,0,3,2:T(8,128)(2,1)S(1)} collective-permute-done((bf16[32,96,10,1]{1,0,3,2:T(8,128)(2,1)S(1)}, bf16[32,96,10,1]{1,0,3,2:T(8,128)(2,1)S(1)}, u32[]{:S(2)}, u32[]{:S(2)}) %collective-permute-start.7) | collective-permute-done | bytes 61472 | tf_op jit(solution)/shard_map/ppermute | solution.py:15
  105.9 2.7 %fusion.1 = bf16[32,96,8,16]{1,0,3,2:T(8,128)(2,1)S(1)} fusion(bf16[32,96,8,16]{1,0,3,2:T(8,128)(2,1)S(1)} %get-tuple-element.19, bf16[3,3,96,96]{3,2,1,0:T(8,128)(2,1)S(1)} %copy-done, bf16[32,96,10,1]{1,0,3,2:T(8,128)(2,1)S(1)} %collective-permute-done.7, bf16[32,96,1,16]{1,0,3,2:T(8,128)(2,1)S(1)} %collective-permute-done.5, ...), kind=kOutput, calls=%fused_computation.4 | convolution fusion | flops 682868736 | bytes 2844672 | tf_op jit(solution)/shard_map/conv_general_dilated | solution.py:26
  108.6 1.4 %copy.48 = bf16[32,96,8,16]{1,3,2,0:T(8,128)(2,1)} copy(bf16[32,96,8,16]{1,0,3,2:T(8,128)(2,1)S(1)} %fusion.1) | data formatting | bytes 1572864
  109.9 1.5 %copy.44 = bf16[16,2,96,8,16]{2,4,0,3,1:T(8,128)(2,1)S(1)} copy(bf16[16,2,96,8,16]{2,4,3,1,0:T(8,128)(2,1)} %bitcast.15) | data formatting | bytes 1572864 | tf_op jit(solution)/shard_map/all_to_all | solution.py:41
  111.4 0.4 fusion.25
  111.9 0.5 copy.45
  112.5 0.3 pad_select_fusion
  112.8 0.3 pad_select_fusion.10
  113.2 0.3 pad_select_fusion.9
  113.5 0.3 pad_select_fusion.8
  113.8 0.3 pad_select_fusion.7
  114.1 0.3 select_reduce_fusion
  114.8 0.3 slice.222
  115.3 0.3 slice.223
  115.5 0.3 pad_select_fusion.4
  117.3 0.5 fusion.8
  117.8 1.3 %copy.47 = bf16[2,96,8,256]{3,2,1,0:T(8,128)(2,1)} copy(bf16[2,96,8,256]{3,1,2,0:T(8,128)(2,1)S(1)} %fusion.8) | data formatting | bytes 1572864
  (95 shorter events, 4.8 us)
Async XLA Ops:
  0.6 34.9 %copy-start = (bf16[3,3,96,96]{3,2,1,0:T(8,128)(2,1)S(1)}, bf16[3,3,96,96]{3,2,1,0:T(8,128)(2,1)}, u32[]{:S(2)}) copy-start(bf16[3,3,96,96]{3,2,1,0:T(8,128)(2,1)} %param.10) | copy-start | bytes 497668
  0.6 12.4 %copy-start.29 = (s32[28]{0:T(128)S(1)}, s32[28]{0:T(128)}, u32[]{:S(2)}) copy-start(s32[28]{0:T(128)} %param.16) | copy-start | bytes 340
  0.7 12.5 %copy-start.9 = (s32[2,8,256]{2,1,0:T(8,128)S(1)}, s32[2,8,256]{2,1,0:T(8,128)}, u32[]{:S(2)}) copy-start(s32[2,8,256]{2,1,0:T(8,128)} %param.15) | copy-start | bytes 49156
  0.7 12.5 %copy-start.6 = (bf16[28,96]{1,0:T(8,128)(2,1)S(1)}, bf16[28,96]{1,0:T(8,128)(2,1)}, u32[]{:S(2)}) copy-start(bf16[28,96]{1,0:T(8,128)(2,1)} %param.13) | copy-start | bytes 16132
  0.7 12.5 %copy-start.2 = (bf16[2,96,8,256]{3,2,1,0:T(8,128)(2,1)S(1)}, bf16[2,96,8,256]{3,2,1,0:T(8,128)(2,1)}, u32[]{:S(2)}) copy-start(bf16[2,96,8,256]{3,2,1,0:T(8,128)(2,1)} %param.17) | copy-start | bytes 2359300
  2.7 15.8 %collective-permute-start = (bf16[32,96,1,16]{1,0,3,2:T(8,128)(2,1)S(1)}, bf16[32,96,1,16]{1,0,3,2:T(8,128)(2,1)S(1)}, u32[]{:S(2)}, u32[]{:S(2)}) collective-permute-start(bf16[32,96,1,16]{1,0,3,2:T(8,128)(2,1)S(1)} %get-tuple-element.28), channel_id=1, source_target_pairs={{0,4},{4,8},{8,12},{12,16},{16,20},{20,24},{24,28},{28,32},{32,36}... | collective-permute-start | bytes 294920 | tf_op jit(solution)/shard_map/ppermute | solution.py:14
  4.6 13.9 %collective-permute-start.1 = (bf16[32,96,1,16]{1,0,3,2:T(8,128)(2,1)S(1)}, bf16[32,96,1,16]{1,0,3,2:T(8,128)(2,1)S(1)}, u32[]{:S(2)}, u32[]{:S(2)}) collective-permute-start(bf16[32,96,1,16]{1,0,3,2:T(8,128)(2,1)S(1)} %get-tuple-element.29), channel_id=1, source_target_pairs={{4,0},{8,4},{12,8},{16,12},{20,16},{24,20},{28,24},{32,28},{36,32}... | collective-permute-start | bytes 294920 | tf_op jit(solution)/shard_map/ppermute | solution.py:15
  13.1 3.2 %copy-start.16 = (pred[28]{0:T(512)(128)(4,1)}, pred[28]{0:T(512)(128)(4,1)S(1)}, u32[]{:S(2)}) copy-start(pred[28]{0:T(512)(128)(4,1)S(1)} %get-tuple-element.36) | copy-start | bytes 88
  13.1 3.7 %copy-start.14 = (pred[28]{0:T(512)(128)(4,1)}, pred[28]{0:T(512)(128)(4,1)S(1)}, u32[]{:S(2)}) copy-start(pred[28]{0:T(512)(128)(4,1)S(1)} %get-tuple-element.37) | copy-start | bytes 88
  13.1 4.1 %copy-start.12 = (pred[28]{0:T(512)(128)(4,1)}, pred[28]{0:T(512)(128)(4,1)S(1)}, u32[]{:S(2)}) copy-start(pred[28]{0:T(512)(128)(4,1)S(1)} %get-tuple-element.38) | copy-start | bytes 88
  13.2 4.6 %copy-start.10 = (pred[28]{0:T(512)(128)(4,1)}, pred[28]{0:T(512)(128)(4,1)S(1)}, u32[]{:S(2)}) copy-start(pred[28]{0:T(512)(128)(4,1)S(1)} %get-tuple-element.35) | copy-start | bytes 88
  17.3 0.7 copy-start.4
  18.5 6.4 %copy-start.28 = (f32[96,5]{0,1:T(8,128)S(1)}, f32[96,5]{0,1:T(8,128)}, u32[]{:S(2)}) copy-start(f32[96,5]{0,1:T(8,128)} %param.11) | copy-start | bytes 5764
  18.8 16.8 %copy-start.3 = (bf16[32,96,8,16]{1,3,2,0:T(8,128)(2,1)S(1)}, bf16[32,96,8,16]{1,3,2,0:T(8,128)(2,1)}, u32[]{:S(2)}) copy-start(bf16[32,96,8,16]{1,3,2,0:T(8,128)(2,1)} %param.9) | copy-start | bytes 2359300
  18.8 16.7 %collective-permute-start.2 = (bf16[32,96,10,1]{1,0,3,2:T(8,128)(2,1)S(1)}, bf16[32,96,10,1]{1,0,3,2:T(8,128)(2,1)}, u32[]{:S(2)}, u32[]{:S(2)}) collective-permute-start(bf16[32,96,10,1]{1,0,3,2:T(8,128)(2,1)S(1)} %get-tuple-element.24), channel_id=1, source_target_pairs={{0,1},{1,2},{2,3},{3,64},{64,65},{65,66},{66,67},{67,128},{128,129... | collective-permute-start | bytes 184328 | tf_op jit(solution)/shard_map/ppermute | solution.py:14
  22.7 12.8 %collective-permute-start.3 = (bf16[32,96,10,1]{1,0,3,2:T(8,128)(2,1)S(1)}, bf16[32,96,10,1]{1,0,3,2:T(8,128)(2,1)}, u32[]{:S(2)}, u32[]{:S(2)}) collective-permute-start(bf16[32,96,10,1]{1,0,3,2:T(8,128)(2,1)S(1)} %get-tuple-element.25), channel_id=1, source_target_pairs={{1,0},{2,1},{3,2},{64,3},{65,64},{66,65},{67,66},{128,67},{129,128... | collective-permute-start | bytes 184328 | tf_op jit(solution)/shard_map/ppermute | solution.py:15
  27.2 32.1 %all-to-all-start = ((bf16[2,96,8,256]{1,2,0,3:T(8,128)(2,1)}), bf16[2,96,8,256]{1,2,0,3:T(8,128)(2,1)}, u32[]{:S(2)}, u32[]{:S(2)}) async-start(bf16[2,96,8,256]{1,2,0,3:T(8,128)(2,1)} %copy.39), calls=%async_computation | async-start | bytes 2097152 | tf_op jit(solution)/shard_map/all_to_all | solution.py:45
  35.5 8.6 %copy-start.18 = (f32[96]{0:T(128)S(1)}, f32[96]{0:T(128)}, u32[]{:S(2)}) copy-start(f32[96]{0:T(128)} %get-tuple-element.30) | copy-start | bytes 1156
  35.5 8.6 %copy-start.20 = (f32[96]{0:T(128)S(1)}, f32[96]{0:T(128)}, u32[]{:S(2)}) copy-start(f32[96]{0:T(128)} %get-tuple-element.31) | copy-start | bytes 1156
  35.5 8.6 %copy-start.22 = (f32[96]{0:T(128)S(1)}, f32[96]{0:T(128)}, u32[]{:S(2)}) copy-start(f32[96]{0:T(128)} %get-tuple-element.32) | copy-start | bytes 1156
  35.5 8.6 %copy-start.24 = (f32[96]{0:T(128)S(1)}, f32[96]{0:T(128)}, u32[]{:S(2)}) copy-start(f32[96]{0:T(128)} %get-tuple-element.33) | copy-start | bytes 1156
  35.5 8.6 %copy-start.26 = (f32[96]{0:T(128)S(1)}, f32[96]{0:T(128)}, u32[]{:S(2)}) copy-start(f32[96]{0:T(128)} %get-tuple-element.34) | copy-start | bytes 1156
  59.2 2.1 %copy-start.1 = (bf16[32,96,8,16]{1,0,3,2:T(8,128)(2,1)S(1)}, bf16[32,96,8,16]{1,0,3,2:T(8,128)(2,1)}, u32[]{:S(2)}) copy-start(bf16[32,96,8,16]{1,0,3,2:T(8,128)(2,1)} %get-tuple-element.9) | copy-start | bytes 2359300
  61.4 9.8 %copy-start.19 = (f32[96]{0:T(128)S(1)}, f32[96]{0:T(128)}, u32[]{:S(2)}) copy-start(f32[96]{0:T(128)} %get-tuple-element.30) | copy-start | bytes 1156
  61.4 9.8 %copy-start.21 = (f32[96]{0:T(128)S(1)}, f32[96]{0:T(128)}, u32[]{:S(2)}) copy-start(f32[96]{0:T(128)} %get-tuple-element.31) | copy-start | bytes 1156
  61.4 9.8 %copy-start.23 = (f32[96]{0:T(128)S(1)}, f32[96]{0:T(128)}, u32[]{:S(2)}) copy-start(f32[96]{0:T(128)} %get-tuple-element.32) | copy-start | bytes 1156
  61.4 9.8 %copy-start.25 = (f32[96]{0:T(128)S(1)}, f32[96]{0:T(128)}, u32[]{:S(2)}) copy-start(f32[96]{0:T(128)} %get-tuple-element.33) | copy-start | bytes 1156
  61.4 9.8 %copy-start.27 = (f32[96]{0:T(128)S(1)}, f32[96]{0:T(128)}, u32[]{:S(2)}) copy-start(f32[96]{0:T(128)} %get-tuple-element.34) | copy-start | bytes 1156
  62.8 47.1 %all-to-all-start.1 = ((bf16[32,96,8,16]{1,3,2,0:T(8,128)(2,1)}), bf16[32,96,8,16]{1,3,2,0:T(8,128)(2,1)}, u32[]{:S(2)}, u32[]{:S(2)}) async-start(bf16[32,96,8,16]{1,3,2,0:T(8,128)(2,1)} %copy.43), calls=%async_computation.1 | async-start | bytes 2097152 | tf_op jit(solution)/shard_map/all_to_all | solution.py:41
  73.1 14.1 %collective-permute-start.4 = (bf16[32,96,1,16]{1,0,3,2:T(8,128)(2,1)S(1)}, bf16[32,96,1,16]{1,0,3,2:T(8,128)(2,1)S(1)}, u32[]{:S(2)}, u32[]{:S(2)}) collective-permute-start(bf16[32,96,1,16]{1,0,3,2:T(8,128)(2,1)S(1)} %get-tuple-element.26), channel_id=1, source_target_pairs={{0,4},{4,8},{8,12},{12,16},{16,20},{20,24},{24,28},{28,32},{32,36}... | collective-permute-start | bytes 294920 | tf_op jit(solution)/shard_map/ppermute | solution.py:14
  75.0 12.2 %collective-permute-start.5 = (bf16[32,96,1,16]{1,0,3,2:T(8,128)(2,1)S(1)}, bf16[32,96,1,16]{1,0,3,2:T(8,128)(2,1)S(1)}, u32[]{:S(2)}, u32[]{:S(2)}) collective-permute-start(bf16[32,96,1,16]{1,0,3,2:T(8,128)(2,1)S(1)} %get-tuple-element.27), channel_id=1, source_target_pairs={{4,0},{8,4},{12,8},{16,12},{20,16},{24,20},{28,24},{32,28},{36,32}... | collective-permute-start | bytes 294920 | tf_op jit(solution)/shard_map/ppermute | solution.py:15
  87.2 12.3 %collective-permute-start.6 = (bf16[32,96,10,1]{1,0,3,2:T(8,128)(2,1)S(1)}, bf16[32,96,10,1]{1,0,3,2:T(8,128)(2,1)S(1)}, u32[]{:S(2)}, u32[]{:S(2)}) collective-permute-start(bf16[32,96,10,1]{1,0,3,2:T(8,128)(2,1)S(1)} %get-tuple-element.22), channel_id=1, source_target_pairs={{0,1},{1,2},{2,3},{3,64},{64,65},{65,66},{66,67},{67,128},{128,129... | collective-permute-start | bytes 184328 | tf_op jit(solution)/shard_map/ppermute | solution.py:14
  97.1 8.8 %collective-permute-start.7 = (bf16[32,96,10,1]{1,0,3,2:T(8,128)(2,1)S(1)}, bf16[32,96,10,1]{1,0,3,2:T(8,128)(2,1)S(1)}, u32[]{:S(2)}, u32[]{:S(2)}) collective-permute-start(bf16[32,96,10,1]{1,0,3,2:T(8,128)(2,1)S(1)} %get-tuple-element.23), channel_id=1, source_target_pairs={{1,0},{2,1},{3,2},{64,3},{65,64},{66,65},{67,66},{128,67},{129,128... | collective-permute-start | bytes 184328 | tf_op jit(solution)/shard_map/ppermute | solution.py:15
  108.5 2.9 %copy-start.5 = (bf16[96,28]{0,1:T(8,128)(2,1)S(1)}, bf16[96,28]{0,1:T(8,128)(2,1)}, u32[]{:S(2)}) copy-start(bf16[96,28]{0,1:T(8,128)(2,1)} %param.12) | copy-start | bytes 16132
  112.5 0.7 copy-start.17
  112.8 0.7 copy-start.15
  113.2 0.6 copy-start.13
  113.5 0.7 copy-start.11
  113.7 0.7 copy-start.8
  116.6 0.7 copy-start.7

commit v10 on v9

--- a/solution.py
+++ b/solution.py
@@ -21,8 +21,7 @@
     return with_halo(field_in, (("row", 2),), 1)
 
 
-def halo_conv(rows, kernel):
-    padded = with_halo(rows, ((("ta", "col"), 3),), 1)
+def valid_conv(padded, kernel):
     return lax.conv_general_dilated(
         padded,
         kernel,
@@ -33,8 +32,8 @@
     )
 
 
-def spatial_conv(field_in, kernel):
-    return halo_conv(row_halo(field_in), kernel)
+def halo_conv(rows, kernel):
+    return valid_conv(with_halo(rows, ((("ta", "col"), 3),), 1), kernel)
 
 
 def to_time(field_in):
@@ -134,9 +133,10 @@
     cot_hidden = time_mix(cot_space, flipped).astype(jnp.bfloat16)
     gate_grad = (slope * cot_hidden.astype(jnp.float32)).astype(jnp.bfloat16)
     kernel_flip = jnp.transpose(conv_weight[::-1, ::-1], (0, 1, 3, 2))
-    features_grad = (cot_hidden.astype(jnp.float32) + spatial_conv(gate_grad, kernel_flip)).astype(
-        jnp.bfloat16
-    )
+    gate_cols = with_halo(gate_grad, ((("ta", "col"), 3),), 1)
+    features_grad = (
+        cot_hidden.astype(jnp.float32) + valid_conv(row_halo(gate_cols), kernel_flip)
+    ).astype(jnp.bfloat16)
     return (updated, features_grad)
 
 

time: 120 us -> 129 us (1.075)
  the two profiles are of different devices: /device:TPU:86 before, /device:TPU:193 now
where the time goes in v10:
time: 129 us; the launch traced here: 128 us
  waiting for transfers between devices  45.4 us (35%)
  starting transfers between devices  41.4 us (32%)
  local copies, waits for them, and re-layouts  16.5 us (13%)
  matrix products  12.9 us (10%)
  other arithmetic  10.5 us (8%)
  between operations  1.46 us (1%)
    ppermute x4, starting transfers between devices, with_halo(): before = lax.ppermute(last, axis, up)  19.8 us
    ppermute x4, waiting for transfers between devices, with_halo(): before = lax.ppermute(last, axis, up)  17.4 us
    ppermute x4, waiting for transfers between devices, with_halo(): after = lax.ppermute(initial, axis, down)  14.3 us
    all_to_all x1, waiting for transfers between devices, to_space(): lax.all_to_all(field_in, ('ta', 'col'), split_axis=3, concat_axis=0, tile...  13.7 us
    ppermute x4, starting transfers between devices, with_halo(): after = lax.ppermute(initial, axis, down)  12.6 us
    conv_general_dilated x2, matrix products, valid_conv(): lax.conv_general_dilated(padded, kernel, window_strides=(1, 1), padding='...  11.2 us
    unnamed x63, local copies, waits for them, and re-layouts  5.54 us
    all_to_all x1, starting transfers between devices, to_time(): lax.all_to_all(field_in, ('ta', 'col'), split_axis=0, concat_axis=3, tile...  4.52 us
  transfers between devices with their start and end apart: 10, of which 4 were waited for; matrix products, arithmetic and copies ran while one was open for 19% of the time, Pallas kernels for 0%

profile of v10, /device:TPU:193, one launch (start us, length us, event | category | flops | bytes accessed | tf_op | source)
XLA Modules:
  0.0 128.1 jit_solution(18378206988211614344)
XLA Ops:
  0.7 2.0 %copy.34 = bf16[32,96,8,16]{1,0,3,2:T(8,128)(2,1)S(1)} copy(bf16[32,96,8,16]{1,3,2,0:T(8,128)(2,1)} %param.9) | data formatting | bytes 1572864 | tf_op args[0]
  2.7 3.7 %collective-permute-start = (bf16[32,96,1,16]{1,0,3,2:T(8,128)(2,1)S(1)}, bf16[32,96,1,16]{1,0,3,2:T(8,128)(2,1)S(1)}, u32[]{:S(2)}, u32[]{:S(2)}) collective-permute-start(bf16[32,96,1,16]{1,0,3,2:T(8,128)(2,1)S(1)} %get-tuple-element.28), channel_id=1, source_target_pairs={{0,4},{4,8},{8,12},{12,16},{16,20},{20,24},{24,28},{28,32},{32,36}... | collective-permute-start | bytes 294920 | tf_op jit(solution)/shard_map/ppermute | solution.py:14
  6.5 1.9 %collective-permute-start.1 = (bf16[32,96,1,16]{1,0,3,2:T(8,128)(2,1)S(1)}, bf16[32,96,1,16]{1,0,3,2:T(8,128)(2,1)S(1)}, u32[]{:S(2)}, u32[]{:S(2)}) collective-permute-start(bf16[32,96,1,16]{1,0,3,2:T(8,128)(2,1)S(1)} %get-tuple-element.29), channel_id=1, source_target_pairs={{4,0},{8,4},{12,8},{16,12},{20,16},{24,20},{28,24},{32,28},{36,32}... | collective-permute-start | bytes 294920 | tf_op jit(solution)/shard_map/ppermute | solution.py:15
  8.8 0.3 pad_select_fusion.1
  9.1 0.3 pad_select_fusion.19
  9.4 0.3 pad_select_fusion.18
  9.7 0.3 pad_select_fusion.17
  10.0 0.3 pad_select_fusion.16
  10.3 0.3 select_reduce_fusion.1
  10.8 0.3 slice.210
  11.6 0.3 pad_select_fusion.13
  12.3 0.3 slice.213
  13.3 0.5 fusion.9
  13.8 5.2 %collective-permute-done.1 = bf16[32,96,1,16]{1,0,3,2:T(8,128)(2,1)S(1)} collective-permute-done((bf16[32,96,1,16]{1,0,3,2:T(8,128)(2,1)S(1)}, bf16[32,96,1,16]{1,0,3,2:T(8,128)(2,1)S(1)}, u32[]{:S(2)}, u32[]{:S(2)}) %collective-permute-start.1) | collective-permute-done | bytes 98336 | tf_op jit(solution)/shard_map/ppermute | solution.py:15
  19.0 0.3 pad_maximum_fusion
  19.3 3.3 %collective-permute-start.2 = (bf16[32,96,10,1]{1,0,3,2:T(8,128)(2,1)S(1)}, bf16[32,96,10,1]{1,0,3,2:T(8,128)(2,1)}, u32[]{:S(2)}, u32[]{:S(2)}) collective-permute-start(bf16[32,96,10,1]{1,0,3,2:T(8,128)(2,1)S(1)} %get-tuple-element.22), channel_id=1, source_target_pairs={{0,1},{1,2},{2,3},{3,64},{64,65},{65,66},{66,67},{67,128},{128,129... | collective-permute-start | bytes 184328 | tf_op jit(solution)/shard_map/ppermute | solution.py:14
  22.6 4.3 %collective-permute-start.3 = (bf16[32,96,10,1]{1,0,3,2:T(8,128)(2,1)S(1)}, bf16[32,96,10,1]{1,0,3,2:T(8,128)(2,1)}, u32[]{:S(2)}, u32[]{:S(2)}) collective-permute-start(bf16[32,96,10,1]{1,0,3,2:T(8,128)(2,1)S(1)} %get-tuple-element.23), channel_id=1, source_target_pairs={{1,0},{2,1},{3,2},{64,3},{65,64},{66,65},{67,66},{128,67},{129,128... | collective-permute-start | bytes 184328 | tf_op jit(solution)/shard_map/ppermute | solution.py:15
  26.9 0.6 slice_bitcast_fusion.4
  27.5 1.7 %copy.39 = bf16[2,96,8,256]{1,2,0,3:T(8,128)(2,1)} copy(bf16[2,96,8,256]{3,1,2,0:T(8,128)(2,1)S(1)} %fusion.9) | data formatting | bytes 1572864 | tf_op jit(solution)/shard_map/optimization_barrier | solution.py:112
  29.2 4.4 %all-to-all-start = ((bf16[2,96,8,256]{1,2,0,3:T(8,128)(2,1)}), bf16[2,96,8,256]{1,2,0,3:T(8,128)(2,1)}, u32[]{:S(2)}, u32[]{:S(2)}) async-start(bf16[2,96,8,256]{1,2,0,3:T(8,128)(2,1)} %copy.39), calls=%async_computation | async-start | bytes 2097152 | tf_op jit(solution)/shard_map/all_to_all | solution.py:44
  33.8 8.5 %add_convert_fusion.2 = (bf16[32,96,8,16]{1,0,3,2:T(8,128)(2,1)S(1)}, f32[32,96,8,16]{1,0,3,2:T(8,128)S(1)}, f32[32,96,8,16]{1,0,3,2:T(8,128)S(1)}) fusion(bf16[32,96,8,16]{1,3,2,0:T(8,128)(2,1)S(1)} %copy-done.3, bf16[3,3,96,96]{3,2,1,0:T(8,128)(2,1)S(1)} %copy-done, bf16[32,96,10,1]{1,0,3,2:T(8,128)(2,1)} %collective-permute-done.3, ...), kind=kOutput, calls=%fused_computation.8 | convolution fusion | flops 706928640 | bytes 5990400 | tf_op jit(solution)/shard_map/conv_general_dilated | solution.py:25
  42.3 3.1 %add_convert_fusion.1 = (bf16[32,96,8,16]{1,0,3,2:T(8,128)(2,1)}, f32[32,96,8,16]{1,0,3,2:T(8,128)S(1)}) fusion(bf16[32,96,8,16]{1,0,3,2:T(8,128)(2,1)S(1)} %get-tuple-element.20, f32[96]{0:T(128)S(1)} %copy-done.24, f32[96]{0:T(128)S(1)} %copy-done.26, f32[96]{0:T(128)S(1)} %copy-done.20, f32[96]{0:T(128)S(1)} %copy-done.22, f32[96]{0:T(128)S(1)} %copy-done.18, ...), kind=kLoop, calls=%fused_computation.7 | loop fusion | flops 9830400 | bytes 6293376 | tf_op jit(solution)/shard_map/convert_element_type | solution.py:117
  45.4 13.7 %all-to-all-done = bf16[2,96,8,256]{1,2,0,3:T(8,128)(2,1)} async-done(((bf16[2,96,8,256]{1,2,0,3:T(8,128)(2,1)}), bf16[2,96,8,256]{1,2,0,3:T(8,128)(2,1)}, u32[]{:S(2)}, u32[]{:S(2)}) %all-to-all-start) | async-done | bytes 786464 | tf_op jit(solution)/shard_map/all_to_all | solution.py:44
  59.1 2.1 %copy.41 = bf16[16,2,96,8,16]{2,1,0,4,3:T(2,128)(2,1)S(1)} copy(bf16[16,2,96,8,16]{2,3,1,4,0:T(8,128)(2,1)} %bitcast.8) | data formatting | bytes 1572864 | tf_op jit(solution)/shard_map/all_to_all | solution.py:44
  61.3 1.4 %copy.43 = bf16[32,96,8,16]{1,3,2,0:T(8,128)(2,1)} copy(bf16[32,96,8,16]{1,0,3,2:T(8,128)(2,1)S(1)} %copy-done.1) | data formatting | bytes 1572864 | tf_op jit(solution)/shard_map/optimization_barrier | solution.py:119
  62.7 4.5 %all-to-all-start.1 = ((bf16[32,96,8,16]{1,3,2,0:T(8,128)(2,1)}), bf16[32,96,8,16]{1,3,2,0:T(8,128)(2,1)}, u32[]{:S(2)}, u32[]{:S(2)}) async-start(bf16[32,96,8,16]{1,3,2,0:T(8,128)(2,1)} %copy.43), calls=%async_computation.1 | async-start | bytes 2097152 | tf_op jit(solution)/shard_map/all_to_all | solution.py:40
  67.2 1.8 %fusion = (bf16[32,96,8,16]{1,0,3,2:T(8,128)(2,1)S(1)}, bf16[32,96,8,16]{1,0,3,2:T(8,128)(2,1)S(1)}) fusion(f32[32,96,8,16]{1,0,3,2:T(8,128)S(1)} %get-tuple-element.11, f32[96]{0:T(128)S(1)} %copy-done.19, f32[96]{0:T(128)S(1)} %copy-done.23, bf16[32,96,8,16]{1,0,3,2:T(8,128)(2,1)S(1)} %bitcast.69, f32[96]{0:T(128)S(1)} %copy-done.21, f32[96]{0:T(128)S(1)} %copy-done.27, ...), kind=kLoop, calls=%fused_computation.3 | loop fusion | flops 7077888 | bytes 3934080 | tf_op jit(solution)/shard_map/convert_element_type | solution.py:134
  69.0 3.1 %collective-permute-start.4 = (bf16[32,96,8,1]{1,0,3,2:T(8,128)(2,1)S(1)}, bf16[32,96,8,1]{1,0,3,2:T(8,128)(2,1)S(1)}, u32[]{:S(2)}, u32[]{:S(2)}) collective-permute-start(bf16[32,96,8,1]{1,0,3,2:T(8,128)(2,1)S(1)} %get-tuple-element.26), channel_id=1, source_target_pairs={{0,1},{1,2},{2,3},{3,64},{64,65},{65,66},{66,67},{67,128},{128,129... | collective-permute-start | bytes 147464 | tf_op jit(solution)/shard_map/ppermute | solution.py:14
  72.1 4.3 %collective-permute-start.5 = (bf16[32,96,8,1]{1,0,3,2:T(8,128)(2,1)S(1)}, bf16[32,96,8,1]{1,0,3,2:T(8,128)(2,1)S(1)}, u32[]{:S(2)}, u32[]{:S(2)}) collective-permute-start(bf16[32,96,8,1]{1,0,3,2:T(8,128)(2,1)S(1)} %get-tuple-element.27), channel_id=1, source_target_pairs={{1,0},{2,1},{3,2},{64,3},{65,64},{66,65},{67,66},{128,67},{129,128... | collective-permute-start | bytes 147464 | tf_op jit(solution)/shard_map/ppermute | solution.py:15
  76.4 17.4 %collective-permute-done.4 = bf16[32,96,8,1]{1,0,3,2:T(8,128)(2,1)S(1)} collective-permute-done((bf16[32,96,8,1]{1,0,3,2:T(8,128)(2,1)S(1)}, bf16[32,96,8,1]{1,0,3,2:T(8,128)(2,1)S(1)}, u32[]{:S(2)}, u32[]{:S(2)}) %collective-permute-start.4) | collective-permute-done | bytes 49184 | tf_op jit(solution)/shard_map/ppermute | solution.py:14
  93.9 9.7 %collective-permute-start.6 = (bf16[32,96,1,18]{1,0,3,2:T(8,128)(2,1)S(1)}, bf16[32,96,1,18]{1,0,3,2:T(8,128)(2,1)S(1)}, u32[]{:S(2)}, u32[]{:S(2)}) collective-permute-start(bf16[32,96,1,18]{1,0,3,2:T(8,128)(2,1)S(1)} %get-tuple-element.24), channel_id=1, source_target_pairs={{0,4},{4,8},{8,12},{12,16},{16,20},{20,24},{24,28},{28,32},{32,36}... | collective-permute-start | bytes 331784 | tf_op jit(solution)/shard_map/ppermute | solution.py:14
  103.6 2.1 %collective-permute-start.7 = (bf16[32,96,1,18]{1,0,3,2:T(8,128)(2,1)S(1)}, bf16[32,96,1,18]{1,0,3,2:T(8,128)(2,1)S(1)}, u32[]{:S(2)}, u32[]{:S(2)}) collective-permute-start(bf16[32,96,1,18]{1,0,3,2:T(8,128)(2,1)S(1)} %get-tuple-element.25), channel_id=1, source_target_pairs={{4,0},{8,4},{12,8},{16,12},{20,16},{24,20},{28,24},{32,28},{36,32}... | collective-permute-start | bytes 331784 | tf_op jit(solution)/shard_map/ppermute | solution.py:15
  105.8 9.1 %collective-permute-done.7 = bf16[32,96,1,18]{1,0,3,2:T(8,128)(2,1)S(1)} collective-permute-done((bf16[32,96,1,18]{1,0,3,2:T(8,128)(2,1)S(1)}, bf16[32,96,1,18]{1,0,3,2:T(8,128)(2,1)S(1)}, u32[]{:S(2)}, u32[]{:S(2)}) %collective-permute-start.7) | collective-permute-done | bytes 110624 | tf_op jit(solution)/shard_map/ppermute | solution.py:15
  114.9 2.7 %fusion.1 = bf16[32,96,8,16]{1,0,3,2:T(8,128)(2,1)S(1)} fusion(bf16[32,96,8,16]{1,0,3,2:T(8,128)(2,1)S(1)} %get-tuple-element.19, bf16[3,3,96,96]{3,2,1,0:T(8,128)(2,1)S(1)} %copy-done, bf16[32,96,1,18]{1,0,3,2:T(8,128)(2,1)S(1)} %collective-permute-done.7, bf16[32,96,8,1]{1,0,3,2:T(8,128)(2,1)S(1)} %collective-permute-done.5, ...), kind=kOutput, calls=%fused_computation.4 | convolution fusion | flops 682868736 | bytes 2844672 | tf_op jit(solution)/shard_map/conv_general_dilated | solution.py:25
  117.6 1.4 %copy.48 = bf16[32,96,8,16]{1,3,2,0:T(8,128)(2,1)} copy(bf16[32,96,8,16]{1,0,3,2:T(8,128)(2,1)S(1)} %fusion.1) | data formatting | bytes 1572864
  119.0 1.5 %copy.44 = bf16[16,2,96,8,16]{2,4,0,3,1:T(8,128)(2,1)S(1)} copy(bf16[16,2,96,8,16]{2,4,3,1,0:T(8,128)(2,1)} %bitcast.15) | data formatting | bytes 1572864 | tf_op jit(solution)/shard_map/all_to_all | solution.py:40
  120.5 0.4 fusion.25
  120.9 0.5 copy.45
  121.5 0.3 pad_select_fusion
  121.8 0.3 pad_select_fusion.10
  122.2 0.3 pad_select_fusion.9
  122.5 0.3 pad_select_fusion.8
  122.8 0.3 pad_select_fusion.7
  123.2 0.3 select_reduce_fusion
  123.8 0.3 slice.222
  124.6 0.3 pad_select_fusion.4
  126.3 0.5 fusion.8
  126.8 1.3 %copy.47 = bf16[2,96,8,256]{3,2,1,0:T(8,128)(2,1)} copy(bf16[2,96,8,256]{3,1,2,0:T(8,128)(2,1)S(1)} %fusion.8) | data formatting | bytes 1572864
  (95 shorter events, 4.9 us)
Async XLA Ops:
  0.6 33.1 %copy-start = (bf16[3,3,96,96]{3,2,1,0:T(8,128)(2,1)S(1)}, bf16[3,3,96,96]{3,2,1,0:T(8,128)(2,1)}, u32[]{:S(2)}) copy-start(bf16[3,3,96,96]{3,2,1,0:T(8,128)(2,1)} %param.10) | copy-start | bytes 497668
  0.6 7.7 %copy-start.29 = (s32[28]{0:T(128)S(1)}, s32[28]{0:T(128)}, u32[]{:S(2)}) copy-start(s32[28]{0:T(128)} %param.16) | copy-start | bytes 340
  0.7 7.8 %copy-start.9 = (s32[2,8,256]{2,1,0:T(8,128)S(1)}, s32[2,8,256]{2,1,0:T(8,128)}, u32[]{:S(2)}) copy-start(s32[2,8,256]{2,1,0:T(8,128)} %param.15) | copy-start | bytes 49156
  0.7 7.8 %copy-start.6 = (bf16[28,96]{1,0:T(8,128)(2,1)S(1)}, bf16[28,96]{1,0:T(8,128)(2,1)}, u32[]{:S(2)}) copy-start(bf16[28,96]{1,0:T(8,128)(2,1)} %param.13) | copy-start | bytes 16132
  0.7 7.8 %copy-start.2 = (bf16[2,96,8,256]{3,2,1,0:T(8,128)(2,1)S(1)}, bf16[2,96,8,256]{3,2,1,0:T(8,128)(2,1)}, u32[]{:S(2)}) copy-start(bf16[2,96,8,256]{3,2,1,0:T(8,128)(2,1)} %param.17) | copy-start | bytes 2359300
  2.7 11.1 %collective-permute-start = (bf16[32,96,1,16]{1,0,3,2:T(8,128)(2,1)S(1)}, bf16[32,96,1,16]{1,0,3,2:T(8,128)(2,1)S(1)}, u32[]{:S(2)}, u32[]{:S(2)}) collective-permute-start(bf16[32,96,1,16]{1,0,3,2:T(8,128)(2,1)S(1)} %get-tuple-element.28), channel_id=1, source_target_pairs={{0,4},{4,8},{8,12},{12,16},{16,20},{20,24},{24,28},{28,32},{32,36}... | collective-permute-start | bytes 294920 | tf_op jit(solution)/shard_map/ppermute | solution.py:14
  6.5 12.5 %collective-permute-start.1 = (bf16[32,96,1,16]{1,0,3,2:T(8,128)(2,1)S(1)}, bf16[32,96,1,16]{1,0,3,2:T(8,128)(2,1)S(1)}, u32[]{:S(2)}, u32[]{:S(2)}) collective-permute-start(bf16[32,96,1,16]{1,0,3,2:T(8,128)(2,1)S(1)} %get-tuple-element.29), channel_id=1, source_target_pairs={{4,0},{8,4},{12,8},{16,12},{20,16},{24,20},{28,24},{32,28},{36,32}... | collective-permute-start | bytes 294920 | tf_op jit(solution)/shard_map/ppermute | solution.py:15
  8.4 3.2 %copy-start.16 = (pred[28]{0:T(512)(128)(4,1)}, pred[28]{0:T(512)(128)(4,1)S(1)}, u32[]{:S(2)}) copy-start(pred[28]{0:T(512)(128)(4,1)S(1)} %get-tuple-element.36) | copy-start | bytes 88
  8.4 3.7 %copy-start.14 = (pred[28]{0:T(512)(128)(4,1)}, pred[28]{0:T(512)(128)(4,1)S(1)}, u32[]{:S(2)}) copy-start(pred[28]{0:T(512)(128)(4,1)S(1)} %get-tuple-element.37) | copy-start | bytes 88
  8.4 4.1 %copy-start.12 = (pred[28]{0:T(512)(128)(4,1)}, pred[28]{0:T(512)(128)(4,1)S(1)}, u32[]{:S(2)}) copy-start(pred[28]{0:T(512)(128)(4,1)S(1)} %get-tuple-element.38) | copy-start | bytes 88
  8.5 4.6 %copy-start.10 = (pred[28]{0:T(512)(128)(4,1)}, pred[28]{0:T(512)(128)(4,1)S(1)}, u32[]{:S(2)}) copy-start(pred[28]{0:T(512)(128)(4,1)S(1)} %get-tuple-element.35) | copy-start | bytes 88
  12.6 0.7 copy-start.4
  13.8 13.1 %copy-start.28 = (f32[96,5]{0,1:T(8,128)S(1)}, f32[96,5]{0,1:T(8,128)}, u32[]{:S(2)}) copy-start(f32[96,5]{0,1:T(8,128)} %param.11) | copy-start | bytes 5764
  19.3 14.5 %copy-start.3 = (bf16[32,96,8,16]{1,3,2,0:T(8,128)(2,1)S(1)}, bf16[32,96,8,16]{1,3,2,0:T(8,128)(2,1)}, u32[]{:S(2)}) copy-start(bf16[32,96,8,16]{1,3,2,0:T(8,128)(2,1)} %param.9) | copy-start | bytes 2359300
  19.3 14.4 %collective-permute-start.2 = (bf16[32,96,10,1]{1,0,3,2:T(8,128)(2,1)S(1)}, bf16[32,96,10,1]{1,0,3,2:T(8,128)(2,1)}, u32[]{:S(2)}, u32[]{:S(2)}) collective-permute-start(bf16[32,96,10,1]{1,0,3,2:T(8,128)(2,1)S(1)} %get-tuple-element.22), channel_id=1, source_target_pairs={{0,1},{1,2},{2,3},{3,64},{64,65},{65,66},{66,67},{67,128},{128,129... | collective-permute-start | bytes 184328 | tf_op jit(solution)/shard_map/ppermute | solution.py:14
  22.6 11.1 %collective-permute-start.3 = (bf16[32,96,10,1]{1,0,3,2:T(8,128)(2,1)S(1)}, bf16[32,96,10,1]{1,0,3,2:T(8,128)(2,1)}, u32[]{:S(2)}, u32[]{:S(2)}) collective-permute-start(bf16[32,96,10,1]{1,0,3,2:T(8,128)(2,1)S(1)} %get-tuple-element.23), channel_id=1, source_target_pairs={{1,0},{2,1},{3,2},{64,3},{65,64},{66,65},{67,66},{128,67},{129,128... | collective-permute-start | bytes 184328 | tf_op jit(solution)/shard_map/ppermute | solution.py:15
  29.2 29.9 %all-to-all-start = ((bf16[2,96,8,256]{1,2,0,3:T(8,128)(2,1)}), bf16[2,96,8,256]{1,2,0,3:T(8,128)(2,1)}, u32[]{:S(2)}, u32[]{:S(2)}) async-start(bf16[2,96,8,256]{1,2,0,3:T(8,128)(2,1)} %copy.39), calls=%async_computation | async-start | bytes 2097152 | tf_op jit(solution)/shard_map/all_to_all | solution.py:44
  33.7 8.6 %copy-start.18 = (f32[96]{0:T(128)S(1)}, f32[96]{0:T(128)}, u32[]{:S(2)}) copy-start(f32[96]{0:T(128)} %get-tuple-element.30) | copy-start | bytes 1156
  33.7 8.6 %copy-start.20 = (f32[96]{0:T(128)S(1)}, f32[96]{0:T(128)}, u32[]{:S(2)}) copy-start(f32[96]{0:T(128)} %get-tuple-element.31) | copy-start | bytes 1156
  33.7 8.6 %copy-start.22 = (f32[96]{0:T(128)S(1)}, f32[96]{0:T(128)}, u32[]{:S(2)}) copy-start(f32[96]{0:T(128)} %get-tuple-element.32) | copy-start | bytes 1156
  33.7 8.6 %copy-start.24 = (f32[96]{0:T(128)S(1)}, f32[96]{0:T(128)}, u32[]{:S(2)}) copy-start(f32[96]{0:T(128)} %get-tuple-element.33) | copy-start | bytes 1156
  33.7 8.6 %copy-start.26 = (f32[96]{0:T(128)S(1)}, f32[96]{0:T(128)}, u32[]{:S(2)}) copy-start(f32[96]{0:T(128)} %get-tuple-element.34) | copy-start | bytes 1156
  59.1 2.1 %copy-start.1 = (bf16[32,96,8,16]{1,0,3,2:T(8,128)(2,1)S(1)}, bf16[32,96,8,16]{1,0,3,2:T(8,128)(2,1)}, u32[]{:S(2)}) copy-start(bf16[32,96,8,16]{1,0,3,2:T(8,128)(2,1)} %get-tuple-element.9) | copy-start | bytes 2359300
  61.2 6.0 %copy-start.19 = (f32[96]{0:T(128)S(1)}, f32[96]{0:T(128)}, u32[]{:S(2)}) copy-start(f32[96]{0:T(128)} %get-tuple-element.30) | copy-start | bytes 1156
  61.3 6.0 %copy-start.21 = (f32[96]{0:T(128)S(1)}, f32[96]{0:T(128)}, u32[]{:S(2)}) copy-start(f32[96]{0:T(128)} %get-tuple-element.31) | copy-start | bytes 1156
  61.3 6.0 %copy-start.23 = (f32[96]{0:T(128)S(1)}, f32[96]{0:T(128)}, u32[]{:S(2)}) copy-start(f32[96]{0:T(128)} %get-tuple-element.32) | copy-start | bytes 1156
  61.3 6.0 %copy-start.25 = (f32[96]{0:T(128)S(1)}, f32[96]{0:T(128)}, u32[]{:S(2)}) copy-start(f32[96]{0:T(128)} %get-tuple-element.33) | copy-start | bytes 1156
  61.3 6.0 %copy-start.27 = (f32[96]{0:T(128)S(1)}, f32[96]{0:T(128)}, u32[]{:S(2)}) copy-start(f32[96]{0:T(128)} %get-tuple-element.34) | copy-start | bytes 1156
  62.7 56.3 %all-to-all-start.1 = ((bf16[32,96,8,16]{1,3,2,0:T(8,128)(2,1)}), bf16[32,96,8,16]{1,3,2,0:T(8,128)(2,1)}, u32[]{:S(2)}, u32[]{:S(2)}) async-start(bf16[32,96,8,16]{1,3,2,0:T(8,128)(2,1)} %copy.43), calls=%async_computation.1 | async-start | bytes 2097152 | tf_op jit(solution)/shard_map/all_to_all | solution.py:40
  69.0 24.8 %collective-permute-start.4 = (bf16[32,96,8,1]{1,0,3,2:T(8,128)(2,1)S(1)}, bf16[32,96,8,1]{1,0,3,2:T(8,128)(2,1)S(1)}, u32[]{:S(2)}, u32[]{:S(2)}) collective-permute-start(bf16[32,96,8,1]{1,0,3,2:T(8,128)(2,1)S(1)} %get-tuple-element.26), channel_id=1, source_target_pairs={{0,1},{1,2},{2,3},{3,64},{64,65},{65,66},{66,67},{67,128},{128,129... | collective-permute-start | bytes 147464 | tf_op jit(solution)/shard_map/ppermute | solution.py:14
  72.1 21.7 %collective-permute-start.5 = (bf16[32,96,8,1]{1,0,3,2:T(8,128)(2,1)S(1)}, bf16[32,96,8,1]{1,0,3,2:T(8,128)(2,1)S(1)}, u32[]{:S(2)}, u32[]{:S(2)}) collective-permute-start(bf16[32,96,8,1]{1,0,3,2:T(8,128)(2,1)S(1)} %get-tuple-element.27), channel_id=1, source_target_pairs={{1,0},{2,1},{3,2},{64,3},{65,64},{66,65},{67,66},{128,67},{129,128... | collective-permute-start | bytes 147464 | tf_op jit(solution)/shard_map/ppermute | solution.py:15
  93.9 11.9 %collective-permute-start.6 = (bf16[32,96,1,18]{1,0,3,2:T(8,128)(2,1)S(1)}, bf16[32,96,1,18]{1,0,3,2:T(8,128)(2,1)S(1)}, u32[]{:S(2)}, u32[]{:S(2)}) collective-permute-start(bf16[32,96,1,18]{1,0,3,2:T(8,128)(2,1)S(1)} %get-tuple-element.24), channel_id=1, source_target_pairs={{0,4},{4,8},{8,12},{12,16},{16,20},{20,24},{24,28},{28,32},{32,36}... | collective-permute-start | bytes 331784 | tf_op jit(solution)/shard_map/ppermute | solution.py:14
  103.6 11.3 %collective-permute-start.7 = (bf16[32,96,1,18]{1,0,3,2:T(8,128)(2,1)S(1)}, bf16[32,96,1,18]{1,0,3,2:T(8,128)(2,1)S(1)}, u32[]{:S(2)}, u32[]{:S(2)}) collective-permute-start(bf16[32,96,1,18]{1,0,3,2:T(8,128)(2,1)S(1)} %get-tuple-element.25), channel_id=1, source_target_pairs={{4,0},{8,4},{12,8},{16,12},{20,16},{24,20},{28,24},{32,28},{36,32}... | collective-permute-start | bytes 331784 | tf_op jit(solution)/shard_map/ppermute | solution.py:15
  117.6 2.9 %copy-start.5 = (bf16[96,28]{0,1:T(8,128)(2,1)S(1)}, bf16[96,28]{0,1:T(8,128)(2,1)}, u32[]{:S(2)}) copy-start(bf16[96,28]{0,1:T(8,128)(2,1)} %param.12) | copy-start | bytes 16132
  121.5 0.7 copy-start.17
  121.8 0.7 copy-start.15
  122.2 0.6 copy-start.13
  122.5 0.7 copy-start.11
  122.8 0.7 copy-start.8
  125.6 0.7 copy-start.7

commit v11 on v9

--- a/solution.py
+++ b/solution.py
@@ -37,12 +37,29 @@
     return halo_conv(row_halo(field_in), kernel)
 
 
+def lane_rows(block):
+    lanes = 128
+    return block.reshape(block.shape[0], -1, lanes)
+
+
 def to_time(field_in):
-    return lax.all_to_all(field_in, ("ta", "col"), split_axis=0, concat_axis=3, tiled=True)
+    blocks = lax.axis_size(("ta", "col"))
+    frames = field_in.shape[0] // blocks
+    sent = lane_rows(field_in.reshape((blocks, frames * field_in.shape[1]) + field_in.shape[2:]))
+    got = lax.all_to_all(sent, ("ta", "col"), split_axis=0, concat_axis=0, tiled=True)
+    got = got.reshape((blocks, frames) + field_in.shape[1:])
+    return jnp.moveaxis(got, 0, 3).reshape(
+        (frames,) + field_in.shape[1:3] + (blocks * field_in.shape[3],)
+    )
 
 
 def to_space(field_in):
-    return lax.all_to_all(field_in, ("ta", "col"), split_axis=3, concat_axis=0, tiled=True)
+    blocks = lax.axis_size(("ta", "col"))
+    width = field_in.shape[3] // blocks
+    split = field_in.reshape(field_in.shape[:3] + (blocks, width))
+    sent = lane_rows(jnp.moveaxis(split, 3, 0))
+    got = lax.all_to_all(sent, ("ta", "col"), split_axis=0, concat_axis=0, tiled=True)
+    return got.reshape((blocks * field_in.shape[0],) + field_in.shape[1:3] + (width,))
 
 
 def time_mix(frames_in, time_taps):

time: 120 us -> 118 us (0.983)
  local copies, waits for them, and re-layouts: 16.6 us -> 23.7 us
  waiting for transfers between devices: 22.4 us -> 17.5 us
  starting transfers between devices: 55.4 us -> 50.6 us
    all_to_all x2, waiting for transfers between devices: 12 us -> 6.44 us  [the longest x1 6.44 us: to_space(): lax.all_to_all(sent, ('ta', 'col'), split_axis=0, concat_axis=0, tiled=True)]
    another operation x0 -> x2, local copies, waits for them, and re-layouts: none -> 5.03 us  [lane_rows(): return block.reshape(block.shape[0], -1, lanes)]
    reshape x0 -> x5, local copies, waits for them, and re-layouts: none -> 4.77 us  [the longest x2 1.98 us: lane_rows(): return block.reshape(block.shape[0], -1, lanes)]
    ppermute x4, starting transfers between devices: 17.6 us -> 13.3 us  [with_halo(): before = lax.ppermute(last, axis, up)]
    ppermute x4, waiting for transfers between devices: 6.38 us -> 9.31 us  [with_halo(): after = lax.ppermute(initial, axis, down)]
    ppermute x4, waiting for transfers between devices: 3.98 us -> 1.72 us  [with_halo(): before = lax.ppermute(last, axis, up)]
    transpose x0 -> x2, local copies, waits for them, and re-layouts: none -> 1.82 us  [the longest x1 1.62 us: to_space(): sent = lane_rows(jnp.moveaxis(split, 3, 0))]
    optimization_barrier x1 -> x0, local copies, waits for them, and re-layouts: 1.39 us -> none  [on_device(): lax.optimization_barrier((to_space(cot_temporal), slope, temporal_space))]
  transfers between devices with their start and end apart: 10 -> 10, of which waited for: 4 -> 5; matrix products, arithmetic and copies ran while one was open for 21% -> 23% of each run, Pallas kernels for 0% -> 0%
where the time goes in v11:
time: 118 us; the launch traced here: 117 us
  starting transfers between devices  50.6 us (43%)
  local copies, waits for them, and re-layouts  23.7 us (20%)
  waiting for transfers between devices  17.5 us (15%)
  matrix products  13 us (11%)
  other arithmetic  10.5 us (9%)
  between operations  1.23 us (1%)
    ppermute x4, starting transfers between devices, with_halo(): after = lax.ppermute(initial, axis, down)  21.1 us
    ppermute x4, starting transfers between devices, with_halo(): before = lax.ppermute(last, axis, up)  13.3 us
    conv_general_dilated x2, matrix products, halo_conv(): lax.conv_general_dilated(padded, kernel, window_strides=(1, 1), padding='...  11.4 us
    ppermute x4, waiting for transfers between devices, with_halo(): after = lax.ppermute(initial, axis, down)  9.31 us
    all_to_all x1, starting transfers between devices, to_time(): lax.all_to_all(sent, ('ta', 'col'), split_axis=0, concat_axis=0, tiled=True)  8.24 us
    all_to_all x1, starting transfers between devices, to_space(): lax.all_to_all(sent, ('ta', 'col'), split_axis=0, concat_axis=0, tiled=True)  7.95 us
    all_to_all x1, waiting for transfers between devices, to_space(): lax.all_to_all(sent, ('ta', 'col'), split_axis=0, concat_axis=0, tiled=True)  6.44 us
    unnamed x23, local copies, waits for them, and re-layouts  5.13 us
  transfers between devices with their start and end apart: 10, of which 5 were waited for; matrix products, arithmetic and copies ran while one was open for 23% of the time, Pallas kernels for 0%

profile of v11, /device:TPU:86, one launch (start us, length us, event | category | flops | bytes accessed | tf_op | source)
XLA Modules:
  0.0 116.5 jit_solution(9507790862169729455)
XLA Ops:
  0.7 2.0 %copy.35 = bf16[32,96,8,16]{1,0,3,2:T(8,128)(2,1)S(1)} copy(bf16[32,96,8,16]{1,3,2,0:T(8,128)(2,1)} %param.9) | data formatting | bytes 1572864 | tf_op args[0]
  2.7 1.9 %collective-permute-start = (bf16[32,96,1,16]{1,0,3,2:T(8,128)(2,1)S(1)}, bf16[32,96,1,16]{1,0,3,2:T(8,128)(2,1)S(1)}, u32[]{:S(2)}, u32[]{:S(2)}) collective-permute-start(bf16[32,96,1,16]{1,0,3,2:T(8,128)(2,1)S(1)} %get-tuple-element.28), channel_id=1, source_target_pairs={{0,4},{4,8},{8,12},{12,16},{16,20},{20,24},{24,28},{28,32},{32,36}... | collective-permute-start | bytes 294920 | tf_op jit(solution)/shard_map/ppermute | solution.py:14
  4.6 8.4 %collective-permute-start.1 = (bf16[32,96,1,16]{1,0,3,2:T(8,128)(2,1)S(1)}, bf16[32,96,1,16]{1,0,3,2:T(8,128)(2,1)S(1)}, u32[]{:S(2)}, u32[]{:S(2)}) collective-permute-start(bf16[32,96,1,16]{1,0,3,2:T(8,128)(2,1)S(1)} %get-tuple-element.29), channel_id=1, source_target_pairs={{4,0},{8,4},{12,8},{16,12},{20,16},{24,20},{28,24},{32,28},{36,32}... | collective-permute-start | bytes 294920 | tf_op jit(solution)/shard_map/ppermute | solution.py:15
  13.5 0.3 pad_select_fusion.1
  13.8 0.3 pad_select_fusion.19
  14.1 0.3 pad_select_fusion.18
  14.4 0.3 pad_select_fusion.17
  14.6 0.3 pad_select_fusion.16
  14.9 0.3 select_reduce_fusion.1
  16.3 0.3 pad_select_fusion.13
  18.0 0.5 fusion.9
  18.5 0.3 pad_maximum_fusion
  18.8 3.7 %collective-permute-start.2 = (bf16[32,96,10,1]{1,0,3,2:T(8,128)(2,1)S(1)}, bf16[32,96,10,1]{1,0,3,2:T(8,128)(2,1)S(1)}, u32[]{:S(2)}, u32[]{:S(2)}) collective-permute-start(bf16[32,96,10,1]{1,0,3,2:T(8,128)(2,1)S(1)} %get-tuple-element.24), channel_id=1, source_target_pairs={{0,1},{1,2},{2,3},{3,64},{64,65},{65,66},{66,67},{67,128},{128,129... | collective-permute-start | bytes 184328 | tf_op jit(solution)/shard_map/ppermute | solution.py:14
  22.6 2.1 %collective-permute-start.3 = (bf16[32,96,10,1]{1,0,3,2:T(8,128)(2,1)S(1)}, bf16[32,96,10,1]{1,0,3,2:T(8,128)(2,1)S(1)}, u32[]{:S(2)}, u32[]{:S(2)}) collective-permute-start(bf16[32,96,10,1]{1,0,3,2:T(8,128)(2,1)S(1)} %get-tuple-element.25), channel_id=1, source_target_pairs={{1,0},{2,1},{3,2},{64,3},{65,64},{66,65},{67,66},{128,67},{129,128... | collective-permute-start | bytes 184328 | tf_op jit(solution)/shard_map/ppermute | solution.py:15
  24.7 0.7 copy.40
  25.4 1.6 %copy.41 = bf16[16,2,96,8,16]{2,1,4,3,0:T(2,128)(2,1)S(1)} copy(bf16[16,2,96,8,16]{2,4,0,3,1:T(8,128)(2,1)S(1)} %bitcast.76) | data formatting | bytes 1572864 | tf_op jit(solution)/shard_map/transpose | solution.py:60
  27.0 0.7 reshape.39
  27.7 1.3 %copy.42 = bf16[16,192,128]{2,1,0:T(8,128)(2,1)} copy(bf16[16,192,128]{1,2,0:T(8,128)(2,1)S(1)} %reshape.39) | data formatting | bytes 1572864 | tf_op jit(solution)/shard_map/reshape | solution.py:42
  29.0 7.9 %all-to-all-start = ((bf16[16,192,128]{2,1,0:T(8,128)(2,1)}), bf16[16,192,128]{2,1,0:T(8,128)(2,1)S(1)}, u32[]{:S(2)}, u32[]{:S(2)}) async-start(bf16[16,192,128]{2,1,0:T(8,128)(2,1)} %copy.42), calls=%async_computation | async-start | bytes 1572864 | tf_op jit(solution)/shard_map/all_to_all | solution.py:61
  37.0 8.8 %add_convert_fusion.2 = (bf16[32,96,8,16]{1,0,3,2:T(8,128)(2,1)S(1)}, f32[32,96,8,16]{1,0,3,2:T(8,128)S(1)}, f32[32,96,8,16]{1,0,3,2:T(8,128)S(1)}) fusion(bf16[32,96,8,16]{1,3,2,0:T(8,128)(2,1)S(1)} %copy-done.3, bf16[3,3,96,96]{3,2,1,0:T(8,128)(2,1)S(1)} %copy-done, bf16[32,96,10,1]{1,0,3,2:T(8,128)(2,1)S(1)} %collective-permute-done.3, ...), kind=kOutput, calls=%fused_computation.8 | convolution fusion | flops 706928640 | bytes 5990400 | tf_op jit(solution)/shard_map/conv_general_dilated | solution.py:26
  45.7 3.1 %add_convert_fusion.1 = (bf16[32,96,8,16]{1,0,3,2:T(8,128)(2,1)}, f32[32,96,8,16]{1,0,3,2:T(8,128)S(1)}) fusion(bf16[32,96,8,16]{1,0,3,2:T(8,128)(2,1)S(1)} %get-tuple-element.20, f32[96]{0:T(128)S(1)} %get-tuple-element.33, f32[96]{0:T(128)S(1)} %get-tuple-element.34, f32[96]{0:T(128)S(1)} %get-tuple-element.31, f32[96]{0:T(128)S(1)} %get-tuple-element.32, ...), kind=kLoop, calls=%fused_computation.7 | loop fusion | flops 9830400 | bytes 6293376 | tf_op jit(solution)/shard_map/convert_element_type | solution.py:135
  48.8 6.4 %all-to-all-done = bf16[16,192,128]{2,1,0:T(8,128)(2,1)S(1)} async-done(((bf16[16,192,128]{2,1,0:T(8,128)(2,1)}), bf16[16,192,128]{2,1,0:T(8,128)(2,1)S(1)}, u32[]{:S(2)}, u32[]{:S(2)}) %all-to-all-start) | async-done | bytes 786464 | tf_op jit(solution)/shard_map/all_to_all | solution.py:61
  55.3 1.7 %copy.43 = bf16[16,192,128]{1,0,2:T(8,128)(2,1)} copy(bf16[16,192,128]{2,1,0:T(8,128)(2,1)S(1)} %all-to-all-done) | data formatting | bytes 1572864 | tf_op jit(solution)/shard_map/all_to_all | solution.py:61
  57.0 1.6 %reshape.40 = bf16[32,96,8,16]{1,0,3,2:T(8,128)(2,1)S(1)} reshape(bf16[16,192,128]{1,0,2:T(8,128)(2,1)} %copy.43) | data formatting | bytes 1572864 | tf_op jit(solution)/shard_map/reshape | solution.py:62
  58.6 2.4 %reshape_reshape.3 = bf16[16,192,128]{1,0,2:T(8,128)(2,1)} reshape(bf16[32,96,8,16]{1,0,3,2:T(8,128)(2,1)} %get-tuple-element.9) | data formatting | bytes 1572864 | tf_op jit(solution)/shard_map/reshape;reshape | solution.py:42
  61.1 2.6 %copy.45 = bf16[16,192,128]{2,1,0:T(8,128)(2,1)} copy(bf16[16,192,128]{1,0,2:T(8,128)(2,1)} %reshape_reshape.3) | data formatting | bytes 1572864 | tf_op jit(solution)/shard_map/reshape;reshape | solution.py:42
  63.7 8.2 %all-to-all-start.1 = ((bf16[16,192,128]{2,1,0:T(8,128)(2,1)}), bf16[16,192,128]{2,1,0:T(8,128)(2,1)}, u32[]{:S(2)}, u32[]{:S(2)}) async-start(bf16[16,192,128]{2,1,0:T(8,128)(2,1)} %copy.45), calls=%async_computation.1 | async-start | bytes 1572864 | tf_op jit(solution)/shard_map/all_to_all | solution.py:49
  71.9 1.7 %fusion = (bf16[32,96,8,16]{1,0,3,2:T(8,128)(2,1)S(1)}, bf16[32,96,8,16]{1,0,3,2:T(8,128)(2,1)S(1)}) fusion(f32[32,96,8,16]{1,0,3,2:T(8,128)S(1)} %get-tuple-element.11, f32[96]{0:T(128)S(1)} %get-tuple-element.30, f32[96]{0:T(128)S(1)} %get-tuple-element.32, bf16[32,96,8,16]{1,0,3,2:T(8,128)(2,1)S(1)} %reshape.40, f32[96]{0:T(128)S(1)} %get-tuple-element.31, ...), kind=kLoop, calls=%fused_computation.3 | loop fusion | flops 7077888 | bytes 3934080 | tf_op jit(solution)/shard_map/convert_element_type | solution.py:152
  73.7 1.9 %collective-permute-start.4 = (bf16[32,96,1,16]{1,0,3,2:T(8,128)(2,1)S(1)}, bf16[32,96,1,16]{1,0,3,2:T(8,128)(2,1)S(1)}, u32[]{:S(2)}, u32[]{:S(2)}) collective-permute-start(bf16[32,96,1,16]{1,0,3,2:T(8,128)(2,1)S(1)} %get-tuple-element.26), channel_id=1, source_target_pairs={{0,4},{4,8},{8,12},{12,16},{16,20},{20,24},{24,28},{28,32},{32,36}... | collective-permute-start | bytes 294920 | tf_op jit(solution)/shard_map/ppermute | solution.py:14
  75.6 8.4 %collective-permute-start.5 = (bf16[32,96,1,16]{1,0,3,2:T(8,128)(2,1)S(1)}, bf16[32,96,1,16]{1,0,3,2:T(8,128)(2,1)S(1)}, u32[]{:S(2)}, u32[]{:S(2)}) collective-permute-start(bf16[32,96,1,16]{1,0,3,2:T(8,128)(2,1)S(1)} %get-tuple-element.27), channel_id=1, source_target_pairs={{4,0},{8,4},{12,8},{16,12},{20,16},{24,20},{28,24},{32,28},{36,32}... | collective-permute-start | bytes 294920 | tf_op jit(solution)/shard_map/ppermute | solution.py:15
  84.1 1.5 %collective-permute-done.4 = bf16[32,96,1,16]{1,0,3,2:T(8,128)(2,1)S(1)} collective-permute-done((bf16[32,96,1,16]{1,0,3,2:T(8,128)(2,1)S(1)}, bf16[32,96,1,16]{1,0,3,2:T(8,128)(2,1)S(1)}, u32[]{:S(2)}, u32[]{:S(2)}) %collective-permute-start.4) | collective-permute-done | bytes 98336 | tf_op jit(solution)/shard_map/ppermute | solution.py:14
  85.6 2.5 %collective-permute-done.5 = bf16[32,96,1,16]{1,0,3,2:T(8,128)(2,1)S(1)} collective-permute-done((bf16[32,96,1,16]{1,0,3,2:T(8,128)(2,1)S(1)}, bf16[32,96,1,16]{1,0,3,2:T(8,128)(2,1)S(1)}, u32[]{:S(2)}, u32[]{:S(2)}) %collective-permute-start.5) | collective-permute-done | bytes 98336 | tf_op jit(solution)/shard_map/ppermute | solution.py:15
  88.1 5.7 %collective-permute-start.6 = (bf16[32,96,10,1]{1,0,3,2:T(8,128)(2,1)S(1)}, bf16[32,96,10,1]{1,0,3,2:T(8,128)(2,1)S(1)}, u32[]{:S(2)}, u32[]{:S(2)}) collective-permute-start(bf16[32,96,10,1]{1,0,3,2:T(8,128)(2,1)S(1)} %get-tuple-element.22), channel_id=1, source_target_pairs={{0,1},{1,2},{2,3},{3,64},{64,65},{65,66},{66,67},{67,128},{128,129... | collective-permute-start | bytes 184328 | tf_op jit(solution)/shard_map/ppermute | solution.py:14
  93.8 2.1 %collective-permute-start.7 = (bf16[32,96,10,1]{1,0,3,2:T(8,128)(2,1)S(1)}, bf16[32,96,10,1]{1,0,3,2:T(8,128)(2,1)S(1)}, u32[]{:S(2)}, u32[]{:S(2)}) collective-permute-start(bf16[32,96,10,1]{1,0,3,2:T(8,128)(2,1)S(1)} %get-tuple-element.23), channel_id=1, source_target_pairs={{1,0},{2,1},{3,2},{64,3},{65,64},{66,65},{67,66},{128,67},{129,128... | collective-permute-start | bytes 184328 | tf_op jit(solution)/shard_map/ppermute | solution.py:15
  96.2 6.8 %collective-permute-done.7 = bf16[32,96,10,1]{1,0,3,2:T(8,128)(2,1)S(1)} collective-permute-done((bf16[32,96,10,1]{1,0,3,2:T(8,128)(2,1)S(1)}, bf16[32,96,10,1]{1,0,3,2:T(8,128)(2,1)S(1)}, u32[]{:S(2)}, u32[]{:S(2)}) %collective-permute-start.7) | collective-permute-done | bytes 61472 | tf_op jit(solution)/shard_map/ppermute | solution.py:15
  103.0 2.6 %fusion.1 = bf16[32,96,8,16]{1,0,3,2:T(8,128)(2,1)S(1)} fusion(bf16[32,96,8,16]{1,0,3,2:T(8,128)(2,1)S(1)} %get-tuple-element.19, bf16[3,3,96,96]{3,2,1,0:T(8,128)(2,1)S(1)} %copy-done, bf16[32,96,10,1]{1,0,3,2:T(8,128)(2,1)S(1)} %collective-permute-done.7, bf16[32,96,1,16]{1,0,3,2:T(8,128)(2,1)S(1)} %collective-permute-done.5, ...), kind=kOutput, calls=%fused_computation.4 | convolution fusion | flops 682868736 | bytes 2844672 | tf_op jit(solution)/shard_map/conv_general_dilated | solution.py:26
  105.6 1.4 %copy.51 = bf16[32,96,8,16]{1,3,2,0:T(8,128)(2,1)} copy(bf16[32,96,8,16]{1,0,3,2:T(8,128)(2,1)S(1)} %fusion.1) | data formatting | bytes 1572864
  107.0 1.4 %copy.46 = bf16[16,192,128]{1,2,0:T(8,128)(2,1)S(1)} copy(bf16[16,192,128]{2,1,0:T(8,128)(2,1)} %all-to-all-done.1) | data formatting | bytes 1572864 | tf_op jit(solution)/shard_map/all_to_all | solution.py:49
  108.4 0.6 reshape.41
  109.3 0.4 fusion.25
  109.7 0.5 copy.48
  110.6 0.3 pad_select_fusion.10
  110.9 0.3 pad_select_fusion.9
  111.5 0.3 pad_select_fusion.7
  111.8 0.3 select_reduce_fusion
  113.3 0.3 pad_select_fusion.4
  114.7 0.5 fusion.8
  115.2 1.3 %copy.50 = bf16[2,96,8,256]{3,2,1,0:T(8,128)(2,1)} copy(bf16[2,96,8,256]{3,1,2,0:T(8,128)(2,1)S(1)} %fusion.8) | data formatting | bytes 1572864
  (62 shorter events, 6.3 us)
Async XLA Ops:
  0.6 36.3 %copy-start = (bf16[3,3,96,96]{3,2,1,0:T(8,128)(2,1)S(1)}, bf16[3,3,96,96]{3,2,1,0:T(8,128)(2,1)}, u32[]{:S(2)}) copy-start(bf16[3,3,96,96]{3,2,1,0:T(8,128)(2,1)} %param.10) | copy-start | bytes 497668
  0.6 12.4 %copy-start.9 = (s32[28]{0:T(128)S(1)}, s32[28]{0:T(128)}, u32[]{:S(2)}) copy-start(s32[28]{0:T(128)} %param.16) | copy-start | bytes 340
  0.7 12.5 %copy-start.7 = (s32[2,8,256]{2,1,0:T(8,128)S(1)}, s32[2,8,256]{2,1,0:T(8,128)}, u32[]{:S(2)}) copy-start(s32[2,8,256]{2,1,0:T(8,128)} %param.15) | copy-start | bytes 49156
  0.7 12.5 %copy-start.5 = (bf16[28,96]{1,0:T(8,128)(2,1)S(1)}, bf16[28,96]{1,0:T(8,128)(2,1)}, u32[]{:S(2)}) copy-start(bf16[28,96]{1,0:T(8,128)(2,1)} %param.13) | copy-start | bytes 16132
  0.7 12.5 %copy-start.1 = (bf16[2,96,8,256]{3,2,1,0:T(8,128)(2,1)S(1)}, bf16[2,96,8,256]{3,2,1,0:T(8,128)(2,1)}, u32[]{:S(2)}) copy-start(bf16[2,96,8,256]{3,2,1,0:T(8,128)(2,1)} %param.17) | copy-start | bytes 2359300
  2.7 15.8 %collective-permute-start = (bf16[32,96,1,16]{1,0,3,2:T(8,128)(2,1)S(1)}, bf16[32,96,1,16]{1,0,3,2:T(8,128)(2,1)S(1)}, u32[]{:S(2)}, u32[]{:S(2)}) collective-permute-start(bf16[32,96,1,16]{1,0,3,2:T(8,128)(2,1)S(1)} %get-tuple-element.28), channel_id=1, source_target_pairs={{0,4},{4,8},{8,12},{12,16},{16,20},{20,24},{24,28},{28,32},{32,36}... | collective-permute-start | bytes 294920 | tf_op jit(solution)/shard_map/ppermute | solution.py:14
  4.6 13.8 %collective-permute-start.1 = (bf16[32,96,1,16]{1,0,3,2:T(8,128)(2,1)S(1)}, bf16[32,96,1,16]{1,0,3,2:T(8,128)(2,1)S(1)}, u32[]{:S(2)}, u32[]{:S(2)}) collective-permute-start(bf16[32,96,1,16]{1,0,3,2:T(8,128)(2,1)S(1)} %get-tuple-element.29), channel_id=1, source_target_pairs={{4,0},{8,4},{12,8},{16,12},{20,16},{24,20},{28,24},{32,28},{36,32}... | collective-permute-start | bytes 294920 | tf_op jit(solution)/shard_map/ppermute | solution.py:15
  17.3 0.7 copy-start.4
  18.4 6.2 %copy-start.8 = (f32[96,5]{0,1:T(8,128)S(1)}, f32[96,5]{0,1:T(8,128)}, u32[]{:S(2)}) copy-start(f32[96,5]{0,1:T(8,128)} %param.11) | copy-start | bytes 5764
  18.8 5.9 %copy-start.2 = (bf16[32,96,10,16]{1,0,3,2:T(8,128)(2,1)}, bf16[32,96,10,16]{1,0,3,2:T(8,128)(2,1)S(1)}, u32[]{:S(2)}) copy-start(bf16[32,96,10,16]{1,0,3,2:T(8,128)(2,1)S(1)} %pad_maximum_fusion) | copy-start | bytes 2949124
  18.8 18.1 %collective-permute-start.2 = (bf16[32,96,10,1]{1,0,3,2:T(8,128)(2,1)S(1)}, bf16[32,96,10,1]{1,0,3,2:T(8,128)(2,1)S(1)}, u32[]{:S(2)}, u32[]{:S(2)}) collective-permute-start(bf16[32,96,10,1]{1,0,3,2:T(8,128)(2,1)S(1)} %get-tuple-element.24), channel_id=1, source_target_pairs={{0,1},{1,2},{2,3},{3,64},{64,65},{65,66},{66,67},{67,128},{128,129... | collective-permute-start | bytes 184328 | tf_op jit(solution)/shard_map/ppermute | solution.py:14
  22.6 14.4 %collective-permute-start.3 = (bf16[32,96,10,1]{1,0,3,2:T(8,128)(2,1)S(1)}, bf16[32,96,10,1]{1,0,3,2:T(8,128)(2,1)S(1)}, u32[]{:S(2)}, u32[]{:S(2)}) collective-permute-start(bf16[32,96,10,1]{1,0,3,2:T(8,128)(2,1)S(1)} %get-tuple-element.25), channel_id=1, source_target_pairs={{1,0},{2,1},{3,2},{64,3},{65,64},{66,65},{67,66},{128,67},{129,128... | collective-permute-start | bytes 184328 | tf_op jit(solution)/shard_map/ppermute | solution.py:15
  27.7 9.2 %copy-start.3 = (bf16[32,96,8,16]{1,3,2,0:T(8,128)(2,1)S(1)}, bf16[32,96,8,16]{1,3,2,0:T(8,128)(2,1)}, u32[]{:S(2)}) copy-start(bf16[32,96,8,16]{1,3,2,0:T(8,128)(2,1)} %param.9) | copy-start | bytes 2359300
  29.0 26.3 %all-to-all-start = ((bf16[16,192,128]{2,1,0:T(8,128)(2,1)}), bf16[16,192,128]{2,1,0:T(8,128)(2,1)S(1)}, u32[]{:S(2)}, u32[]{:S(2)}) async-start(bf16[16,192,128]{2,1,0:T(8,128)(2,1)} %copy.42), calls=%async_computation | async-start | bytes 1572864 | tf_op jit(solution)/shard_map/all_to_all | solution.py:61
  63.7 43.3 %all-to-all-start.1 = ((bf16[16,192,128]{2,1,0:T(8,128)(2,1)}), bf16[16,192,128]{2,1,0:T(8,128)(2,1)}, u32[]{:S(2)}, u32[]{:S(2)}) async-start(bf16[16,192,128]{2,1,0:T(8,128)(2,1)} %copy.45), calls=%async_computation.1 | async-start | bytes 1572864 | tf_op jit(solution)/shard_map/all_to_all | solution.py:49
  73.7 11.9 %collective-permute-start.4 = (bf16[32,96,1,16]{1,0,3,2:T(8,128)(2,1)S(1)}, bf16[32,96,1,16]{1,0,3,2:T(8,128)(2,1)S(1)}, u32[]{:S(2)}, u32[]{:S(2)}) collective-permute-start(bf16[32,96,1,16]{1,0,3,2:T(8,128)(2,1)S(1)} %get-tuple-element.26), channel_id=1, source_target_pairs={{0,4},{4,8},{8,12},{12,16},{16,20},{20,24},{24,28},{28,32},{32,36}... | collective-permute-start | bytes 294920 | tf_op jit(solution)/shard_map/ppermute | solution.py:14
  75.6 12.5 %collective-permute-start.5 = (bf16[32,96,1,16]{1,0,3,2:T(8,128)(2,1)S(1)}, bf16[32,96,1,16]{1,0,3,2:T(8,128)(2,1)S(1)}, u32[]{:S(2)}, u32[]{:S(2)}) collective-permute-start(bf16[32,96,1,16]{1,0,3,2:T(8,128)(2,1)S(1)} %get-tuple-element.27), channel_id=1, source_target_pairs={{4,0},{8,4},{12,8},{16,12},{20,16},{24,20},{28,24},{32,28},{36,32}... | collective-permute-start | bytes 294920 | tf_op jit(solution)/shard_map/ppermute | solution.py:15
  88.1 8.1 %collective-permute-start.6 = (bf16[32,96,10,1]{1,0,3,2:T(8,128)(2,1)S(1)}, bf16[32,96,10,1]{1,0,3,2:T(8,128)(2,1)S(1)}, u32[]{:S(2)}, u32[]{:S(2)}) collective-permute-start(bf16[32,96,10,1]{1,0,3,2:T(8,128)(2,1)S(1)} %get-tuple-element.22), channel_id=1, source_target_pairs={{0,1},{1,2},{2,3},{3,64},{64,65},{65,66},{66,67},{67,128},{128,129... | collective-permute-start | bytes 184328 | tf_op jit(solution)/shard_map/ppermute | solution.py:14
  93.8 9.2 %collective-permute-start.7 = (bf16[32,96,10,1]{1,0,3,2:T(8,128)(2,1)S(1)}, bf16[32,96,10,1]{1,0,3,2:T(8,128)(2,1)S(1)}, u32[]{:S(2)}, u32[]{:S(2)}) collective-permute-start(bf16[32,96,10,1]{1,0,3,2:T(8,128)(2,1)S(1)} %get-tuple-element.23), channel_id=1, source_target_pairs={{1,0},{2,1},{3,2},{64,3},{65,64},{66,65},{67,66},{128,67},{129,128... | collective-permute-start | bytes 184328 | tf_op jit(solution)/shard_map/ppermute | solution.py:15
  111.5 0.7 copy-start.6

commit v12 on v11

--- a/solution.py
+++ b/solution.py
@@ -4,15 +4,19 @@
 from jax.sharding import PartitionSpec as P
 
 
-def with_halo(array, sides, width):
+def with_halo(array, sides, width, dense=False):
     for axis, dim in sides:
         devices, length = (lax.axis_size(axis), array.shape[dim])
         up = [(i, (i + 1) % devices) for i in range(devices - 1)]
         down = [(j, i) for i, j in up]
         last = lax.slice_in_dim(array, length - width, length, axis=dim)
         initial = lax.slice_in_dim(array, 0, width, axis=dim)
-        before = lax.ppermute(last, axis, up)
-        after = lax.ppermute(initial, axis, down)
+        if dense:
+            before = lax.ppermute(lane_rows(last[None]), axis, up).reshape(last.shape)
+            after = lax.ppermute(lane_rows(initial[None]), axis, down).reshape(initial.shape)
+        else:
+            before = lax.ppermute(last, axis, up)
+            after = lax.ppermute(initial, axis, down)
         array = jnp.concatenate([before, array, after], axis=dim)
     return array
 
@@ -31,10 +35,6 @@
         dimension_numbers=("NCHW", "HWIO", "NCHW"),
         preferred_element_type=jnp.float32,
     )
-
-
-def spatial_conv(field_in, kernel):
-    return halo_conv(row_halo(field_in), kernel)
 
 
 def lane_rows(block):
@@ -151,7 +151,8 @@
     cot_hidden = time_mix(cot_space, flipped).astype(jnp.bfloat16)
     gate_grad = (slope * cot_hidden.astype(jnp.float32)).astype(jnp.bfloat16)
     kernel_flip = jnp.transpose(conv_weight[::-1, ::-1], (0, 1, 3, 2))
-    features_grad = (cot_hidden.astype(jnp.float32) + spatial_conv(gate_grad, kernel_flip)).astype(
+    gate_rows = with_halo(gate_grad, (("row", 2),), 1, dense=True)
+    features_grad = (cot_hidden.astype(jnp.float32) + halo_conv(gate_rows, kernel_flip)).astype(
         jnp.bfloat16
     )
     return (updated, features_grad)

time: 118 us -> 122 us (1.034)
  local copies, waits for them, and re-layouts: 23.7 us -> 27.9 us
  other arithmetic: 10.5 us -> 14.2 us
  waiting for transfers between devices: 17.5 us -> 15 us
  starting transfers between devices: 50.6 us -> 48.9 us
    ppermute x0 -> x2, starting transfers between devices: none -> 10.4 us  [the longest x1 8.45 us: with_halo(): lax.ppermute(lane_rows(initial[None]), axis, down).reshape(initial.shape)]
    ppermute x4 -> x3, starting transfers between devices: 21.1 us -> 14.1 us  [with_halo(): after = lax.ppermute(initial, axis, down)]
    ppermute x4 -> x3, starting transfers between devices: 13.3 us -> 8.13 us  [with_halo(): before = lax.ppermute(last, axis, up)]
    convert_element_type x1, other arithmetic: 1.75 us -> 6.24 us  [on_device(): gate_grad = (slope * cot_hidden.astype(jnp.float32)).astype(jnp.bfloat16)]
    ppermute x4 -> x3, waiting for transfers between devices: 9.31 us -> 5.02 us  [with_halo(): after = lax.ppermute(initial, axis, down)]
    ppermute x0 -> x2, waiting for transfers between devices: none -> 2.3 us  [the longest x1 1.3 us: with_halo(): before = lax.ppermute(lane_rows(last[None]), axis, up).reshape(last.shape)]
    reshape x0 -> x4, local copies, waits for them, and re-layouts: none -> 1.69 us  [the longest x2 0.84 us: with_halo(): before = lax.ppermute(lane_rows(last[None]), axis, up).reshape(last.shape)]
    ppermute x4 -> x3, waiting for transfers between devices: 1.72 us -> 0.37 us  [with_halo(): before = lax.ppermute(last, axis, up)]
  transfers between devices with their start and end apart: 10 -> 10, of which waited for: 5 -> 5; matrix products, arithmetic and copies ran while one was open for 23% -> 28% of each run, Pallas kernels for 0% -> 0%
where the time goes in v12:
time: 122 us; the launch traced here: 120 us
  starting transfers between devices  48.9 us (40%)
  local copies, waits for them, and re-layouts  27.9 us (23%)
  waiting for transfers between devices  15 us (12%)
  other arithmetic  14.2 us (12%)
  matrix products  13 us (11%)
  between operations  1.29 us (1%)
    ppermute x3, starting transfers between devices, with_halo(): after = lax.ppermute(initial, axis, down)  14.1 us
    conv_general_dilated x2, matrix products, halo_conv(): lax.conv_general_dilated(padded, kernel, window_strides=(1, 1), padding='...  11.3 us
    ppermute x1, starting transfers between devices, with_halo(): lax.ppermute(lane_rows(initial[None]), axis, down).reshape(initial.shape)  8.45 us
    all_to_all x1, starting transfers between devices, to_time(): lax.all_to_all(sent, ('ta', 'col'), split_axis=0, concat_axis=0, tiled=True)  8.35 us
    ppermute x3, starting transfers between devices, with_halo(): before = lax.ppermute(last, axis, up)  8.13 us
    all_to_all x1, starting transfers between devices, to_space(): lax.all_to_all(sent, ('ta', 'col'), split_axis=0, concat_axis=0, tiled=True)  7.95 us
    all_to_all x1, waiting for transfers between devices, to_space(): lax.all_to_all(sent, ('ta', 'col'), split_axis=0, concat_axis=0, tiled=True)  7.31 us
    convert_element_type x1, other arithmetic, on_device(): gate_grad = (slope * cot_hidden.astype(jnp.float32)).astype(jnp.bfloat16)  6.24 us
  transfers between devices with their start and end apart: 10, of which 5 were waited for; matrix products, arithmetic and copies ran while one was open for 28% of the time, Pallas kernels for 0%

profile of v12, /device:TPU:86, one launch (start us, length us, event | category | flops | bytes accessed | tf_op | source)
XLA Modules:
  0.0 120.3 jit_solution(2913081399017739544)
XLA Ops:
  0.7 2.0 %copy.39 = bf16[32,96,8,16]{1,0,3,2:T(8,128)(2,1)S(1)} copy(bf16[32,96,8,16]{1,3,2,0:T(8,128)(2,1)} %param.9) | data formatting | bytes 1572864 | tf_op args[0]
  2.7 1.9 %collective-permute-start = (bf16[32,96,1,16]{1,0,3,2:T(8,128)(2,1)S(1)}, bf16[32,96,1,16]{1,0,3,2:T(8,128)(2,1)S(1)}, u32[]{:S(2)}, u32[]{:S(2)}) collective-permute-start(bf16[32,96,1,16]{1,0,3,2:T(8,128)(2,1)S(1)} %get-tuple-element.28), channel_id=1, source_target_pairs={{0,4},{4,8},{8,12},{12,16},{16,20},{20,24},{24,28},{28,32},{32,36}... | collective-permute-start | bytes 294920 | tf_op jit(solution)/shard_map/ppermute | solution.py:18
  4.6 8.4 %collective-permute-start.1 = (bf16[32,96,1,16]{1,0,3,2:T(8,128)(2,1)S(1)}, bf16[32,96,1,16]{1,0,3,2:T(8,128)(2,1)S(1)}, u32[]{:S(2)}, u32[]{:S(2)}) collective-permute-start(bf16[32,96,1,16]{1,0,3,2:T(8,128)(2,1)S(1)} %get-tuple-element.29), channel_id=1, source_target_pairs={{4,0},{8,4},{12,8},{16,12},{20,16},{24,20},{28,24},{32,28},{36,32}... | collective-permute-start | bytes 294920 | tf_op jit(solution)/shard_map/ppermute | solution.py:19
  14.9 0.3 select_reduce_fusion.1
  18.0 0.5 fusion.9
  18.5 0.3 pad_maximum_fusion
  18.8 3.7 %collective-permute-start.2 = (bf16[32,96,10,1]{1,0,3,2:T(8,128)(2,1)S(1)}, bf16[32,96,10,1]{1,0,3,2:T(8,128)(2,1)S(1)}, u32[]{:S(2)}, u32[]{:S(2)}) collective-permute-start(bf16[32,96,10,1]{1,0,3,2:T(8,128)(2,1)S(1)} %get-tuple-element.24), channel_id=1, source_target_pairs={{0,1},{1,2},{2,3},{3,64},{64,65},{65,66},{66,67},{67,128},{128,129... | collective-permute-start | bytes 184328 | tf_op jit(solution)/shard_map/ppermute | solution.py:18
  22.6 2.1 %collective-permute-start.3 = (bf16[32,96,10,1]{1,0,3,2:T(8,128)(2,1)S(1)}, bf16[32,96,10,1]{1,0,3,2:T(8,128)(2,1)S(1)}, u32[]{:S(2)}, u32[]{:S(2)}) collective-permute-start(bf16[32,96,10,1]{1,0,3,2:T(8,128)(2,1)S(1)} %get-tuple-element.25), channel_id=1, source_target_pairs={{1,0},{2,1},{3,2},{64,3},{65,64},{66,65},{67,66},{128,67},{129,128... | collective-permute-start | bytes 184328 | tf_op jit(solution)/shard_map/ppermute | solution.py:19
  24.7 0.7 copy.44
  25.4 1.6 %copy.45 = bf16[16,2,96,8,16]{2,1,4,3,0:T(2,128)(2,1)S(1)} copy(bf16[16,2,96,8,16]{2,4,0,3,1:T(8,128)(2,1)S(1)} %bitcast.84) | data formatting | bytes 1572864 | tf_op jit(solution)/shard_map/transpose | solution.py:60
  27.0 0.7 reshape.45
  27.7 1.3 %copy.46 = bf16[16,192,128]{2,1,0:T(8,128)(2,1)} copy(bf16[16,192,128]{1,2,0:T(8,128)(2,1)S(1)} %reshape.45) | data formatting | bytes 1572864 | tf_op jit(solution)/shard_map/reshape | solution.py:42
  29.0 7.9 %all-to-all-start = ((bf16[16,192,128]{2,1,0:T(8,128)(2,1)}), bf16[16,192,128]{2,1,0:T(8,128)(2,1)}, u32[]{:S(2)}, u32[]{:S(2)}) async-start(bf16[16,192,128]{2,1,0:T(8,128)(2,1)} %copy.46), calls=%async_computation | async-start | bytes 1572864 | tf_op jit(solution)/shard_map/all_to_all | solution.py:61
  37.0 8.7 %add_convert_fusion.2 = (bf16[32,96,8,16]{1,0,3,2:T(8,128)(2,1)S(1)}, f32[32,96,8,16]{1,0,3,2:T(8,128)S(1)}, f32[32,96,8,16]{1,0,3,2:T(8,128)S(1)}) fusion(bf16[32,96,8,16]{1,3,2,0:T(8,128)(2,1)} %param.9, bf16[3,3,96,96]{3,2,1,0:T(8,128)(2,1)S(1)} %copy-done, bf16[32,96,10,1]{1,0,3,2:T(8,128)(2,1)S(1)} %collective-permute-done.3, ...), kind=kOutput, calls=%fused_computation.8 | convolution fusion | flops 706928640 | bytes 5990400 | tf_op jit(solution)/shard_map/conv_general_dilated | solution.py:30
  45.6 2.3 %add_convert_fusion.1 = (bf16[32,96,8,16]{1,0,3,2:T(8,128)(2,1)S(1)}, f32[32,96,8,16]{1,0,3,2:T(8,128)S(1)}) fusion(bf16[32,96,8,16]{1,0,3,2:T(8,128)(2,1)S(1)} %get-tuple-element.20, f32[96]{0:T(128)S(1)} %get-tuple-element.33, f32[96]{0:T(128)S(1)} %get-tuple-element.34, f32[96]{0:T(128)S(1)} %get-tuple-element.31, f32[96]{0:T(128)S(1)} %get-tuple-element.32, ...), kind=kLoop, calls=%fused_computation.7 | loop fusion | flops 9830400 | bytes 6293376 | tf_op jit(solution)/shard_map/convert_element_type | solution.py:135
  48.0 7.3 %all-to-all-done = bf16[16,192,128]{2,1,0:T(8,128)(2,1)} async-done(((bf16[16,192,128]{2,1,0:T(8,128)(2,1)}), bf16[16,192,128]{2,1,0:T(8,128)(2,1)}, u32[]{:S(2)}, u32[]{:S(2)}) %all-to-all-start) | async-done | bytes 786464 | tf_op jit(solution)/shard_map/all_to_all | solution.py:61
  55.3 2.6 %copy.47 = bf16[16,192,128]{1,0,2:T(8,128)(2,1)} copy(bf16[16,192,128]{2,1,0:T(8,128)(2,1)} %all-to-all-done) | data formatting | bytes 1572864 | tf_op jit(solution)/shard_map/all_to_all | solution.py:61
  57.9 2.4 %reshape.46 = bf16[32,96,8,16]{1,0,3,2:T(8,128)(2,1)} reshape(bf16[16,192,128]{1,0,2:T(8,128)(2,1)} %copy.47) | data formatting | bytes 1572864 | tf_op jit(solution)/shard_map/reshape | solution.py:62
  60.3 1.5 %reshape_reshape.3 = bf16[16,192,128]{1,0,2:T(8,128)(2,1)} reshape(bf16[32,96,8,16]{1,0,3,2:T(8,128)(2,1)S(1)} %get-tuple-element.9) | data formatting | bytes 1572864 | tf_op jit(solution)/shard_map/reshape;reshape | solution.py:42
  61.8 2.6 %copy.49 = bf16[16,192,128]{2,1,0:T(8,128)(2,1)} copy(bf16[16,192,128]{1,0,2:T(8,128)(2,1)} %reshape_reshape.3) | data formatting | bytes 1572864 | tf_op jit(solution)/shard_map/reshape;reshape | solution.py:42
  64.4 8.3 %all-to-all-start.1 = ((bf16[16,192,128]{2,1,0:T(8,128)(2,1)}), bf16[16,192,128]{2,1,0:T(8,128)(2,1)}, u32[]{:S(2)}, u32[]{:S(2)}) async-start(bf16[16,192,128]{2,1,0:T(8,128)(2,1)} %copy.49), calls=%async_computation.1 | async-start | bytes 1572864 | tf_op jit(solution)/shard_map/all_to_all | solution.py:49
  72.7 6.2 %fusion = (bf16[32,96,8,16]{1,0,3,2:T(8,128)(2,1)S(1)}, bf16[32,96,8,16]{1,0,3,2:T(8,128)(2,1)}) fusion(f32[32,96,8,16]{1,0,3,2:T(8,128)S(1)} %get-tuple-element.11, f32[96]{0:T(128)S(1)} %get-tuple-element.30, f32[96]{0:T(128)S(1)} %get-tuple-element.32, bf16[32,96,8,16]{1,0,3,2:T(8,128)(2,1)} %reshape.46, f32[96]{0:T(128)S(1)} %get-tuple-element.31, ...), kind=kLoop, calls=%fused_computation.3 | loop fusion | flops 7077888 | bytes 3934080 | tf_op jit(solution)/shard_map/convert_element_type | solution.py:152
  79.0 0.4 copy.54
  79.4 0.5 reshape_broadcast_in_dim.6
  79.9 1.9 %collective-permute-start.4 = (bf16[1,384,128]{2,1,0:T(8,128)(2,1)S(1)}, bf16[1,384,128]{2,1,0:T(8,128)(2,1)S(1)}, u32[]{:S(2)}, u32[]{:S(2)}) collective-permute-start(bf16[1,384,128]{2,1,0:T(8,128)(2,1)S(1)} %reshape_broadcast_in_dim.6), channel_id=1, source_target_pairs={{0,4},{4,8},{8,12},{12,16},{16,20},{20,24},{24,28},{28,32},{32,36}... | collective-permute-start | bytes 294920 | tf_op jit(solution)/shard_map/ppermute | solution.py:15
  81.8 0.4 copy.55
  82.2 0.5 reshape_broadcast_in_dim.7
  82.7 8.4 %collective-permute-start.5 = (bf16[1,384,128]{2,1,0:T(8,128)(2,1)S(1)}, bf16[1,384,128]{2,1,0:T(8,128)(2,1)S(1)}, u32[]{:S(2)}, u32[]{:S(2)}) collective-permute-start(bf16[1,384,128]{2,1,0:T(8,128)(2,1)S(1)} %reshape_broadcast_in_dim.7), channel_id=1, source_target_pairs={{4,0},{8,4},{12,8},{16,12},{20,16},{24,20},{28,24},{32,28},{36,32}... | collective-permute-start | bytes 294920 | tf_op jit(solution)/shard_map/ppermute | solution.py:16
  91.2 1.3 %collective-permute-done.4 = bf16[1,384,128]{2,1,0:T(8,128)(2,1)S(1)} collective-permute-done((bf16[1,384,128]{2,1,0:T(8,128)(2,1)S(1)}, bf16[1,384,128]{2,1,0:T(8,128)(2,1)S(1)}, u32[]{:S(2)}, u32[]{:S(2)}) %collective-permute-start.4) | collective-permute-done | bytes 98336 | tf_op jit(solution)/shard_map/ppermute | solution.py:15
  92.5 0.5 reshape.49
  93.0 0.3 copy.56
  93.4 1.0 collective-permute-done.5
  94.4 0.5 reshape.50
  94.9 0.3 copy.57
  95.3 2.5 %collective-permute-start.6 = (bf16[32,96,10,1]{1,0,3,2:T(8,128)(2,1)S(1)}, bf16[32,96,10,1]{1,0,3,2:T(8,128)(2,1)S(1)}, u32[]{:S(2)}, u32[]{:S(2)}) collective-permute-start(bf16[32,96,10,1]{1,0,3,2:T(8,128)(2,1)S(1)} %get-tuple-element.22), channel_id=1, source_target_pairs={{0,1},{1,2},{2,3},{3,64},{64,65},{65,66},{66,67},{67,128},{128,129... | collective-permute-start | bytes 184328 | tf_op jit(solution)/shard_map/ppermute | solution.py:18
  97.7 3.6 %collective-permute-start.7 = (bf16[32,96,10,1]{1,0,3,2:T(8,128)(2,1)S(1)}, bf16[32,96,10,1]{1,0,3,2:T(8,128)(2,1)S(1)}, u32[]{:S(2)}, u32[]{:S(2)}) collective-permute-start(bf16[32,96,10,1]{1,0,3,2:T(8,128)(2,1)S(1)} %get-tuple-element.23), channel_id=1, source_target_pairs={{1,0},{2,1},{3,2},{64,3},{65,64},{66,65},{67,66},{128,67},{129,128... | collective-permute-start | bytes 184328 | tf_op jit(solution)/shard_map/ppermute | solution.py:19
  101.3 0.4 collective-permute-done.6
  101.7 5.0 %collective-permute-done.7 = bf16[32,96,10,1]{1,0,3,2:T(8,128)(2,1)S(1)} collective-permute-done((bf16[32,96,10,1]{1,0,3,2:T(8,128)(2,1)S(1)}, bf16[32,96,10,1]{1,0,3,2:T(8,128)(2,1)S(1)}, u32[]{:S(2)}, u32[]{:S(2)}) %collective-permute-start.7) | collective-permute-done | bytes 61472 | tf_op jit(solution)/shard_map/ppermute | solution.py:19
  106.7 2.7 %fusion.1 = bf16[32,96,8,16]{1,0,3,2:T(8,128)(2,1)S(1)} fusion(bf16[32,96,8,16]{1,0,3,2:T(8,128)(2,1)S(1)} %copy-done.4, bf16[3,3,96,96]{3,2,1,0:T(8,128)(2,1)S(1)} %copy-done, bf16[32,96,10,1]{1,0,3,2:T(8,128)(2,1)S(1)} %collective-permute-done.7, bf16[32,96,1,16]{1,0,3,2:T(8,128)(2,1)S(1)} %copy.57, bf16[32,96,8,16]{1,0,3,2:T(8,128)(2,1)S(1)} %get-tuple-element.18, ...), kind=kOutput, calls=%fused_computation.4 | convolution fusion | flops 682868736 | bytes 2844672 | tf_op jit(solution)/shard_map/conv_general_dilated | solution.py:30
  109.4 1.4 %copy.59 = bf16[32,96,8,16]{1,3,2,0:T(8,128)(2,1)} copy(bf16[32,96,8,16]{1,0,3,2:T(8,128)(2,1)S(1)} %fusion.1) | data formatting | bytes 1572864
  110.8 1.4 %copy.50 = bf16[16,192,128]{1,2,0:T(8,128)(2,1)S(1)} copy(bf16[16,192,128]{2,1,0:T(8,128)(2,1)} %all-to-all-done.1) | data formatting | bytes 1572864 | tf_op jit(solution)/shard_map/all_to_all | solution.py:49
  112.2 0.6 reshape.47
  113.1 0.4 fusion.25
  113.5 0.5 copy.52
  115.6 0.3 select_reduce_fusion
  117.0 0.3 pad_select_fusion.4
  118.5 0.5 fusion.8
  119.0 1.3 %copy.58 = bf16[2,96,8,256]{3,2,1,0:T(8,128)(2,1)} copy(bf16[2,96,8,256]{3,1,2,0:T(8,128)(2,1)S(1)} %fusion.8) | data formatting | bytes 1572864
  (72 shorter events, 8.6 us)
Async XLA Ops:
  0.6 36.3 %copy-start = (bf16[3,3,96,96]{3,2,1,0:T(8,128)(2,1)S(1)}, bf16[3,3,96,96]{3,2,1,0:T(8,128)(2,1)}, u32[]{:S(2)}) copy-start(bf16[3,3,96,96]{3,2,1,0:T(8,128)(2,1)} %param.10) | copy-start | bytes 497668
  0.6 12.4 %copy-start.10 = (s32[28]{0:T(128)S(1)}, s32[28]{0:T(128)}, u32[]{:S(2)}) copy-start(s32[28]{0:T(128)} %param.16) | copy-start | bytes 340
  0.7 12.5 %copy-start.8 = (s32[2,8,256]{2,1,0:T(8,128)S(1)}, s32[2,8,256]{2,1,0:T(8,128)}, u32[]{:S(2)}) copy-start(s32[2,8,256]{2,1,0:T(8,128)} %param.15) | copy-start | bytes 49156
  0.7 12.5 %copy-start.6 = (bf16[28,96]{1,0:T(8,128)(2,1)S(1)}, bf16[28,96]{1,0:T(8,128)(2,1)}, u32[]{:S(2)}) copy-start(bf16[28,96]{1,0:T(8,128)(2,1)} %param.13) | copy-start | bytes 16132
  0.7 12.5 %copy-start.1 = (bf16[2,96,8,256]{3,2,1,0:T(8,128)(2,1)S(1)}, bf16[2,96,8,256]{3,2,1,0:T(8,128)(2,1)}, u32[]{:S(2)}) copy-start(bf16[2,96,8,256]{3,2,1,0:T(8,128)(2,1)} %param.17) | copy-start | bytes 2359300
  2.7 15.8 %collective-permute-start = (bf16[32,96,1,16]{1,0,3,2:T(8,128)(2,1)S(1)}, bf16[32,96,1,16]{1,0,3,2:T(8,128)(2,1)S(1)}, u32[]{:S(2)}, u32[]{:S(2)}) collective-permute-start(bf16[32,96,1,16]{1,0,3,2:T(8,128)(2,1)S(1)} %get-tuple-element.28), channel_id=1, source_target_pairs={{0,4},{4,8},{8,12},{12,16},{16,20},{20,24},{24,28},{28,32},{32,36}... | collective-permute-start | bytes 294920 | tf_op jit(solution)/shard_map/ppermute | solution.py:18
  4.6 13.8 %collective-permute-start.1 = (bf16[32,96,1,16]{1,0,3,2:T(8,128)(2,1)S(1)}, bf16[32,96,1,16]{1,0,3,2:T(8,128)(2,1)S(1)}, u32[]{:S(2)}, u32[]{:S(2)}) collective-permute-start(bf16[32,96,1,16]{1,0,3,2:T(8,128)(2,1)S(1)} %get-tuple-element.29), channel_id=1, source_target_pairs={{4,0},{8,4},{12,8},{16,12},{20,16},{24,20},{28,24},{32,28},{36,32}... | collective-permute-start | bytes 294920 | tf_op jit(solution)/shard_map/ppermute | solution.py:19
  17.3 0.7 copy-start.5
  18.4 6.2 %copy-start.9 = (f32[96,5]{0,1:T(8,128)S(1)}, f32[96,5]{0,1:T(8,128)}, u32[]{:S(2)}) copy-start(f32[96,5]{0,1:T(8,128)} %param.11) | copy-start | bytes 5764
  18.8 5.9 %copy-start.2 = (bf16[32,96,10,16]{1,0,3,2:T(8,128)(2,1)}, bf16[32,96,10,16]{1,0,3,2:T(8,128)(2,1)S(1)}, u32[]{:S(2)}) copy-start(bf16[32,96,10,16]{1,0,3,2:T(8,128)(2,1)S(1)} %pad_maximum_fusion) | copy-start | bytes 2949124
  18.8 18.1 %collective-permute-start.2 = (bf16[32,96,10,1]{1,0,3,2:T(8,128)(2,1)S(1)}, bf16[32,96,10,1]{1,0,3,2:T(8,128)(2,1)S(1)}, u32[]{:S(2)}, u32[]{:S(2)}) collective-permute-start(bf16[32,96,10,1]{1,0,3,2:T(8,128)(2,1)S(1)} %get-tuple-element.24), channel_id=1, source_target_pairs={{0,1},{1,2},{2,3},{3,64},{64,65},{65,66},{66,67},{67,128},{128,129... | collective-permute-start | bytes 184328 | tf_op jit(solution)/shard_map/ppermute | solution.py:18
  22.6 14.4 %collective-permute-start.3 = (bf16[32,96,10,1]{1,0,3,2:T(8,128)(2,1)S(1)}, bf16[32,96,10,1]{1,0,3,2:T(8,128)(2,1)S(1)}, u32[]{:S(2)}, u32[]{:S(2)}) collective-permute-start(bf16[32,96,10,1]{1,0,3,2:T(8,128)(2,1)S(1)} %get-tuple-element.25), channel_id=1, source_target_pairs={{1,0},{2,1},{3,2},{64,3},{65,64},{66,65},{67,66},{128,67},{129,128... | collective-permute-start | bytes 184328 | tf_op jit(solution)/shard_map/ppermute | solution.py:19
  27.7 9.2 %copy-start.3 = (bf16[32,96,10,16]{1,0,3,2:T(8,128)(2,1)S(1)}, bf16[32,96,10,16]{1,0,3,2:T(8,128)(2,1)}, u32[]{:S(2)}) copy-start(bf16[32,96,10,16]{1,0,3,2:T(8,128)(2,1)} %copy-done.2) | copy-start | bytes 2949124
  29.0 26.3 %all-to-all-start = ((bf16[16,192,128]{2,1,0:T(8,128)(2,1)}), bf16[16,192,128]{2,1,0:T(8,128)(2,1)}, u32[]{:S(2)}, u32[]{:S(2)}) async-start(bf16[16,192,128]{2,1,0:T(8,128)(2,1)} %copy.46), calls=%async_computation | async-start | bytes 1572864 | tf_op jit(solution)/shard_map/all_to_all | solution.py:61
  64.4 46.4 %all-to-all-start.1 = ((bf16[16,192,128]{2,1,0:T(8,128)(2,1)}), bf16[16,192,128]{2,1,0:T(8,128)(2,1)}, u32[]{:S(2)}, u32[]{:S(2)}) async-start(bf16[16,192,128]{2,1,0:T(8,128)(2,1)} %copy.49), calls=%async_computation.1 | async-start | bytes 1572864 | tf_op jit(solution)/shard_map/all_to_all | solution.py:49
  79.9 12.6 %collective-permute-start.4 = (bf16[1,384,128]{2,1,0:T(8,128)(2,1)S(1)}, bf16[1,384,128]{2,1,0:T(8,128)(2,1)S(1)}, u32[]{:S(2)}, u32[]{:S(2)}) collective-permute-start(bf16[1,384,128]{2,1,0:T(8,128)(2,1)S(1)} %reshape_broadcast_in_dim.6), channel_id=1, source_target_pairs={{0,4},{4,8},{8,12},{12,16},{16,20},{20,24},{24,28},{28,32},{32,36}... | collective-permute-start | bytes 294920 | tf_op jit(solution)/shard_map/ppermute | solution.py:15
  82.7 11.6 %collective-permute-start.5 = (bf16[1,384,128]{2,1,0:T(8,128)(2,1)S(1)}, bf16[1,384,128]{2,1,0:T(8,128)(2,1)S(1)}, u32[]{:S(2)}, u32[]{:S(2)}) collective-permute-start(bf16[1,384,128]{2,1,0:T(8,128)(2,1)S(1)} %reshape_broadcast_in_dim.7), channel_id=1, source_target_pairs={{4,0},{8,4},{12,8},{16,12},{20,16},{24,20},{28,24},{32,28},{36,32}... | collective-permute-start | bytes 294920 | tf_op jit(solution)/shard_map/ppermute | solution.py:16
  93.0 13.7 %copy-start.4 = (bf16[32,96,8,16]{1,0,3,2:T(8,128)(2,1)S(1)}, bf16[32,96,8,16]{1,0,3,2:T(8,128)(2,1)}, u32[]{:S(2)}) copy-start(bf16[32,96,8,16]{1,0,3,2:T(8,128)(2,1)} %get-tuple-element.19) | copy-start | bytes 2359300
  95.3 6.4 %collective-permute-start.6 = (bf16[32,96,10,1]{1,0,3,2:T(8,128)(2,1)S(1)}, bf16[32,96,10,1]{1,0,3,2:T(8,128)(2,1)S(1)}, u32[]{:S(2)}, u32[]{:S(2)}) collective-permute-start(bf16[32,96,10,1]{1,0,3,2:T(8,128)(2,1)S(1)} %get-tuple-element.22), channel_id=1, source_target_pairs={{0,1},{1,2},{2,3},{3,64},{64,65},{65,66},{66,67},{67,128},{128,129... | collective-permute-start | bytes 184328 | tf_op jit(solution)/shard_map/ppermute | solution.py:18
  97.7 9.0 %collective-permute-start.7 = (bf16[32,96,10,1]{1,0,3,2:T(8,128)(2,1)S(1)}, bf16[32,96,10,1]{1,0,3,2:T(8,128)(2,1)S(1)}, u32[]{:S(2)}, u32[]{:S(2)}) collective-permute-start(bf16[32,96,10,1]{1,0,3,2:T(8,128)(2,1)S(1)} %get-tuple-element.23), channel_id=1, source_target_pairs={{1,0},{2,1},{3,2},{64,3},{65,64},{66,65},{67,66},{128,67},{129,128... | collective-permute-start | bytes 184328 | tf_op jit(solution)/shard_map/ppermute | solution.py:19
  115.3 0.7 copy-start.7

commit v13 on v11

--- a/solution.py
+++ b/solution.py
@@ -134,9 +134,7 @@
     hidden_state = (features.astype(jnp.float32) + gelu_value).astype(jnp.bfloat16)
     temporal_space = time_mix(hidden_state, time_weight).astype(jnp.bfloat16)
     flipped = time_weight[:, ::-1]
-    cot_space, slope, temporal_space = lax.optimization_barrier(
-        (to_space(cot_temporal), slope, temporal_space)
-    )
+    cot_space, slope = lax.optimization_barrier((to_space(cot_temporal), slope))
     temporal = to_time(temporal_space)
     band_vals = jnp.einsum("fcqw,cb->fbqw", temporal, band_out, preferred_element_type=jnp.float32)
     masked_band_sum = disperse(band_vals * mask_float, bits, width_wide)

time: 118 us -> 120 us (1.017)
  local copies, waits for them, and re-layouts: 23.7 us -> 18.2 us
  other arithmetic: 10.5 us -> 15.2 us
  starting transfers between devices: 50.6 us -> 53.5 us
    convert_element_type x1, other arithmetic: 1.75 us -> 7.68 us  [on_device(): gate_grad = (slope * cot_hidden.astype(jnp.float32)).astype(jnp.bfloat16)]
    ppermute x4, starting transfers between devices: 13.3 us -> 16 us  [with_halo(): before = lax.ppermute(last, axis, up)]
    another operation x2, local copies, waits for them, and re-layouts: 5.03 us -> 2.35 us  [lane_rows(): return block.reshape(block.shape[0], -1, lanes)]
    ppermute x4, waiting for transfers between devices: 9.31 us -> 7.13 us  [with_halo(): after = lax.ppermute(initial, axis, down)]
    all_to_all x1, waiting for transfers between devices: 6.44 us -> 8.41 us  [to_space(): lax.all_to_all(sent, ('ta', 'col'), split_axis=0, concat_axis=0, tiled=True)]
    convert_element_type x1, other arithmetic: 3.1 us -> 1.87 us  [on_device(): (features.astype(jnp.float32) + gelu_value).astype(jnp.bfloat16)]
    ppermute x4, waiting for transfers between devices: 1.72 us -> 2.93 us  [with_halo(): before = lax.ppermute(last, axis, up)]
    unnamed x23 -> x27, local copies, waits for them, and re-layouts: 5.13 us -> 5.12 us
  transfers between devices with their start and end apart: 10 -> 10, of which waited for: 5 -> 5; matrix products, arithmetic and copies ran while one was open for 23% -> 19% of each run, Pallas kernels for 0% -> 0%
where the time goes in v13:
time: 120 us; the launch traced here: 119 us
  starting transfers between devices  53.5 us (45%)
  waiting for transfers between devices  18.5 us (15%)
  local copies, waits for them, and re-layouts  18.2 us (15%)
  other arithmetic  15.2 us (13%)
  matrix products  12.4 us (10%)
  between operations  1.25 us (1%)
    ppermute x4, starting transfers between devices, with_halo(): after = lax.ppermute(initial, axis, down)  21.1 us
    ppermute x4, starting transfers between devices, with_halo(): before = lax.ppermute(last, axis, up)  16 us
    conv_general_dilated x2, matrix products, halo_conv(): lax.conv_general_dilated(padded, kernel, window_strides=(1, 1), padding='...  10.7 us
    all_to_all x1, waiting for transfers between devices, to_space(): lax.all_to_all(sent, ('ta', 'col'), split_axis=0, concat_axis=0, tiled=True)  8.41 us
    all_to_all x1, starting transfers between devices, to_time(): lax.all_to_all(sent, ('ta', 'col'), split_axis=0, concat_axis=0, tiled=True)  8.38 us
    all_to_all x1, starting transfers between devices, to_space(): lax.all_to_all(sent, ('ta', 'col'), split_axis=0, concat_axis=0, tiled=True)  7.95 us
    convert_element_type x1, other arithmetic, on_device(): gate_grad = (slope * cot_hidden.astype(jnp.float32)).astype(jnp.bfloat16)  7.68 us
    ppermute x4, waiting for transfers between devices, with_halo(): after = lax.ppermute(initial, axis, down)  7.13 us
  transfers between devices with their start and end apart: 10, of which 5 were waited for; matrix products, arithmetic and copies ran while one was open for 19% of the time, Pallas kernels for 0%

profile of v13, /device:TPU:86, one launch (start us, length us, event | category | flops | bytes accessed | tf_op | source)
XLA Modules:
  0.0 119.0 jit_solution(11568591550216208795)
XLA Ops:
  0.7 2.0 %copy.35 = bf16[32,96,8,16]{1,0,3,2:T(8,128)(2,1)S(1)} copy(bf16[32,96,8,16]{1,3,2,0:T(8,128)(2,1)} %param.9) | data formatting | bytes 1572864 | tf_op args[0]
  2.7 1.9 %collective-permute-start = (bf16[32,96,1,16]{1,0,3,2:T(8,128)(2,1)S(1)}, bf16[32,96,1,16]{1,0,3,2:T(8,128)(2,1)S(1)}, u32[]{:S(2)}, u32[]{:S(2)}) collective-permute-start(bf16[32,96,1,16]{1,0,3,2:T(8,128)(2,1)S(1)} %get-tuple-element.26), channel_id=1, source_target_pairs={{0,4},{4,8},{8,12},{12,16},{16,20},{20,24},{24,28},{28,32},{32,36}... | collective-permute-start | bytes 294920 | tf_op jit(solution)/shard_map/ppermute | solution.py:14
  4.6 8.4 %collective-permute-start.1 = (bf16[32,96,1,16]{1,0,3,2:T(8,128)(2,1)S(1)}, bf16[32,96,1,16]{1,0,3,2:T(8,128)(2,1)S(1)}, u32[]{:S(2)}, u32[]{:S(2)}) collective-permute-start(bf16[32,96,1,16]{1,0,3,2:T(8,128)(2,1)S(1)} %get-tuple-element.27), channel_id=1, source_target_pairs={{4,0},{8,4},{12,8},{16,12},{20,16},{24,20},{28,24},{32,28},{36,32}... | collective-permute-start | bytes 294920 | tf_op jit(solution)/shard_map/ppermute | solution.py:15
  13.5 0.3 pad_select_fusion.1
  14.1 0.3 pad_select_fusion.18
  14.4 0.3 pad_select_fusion.17
  14.6 0.3 pad_select_fusion.16
  14.9 0.3 select_reduce_fusion.1
  16.3 0.3 pad_select_fusion.13
  18.0 0.5 fusion.9
  18.5 0.3 pad_maximum_fusion
  18.8 3.7 %collective-permute-start.2 = (bf16[32,96,10,1]{1,0,3,2:T(8,128)(2,1)S(1)}, bf16[32,96,10,1]{1,0,3,2:T(8,128)(2,1)S(1)}, u32[]{:S(2)}, u32[]{:S(2)}) collective-permute-start(bf16[32,96,10,1]{1,0,3,2:T(8,128)(2,1)S(1)} %get-tuple-element.22), channel_id=1, source_target_pairs={{0,1},{1,2},{2,3},{3,64},{64,65},{65,66},{66,67},{67,128},{128,129... | collective-permute-start | bytes 184328 | tf_op jit(solution)/shard_map/ppermute | solution.py:14
  22.6 2.1 %collective-permute-start.3 = (bf16[32,96,10,1]{1,0,3,2:T(8,128)(2,1)S(1)}, bf16[32,96,10,1]{1,0,3,2:T(8,128)(2,1)S(1)}, u32[]{:S(2)}, u32[]{:S(2)}) collective-permute-start(bf16[32,96,10,1]{1,0,3,2:T(8,128)(2,1)S(1)} %get-tuple-element.23), channel_id=1, source_target_pairs={{1,0},{2,1},{3,2},{64,3},{65,64},{66,65},{67,66},{128,67},{129,128... | collective-permute-start | bytes 184328 | tf_op jit(solution)/shard_map/ppermute | solution.py:15
  24.7 0.7 copy.46
  25.4 1.6 %copy.47 = bf16[16,2,96,8,16]{2,1,4,3,0:T(2,128)(2,1)S(1)} copy(bf16[16,2,96,8,16]{2,4,0,3,1:T(8,128)(2,1)S(1)} %bitcast.76) | data formatting | bytes 1572864 | tf_op jit(solution)/shard_map/transpose | solution.py:60
  27.0 0.7 reshape.41
  27.7 1.3 %copy.48 = bf16[16,192,128]{2,1,0:T(8,128)(2,1)} copy(bf16[16,192,128]{1,2,0:T(8,128)(2,1)S(1)} %reshape.41) | data formatting | bytes 1572864 | tf_op jit(solution)/shard_map/reshape | solution.py:42
  29.0 7.9 %all-to-all-start.1 = ((bf16[16,192,128]{2,1,0:T(8,128)(2,1)}), bf16[16,192,128]{2,1,0:T(8,128)(2,1)S(1)}, u32[]{:S(2)}, u32[]{:S(2)}) async-start(bf16[16,192,128]{2,1,0:T(8,128)(2,1)} %copy.48), calls=%async_computation.1 | async-start | bytes 1572864 | tf_op jit(solution)/shard_map/all_to_all | solution.py:61
  37.0 8.0 %multiply_add_fusion = (f32[32,96,8,16]{1,0,3,2:T(8,128)}, f32[32,96,8,16]{1,0,3,2:T(8,128)S(1)}, f32[32,96,8,16]{1,0,3,2:T(8,128)S(1)}) fusion(bf16[3,3,96,96]{3,2,1,0:T(8,128)(2,1)S(1)} %copy-done, bf16[32,96,10,1]{1,0,3,2:T(8,128)(2,1)S(1)} %collective-permute-done.3, bf16[32,96,10,16]{1,0,3,2:T(8,128)(2,1)S(1)} %copy-done.4, ...), kind=kOutput, calls=%fused_computation.7 | convolution fusion | flops 707321856 | bytes 5990400 | tf_op jit(solution)/shard_map/conv_general_dilated | solution.py:26
  45.0 1.9 %add_convert_fusion.2 = bf16[32,96,8,16]{1,0,3,2:T(8,128)(2,1)} fusion(f32[32,96,8,16]{1,0,3,2:T(8,128)S(1)} %get-tuple-element.19, f32[32,96,8,16]{1,0,3,2:T(8,128)S(1)} %get-tuple-element.40, bf16[32,96,8,16]{1,3,2,0:T(8,128)(2,1)S(1)} %copy-done.1), kind=kLoop, calls=%fused_computation.9 | loop fusion | flops 1966080 | bytes 4718592 | tf_op jit(solution)/shard_map/convert_element_type | solution.py:134
  46.9 8.4 %all-to-all-done.1 = bf16[16,192,128]{2,1,0:T(8,128)(2,1)S(1)} async-done(((bf16[16,192,128]{2,1,0:T(8,128)(2,1)}), bf16[16,192,128]{2,1,0:T(8,128)(2,1)S(1)}, u32[]{:S(2)}, u32[]{:S(2)}) %all-to-all-start.1) | async-done | bytes 786464 | tf_op jit(solution)/shard_map/all_to_all | solution.py:61
  55.3 0.9 copy.49
  56.2 0.6 reshape.42
  56.8 7.7 %fusion = (bf16[32,96,8,16]{1,0,3,2:T(8,128)(2,1)S(1)}, bf16[32,96,8,16]{1,0,3,2:T(8,128)(2,1)}, bf16[32,96,8,16]{1,0,3,2:T(8,128)(2,1)S(1)}) fusion(f32[32,96,8,16]{1,0,3,2:T(8,128)} %get-tuple-element.9, f32[96]{0:T(128)S(1)} %get-tuple-element.28, f32[96]{0:T(128)S(1)} %get-tuple-element.30, bf16[32,96,8,16]{1,0,3,2:T(8,128)(2,1)S(1)} %reshape.42, ...), kind=kLoop, calls=%fused_computation.3 | loop fusion | flops 12976128 | bytes 5506944 | tf_op jit(solution)/shard_map/convert_element_type | solution.py:150
  64.5 0.7 reshape_reshape.3
  65.2 1.6 %copy.41 = bf16[16,192,128]{2,1,0:T(8,128)(2,1)} copy(bf16[16,192,128]{1,0,2:T(8,128)(2,1)S(1)} %reshape_reshape.3) | data formatting | bytes 1572864 | tf_op jit(solution)/shard_map/reshape;reshape | solution.py:42
  66.8 8.4 %all-to-all-start = ((bf16[16,192,128]{2,1,0:T(8,128)(2,1)}), bf16[16,192,128]{2,1,0:T(8,128)(2,1)S(1)}, u32[]{:S(2)}, u32[]{:S(2)}) async-start(bf16[16,192,128]{2,1,0:T(8,128)(2,1)} %copy.41), calls=%async_computation | async-start | bytes 1572864 | tf_op jit(solution)/shard_map/all_to_all | solution.py:49
  75.2 1.9 %collective-permute-start.4 = (bf16[32,96,1,16]{1,0,3,2:T(8,128)(2,1)S(1)}, bf16[32,96,1,16]{1,0,3,2:T(8,128)(2,1)S(1)}, u32[]{:S(2)}, u32[]{:S(2)}) collective-permute-start(bf16[32,96,1,16]{1,0,3,2:T(8,128)(2,1)S(1)} %get-tuple-element.24), channel_id=1, source_target_pairs={{0,4},{4,8},{8,12},{12,16},{16,20},{20,24},{24,28},{28,32},{32,36}... | collective-permute-start | bytes 294920 | tf_op jit(solution)/shard_map/ppermute | solution.py:14
  77.2 8.4 %collective-permute-start.5 = (bf16[32,96,1,16]{1,0,3,2:T(8,128)(2,1)S(1)}, bf16[32,96,1,16]{1,0,3,2:T(8,128)(2,1)S(1)}, u32[]{:S(2)}, u32[]{:S(2)}) collective-permute-start(bf16[32,96,1,16]{1,0,3,2:T(8,128)(2,1)S(1)} %get-tuple-element.25), channel_id=1, source_target_pairs={{4,0},{8,4},{12,8},{16,12},{20,16},{24,20},{28,24},{32,28},{36,32}... | collective-permute-start | bytes 294920 | tf_op jit(solution)/shard_map/ppermute | solution.py:15
  85.6 2.7 %collective-permute-done.4 = bf16[32,96,1,16]{1,0,3,2:T(8,128)(2,1)S(1)} collective-permute-done((bf16[32,96,1,16]{1,0,3,2:T(8,128)(2,1)S(1)}, bf16[32,96,1,16]{1,0,3,2:T(8,128)(2,1)S(1)}, u32[]{:S(2)}, u32[]{:S(2)}) %collective-permute-start.4) | collective-permute-done | bytes 98336 | tf_op jit(solution)/shard_map/ppermute | solution.py:14
  88.3 0.3 collective-permute-done.5
  88.7 8.4 %collective-permute-start.6 = (bf16[32,96,10,1]{1,0,3,2:T(8,128)(2,1)S(1)}, bf16[32,96,10,1]{1,0,3,2:T(8,128)(2,1)S(1)}, u32[]{:S(2)}, u32[]{:S(2)}) collective-permute-start(bf16[32,96,10,1]{1,0,3,2:T(8,128)(2,1)S(1)} %get-tuple-element.20), channel_id=1, source_target_pairs={{0,1},{1,2},{2,3},{3,64},{64,65},{65,66},{66,67},{67,128},{128,129... | collective-permute-start | bytes 184328 | tf_op jit(solution)/shard_map/ppermute | solution.py:14
  97.1 2.1 %collective-permute-start.7 = (bf16[32,96,10,1]{1,0,3,2:T(8,128)(2,1)S(1)}, bf16[32,96,10,1]{1,0,3,2:T(8,128)(2,1)S(1)}, u32[]{:S(2)}, u32[]{:S(2)}) collective-permute-start(bf16[32,96,10,1]{1,0,3,2:T(8,128)(2,1)S(1)} %get-tuple-element.21), channel_id=1, source_target_pairs={{1,0},{2,1},{3,2},{64,3},{65,64},{66,65},{67,66},{128,67},{129,128... | collective-permute-start | bytes 184328 | tf_op jit(solution)/shard_map/ppermute | solution.py:15
  99.5 6.8 %collective-permute-done.7 = bf16[32,96,10,1]{1,0,3,2:T(8,128)(2,1)S(1)} collective-permute-done((bf16[32,96,10,1]{1,0,3,2:T(8,128)(2,1)S(1)}, bf16[32,96,10,1]{1,0,3,2:T(8,128)(2,1)S(1)}, u32[]{:S(2)}, u32[]{:S(2)}) %collective-permute-start.7) | collective-permute-done | bytes 61472 | tf_op jit(solution)/shard_map/ppermute | solution.py:15
  106.3 2.7 %fusion.1 = bf16[32,96,8,16]{1,0,3,2:T(8,128)(2,1)S(1)} fusion(bf16[32,96,8,16]{1,0,3,2:T(8,128)(2,1)S(1)} %copy-done.5, bf16[3,3,96,96]{3,2,1,0:T(8,128)(2,1)S(1)} %copy-done, bf16[32,96,10,1]{1,0,3,2:T(8,128)(2,1)S(1)} %collective-permute-done.7, bf16[32,96,1,16]{1,0,3,2:T(8,128)(2,1)S(1)} %collective-permute-done.5, ...), kind=kOutput, calls=%fused_computation.4 | convolution fusion | flops 682868736 | bytes 2844672 | tf_op jit(solution)/shard_map/conv_general_dilated | solution.py:26
  109.0 1.4 %copy.51 = bf16[32,96,8,16]{1,3,2,0:T(8,128)(2,1)} copy(bf16[32,96,8,16]{1,0,3,2:T(8,128)(2,1)S(1)} %fusion.1) | data formatting | bytes 1572864
  110.4 0.5 copy.42
  110.9 0.6 reshape.38
  111.7 0.4 fusion.25
  112.2 0.5 copy.44
  112.8 0.3 pad_select_fusion
  113.1 0.3 pad_select_fusion.10
  113.4 0.3 pad_select_fusion.9
  113.9 0.3 pad_select_fusion.7
  114.2 0.3 select_reduce_fusion
  115.7 0.3 pad_select_fusion.4
  117.2 0.5 fusion.8
  117.7 1.3 %copy.50 = bf16[2,96,8,256]{3,2,1,0:T(8,128)(2,1)} copy(bf16[2,96,8,256]{3,1,2,0:T(8,128)(2,1)S(1)} %fusion.8) | data formatting | bytes 1572864
  (66 shorter events, 6.3 us)
Async XLA Ops:
  0.6 36.3 %copy-start = (bf16[3,3,96,96]{3,2,1,0:T(8,128)(2,1)S(1)}, bf16[3,3,96,96]{3,2,1,0:T(8,128)(2,1)}, u32[]{:S(2)}) copy-start(bf16[3,3,96,96]{3,2,1,0:T(8,128)(2,1)} %param.10) | copy-start | bytes 497668
  0.6 12.4 %copy-start.11 = (s32[28]{0:T(128)S(1)}, s32[28]{0:T(128)}, u32[]{:S(2)}) copy-start(s32[28]{0:T(128)} %param.16) | copy-start | bytes 340
  0.7 12.5 %copy-start.9 = (s32[2,8,256]{2,1,0:T(8,128)S(1)}, s32[2,8,256]{2,1,0:T(8,128)}, u32[]{:S(2)}) copy-start(s32[2,8,256]{2,1,0:T(8,128)} %param.15) | copy-start | bytes 49156
  0.7 12.5 %copy-start.7 = (bf16[28,96]{1,0:T(8,128)(2,1)S(1)}, bf16[28,96]{1,0:T(8,128)(2,1)}, u32[]{:S(2)}) copy-start(bf16[28,96]{1,0:T(8,128)(2,1)} %param.13) | copy-start | bytes 16132
  0.7 12.5 %copy-start.2 = (bf16[2,96,8,256]{3,2,1,0:T(8,128)(2,1)S(1)}, bf16[2,96,8,256]{3,2,1,0:T(8,128)(2,1)}, u32[]{:S(2)}) copy-start(bf16[2,96,8,256]{3,2,1,0:T(8,128)(2,1)} %param.17) | copy-start | bytes 2359300
  2.7 15.8 %collective-permute-start = (bf16[32,96,1,16]{1,0,3,2:T(8,128)(2,1)S(1)}, bf16[32,96,1,16]{1,0,3,2:T(8,128)(2,1)S(1)}, u32[]{:S(2)}, u32[]{:S(2)}) collective-permute-start(bf16[32,96,1,16]{1,0,3,2:T(8,128)(2,1)S(1)} %get-tuple-element.26), channel_id=1, source_target_pairs={{0,4},{4,8},{8,12},{12,16},{16,20},{20,24},{24,28},{28,32},{32,36}... | collective-permute-start | bytes 294920 | tf_op jit(solution)/shard_map/ppermute | solution.py:14
  4.6 13.8 %collective-permute-start.1 = (bf16[32,96,1,16]{1,0,3,2:T(8,128)(2,1)S(1)}, bf16[32,96,1,16]{1,0,3,2:T(8,128)(2,1)S(1)}, u32[]{:S(2)}, u32[]{:S(2)}) collective-permute-start(bf16[32,96,1,16]{1,0,3,2:T(8,128)(2,1)S(1)} %get-tuple-element.27), channel_id=1, source_target_pairs={{4,0},{8,4},{12,8},{16,12},{20,16},{24,20},{28,24},{32,28},{36,32}... | collective-permute-start | bytes 294920 | tf_op jit(solution)/shard_map/ppermute | solution.py:15
  17.3 0.7 copy-start.6
  18.4 6.2 %copy-start.10 = (f32[96,5]{0,1:T(8,128)S(1)}, f32[96,5]{0,1:T(8,128)}, u32[]{:S(2)}) copy-start(f32[96,5]{0,1:T(8,128)} %param.11) | copy-start | bytes 5764
  18.8 5.9 %copy-start.3 = (bf16[32,96,10,16]{1,0,3,2:T(8,128)(2,1)}, bf16[32,96,10,16]{1,0,3,2:T(8,128)(2,1)S(1)}, u32[]{:S(2)}) copy-start(bf16[32,96,10,16]{1,0,3,2:T(8,128)(2,1)S(1)} %pad_maximum_fusion) | copy-start | bytes 2949124
  18.8 18.1 %collective-permute-start.2 = (bf16[32,96,10,1]{1,0,3,2:T(8,128)(2,1)S(1)}, bf16[32,96,10,1]{1,0,3,2:T(8,128)(2,1)S(1)}, u32[]{:S(2)}, u32[]{:S(2)}) collective-permute-start(bf16[32,96,10,1]{1,0,3,2:T(8,128)(2,1)S(1)} %get-tuple-element.22), channel_id=1, source_target_pairs={{0,1},{1,2},{2,3},{3,64},{64,65},{65,66},{66,67},{67,128},{128,129... | collective-permute-start | bytes 184328 | tf_op jit(solution)/shard_map/ppermute | solution.py:14
  22.6 14.4 %collective-permute-start.3 = (bf16[32,96,10,1]{1,0,3,2:T(8,128)(2,1)S(1)}, bf16[32,96,10,1]{1,0,3,2:T(8,128)(2,1)S(1)}, u32[]{:S(2)}, u32[]{:S(2)}) collective-permute-start(bf16[32,96,10,1]{1,0,3,2:T(8,128)(2,1)S(1)} %get-tuple-element.23), channel_id=1, source_target_pairs={{1,0},{2,1},{3,2},{64,3},{65,64},{66,65},{67,66},{128,67},{129,128... | collective-permute-start | bytes 184328 | tf_op jit(solution)/shard_map/ppermute | solution.py:15
  27.7 9.3 %copy-start.4 = (bf16[32,96,10,16]{1,0,3,2:T(8,128)(2,1)S(1)}, bf16[32,96,10,16]{1,0,3,2:T(8,128)(2,1)}, u32[]{:S(2)}) copy-start(bf16[32,96,10,16]{1,0,3,2:T(8,128)(2,1)} %copy-done.3) | copy-start | bytes 2949124
  29.0 26.3 %all-to-all-start.1 = ((bf16[16,192,128]{2,1,0:T(8,128)(2,1)}), bf16[16,192,128]{2,1,0:T(8,128)(2,1)S(1)}, u32[]{:S(2)}, u32[]{:S(2)}) async-start(bf16[16,192,128]{2,1,0:T(8,128)(2,1)} %copy.48), calls=%async_computation.1 | async-start | bytes 1572864 | tf_op jit(solution)/shard_map/all_to_all | solution.py:61
  36.9 8.1 %copy-start.1 = (bf16[32,96,8,16]{1,3,2,0:T(8,128)(2,1)S(1)}, bf16[32,96,8,16]{1,3,2,0:T(8,128)(2,1)}, u32[]{:S(2)}) copy-start(bf16[32,96,8,16]{1,3,2,0:T(8,128)(2,1)} %param.9) | copy-start | bytes 2359300
  66.8 39.5 %copy-start.5 = (bf16[32,96,8,16]{1,0,3,2:T(8,128)(2,1)S(1)}, bf16[32,96,8,16]{1,0,3,2:T(8,128)(2,1)}, u32[]{:S(2)}) copy-start(bf16[32,96,8,16]{1,0,3,2:T(8,128)(2,1)} %get-tuple-element.17) | copy-start | bytes 2359300
  66.8 43.5 %all-to-all-start = ((bf16[16,192,128]{2,1,0:T(8,128)(2,1)}), bf16[16,192,128]{2,1,0:T(8,128)(2,1)S(1)}, u32[]{:S(2)}, u32[]{:S(2)}) async-start(bf16[16,192,128]{2,1,0:T(8,128)(2,1)} %copy.41), calls=%async_computation | async-start | bytes 1572864 | tf_op jit(solution)/shard_map/all_to_all | solution.py:49
  75.2 13.1 %collective-permute-start.4 = (bf16[32,96,1,16]{1,0,3,2:T(8,128)(2,1)S(1)}, bf16[32,96,1,16]{1,0,3,2:T(8,128)(2,1)S(1)}, u32[]{:S(2)}, u32[]{:S(2)}) collective-permute-start(bf16[32,96,1,16]{1,0,3,2:T(8,128)(2,1)S(1)} %get-tuple-element.24), channel_id=1, source_target_pairs={{0,4},{4,8},{8,12},{12,16},{16,20},{20,24},{24,28},{28,32},{32,36}... | collective-permute-start | bytes 294920 | tf_op jit(solution)/shard_map/ppermute | solution.py:14
  77.2 11.5 %collective-permute-start.5 = (bf16[32,96,1,16]{1,0,3,2:T(8,128)(2,1)S(1)}, bf16[32,96,1,16]{1,0,3,2:T(8,128)(2,1)S(1)}, u32[]{:S(2)}, u32[]{:S(2)}) collective-permute-start(bf16[32,96,1,16]{1,0,3,2:T(8,128)(2,1)S(1)} %get-tuple-element.25), channel_id=1, source_target_pairs={{4,0},{8,4},{12,8},{16,12},{20,16},{24,20},{28,24},{32,28},{36,32}... | collective-permute-start | bytes 294920 | tf_op jit(solution)/shard_map/ppermute | solution.py:15
  88.7 10.8 %collective-permute-start.6 = (bf16[32,96,10,1]{1,0,3,2:T(8,128)(2,1)S(1)}, bf16[32,96,10,1]{1,0,3,2:T(8,128)(2,1)S(1)}, u32[]{:S(2)}, u32[]{:S(2)}) collective-permute-start(bf16[32,96,10,1]{1,0,3,2:T(8,128)(2,1)S(1)} %get-tuple-element.20), channel_id=1, source_target_pairs={{0,1},{1,2},{2,3},{3,64},{64,65},{65,66},{66,67},{67,128},{128,129... | collective-permute-start | bytes 184328 | tf_op jit(solution)/shard_map/ppermute | solution.py:14
  97.1 9.2 %collective-permute-start.7 = (bf16[32,96,10,1]{1,0,3,2:T(8,128)(2,1)S(1)}, bf16[32,96,10,1]{1,0,3,2:T(8,128)(2,1)S(1)}, u32[]{:S(2)}, u32[]{:S(2)}) collective-permute-start(bf16[32,96,10,1]{1,0,3,2:T(8,128)(2,1)S(1)} %get-tuple-element.21), channel_id=1, source_target_pairs={{1,0},{2,1},{3,2},{64,3},{65,64},{66,65},{67,66},{128,67},{129,128... | collective-permute-start | bytes 184328 | tf_op jit(solution)/shard_map/ppermute | solution.py:15
  113.9 0.7 copy-start.8

commit v14 on v11

--- a/solution.py
+++ b/solution.py
@@ -53,13 +53,16 @@
     )
 
 
-def to_space(field_in):
+def space_blocks(field_in):
     blocks = lax.axis_size(("ta", "col"))
-    width = field_in.shape[3] // blocks
-    split = field_in.reshape(field_in.shape[:3] + (blocks, width))
-    sent = lane_rows(jnp.moveaxis(split, 3, 0))
+    split = field_in.reshape(field_in.shape[:3] + (blocks, field_in.shape[3] // blocks))
+    return lane_rows(jnp.moveaxis(split, 3, 0))
+
+
+def to_space(sent, like):
+    blocks = lax.axis_size(("ta", "col"))
     got = lax.all_to_all(sent, ("ta", "col"), split_axis=0, concat_axis=0, tiled=True)
-    return got.reshape((blocks * field_in.shape[0],) + field_in.shape[1:3] + (width,))
+    return got.reshape((blocks * like.shape[0],) + like.shape[1:3] + (like.shape[3] // blocks,))
 
 
 def time_mix(frames_in, time_taps):
@@ -127,7 +130,7 @@
         + jnp.einsum("fbqw,cb->fcqw", band_grad, band_out, preferred_element_type=jnp.float32)
     ).astype(jnp.bfloat16)
     feature_rows = row_halo(features)
-    feature_rows, cot_temporal = lax.optimization_barrier((feature_rows, cot_temporal))
+    feature_rows, cot_sent = lax.optimization_barrier((feature_rows, space_blocks(cot_temporal)))
     pre_act = halo_conv(feature_rows, conv_weight)
     gelu_value, pullback = jax.vjp(gelu_exact, pre_act)
     slope = pullback(jnp.ones_like(pre_act))[0]
@@ -135,7 +138,7 @@
     temporal_space = time_mix(hidden_state, time_weight).astype(jnp.bfloat16)
     flipped = time_weight[:, ::-1]
     cot_space, slope, temporal_space = lax.optimization_barrier(
-        (to_space(cot_temporal), slope, temporal_space)
+        (to_space(cot_sent, cot_temporal), slope, temporal_space)
     )
     temporal = to_time(temporal_space)
     band_vals = jnp.einsum("fcqw,cb->fbqw", temporal, band_out, preferred_element_type=jnp.float32)

time: 118 us -> 117 us (level)
  waiting for transfers between devices: 17.5 us -> 13 us
  local copies, waits for them, and re-layouts: 23.7 us -> 25.4 us
    ppermute x4, waiting for transfers between devices: 9.31 us -> 6.42 us  [with_halo(): after = lax.ppermute(initial, axis, down)]
    all_to_all x1, waiting for transfers between devices: 6.44 us -> 3.76 us  [to_space(): lax.all_to_all(sent, ('ta', 'col'), split_axis=0, concat_axis=0, tiled=True)]
    reshape x2 -> x1, local copies, waits for them, and re-layouts: 1.98 us -> 0.72 us  [lane_rows(): return block.reshape(block.shape[0], -1, lanes)]
where the time goes in v14:
time: 117 us; the launch traced here: 115 us
  starting transfers between devices  50.9 us (44%)
  local copies, waits for them, and re-layouts  25.4 us (22%)
  matrix products  13 us (11%)
  waiting for transfers between devices  13 us (11%)
  other arithmetic  11.4 us (10%)
  between operations  1.2 us (1%)
    ppermute x4, starting transfers between devices, with_halo(): after = lax.ppermute(initial, axis, down)  21.1 us
    ppermute x4, starting transfers between devices, with_halo(): before = lax.ppermute(last, axis, up)  13.3 us
    conv_general_dilated x2, matrix products, halo_conv(): lax.conv_general_dilated(padded, kernel, window_strides=(1, 1), padding='...  11.4 us
    all_to_all x1, starting transfers between devices, to_time(): lax.all_to_all(sent, ('ta', 'col'), split_axis=0, concat_axis=0, tiled=True)  8.5 us
    all_to_all x1, starting transfers between devices, to_space(): lax.all_to_all(sent, ('ta', 'col'), split_axis=0, concat_axis=0, tiled=True)  7.95 us
    ppermute x4, waiting for transfers between devices, with_halo(): after = lax.ppermute(initial, axis, down)  6.42 us
    unnamed x23, local copies, waits for them, and re-layouts  6.18 us
    another operation x2, local copies, waits for them, and re-layouts, lane_rows(): return block.reshape(block.shape[0], -1, lanes)  5.03 us
  transfers between devices with their start and end apart: 10, of which 5 were waited for; matrix products, arithmetic and copies ran while one was open for 23% of the time, Pallas kernels for 0%

profile of v14, /device:TPU:86, one launch (start us, length us, event | category | flops | bytes accessed | tf_op | source)
XLA Modules:
  0.0 114.9 jit_solution(12656611840947710909)
XLA Ops:
  0.7 2.0 %copy.35 = bf16[32,96,8,16]{1,0,3,2:T(8,128)(2,1)S(1)} copy(bf16[32,96,8,16]{1,3,2,0:T(8,128)(2,1)} %param.9) | data formatting | bytes 1572864 | tf_op args[0]
  2.7 0.7 fusion.50
  3.4 1.9 %collective-permute-start = (bf16[32,96,1,16]{1,0,3,2:T(8,128)(2,1)}, bf16[32,96,1,16]{1,0,3,2:T(8,128)(2,1)S(1)}, u32[]{:S(2)}, u32[]{:S(2)}) collective-permute-start(bf16[32,96,1,16]{1,0,3,2:T(8,128)(2,1)} %get-tuple-element.28), channel_id=1, source_target_pairs={{0,4},{4,8},{8,12},{12,16},{16,20},{20,24},{24,28},{28,32},{32,36}... | collective-permute-start | bytes 294920 | tf_op jit(solution)/shard_map/ppermute | solution.py:14
  5.3 8.4 %collective-permute-start.1 = (bf16[32,96,1,16]{1,0,3,2:T(8,128)(2,1)}, bf16[32,96,1,16]{1,0,3,2:T(8,128)(2,1)}, u32[]{:S(2)}, u32[]{:S(2)}) collective-permute-start(bf16[32,96,1,16]{1,0,3,2:T(8,128)(2,1)} %get-tuple-element.29), channel_id=1, source_target_pairs={{4,0},{8,4},{12,8},{16,12},{20,16},{24,20},{28,24},{32,28},{36,32}... | collective-permute-start | bytes 294920 | tf_op jit(solution)/shard_map/ppermute | solution.py:15
  14.2 0.3 pad_select_fusion.1
  14.5 0.3 pad_select_fusion.19
  14.8 0.3 pad_select_fusion.18
  15.0 0.3 pad_select_fusion.17
  15.3 0.3 pad_select_fusion.16
  15.6 0.3 select_reduce_fusion.1
  16.9 0.3 pad_select_fusion.13
  18.6 0.5 fusion.9
  19.1 0.7 copy.40
  19.8 1.6 %copy.41 = bf16[16,2,96,8,16]{2,1,4,3,0:T(2,128)(2,1)S(1)} copy(bf16[16,2,96,8,16]{2,4,0,3,1:T(8,128)(2,1)S(1)} %bitcast.76) | data formatting | bytes 1572864 | tf_op jit(solution)/shard_map/transpose | solution.py:59
  21.4 0.7 reshape.39
  22.2 1.2 %pad_maximum_fusion = bf16[32,96,10,16]{1,0,3,2:T(8,128)(2,1)S(1)} fusion(bf16[32,96,1,16]{1,0,3,2:T(8,128)(2,1)} %collective-permute-done.1, bf16[32,96,8,16]{1,0,3,2:T(8,128)(2,1)S(1)} %copy.35, bf16[32,96,1,16]{1,0,3,2:T(8,128)(2,1)S(1)} %collective-permute-done), kind=kLoop, calls=%fused_computation.42 | loop fusion | flops 983040 | bytes 1966080 | tf_op jit(solution)/shard_map/concatenate | solution.py:16
  23.4 1.1 copy-done.2
  24.5 3.9 %collective-permute-start.2 = (bf16[32,96,10,1]{1,0,3,2:T(8,128)(2,1)S(1)}, bf16[32,96,10,1]{1,0,3,2:T(8,128)(2,1)S(1)}, u32[]{:S(2)}, u32[]{:S(2)}) collective-permute-start(bf16[32,96,10,1]{1,0,3,2:T(8,128)(2,1)S(1)} %get-tuple-element.24), channel_id=1, source_target_pairs={{0,1},{1,2},{2,3},{3,64},{64,65},{65,66},{66,67},{67,128},{128,129... | collective-permute-start | bytes 184328 | tf_op jit(solution)/shard_map/ppermute | solution.py:14
  28.4 2.1 %collective-permute-start.3 = (bf16[32,96,10,1]{1,0,3,2:T(8,128)(2,1)S(1)}, bf16[32,96,10,1]{1,0,3,2:T(8,128)(2,1)S(1)}, u32[]{:S(2)}, u32[]{:S(2)}) collective-permute-start(bf16[32,96,10,1]{1,0,3,2:T(8,128)(2,1)S(1)} %get-tuple-element.25), channel_id=1, source_target_pairs={{1,0},{2,1},{3,2},{64,3},{65,64},{66,65},{67,66},{128,67},{129,128... | collective-permute-start | bytes 184328 | tf_op jit(solution)/shard_map/ppermute | solution.py:15
  30.5 1.3 %copy.42 = bf16[16,192,128]{2,1,0:T(8,128)(2,1)} copy(bf16[16,192,128]{1,2,0:T(8,128)(2,1)S(1)} %reshape.39) | data formatting | bytes 1572864 | tf_op jit(solution)/shard_map/optimization_barrier | solution.py:133
  31.7 7.9 %all-to-all-start = ((bf16[16,192,128]{2,1,0:T(8,128)(2,1)}), bf16[16,192,128]{2,1,0:T(8,128)(2,1)S(1)}, u32[]{:S(2)}, u32[]{:S(2)}) async-start(bf16[16,192,128]{2,1,0:T(8,128)(2,1)} %copy.42), calls=%async_computation | async-start | bytes 1572864 | tf_op jit(solution)/shard_map/all_to_all | solution.py:64
  39.7 8.8 %add_convert_fusion.2 = (bf16[32,96,8,16]{1,0,3,2:T(8,128)(2,1)S(1)}, f32[32,96,8,16]{1,0,3,2:T(8,128)S(1)}, f32[32,96,8,16]{1,0,3,2:T(8,128)S(1)}) fusion(bf16[32,96,8,16]{1,3,2,0:T(8,128)(2,1)S(1)} %copy-done.3, bf16[3,3,96,96]{3,2,1,0:T(8,128)(2,1)S(1)} %copy-done, bf16[32,96,10,1]{1,0,3,2:T(8,128)(2,1)S(1)} %collective-permute-done.3, ...), kind=kOutput, calls=%fused_computation.8 | convolution fusion | flops 706928640 | bytes 5990400 | tf_op jit(solution)/shard_map/conv_general_dilated | solution.py:26
  48.5 3.1 %add_convert_fusion.1 = (bf16[32,96,8,16]{1,0,3,2:T(8,128)(2,1)}, f32[32,96,8,16]{1,0,3,2:T(8,128)S(1)}) fusion(bf16[32,96,8,16]{1,0,3,2:T(8,128)(2,1)S(1)} %get-tuple-element.20, f32[96]{0:T(128)S(1)} %get-tuple-element.33, f32[96]{0:T(128)S(1)} %get-tuple-element.34, f32[96]{0:T(128)S(1)} %get-tuple-element.31, f32[96]{0:T(128)S(1)} %get-tuple-element.32, ...), kind=kLoop, calls=%fused_computation.7 | loop fusion | flops 9830400 | bytes 6293376 | tf_op jit(solution)/shard_map/convert_element_type | solution.py:138
  51.6 3.8 %all-to-all-done = bf16[16,192,128]{2,1,0:T(8,128)(2,1)S(1)} async-done(((bf16[16,192,128]{2,1,0:T(8,128)(2,1)}), bf16[16,192,128]{2,1,0:T(8,128)(2,1)S(1)}, u32[]{:S(2)}, u32[]{:S(2)}) %all-to-all-start) | async-done | bytes 786464 | tf_op jit(solution)/shard_map/all_to_all | solution.py:64
  55.4 1.7 %copy.43 = bf16[16,192,128]{1,0,2:T(8,128)(2,1)} copy(bf16[16,192,128]{2,1,0:T(8,128)(2,1)S(1)} %all-to-all-done) | data formatting | bytes 1572864 | tf_op jit(solution)/shard_map/all_to_all | solution.py:64
  57.0 1.6 %reshape.40 = bf16[32,96,8,16]{1,0,3,2:T(8,128)(2,1)S(1)} reshape(bf16[16,192,128]{1,0,2:T(8,128)(2,1)} %copy.43) | data formatting | bytes 1572864 | tf_op jit(solution)/shard_map/reshape | solution.py:65
  58.7 2.4 %reshape_reshape.3 = bf16[16,192,128]{1,0,2:T(8,128)(2,1)} reshape(bf16[32,96,8,16]{1,0,3,2:T(8,128)(2,1)} %get-tuple-element.9) | data formatting | bytes 1572864 | tf_op jit(solution)/shard_map/reshape;reshape | solution.py:42
  61.1 2.6 %copy.45 = bf16[16,192,128]{2,1,0:T(8,128)(2,1)} copy(bf16[16,192,128]{1,0,2:T(8,128)(2,1)} %reshape_reshape.3) | data formatting | bytes 1572864 | tf_op jit(solution)/shard_map/reshape;reshape | solution.py:42
  63.7 8.5 %all-to-all-start.1 = ((bf16[16,192,128]{2,1,0:T(8,128)(2,1)}), bf16[16,192,128]{2,1,0:T(8,128)(2,1)}, u32[]{:S(2)}, u32[]{:S(2)}) async-start(bf16[16,192,128]{2,1,0:T(8,128)(2,1)} %copy.45), calls=%async_computation.1 | async-start | bytes 1572864 | tf_op jit(solution)/shard_map/all_to_all | solution.py:49
  72.2 1.8 %fusion = (bf16[32,96,8,16]{1,0,3,2:T(8,128)(2,1)S(1)}, bf16[32,96,8,16]{1,0,3,2:T(8,128)(2,1)S(1)}) fusion(f32[32,96,8,16]{1,0,3,2:T(8,128)S(1)} %get-tuple-element.11, f32[96]{0:T(128)S(1)} %get-tuple-element.30, f32[96]{0:T(128)S(1)} %get-tuple-element.32, bf16[32,96,8,16]{1,0,3,2:T(8,128)(2,1)S(1)} %reshape.40, f32[96]{0:T(128)S(1)} %get-tuple-element.31, ...), kind=kLoop, calls=%fused_computation.3 | loop fusion | flops 7077888 | bytes 3934080 | tf_op jit(solution)/shard_map/convert_element_type | solution.py:155
  74.0 1.9 %collective-permute-start.4 = (bf16[32,96,1,16]{1,0,3,2:T(8,128)(2,1)S(1)}, bf16[32,96,1,16]{1,0,3,2:T(8,128)(2,1)S(1)}, u32[]{:S(2)}, u32[]{:S(2)}) collective-permute-start(bf16[32,96,1,16]{1,0,3,2:T(8,128)(2,1)S(1)} %get-tuple-element.26), channel_id=1, source_target_pairs={{0,4},{4,8},{8,12},{12,16},{16,20},{20,24},{24,28},{28,32},{32,36}... | collective-permute-start | bytes 294920 | tf_op jit(solution)/shard_map/ppermute | solution.py:14
  75.9 8.4 %collective-permute-start.5 = (bf16[32,96,1,16]{1,0,3,2:T(8,128)(2,1)S(1)}, bf16[32,96,1,16]{1,0,3,2:T(8,128)(2,1)S(1)}, u32[]{:S(2)}, u32[]{:S(2)}) collective-permute-start(bf16[32,96,1,16]{1,0,3,2:T(8,128)(2,1)S(1)} %get-tuple-element.27), channel_id=1, source_target_pairs={{4,0},{8,4},{12,8},{16,12},{20,16},{24,20},{28,24},{32,28},{36,32}... | collective-permute-start | bytes 294920 | tf_op jit(solution)/shard_map/ppermute | solution.py:15
  84.4 2.6 %collective-permute-done.4 = bf16[32,96,1,16]{1,0,3,2:T(8,128)(2,1)S(1)} collective-permute-done((bf16[32,96,1,16]{1,0,3,2:T(8,128)(2,1)S(1)}, bf16[32,96,1,16]{1,0,3,2:T(8,128)(2,1)S(1)}, u32[]{:S(2)}, u32[]{:S(2)}) %collective-permute-start.4) | collective-permute-done | bytes 98336 | tf_op jit(solution)/shard_map/ppermute | solution.py:14
  87.2 5.6 %collective-permute-start.6 = (bf16[32,96,10,1]{1,0,3,2:T(8,128)(2,1)S(1)}, bf16[32,96,10,1]{1,0,3,2:T(8,128)(2,1)S(1)}, u32[]{:S(2)}, u32[]{:S(2)}) collective-permute-start(bf16[32,96,10,1]{1,0,3,2:T(8,128)(2,1)S(1)} %get-tuple-element.22), channel_id=1, source_target_pairs={{0,1},{1,2},{2,3},{3,64},{64,65},{65,66},{66,67},{67,128},{128,129... | collective-permute-start | bytes 184328 | tf_op jit(solution)/shard_map/ppermute | solution.py:14
  92.8 2.1 %collective-permute-start.7 = (bf16[32,96,10,1]{1,0,3,2:T(8,128)(2,1)S(1)}, bf16[32,96,10,1]{1,0,3,2:T(8,128)(2,1)S(1)}, u32[]{:S(2)}, u32[]{:S(2)}) collective-permute-start(bf16[32,96,10,1]{1,0,3,2:T(8,128)(2,1)S(1)} %get-tuple-element.23), channel_id=1, source_target_pairs={{1,0},{2,1},{3,2},{64,3},{65,64},{66,65},{67,66},{128,67},{129,128... | collective-permute-start | bytes 184328 | tf_op jit(solution)/shard_map/ppermute | solution.py:15
  95.2 6.2 %collective-permute-done.7 = bf16[32,96,10,1]{1,0,3,2:T(8,128)(2,1)S(1)} collective-permute-done((bf16[32,96,10,1]{1,0,3,2:T(8,128)(2,1)S(1)}, bf16[32,96,10,1]{1,0,3,2:T(8,128)(2,1)S(1)}, u32[]{:S(2)}, u32[]{:S(2)}) %collective-permute-start.7) | collective-permute-done | bytes 61472 | tf_op jit(solution)/shard_map/ppermute | solution.py:15
  101.4 2.6 %fusion.1 = bf16[32,96,8,16]{1,0,3,2:T(8,128)(2,1)S(1)} fusion(bf16[32,96,8,16]{1,0,3,2:T(8,128)(2,1)S(1)} %get-tuple-element.19, bf16[3,3,96,96]{3,2,1,0:T(8,128)(2,1)S(1)} %copy-done, bf16[32,96,10,1]{1,0,3,2:T(8,128)(2,1)S(1)} %collective-permute-done.7, bf16[32,96,1,16]{1,0,3,2:T(8,128)(2,1)S(1)} %collective-permute-done.5, ...), kind=kOutput, calls=%fused_computation.4 | convolution fusion | flops 682868736 | bytes 2844672 | tf_op jit(solution)/shard_map/conv_general_dilated | solution.py:26
  104.0 1.4 %copy.51 = bf16[32,96,8,16]{1,3,2,0:T(8,128)(2,1)} copy(bf16[32,96,8,16]{1,0,3,2:T(8,128)(2,1)S(1)} %fusion.1) | data formatting | bytes 1572864
  105.4 1.4 %copy.46 = bf16[16,192,128]{1,2,0:T(8,128)(2,1)S(1)} copy(bf16[16,192,128]{2,1,0:T(8,128)(2,1)} %all-to-all-done.1) | data formatting | bytes 1572864 | tf_op jit(solution)/shard_map/all_to_all | solution.py:49
  106.9 0.6 reshape.41
  107.7 0.4 fusion.25
  108.2 0.5 copy.48
  108.8 0.3 pad_select_fusion
  109.9 0.3 pad_select_fusion.7
  110.2 0.3 select_reduce_fusion
  111.7 0.3 pad_select_fusion.4
  113.1 0.5 fusion.8
  113.6 1.3 %copy.50 = bf16[2,96,8,256]{3,2,1,0:T(8,128)(2,1)} copy(bf16[2,96,8,256]{3,1,2,0:T(8,128)(2,1)S(1)} %fusion.8) | data formatting | bytes 1572864
  (62 shorter events, 6.7 us)
Async XLA Ops:
  0.6 39.1 %copy-start = (bf16[3,3,96,96]{3,2,1,0:T(8,128)(2,1)S(1)}, bf16[3,3,96,96]{3,2,1,0:T(8,128)(2,1)}, u32[]{:S(2)}) copy-start(bf16[3,3,96,96]{3,2,1,0:T(8,128)(2,1)} %param.10) | copy-start | bytes 497668
  0.6 13.1 %copy-start.9 = (s32[28]{0:T(128)S(1)}, s32[28]{0:T(128)}, u32[]{:S(2)}) copy-start(s32[28]{0:T(128)} %param.16) | copy-start | bytes 340
  0.7 13.1 %copy-start.7 = (s32[2,8,256]{2,1,0:T(8,128)S(1)}, s32[2,8,256]{2,1,0:T(8,128)}, u32[]{:S(2)}) copy-start(s32[2,8,256]{2,1,0:T(8,128)} %param.15) | copy-start | bytes 49156
  0.7 13.2 %copy-start.1 = (bf16[2,96,8,256]{3,2,1,0:T(8,128)(2,1)S(1)}, bf16[2,96,8,256]{3,2,1,0:T(8,128)(2,1)}, u32[]{:S(2)}) copy-start(bf16[2,96,8,256]{3,2,1,0:T(8,128)(2,1)} %param.17) | copy-start | bytes 2359300
  0.7 13.2 %copy-start.5 = (bf16[28,96]{1,0:T(8,128)(2,1)S(1)}, bf16[28,96]{1,0:T(8,128)(2,1)}, u32[]{:S(2)}) copy-start(bf16[28,96]{1,0:T(8,128)(2,1)} %param.13) | copy-start | bytes 16132
  3.4 18.8 %collective-permute-start = (bf16[32,96,1,16]{1,0,3,2:T(8,128)(2,1)}, bf16[32,96,1,16]{1,0,3,2:T(8,128)(2,1)S(1)}, u32[]{:S(2)}, u32[]{:S(2)}) collective-permute-start(bf16[32,96,1,16]{1,0,3,2:T(8,128)(2,1)} %get-tuple-element.28), channel_id=1, source_target_pairs={{0,4},{4,8},{8,12},{12,16},{16,20},{20,24},{24,28},{28,32},{32,36}... | collective-permute-start | bytes 294920 | tf_op jit(solution)/shard_map/ppermute | solution.py:14
  5.3 16.9 %collective-permute-start.1 = (bf16[32,96,1,16]{1,0,3,2:T(8,128)(2,1)}, bf16[32,96,1,16]{1,0,3,2:T(8,128)(2,1)}, u32[]{:S(2)}, u32[]{:S(2)}) collective-permute-start(bf16[32,96,1,16]{1,0,3,2:T(8,128)(2,1)} %get-tuple-element.29), channel_id=1, source_target_pairs={{4,0},{8,4},{12,8},{16,12},{20,16},{24,20},{28,24},{32,28},{36,32}... | collective-permute-start | bytes 294920 | tf_op jit(solution)/shard_map/ppermute | solution.py:15
  17.9 0.7 copy-start.4
  22.1 8.3 %copy-start.8 = (f32[96,5]{0,1:T(8,128)S(1)}, f32[96,5]{0,1:T(8,128)}, u32[]{:S(2)}) copy-start(f32[96,5]{0,1:T(8,128)} %param.11) | copy-start | bytes 5764
  23.4 1.1 copy-start.2
  24.5 15.3 %copy-start.3 = (bf16[32,96,8,16]{1,3,2,0:T(8,128)(2,1)S(1)}, bf16[32,96,8,16]{1,3,2,0:T(8,128)(2,1)}, u32[]{:S(2)}) copy-start(bf16[32,96,8,16]{1,3,2,0:T(8,128)(2,1)} %param.9) | copy-start | bytes 2359300
  24.5 15.2 %collective-permute-start.2 = (bf16[32,96,10,1]{1,0,3,2:T(8,128)(2,1)S(1)}, bf16[32,96,10,1]{1,0,3,2:T(8,128)(2,1)S(1)}, u32[]{:S(2)}, u32[]{:S(2)}) collective-permute-start(bf16[32,96,10,1]{1,0,3,2:T(8,128)(2,1)S(1)} %get-tuple-element.24), channel_id=1, source_target_pairs={{0,1},{1,2},{2,3},{3,64},{64,65},{65,66},{66,67},{67,128},{128,129... | collective-permute-start | bytes 184328 | tf_op jit(solution)/shard_map/ppermute | solution.py:14
  28.4 11.3 %collective-permute-start.3 = (bf16[32,96,10,1]{1,0,3,2:T(8,128)(2,1)S(1)}, bf16[32,96,10,1]{1,0,3,2:T(8,128)(2,1)S(1)}, u32[]{:S(2)}, u32[]{:S(2)}) collective-permute-start(bf16[32,96,10,1]{1,0,3,2:T(8,128)(2,1)S(1)} %get-tuple-element.25), channel_id=1, source_target_pairs={{1,0},{2,1},{3,2},{64,3},{65,64},{66,65},{67,66},{128,67},{129,128... | collective-permute-start | bytes 184328 | tf_op jit(solution)/shard_map/ppermute | solution.py:15
  31.7 23.6 %all-to-all-start = ((bf16[16,192,128]{2,1,0:T(8,128)(2,1)}), bf16[16,192,128]{2,1,0:T(8,128)(2,1)S(1)}, u32[]{:S(2)}, u32[]{:S(2)}) async-start(bf16[16,192,128]{2,1,0:T(8,128)(2,1)} %copy.42), calls=%async_computation | async-start | bytes 1572864 | tf_op jit(solution)/shard_map/all_to_all | solution.py:64
  63.7 41.7 %all-to-all-start.1 = ((bf16[16,192,128]{2,1,0:T(8,128)(2,1)}), bf16[16,192,128]{2,1,0:T(8,128)(2,1)}, u32[]{:S(2)}, u32[]{:S(2)}) async-start(bf16[16,192,128]{2,1,0:T(8,128)(2,1)} %copy.45), calls=%async_computation.1 | async-start | bytes 1572864 | tf_op jit(solution)/shard_map/all_to_all | solution.py:49
  74.0 13.0 %collective-permute-start.4 = (bf16[32,96,1,16]{1,0,3,2:T(8,128)(2,1)S(1)}, bf16[32,96,1,16]{1,0,3,2:T(8,128)(2,1)S(1)}, u32[]{:S(2)}, u32[]{:S(2)}) collective-permute-start(bf16[32,96,1,16]{1,0,3,2:T(8,128)(2,1)S(1)} %get-tuple-element.26), channel_id=1, source_target_pairs={{0,4},{4,8},{8,12},{12,16},{16,20},{20,24},{24,28},{28,32},{32,36}... | collective-permute-start | bytes 294920 | tf_op jit(solution)/shard_map/ppermute | solution.py:14
  75.9 11.2 %collective-permute-start.5 = (bf16[32,96,1,16]{1,0,3,2:T(8,128)(2,1)S(1)}, bf16[32,96,1,16]{1,0,3,2:T(8,128)(2,1)S(1)}, u32[]{:S(2)}, u32[]{:S(2)}) collective-permute-start(bf16[32,96,1,16]{1,0,3,2:T(8,128)(2,1)S(1)} %get-tuple-element.27), channel_id=1, source_target_pairs={{4,0},{8,4},{12,8},{16,12},{20,16},{24,20},{28,24},{32,28},{36,32}... | collective-permute-start | bytes 294920 | tf_op jit(solution)/shard_map/ppermute | solution.py:15
  87.2 7.9 %collective-permute-start.6 = (bf16[32,96,10,1]{1,0,3,2:T(8,128)(2,1)S(1)}, bf16[32,96,10,1]{1,0,3,2:T(8,128)(2,1)S(1)}, u32[]{:S(2)}, u32[]{:S(2)}) collective-permute-start(bf16[32,96,10,1]{1,0,3,2:T(8,128)(2,1)S(1)} %get-tuple-element.22), channel_id=1, source_target_pairs={{0,1},{1,2},{2,3},{3,64},{64,65},{65,66},{66,67},{67,128},{128,129... | collective-permute-start | bytes 184328 | tf_op jit(solution)/shard_map/ppermute | solution.py:14
  92.8 8.6 %collective-permute-start.7 = (bf16[32,96,10,1]{1,0,3,2:T(8,128)(2,1)S(1)}, bf16[32,96,10,1]{1,0,3,2:T(8,128)(2,1)S(1)}, u32[]{:S(2)}, u32[]{:S(2)}) collective-permute-start(bf16[32,96,10,1]{1,0,3,2:T(8,128)(2,1)S(1)} %get-tuple-element.23), channel_id=1, source_target_pairs={{1,0},{2,1},{3,2},{64,3},{65,64},{66,65},{67,66},{128,67},{129,128... | collective-permute-start | bytes 184328 | tf_op jit(solution)/shard_map/ppermute | solution.py:15
  109.9 0.7 copy-start.6
